TPU v7x, 512 devices: a whole 4x8x8 slice. The times are simulated.
512 devices in a mesh: dp: 64 (over y, z), tx: 2 (over core), ty: 4 (over x).
Axes of the slice: x: 4, y: 8, z: 8, core: 2. Of those that a mesh axis runs over, the one named last changes fastest.
Arguments:
- tokens: bfloat16 [32768, 2048], P('dp', 'tx'), may hold values from -6 to 6
- query_weight: bfloat16 [2048, 4, 512], P(None, 'ty', 'tx'), may hold values from -0.25 to 0.25
- key_value_weight: bfloat16 [2048, 4, 128], P(None, 'ty'), may hold values from -0.125 to 0.125
- output_weight: bfloat16 [4, 512, 2048], P('ty', 'tx'), may hold values from -0.5 to 0.5
- cache: bfloat16 [64, 4, 2048, 128], P('dp', 'ty'), may hold values from -300 to 300
- lengths: int32 [64], replicated, may hold values from 0 to 8192, as said below
- offsets: int32 [64], replicated, may hold values from 0 to 2047
- slots: int32 [64], replicated, may hold values from 0 to 63, each once
Outputs:
- mixed: bfloat16 [32768, 2048], P('dp', ('tx', 'ty'))
- new_cache: bfloat16 [64, 4, 2048, 128], P('dp', 'ty')
Inputs may be any that keep to these rules, and one draw needn't show every extreme that they name: `lengths`: some request has exactly 8192 cached positions. `slots`: every slot belongs to exactly one request.
All inputs are finite; a program needn't handle non-finite values.
Results may differ from a plain program's by a relative error of at most 0.012.
The roundings to bfloat16 on the way count: a program that leaves them out, or rounds other values in their place, can miss the bound.
Values may be sent and summed in bfloat16 or wider, within the bound.
No kernel may reach another device: no remote copies, remote signals or barrier semaphores. Data moves between devices by JAX's collectives and lax.ppermute only.
A program may use at most 64 MiB of HBM per device.

v0:
```python
import math

import jax
import jax.numpy as jnp
from jax import lax
from jax.sharding import PartitionSpec as P

HEAD_SIZE = 64
WINDOW_LENGTH = 2048


EPS = 1e-05


def apply_rotary(values, token_positions):
    width = values.shape[-1]
    half_width = width // 2
    freqs = jnp.exp(jnp.arange(half_width, dtype=jnp.float32) * (-2.0 * math.log(10000.0) / width))
    angles = token_positions.astype(jnp.float32)[:, None] * freqs[None, :]
    cosine = jnp.cos(angles)[:, None, :]
    sine = jnp.sin(angles)[:, None, :]
    leading = values[..., :half_width]
    trailing = values[..., half_width:]
    return jnp.concatenate(
        [leading * cosine - trailing * sine, trailing * cosine + leading * sine], axis=-1
    )


def carry_in(window):
    return lax.all_to_all(window, "dp", split_axis=0, concat_axis=0, tiled=True)


def carry_out(window):
    return lax.all_to_all(window, "dp", split_axis=0, concat_axis=0, tiled=True)


def reorder(window, order, groups):
    columns = window.shape[1]
    blocks = window.reshape(groups, window.shape[0] // groups, columns)
    return jnp.take(blocks, order, axis=0).reshape(window.shape[0], columns)


def per_device(
    tokens, query_weight, key_value_weight, output_weight, cache, lengths, offsets, slots
):
    request = lax.axis_index("dp")
    groups = lax.axis_size("dp")
    whole = lax.all_gather(tokens, "tx", axis=1, tiled=True)
    rows_new = whole.shape[0]
    width = whole.shape[1]
    floats = whole.astype(jnp.float32)
    normalized_input = (
        floats * lax.rsqrt(jnp.mean(floats * floats, axis=1, keepdims=True) + EPS)
    ).astype(jnp.bfloat16)
    owners = jnp.arange(slots.shape[0], dtype=jnp.int32)
    inverse = jnp.sum(jnp.where(slots[None, :] == owners[:, None], owners[None, :], 0), axis=1)
    spread_in = carry_in(cache[0, 0])
    window = carry_in(reorder(spread_in, slots, groups))
    query_cols = query_weight.shape[2]
    heads = query_cols // HEAD_SIZE
    queries = jnp.dot(
        normalized_input,
        query_weight.reshape(width, query_cols),
        preferred_element_type=jnp.float32,
    )
    rotation_pairs = jnp.dot(
        normalized_input,
        key_value_weight.reshape(width, 2 * HEAD_SIZE),
        preferred_element_type=jnp.float32,
    )
    length = lengths[request]
    offset = offsets[request]
    token_positions = length + jnp.arange(rows_new, dtype=jnp.int32)
    query_rotated = apply_rotary(
        queries.reshape(rows_new, heads, HEAD_SIZE), token_positions
    ).astype(jnp.bfloat16)
    new_keys = apply_rotary(rotation_pairs[:, None, :HEAD_SIZE], token_positions)[:, 0].astype(
        jnp.bfloat16
    )
    new_values = rotation_pairs[:, HEAD_SIZE:].astype(jnp.bfloat16)
    factor = 1.0 / math.sqrt(HEAD_SIZE)
    rows = jnp.arange(rows_new, dtype=jnp.int32)
    new_mask = rows[None, :] <= rows[:, None]
    cycle = jnp.arange(WINDOW_LENGTH, dtype=jnp.int32)
    held = length - 1 - jnp.mod(offset - 1 - cycle, WINDOW_LENGTH)
    cache_mask = (held[None, :] >= 0) & (held[None, :] > token_positions[:, None] - WINDOW_LENGTH)
    mask_all = jnp.concatenate([cache_mask, new_mask], axis=1)
    keys_all = jnp.concatenate([window[:, :HEAD_SIZE], new_keys], axis=0)
    values_all = jnp.concatenate([window[:, HEAD_SIZE:], new_values], axis=0)

    def one_head(query_rows):
        scores = (
            jnp.einsum("qd,kd->qk", query_rows, keys_all, preferred_element_type=jnp.float32)
            * factor
        )
        scores = jnp.where(mask_all, scores, -jnp.inf)
        top = jnp.max(scores, axis=1, keepdims=True)
        powers = jnp.exp(scores - top)
        total = jnp.sum(powers, axis=1, keepdims=True)
        weights = powers.astype(jnp.bfloat16)
        summed = jnp.dot(weights, values_all, preferred_element_type=jnp.float32)
        return (summed / total).astype(jnp.bfloat16)

    outputs = lax.map(one_head, jnp.transpose(query_rotated, (1, 0, 2)))
    attended = jnp.transpose(outputs, (1, 0, 2)).reshape(rows_new, heads * HEAD_SIZE)
    rolled = jnp.roll(window, -offset, axis=0)
    entry = jnp.concatenate([new_keys, new_values], axis=1)
    updated = jnp.roll(jnp.concatenate([entry, rolled[rows_new:]], axis=0), offset, axis=0)
    spread_out = carry_out(updated)
    returned = carry_out(reorder(spread_out, inverse, groups))
    new_cache = returned[None, None]
    out_rows = output_weight.reshape(output_weight.shape[1], width)
    partial_value = jnp.dot(attended, out_rows, preferred_element_type=jnp.float32)
    summed_out = lax.psum_scatter(partial_value, ("tx", "ty"), scatter_dimension=1, tiled=True)
    mixed = summed_out.astype(jnp.bfloat16)
    return (mixed, new_cache)


def solution(mesh):
    return jax.shard_map(
        per_device,
        mesh=mesh,
        in_specs=(
            P("dp", "tx"),
            P(None, "ty", "tx"),
            P(None, "ty", None),
            P("ty", "tx", None),
            P("dp", "ty", None, None),
            P(),
            P(),
            P(),
        ),
        out_specs=(P("dp", ("tx", "ty")), P("dp", "ty", None, None)),
        check_vma=False,
    )
```

profile of v0, /device:TPU:6, one launch (start us, length us, event | category | flops | bytes accessed | tf_op | source)
XLA Modules:
  0.0 170.9 jit_solution(11235077658752642387)
XLA Ops:
  7.9 16.6 %all-to-all-start = ((bf16[64,32,128]{2,1,0:T(8,128)(2,1)}), bf16[64,32,128]{2,1,0:T(8,128)(2,1)S(1)}, u32[]{:S(2)}, u32[]{:S(2)}) async-start(bf16[64,32,128]{2,1,0:T(8,128)(2,1)} %bitcast.56), calls=%async_computation | async-start | bytes 1048576 | tf_op jit(solution)/shard_map/all_to_all | solution.py:30
  30.5 2.3 %copy.20 = bf16[2048,1,256]{0,2,1:T(8,128)(2,1)} copy(bf16[2048,1,256]{2,0,1:T(8,128)(2,1)} %param.15) | data formatting | bytes 2097152 | tf_op args[1]
  32.8 11.0 %all-to-all-done = bf16[64,32,128]{2,1,0:T(8,128)(2,1)S(1)} async-done(((bf16[64,32,128]{2,1,0:T(8,128)(2,1)}), bf16[64,32,128]{2,1,0:T(8,128)(2,1)S(1)}, u32[]{:S(2)}, u32[]{:S(2)}) %all-to-all-start) | async-done | bytes 524320 | tf_op jit(solution)/shard_map/all_to_all | solution.py:30
  45.4 5.3 %all-to-all-start.1 = ((bf16[64,32,128]{2,1,0:T(8,128)(2,1)}), bf16[64,32,128]{2,1,0:T(8,128)(2,1)S(1)}, u32[]{:S(2)}, u32[]{:S(2)}) async-start(bf16[64,32,128]{2,1,0:T(8,128)(2,1)} %broadcast_select_fusion.1), calls=%async_computation.1 | async-start | bytes 1048576 | tf_op jit(solution)/shard_map/all_to_all | solution.py:30
  52.0 17.6 %all-to-all-done.1 = bf16[64,32,128]{2,1,0:T(8,128)(2,1)S(1)} async-done(((bf16[64,32,128]{2,1,0:T(8,128)(2,1)}), bf16[64,32,128]{2,1,0:T(8,128)(2,1)S(1)}, u32[]{:S(2)}, u32[]{:S(2)}) %all-to-all-start.1) | async-done | bytes 524320 | tf_op jit(solution)/shard_map/all_to_all | solution.py:30
  70.7 2.1 %fusion.20 = f32[512]{0:T(512)S(1)} fusion(bf16[512,2048]{1,0:T(8,128)(2,1)} %all-gather.2.cloned.1.call-done), kind=kLoop, calls=%fused_computation.18 | loop fusion | flops 3145216 | bytes 2099200 | tf_op jit(solution)/shard_map/reduce_sum | solution.py:53
  72.7 2.6 %fusion.26 = f32[512,128]{0,1:T(8,128)S(1)} fusion(bf16[512,2048]{1,0:T(8,128)(2,1)} %all-gather.2.cloned.1.call-done, f32[512]{0:T(512)S(1)} %add_rsqrt_fusion, bf16[2048,1,128]{2,0,1:T(8,128)(2,1)} %param.16), kind=kOutput, calls=%fused_computation.32 | convolution fusion | flops 271581184 | bytes 2885632 | tf_op jit(solution)/shard_map/dot_general | solution.py:66
  77.3 2.7 %fusion.22 = f32[512,4,64]{0,2,1:T(8,128)S(1)} fusion(bf16[4,64,2048]{2,1,0:T(8,128)(2,1)} %bitcast.54, bf16[512,2048]{1,0:T(8,128)(2,1)} %all-gather.2.cloned.1.call-done, f32[512]{0:T(512)S(1)} %add_rsqrt_fusion), kind=kOutput, calls=%fused_computation.21 | convolution fusion | flops 540016640 | bytes 3672064 | tf_op jit(solution)/shard_map/dot_general | solution.py:61
  80.8 2.3 %pad_maximum_fusion = (bf16[2560,64]{1,0:T(8,128)(2,1)S(1)}, bf16[2560,64]{1,0:T(8,128)(2,1)}) fusion(bf16[512,64]{1,0:T(8,128)(2,1)S(1)} %copy-done.6, bf16[2048,64]{1,0:T(8,128)(2,1)} %get-tuple-element.72, bf16[512,64]{1,0:T(8,128)(2,1)S(1)} %copy-done.7, bf16[2048,64]{1,0:T(8,128)(2,1)} %get-tuple-element.71), kind=kLoop, calls=%fused_computation.33 | loop fusion | flops 1310720 | bytes 1310720 | tf_op jit(solution)/shard_map/concatenate | solution.py:88
  83.1 18.8 %while.10 = (s32[]{:T(128)}, bf16[4,512,64]{1,2,0:T(8,128)(2,1)}, bf16[4,512,64]{1,2,0:T(8,128)(2,1)}, bf16[2560,64]{1,0:T(8,128)(2,1)S(1)}, pred[512,2560]{1,0:...) while((s32[]{:T(128)}, bf16[4,512,64]{1,2,0:T(8,128)(2,1)}, bf16[4,512,64]{1,2,0:T(8,128)(2,1)}, ...), condition=%wide.region_4.6_spmd, body=%wide.region_1.5_spmd.sunk | while | flops 344783872 | bytes 19146872 | solution.py:104
  83.1 2.0 %fusion.64 = (f32[512]{0:T(512)S(1)}, f32[512,2560]{1,0:T(8,128)S(1)}) fusion(pred[512,2560]{1,0:T(32,128)(4,1)S(1)} %get-tuple-element.138, bf16[2560,64]{1,0:T(8,128)(2,1)S(1)} %get-tuple-element.137, bf16[4,512,64]{1,2,0:T(8,128)(2,1)} %get-tuple-element.136, s32[]{:T(128)S(6)} %copy.29), kind=kOutput, calls=%fused_computation.83.clone.1 | convolution fusion | flops 171703808 | bytes 6948868 | tf_op jit(solution)/shard_map/while/body/eval_jaxpr/qd,kd->qk/dot_general | solution.py:93
  86.2 1.6 fusion.66
  87.8 2.0 %fusion.64 = (f32[512]{0:T(512)S(1)}, f32[512,2560]{1,0:T(8,128)S(1)}) fusion(pred[512,2560]{1,0:T(32,128)(4,1)S(1)} %get-tuple-element.138, bf16[2560,64]{1,0:T(8,128)(2,1)S(1)} %get-tuple-element.137, bf16[4,512,64]{1,2,0:T(8,128)(2,1)} %get-tuple-element.136, s32[]{:T(128)S(6)} %copy.29), kind=kOutput, calls=%fused_computation.83.clone.1 | convolution fusion | flops 171703808 | bytes 6948868 | tf_op jit(solution)/shard_map/while/body/eval_jaxpr/qd,kd->qk/dot_general | solution.py:93
  90.9 1.6 fusion.66
  92.5 2.0 %fusion.64 = (f32[512]{0:T(512)S(1)}, f32[512,2560]{1,0:T(8,128)S(1)}) fusion(pred[512,2560]{1,0:T(32,128)(4,1)S(1)} %get-tuple-element.138, bf16[2560,64]{1,0:T(8,128)(2,1)S(1)} %get-tuple-element.137, bf16[4,512,64]{1,2,0:T(8,128)(2,1)} %get-tuple-element.136, s32[]{:T(128)S(6)} %copy.29), kind=kOutput, calls=%fused_computation.83.clone.1 | convolution fusion | flops 171703808 | bytes 6948868 | tf_op jit(solution)/shard_map/while/body/eval_jaxpr/qd,kd->qk/dot_general | solution.py:93
  95.6 1.6 fusion.66
  97.2 2.0 %fusion.64 = (f32[512]{0:T(512)S(1)}, f32[512,2560]{1,0:T(8,128)S(1)}) fusion(pred[512,2560]{1,0:T(32,128)(4,1)S(1)} %get-tuple-element.138, bf16[2560,64]{1,0:T(8,128)(2,1)S(1)} %get-tuple-element.137, bf16[4,512,64]{1,2,0:T(8,128)(2,1)} %get-tuple-element.136, s32[]{:T(128)S(6)} %copy.29), kind=kOutput, calls=%fused_computation.83.clone.1 | convolution fusion | flops 171703808 | bytes 6948868 | tf_op jit(solution)/shard_map/while/body/eval_jaxpr/qd,kd->qk/dot_general | solution.py:93
  100.2 1.6 fusion.66
  101.9 3.6 %fusion.24 = f32[512,2048]{1,0:T(8,128)} fusion(bf16[512,256]{0,1:T(8,128)(2,1)} %bitcast.55, bf16[1,256,2048]{2,1,0:T(8,128)(2,1)S(1)} %copy-done), kind=kOutput, calls=%fused_computation.29 | convolution fusion | flops 536870912 | bytes 5505024 | tf_op jit(solution)/shard_map/dot_general | solution.py:113
  109.8 4.1 %fusion.30 = bf16[2048,128]{1,0:T(8,128)(2,1)} fusion(s32[]{:T(128)S(6)} %select_n.54, bf16[512,128]{1,0:T(8,128)(2,1)S(1)} %copy.24, bf16[1536,128]{1,0:T(8,128)(2,1)S(1)} %fusion.33), kind=kLoop, calls=%fused_computation.36 | loop fusion | flops 2097152 | bytes 1048580 | tf_op jit(solution)/shard_map/jit(_roll_dynamic)/concatenate | solution.py:108
  113.9 5.4 %all-to-all-start.2 = ((bf16[64,32,128]{2,1,0:T(8,128)(2,1)}), bf16[64,32,128]{2,1,0:T(8,128)(2,1)S(1)}, u32[]{:S(2)}, u32[]{:S(2)}) async-start(bf16[64,32,128]{2,1,0:T(8,128)(2,1)} %bitcast.17), calls=%async_computation.3 | async-start | bytes 1048576 | tf_op jit(solution)/shard_map/all_to_all | solution.py:34
  119.5 18.4 %all-to-all-done.2 = bf16[64,32,128]{2,1,0:T(8,128)(2,1)S(1)} async-done(((bf16[64,32,128]{2,1,0:T(8,128)(2,1)}), bf16[64,32,128]{2,1,0:T(8,128)(2,1)S(1)}, u32[]{:S(2)}, u32[]{:S(2)}) %all-to-all-start.2) | async-done | bytes 524320 | tf_op jit(solution)/shard_map/all_to_all | solution.py:34
  138.6 22.9 %all_to_all.33 = bf16[64,32,128]{2,1,0:T(8,128)(2,1)S(1)} all-to-all(bf16[64,32,128]{2,1,0:T(8,128)(2,1)S(1)} %broadcast_select_fusion), channel_id=1, replica_groups=mesh['dp'=64,'tx'=2,'ty'=4] {'dp'}, dimensions={0} | all-to-all | bytes 1048576 | tf_op jit(solution)/shard_map/all_to_all | solution.py:34
  161.5 1.8 %convert_element_type.33 = bf16[512,256]{1,0:T(8,128)(2,1)} convert(f32[512,256]{1,0:T(8,128)} %reduce-scatter.2.cloned.1.call-done) | non-fusion elementwise | flops 131072 | bytes 786432 | tf_op jit(solution)/shard_map/convert_element_type | solution.py:115
  (71 shorter events, 19.7 us)
Async XLA Ops:
  7.2 94.7 %copy-start = (bf16[1,256,2048]{2,1,0:T(8,128)(2,1)S(1)}, bf16[1,256,2048]{2,1,0:T(8,128)(2,1)}, u32[]{:S(2)}) copy-start(bf16[1,256,2048]{2,1,0:T(8,128)(2,1)} %param.17) | copy-start | bytes 3145732
  7.2 25.6 %copy-start.8 = (s32[64]{0:T(128)S(1)}, s32[64]{0:T(128)}, u32[]{:S(2)}) copy-start(s32[64]{0:T(128)} %param.21) | copy-start | bytes 772
  7.2 63.5 %all-gather.2.cloned.1.call-start = ((), (), s32[]{:S(2)}) async-start(), calls=%async_computation.5 | async-start | bytes 3145728 | tf_op jit(solution)/shard_map/all_gather | solution.py:48
  7.9 35.9 %all-to-all-start = ((bf16[64,32,128]{2,1,0:T(8,128)(2,1)}), bf16[64,32,128]{2,1,0:T(8,128)(2,1)S(1)}, u32[]{:S(2)}, u32[]{:S(2)}) async-start(bf16[64,32,128]{2,1,0:T(8,128)(2,1)} %bitcast.56), calls=%async_computation | async-start | bytes 1048576 | tf_op jit(solution)/shard_map/all_to_all | solution.py:30
  45.4 24.1 %all-to-all-start.1 = ((bf16[64,32,128]{2,1,0:T(8,128)(2,1)}), bf16[64,32,128]{2,1,0:T(8,128)(2,1)S(1)}, u32[]{:S(2)}, u32[]{:S(2)}) async-start(bf16[64,32,128]{2,1,0:T(8,128)(2,1)} %broadcast_select_fusion.1), calls=%async_computation.1 | async-start | bytes 1048576 | tf_op jit(solution)/shard_map/all_to_all | solution.py:30
  50.7 110.8 %reduce-scatter.2.cloned.1.call-start = ((), (), s32[]{:S(2)}) async-start(), calls=%async_computation.6 | async-start | bytes 4718592 | tf_op jit(solution)/shard_map/reduce_scatter | solution.py:114
  75.4 5.4 %copy-start.2 = (bf16[512,64]{0,1:T(8,128)(2,1)}, bf16[512,64]{0,1:T(8,128)(2,1)S(1)}, u32[]{:S(2)}) copy-start(bf16[512,64]{0,1:T(8,128)(2,1)S(1)} %slice.59) | copy-start | bytes 196612
  75.7 5.1 %copy-start.4 = (bf16[512,64]{0,1:T(8,128)(2,1)}, bf16[512,64]{0,1:T(8,128)(2,1)S(1)}, u32[]{:S(2)}) copy-start(bf16[512,64]{0,1:T(8,128)(2,1)S(1)} %maximum_bitcast_fusion.1) | copy-start | bytes 196612
  77.2 3.5 %copy-start.6 = (bf16[512,64]{1,0:T(8,128)(2,1)S(1)}, bf16[512,64]{1,0:T(8,128)(2,1)}, u32[]{:S(2)}) copy-start(bf16[512,64]{1,0:T(8,128)(2,1)} %copy.21) | copy-start | bytes 196612
  77.2 3.5 %copy-start.7 = (bf16[512,64]{1,0:T(8,128)(2,1)S(1)}, bf16[512,64]{1,0:T(8,128)(2,1)}, u32[]{:S(2)}) copy-start(bf16[512,64]{1,0:T(8,128)(2,1)} %copy.22) | copy-start | bytes 196612
  85.1 1.1 copy-start.1
  89.8 1.1 copy-start.1
  94.5 1.1 copy-start.1
  99.2 1.1 copy-start.1
  105.5 4.1 %copy-start.3 = (bf16[512,64]{0,1:T(8,128)(2,1)S(1)}, bf16[512,64]{0,1:T(8,128)(2,1)}, u32[]{:S(2)}) copy-start(bf16[512,64]{0,1:T(8,128)(2,1)} %copy-done.2) | copy-start | bytes 196612
  105.5 4.1 %copy-start.5 = (bf16[512,64]{0,1:T(8,128)(2,1)S(1)}, bf16[512,64]{0,1:T(8,128)(2,1)}, u32[]{:S(2)}) copy-start(bf16[512,64]{0,1:T(8,128)(2,1)} %copy-done.4) | copy-start | bytes 196612
  113.9 23.9 %all-to-all-start.2 = ((bf16[64,32,128]{2,1,0:T(8,128)(2,1)}), bf16[64,32,128]{2,1,0:T(8,128)(2,1)S(1)}, u32[]{:S(2)}, u32[]{:S(2)}) async-start(bf16[64,32,128]{2,1,0:T(8,128)(2,1)} %bitcast.17), calls=%async_computation.3 | async-start | bytes 1048576 | tf_op jit(solution)/shard_map/all_to_all | solution.py:34
Sparse Core Ops, SparseCore 0:
  10.1 23.2 all-gather.1
  105.7 49.0 reduce-scatter.1
where the time goes:
time: 172 us; the launch traced here: 171 us
  waiting for transfers between devices  47.6 us (28%)
  starting transfers between devices  27.4 us (16%)
  matrix products  23.3 us (14%)
  blocking collectives  22.9 us (13%)
  other arithmetic  20.7 us (12%)
  between operations  18.2 us (11%)
  local copies, waits for them, and re-layouts  10.8 us (6%)
    all_to_all x2, waiting for transfers between devices, carry_in(): return lax.all_to_all(window, 'dp', split_axis=0, concat_axis=0, tiled=True)  28.5 us
    all_to_all x1, blocking collectives, carry_out(): return lax.all_to_all(window, 'dp', split_axis=0, concat_axis=0, tiled=True)  22.9 us
    all_to_all x2, starting transfers between devices, carry_in(): return lax.all_to_all(window, 'dp', split_axis=0, concat_axis=0, tiled=True)  21.9 us
    all_to_all x1, waiting for transfers between devices, carry_out(): return lax.all_to_all(window, 'dp', split_axis=0, concat_axis=0, tiled=True)  18.4 us
    dot_general x4, matrix products, one_head(): jnp.einsum('qd,kd->qk', query_rows, keys_all, preferred_element_type=jnp....  7.91 us
    dot_general x4, matrix products, one_head(): summed = jnp.dot(weights, values_all, preferred_element_type=jnp.float32)  6.48 us
    all_to_all x1, starting transfers between devices, carry_out(): return lax.all_to_all(window, 'dp', split_axis=0, concat_axis=0, tiled=True)  5.42 us
    concatenate x1, other arithmetic, per_device(): jnp.roll(jnp.concatenate([entry, rolled[rows_new:]], axis=0), offset, axi...  4.14 us
  transfers between devices with their start and end apart: 5, of which 3 were waited for; matrix products, arithmetic and copies ran while one was open for 10% of the time, Pallas kernels for 0%

commit v1 on v0

--- a/solution.py
+++ b/solution.py
@@ -54,8 +54,13 @@
     ).astype(jnp.bfloat16)
     owners = jnp.arange(slots.shape[0], dtype=jnp.int32)
     inverse = jnp.sum(jnp.where(slots[None, :] == owners[:, None], owners[None, :], 0), axis=1)
-    spread_in = carry_in(cache[0, 0])
-    window = carry_in(reorder(spread_in, slots, groups))
+    stored = cache[0, 0]
+    halves = lax.axis_size("tx")
+    half_rows = stored.shape[0] // halves
+    mine = lax.dynamic_slice_in_dim(stored, lax.axis_index("tx") * half_rows, half_rows, axis=0)
+    spread_in = carry_in(mine)
+    window_part = carry_in(reorder(spread_in, slots, groups))
+    window = lax.all_gather(window_part, "tx", axis=0, tiled=True)
     query_cols = query_weight.shape[2]
     heads = query_cols // HEAD_SIZE
     queries = jnp.dot(
@@ -103,12 +108,13 @@
 
     outputs = lax.map(one_head, jnp.transpose(query_rotated, (1, 0, 2)))
     attended = jnp.transpose(outputs, (1, 0, 2)).reshape(rows_new, heads * HEAD_SIZE)
-    rolled = jnp.roll(window, -offset, axis=0)
     entry = jnp.concatenate([new_keys, new_values], axis=1)
-    updated = jnp.roll(jnp.concatenate([entry, rolled[rows_new:]], axis=0), offset, axis=0)
-    spread_out = carry_out(updated)
-    returned = carry_out(reorder(spread_out, inverse, groups))
-    new_cache = returned[None, None]
+    spread_out = carry_out(entry)
+    arrived = carry_out(reorder(spread_out, inverse, groups))
+    own_offset = offsets[inverse[request]]
+    rolled = jnp.roll(stored, -own_offset, axis=0)
+    updated = jnp.roll(jnp.concatenate([arrived, rolled[rows_new:]], axis=0), own_offset, axis=0)
+    new_cache = updated[None, None]
     out_rows = output_weight.reshape(output_weight.shape[1], width)
     partial_value = jnp.dot(attended, out_rows, preferred_element_type=jnp.float32)
     summed_out = lax.psum_scatter(partial_value, ("tx", "ty"), scatter_dimension=1, tiled=True)

time: 172 us -> 165 us (0.959)
  the two profiles are of different devices: /device:TPU:6 before, /device:TPU:1 now
where the time goes in v1:
time: 165 us; the launch traced here: 164 us
  waiting for transfers between devices  41 us (25%)
  starting transfers between devices  37.1 us (22%)
  other arithmetic  24 us (15%)
  matrix products  23.4 us (14%)
  between operations  20 us (12%)
  local copies, waits for them, and re-layouts  12.8 us (8%)
  blocking collectives  5.49 us (3%)
    all_to_all x2, starting transfers between devices, carry_in(): return lax.all_to_all(window, 'dp', split_axis=0, concat_axis=0, tiled=True)  27.6 us
    all_to_all x2, waiting for transfers between devices, carry_out(): return lax.all_to_all(window, 'dp', split_axis=0, concat_axis=0, tiled=True)  19.1 us
    all_to_all x2, waiting for transfers between devices, carry_in(): return lax.all_to_all(window, 'dp', split_axis=0, concat_axis=0, tiled=True)  10.7 us
    reduce_scatter x1, waiting for transfers between devices, per_device(): lax.psum_scatter(partial_value, ('tx', 'ty'), scatter_dimension=1, tiled=...  10.4 us
    all_to_all x2, starting transfers between devices, carry_out(): return lax.all_to_all(window, 'dp', split_axis=0, concat_axis=0, tiled=True)  9.42 us
    dot_general x4, matrix products, one_head(): jnp.einsum('qd,kd->qk', query_rows, keys_all, preferred_element_type=jnp....  7.92 us
    dot_general x4, matrix products, one_head(): summed = jnp.dot(weights, values_all, preferred_element_type=jnp.float32)  6.48 us
    all_gather x1, blocking collectives, per_device(): window = lax.all_gather(window_part, 'tx', axis=0, tiled=True)  5.49 us
  transfers between devices with their start and end apart: 6, of which 5 were waited for; matrix products, arithmetic and copies ran while one was open for 14% of the time, Pallas kernels for 0%

profile of v1, /device:TPU:1, one launch (start us, length us, event | category | flops | bytes accessed | tf_op | source)
XLA Modules:
  0.0 163.7 jit_solution(5020927083020710102)
XLA Ops:
  7.9 1.7 %constant_dynamic-slice_fusion = bf16[1,1,1024,128]{3,2,1,0:T(8,128)(2,1)} fusion(bf16[1,1,2048,128]{3,2,1,0:T(8,128)(2,1)} %param.16, s32[]{:T(128)S(6)} %select_n.76), kind=kLoop, calls=%fused_computation.84 | loop fusion | bytes 524292 | tf_op jit(solution)/shard_map/dynamic_slice | solution.py:60
  9.6 17.1 %all-to-all-start = ((bf16[64,16,128]{2,1,0:T(8,128)(2,1)}), bf16[64,16,128]{2,1,0:T(8,128)(2,1)S(1)}, u32[]{:S(2)}, u32[]{:S(2)}) async-start(bf16[64,16,128]{2,1,0:T(8,128)(2,1)} %bitcast.8), calls=%async_computation | async-start | bytes 524288 | tf_op jit(solution)/shard_map/all_to_all | solution.py:30
  37.4 1.9 %all-to-all-done = bf16[64,16,128]{2,1,0:T(8,128)(2,1)S(1)} async-done(((bf16[64,16,128]{2,1,0:T(8,128)(2,1)}), bf16[64,16,128]{2,1,0:T(8,128)(2,1)S(1)}, u32[]{:S(2)}, u32[]{:S(2)}) %all-to-all-start) | async-done | bytes 262176 | tf_op jit(solution)/shard_map/all_to_all | solution.py:30
  40.8 10.5 %all-to-all-start.1 = ((bf16[64,16,128]{2,1,0:T(8,128)(2,1)}), bf16[64,16,128]{2,1,0:T(8,128)(2,1)}, u32[]{:S(2)}, u32[]{:S(2)}) async-start(bf16[64,16,128]{2,1,0:T(8,128)(2,1)} %broadcast_select_fusion), calls=%async_computation.1 | async-start | bytes 524288 | tf_op jit(solution)/shard_map/all_to_all | solution.py:30
  52.3 2.3 %copy.20 = bf16[2048,1,256]{0,2,1:T(8,128)(2,1)} copy(bf16[2048,1,256]{2,0,1:T(8,128)(2,1)} %param.13) | data formatting | bytes 2097152 | tf_op args[1]
  54.8 8.8 %all-to-all-done.1 = bf16[64,16,128]{2,1,0:T(8,128)(2,1)} async-done(((bf16[64,16,128]{2,1,0:T(8,128)(2,1)}), bf16[64,16,128]{2,1,0:T(8,128)(2,1)}, u32[]{:S(2)}, u32[]{:S(2)}) %all-to-all-start.1) | async-done | bytes 262176 | tf_op jit(solution)/shard_map/all_to_all | solution.py:30
  63.6 5.5 %all_gather.7 = bf16[2048,128]{1,0:T(8,128)(2,1)S(1)} all-gather(bf16[1024,128]{1,0:T(8,128)(2,1)} %bitcast.9), channel_id=1, replica_groups=mesh['dp'=64,'tx'=2,'ty'=4] {'tx'}, dimensions={0}, use_global_device_ids=true | all-gather | bytes 786432 | tf_op jit(solution)/shard_map/all_gather | solution.py:63
  70.0 2.1 %fusion.20 = f32[512]{0:T(512)S(1)} fusion(bf16[512,2048]{1,0:T(8,128)(2,1)} %all-gather.2.cloned.1.call-done), kind=kLoop, calls=%fused_computation.18 | loop fusion | flops 3145216 | bytes 2099200 | tf_op jit(solution)/shard_map/reduce_sum | solution.py:53
  72.1 2.6 %fusion.26 = f32[512,128]{0,1:T(8,128)S(1)} fusion(bf16[512,2048]{1,0:T(8,128)(2,1)} %all-gather.2.cloned.1.call-done, f32[512]{0:T(512)S(1)} %add_rsqrt_fusion, bf16[2048,1,128]{2,0,1:T(8,128)(2,1)} %param.14), kind=kOutput, calls=%fused_computation.32 | convolution fusion | flops 271581184 | bytes 2885632 | tf_op jit(solution)/shard_map/dot_general | solution.py:71
  76.7 2.7 %fusion.22 = f32[512,4,64]{0,2,1:T(8,128)S(1)} fusion(bf16[4,64,2048]{2,1,0:T(8,128)(2,1)} %bitcast.61, bf16[512,2048]{1,0:T(8,128)(2,1)} %all-gather.2.cloned.1.call-done, f32[512]{0:T(512)S(1)} %add_rsqrt_fusion), kind=kOutput, calls=%fused_computation.21 | convolution fusion | flops 540016640 | bytes 3672064 | tf_op jit(solution)/shard_map/dot_general | solution.py:66
  81.1 2.1 %pad_maximum_fusion = (bf16[2560,64]{1,0:T(8,128)(2,1)S(1)}, bf16[2560,64]{1,0:T(8,128)(2,1)}) fusion(bf16[512,64]{1,0:T(8,128)(2,1)S(1)} %copy-done.7, bf16[2048,64]{1,0:T(8,128)(2,1)} %get-tuple-element.71, bf16[512,64]{1,0:T(8,128)(2,1)S(1)} %copy-done.8, bf16[2048,64]{1,0:T(8,128)(2,1)S(1)} %get-tuple-element.70), kind=kLoop, calls=%fused_computation.33 | loop fusion | flops 1310720 | bytes 1310720 | tf_op jit(solution)/shard_map/concatenate | solution.py:93
  83.2 18.8 %while.10 = (s32[]{:T(128)}, bf16[4,512,64]{1,2,0:T(8,128)(2,1)}, bf16[4,512,64]{1,2,0:T(8,128)(2,1)}, bf16[2560,64]{1,0:T(8,128)(2,1)S(1)}, pred[512,2560]{1,0:...) while((s32[]{:T(128)}, bf16[4,512,64]{1,2,0:T(8,128)(2,1)}, bf16[4,512,64]{1,2,0:T(8,128)(2,1)}, ...), condition=%wide.region_4.5_spmd, body=%wide.region_1.4_spmd.sunk | while | flops 344783872 | bytes 19147880 | solution.py:109
  83.2 2.0 %fusion.67 = (f32[512]{0:T(512)S(1)}, f32[512,2560]{1,0:T(8,128)S(1)}) fusion(pred[512,2560]{1,0:T(32,128)(4,1)S(1)} %get-tuple-element.139, bf16[2560,64]{1,0:T(8,128)(2,1)S(1)} %get-tuple-element.138, bf16[4,512,64]{1,2,0:T(8,128)(2,1)} %get-tuple-element.137, s32[]{:T(128)} %get-tuple-element.128), kind=kOutput, calls=%fused_computation.87.clone.1 | convolution fusion | flops 171703808 | bytes 6949376 | tf_op jit(solution)/shard_map/while/body/eval_jaxpr/qd,kd->qk/dot_general | solution.py:98
  87.9 2.0 %fusion.67 = (f32[512]{0:T(512)S(1)}, f32[512,2560]{1,0:T(8,128)S(1)}) fusion(pred[512,2560]{1,0:T(32,128)(4,1)S(1)} %get-tuple-element.139, bf16[2560,64]{1,0:T(8,128)(2,1)S(1)} %get-tuple-element.138, bf16[4,512,64]{1,2,0:T(8,128)(2,1)} %get-tuple-element.137, s32[]{:T(128)} %get-tuple-element.128), kind=kOutput, calls=%fused_computation.87.clone.1 | convolution fusion | flops 171703808 | bytes 6949376 | tf_op jit(solution)/shard_map/while/body/eval_jaxpr/qd,kd->qk/dot_general | solution.py:98
  92.6 2.0 %fusion.67 = (f32[512]{0:T(512)S(1)}, f32[512,2560]{1,0:T(8,128)S(1)}) fusion(pred[512,2560]{1,0:T(32,128)(4,1)S(1)} %get-tuple-element.139, bf16[2560,64]{1,0:T(8,128)(2,1)S(1)} %get-tuple-element.138, bf16[4,512,64]{1,2,0:T(8,128)(2,1)} %get-tuple-element.137, s32[]{:T(128)} %get-tuple-element.128), kind=kOutput, calls=%fused_computation.87.clone.1 | convolution fusion | flops 171703808 | bytes 6949376 | tf_op jit(solution)/shard_map/while/body/eval_jaxpr/qd,kd->qk/dot_general | solution.py:98
  97.3 2.0 %fusion.67 = (f32[512]{0:T(512)S(1)}, f32[512,2560]{1,0:T(8,128)S(1)}) fusion(pred[512,2560]{1,0:T(32,128)(4,1)S(1)} %get-tuple-element.139, bf16[2560,64]{1,0:T(8,128)(2,1)S(1)} %get-tuple-element.138, bf16[4,512,64]{1,2,0:T(8,128)(2,1)} %get-tuple-element.137, s32[]{:T(128)} %get-tuple-element.128), kind=kOutput, calls=%fused_computation.87.clone.1 | convolution fusion | flops 171703808 | bytes 6949376 | tf_op jit(solution)/shard_map/while/body/eval_jaxpr/qd,kd->qk/dot_general | solution.py:98
  102.0 3.7 %fusion.24 = f32[512,2048]{1,0:T(8,128)} fusion(bf16[512,256]{0,1:T(8,128)(2,1)} %bitcast.62, bf16[1,256,2048]{2,1,0:T(8,128)(2,1)S(1)} %copy-done), kind=kOutput, calls=%fused_computation.29 | convolution fusion | flops 536870912 | bytes 5505024 | tf_op jit(solution)/shard_map/dot_general | solution.py:119
  106.5 4.6 %all-to-all-start.2 = ((bf16[64,8,128]{2,1,0:T(8,128)(2,1)}), bf16[64,8,128]{2,1,0:T(8,128)(2,1)S(1)}, u32[]{:S(2)}, u32[]{:S(2)}) async-start(bf16[64,8,128]{2,1,0:T(8,128)(2,1)} %bitcast.17), calls=%async_computation.3 | async-start | bytes 262144 | tf_op jit(solution)/shard_map/all_to_all | solution.py:34
  111.2 11.6 %all-to-all-done.2 = bf16[64,8,128]{2,1,0:T(8,128)(2,1)S(1)} async-done(((bf16[64,8,128]{2,1,0:T(8,128)(2,1)}), bf16[64,8,128]{2,1,0:T(8,128)(2,1)S(1)}, u32[]{:S(2)}, u32[]{:S(2)}) %all-to-all-start.2) | async-done | bytes 131104 | tf_op jit(solution)/shard_map/all_to_all | solution.py:34
  124.2 4.8 %all-to-all-start.3 = ((bf16[64,8,128]{2,1,0:T(8,128)(2,1)}), bf16[64,8,128]{2,1,0:T(8,128)(2,1)S(1)}, u32[]{:S(2)}, u32[]{:S(2)}) async-start(bf16[64,8,128]{2,1,0:T(8,128)(2,1)} %broadcast_select_fusion.1), calls=%async_computation.4 | async-start | bytes 262144 | tf_op jit(solution)/shard_map/all_to_all | solution.py:34
  133.1 7.5 %all-to-all-done.3 = bf16[64,8,128]{2,1,0:T(8,128)(2,1)S(1)} async-done(((bf16[64,8,128]{2,1,0:T(8,128)(2,1)}), bf16[64,8,128]{2,1,0:T(8,128)(2,1)S(1)}, u32[]{:S(2)}, u32[]{:S(2)}) %all-to-all-start.3) | async-done | bytes 131104 | tf_op jit(solution)/shard_map/all_to_all | solution.py:34
  140.6 4.1 %fusion.31 = bf16[1,1,2048,128]{3,2,1,0:T(8,128)(2,1)} fusion(s32[]{:T(128)S(6)} %select_n.89, bf16[512,128]{1,0:T(8,128)(2,1)S(1)} %bitcast.63, bf16[1536,128]{1,0:T(8,128)(2,1)S(1)} %fusion.34), kind=kLoop, calls=%fused_computation.37 | loop fusion | flops 2097152 | bytes 1048580 | tf_op jit(solution)/shard_map/broadcast_in_dim | solution.py:117
  144.7 10.4 %reduce-scatter.2.cloned.1.call-done = f32[512,256]{1,0:T(8,128)} async-done(((f32[512,2048]{1,0:T(8,128)}), f32[512,256]{1,0:T(8,128)}) %reduce-scatter.2.cloned.1.call-update) | async-done | bytes 524304 | tf_op jit(solution)/shard_map/reduce_scatter | solution.py:120
  155.1 1.8 %convert_element_type.33 = bf16[512,256]{1,0:T(8,128)(2,1)} convert(f32[512,256]{1,0:T(8,128)} %reduce-scatter.2.cloned.1.call-done) | non-fusion elementwise | flops 131072 | bytes 786432 | tf_op jit(solution)/shard_map/convert_element_type | solution.py:121
  (74 shorter events, 29.9 us)
Async XLA Ops:
  7.2 94.8 %copy-start = (bf16[1,256,2048]{2,1,0:T(8,128)(2,1)S(1)}, bf16[1,256,2048]{2,1,0:T(8,128)(2,1)}, u32[]{:S(2)}) copy-start(bf16[1,256,2048]{2,1,0:T(8,128)(2,1)} %param.15) | copy-start | bytes 3145732
  7.2 62.9 %all-gather.2.cloned.1.call-start = ((), (), s32[]{:S(2)}) async-start(), calls=%async_computation.5 | async-start | bytes 3145728 | tf_op jit(solution)/shard_map/all_gather | solution.py:48
  9.6 29.7 %all-to-all-start = ((bf16[64,16,128]{2,1,0:T(8,128)(2,1)}), bf16[64,16,128]{2,1,0:T(8,128)(2,1)S(1)}, u32[]{:S(2)}, u32[]{:S(2)}) async-start(bf16[64,16,128]{2,1,0:T(8,128)(2,1)} %bitcast.8), calls=%async_computation | async-start | bytes 524288 | tf_op jit(solution)/shard_map/all_to_all | solution.py:30
  40.8 22.8 %all-to-all-start.1 = ((bf16[64,16,128]{2,1,0:T(8,128)(2,1)}), bf16[64,16,128]{2,1,0:T(8,128)(2,1)}, u32[]{:S(2)}, u32[]{:S(2)}) async-start(bf16[64,16,128]{2,1,0:T(8,128)(2,1)} %broadcast_select_fusion), calls=%async_computation.1 | async-start | bytes 524288 | tf_op jit(solution)/shard_map/all_to_all | solution.py:30
  51.3 103.8 %reduce-scatter.2.cloned.1.call-start = ((), (), s32[]{:S(2)}) async-start(), calls=%async_computation.6 | async-start | bytes 4718592 | tf_op jit(solution)/shard_map/reduce_scatter | solution.py:120
  74.8 6.3 %copy-start.3 = (bf16[512,64]{0,1:T(8,128)(2,1)}, bf16[512,64]{0,1:T(8,128)(2,1)S(1)}, u32[]{:S(2)}) copy-start(bf16[512,64]{0,1:T(8,128)(2,1)S(1)} %slice.59) | copy-start | bytes 196612
  75.1 5.9 %copy-start.5 = (bf16[512,64]{0,1:T(8,128)(2,1)}, bf16[512,64]{0,1:T(8,128)(2,1)S(1)}, u32[]{:S(2)}) copy-start(bf16[512,64]{0,1:T(8,128)(2,1)S(1)} %maximum_bitcast_fusion.1) | copy-start | bytes 196612
  76.6 4.4 %copy-start.7 = (bf16[512,64]{1,0:T(8,128)(2,1)S(1)}, bf16[512,64]{1,0:T(8,128)(2,1)}, u32[]{:S(2)}) copy-start(bf16[512,64]{1,0:T(8,128)(2,1)} %copy.21) | copy-start | bytes 196612
  76.6 4.4 %copy-start.8 = (bf16[512,64]{1,0:T(8,128)(2,1)S(1)}, bf16[512,64]{1,0:T(8,128)(2,1)}, u32[]{:S(2)}) copy-start(bf16[512,64]{1,0:T(8,128)(2,1)} %copy.22) | copy-start | bytes 196612
  85.2 1.1 copy-start.1
  89.9 1.1 copy-start.1
  94.6 1.1 copy-start.1
  99.3 1.1 copy-start.1
  102.0 3.7 %copy-start.4 = (bf16[512,64]{0,1:T(8,128)(2,1)S(1)}, bf16[512,64]{0,1:T(8,128)(2,1)}, u32[]{:S(2)}) copy-start(bf16[512,64]{0,1:T(8,128)(2,1)} %copy-done.3) | copy-start | bytes 196612
  102.0 3.7 %copy-start.6 = (bf16[512,64]{0,1:T(8,128)(2,1)S(1)}, bf16[512,64]{0,1:T(8,128)(2,1)}, u32[]{:S(2)}) copy-start(bf16[512,64]{0,1:T(8,128)(2,1)} %copy-done.5) | copy-start | bytes 196612
  105.7 25.9 %copy-start.2 = (bf16[1,1,2048,128]{3,2,1,0:T(8,128)(2,1)S(1)}, bf16[1,1,2048,128]{3,2,1,0:T(8,128)(2,1)}, u32[]{:S(2)}) copy-start(bf16[1,1,2048,128]{3,2,1,0:T(8,128)(2,1)} %param.16) | copy-start | bytes 1572868
  106.5 16.2 %all-to-all-start.2 = ((bf16[64,8,128]{2,1,0:T(8,128)(2,1)}), bf16[64,8,128]{2,1,0:T(8,128)(2,1)S(1)}, u32[]{:S(2)}, u32[]{:S(2)}) async-start(bf16[64,8,128]{2,1,0:T(8,128)(2,1)} %bitcast.17), calls=%async_computation.3 | async-start | bytes 262144 | tf_op jit(solution)/shard_map/all_to_all | solution.py:34
  124.2 16.4 %all-to-all-start.3 = ((bf16[64,8,128]{2,1,0:T(8,128)(2,1)}), bf16[64,8,128]{2,1,0:T(8,128)(2,1)S(1)}, u32[]{:S(2)}, u32[]{:S(2)}) async-start(bf16[64,8,128]{2,1,0:T(8,128)(2,1)} %broadcast_select_fusion.1), calls=%async_computation.4 | async-start | bytes 262144 | tf_op jit(solution)/shard_map/all_to_all | solution.py:34
Sparse Core Ops, SparseCore 0:
  10.1 25.6 all-gather.1
  105.8 49.2 reduce-scatter.1

commit v2 on v1

--- a/solution.py
+++ b/solution.py
@@ -59,8 +59,6 @@
     half_rows = stored.shape[0] // halves
     mine = lax.dynamic_slice_in_dim(stored, lax.axis_index("tx") * half_rows, half_rows, axis=0)
     spread_in = carry_in(mine)
-    window_part = carry_in(reorder(spread_in, slots, groups))
-    window = lax.all_gather(window_part, "tx", axis=0, tiled=True)
     query_cols = query_weight.shape[2]
     heads = query_cols // HEAD_SIZE
     queries = jnp.dot(
@@ -83,6 +81,20 @@
         jnp.bfloat16
     )
     new_values = rotation_pairs[:, HEAD_SIZE:].astype(jnp.bfloat16)
+    entry = jnp.concatenate([new_keys, new_values], axis=1)
+    window_chunk = half_rows // groups
+    entry_chunk = rows_new // groups
+    payload = jnp.concatenate(
+        [
+            reorder(spread_in, slots, groups).reshape(groups, window_chunk, -1),
+            entry.reshape(groups, entry_chunk, -1),
+        ],
+        axis=1,
+    ).reshape(groups * (window_chunk + entry_chunk), -1)
+    delivered = carry_in(payload).reshape(groups, window_chunk + entry_chunk, -1)
+    window_part = delivered[:, :window_chunk].reshape(half_rows, -1)
+    entry_parts = delivered[:, window_chunk:].reshape(rows_new, -1)
+    window = lax.all_gather(window_part, "tx", axis=0, tiled=True)
     factor = 1.0 / math.sqrt(HEAD_SIZE)
     rows = jnp.arange(rows_new, dtype=jnp.int32)
     new_mask = rows[None, :] <= rows[:, None]
@@ -108,16 +120,15 @@
 
     outputs = lax.map(one_head, jnp.transpose(query_rotated, (1, 0, 2)))
     attended = jnp.transpose(outputs, (1, 0, 2)).reshape(rows_new, heads * HEAD_SIZE)
-    entry = jnp.concatenate([new_keys, new_values], axis=1)
-    spread_out = carry_out(entry)
-    arrived = carry_out(reorder(spread_out, inverse, groups))
+    arrived = carry_out(reorder(entry_parts, inverse, groups))
     own_offset = offsets[inverse[request]]
     rolled = jnp.roll(stored, -own_offset, axis=0)
     updated = jnp.roll(jnp.concatenate([arrived, rolled[rows_new:]], axis=0), own_offset, axis=0)
     new_cache = updated[None, None]
     out_rows = output_weight.reshape(output_weight.shape[1], width)
     partial_value = jnp.dot(attended, out_rows, preferred_element_type=jnp.float32)
-    summed_out = lax.psum_scatter(partial_value, ("tx", "ty"), scatter_dimension=1, tiled=True)
+    across_cores = lax.psum_scatter(partial_value, "tx", scatter_dimension=1, tiled=True)
+    summed_out = lax.psum_scatter(across_cores, "ty", scatter_dimension=1, tiled=True)
     mixed = summed_out.astype(jnp.bfloat16)
     return (mixed, new_cache)
 

time: 165 us -> 163 us (0.988)
  starting transfers between devices: 37.1 us -> 40 us
  local copies, waits for them, and re-layouts: 12.8 us -> 10.7 us
  other arithmetic: 24 us -> 22.3 us
    reduce_scatter x1 -> x2, waiting for transfers between devices: 10.4 us -> 23.2 us  [the longest x1 14.2 us: per_device(): lax.psum_scatter(partial_value, 'tx', scatter_dimension=1, tiled=True)]
    all_to_all x2 -> x1, waiting for transfers between devices: 19.1 us -> 7.24 us  [carry_out(): return lax.all_to_all(window, 'dp', split_axis=0, concat_axis=0, tiled=True)]
    all_to_all x2 -> x1, starting transfers between devices: 9.42 us -> 12.3 us  [carry_out(): return lax.all_to_all(window, 'dp', split_axis=0, concat_axis=0, tiled=True)]
    all_to_all x2, waiting for transfers between devices: 10.7 us -> 8.53 us  [carry_in(): return lax.all_to_all(window, 'dp', split_axis=0, concat_axis=0, tiled=True)]
  transfers between devices with their start and end apart: 6 -> 6, of which waited for: 5 -> 5; matrix products, arithmetic and copies ran while one was open for 14% -> 15% of each run, Pallas kernels for 0% -> 0%
where the time goes in v2:
time: 163 us; the launch traced here: 162 us
  starting transfers between devices  40 us (25%)
  waiting for transfers between devices  39.7 us (24%)
  matrix products  23.2 us (14%)
  other arithmetic  22.3 us (14%)
  between operations  19.8 us (12%)
  local copies, waits for them, and re-layouts  10.7 us (7%)
  blocking collectives  6.03 us (4%)
    all_to_all x2, starting transfers between devices, carry_in(): return lax.all_to_all(window, 'dp', split_axis=0, concat_axis=0, tiled=True)  27.6 us
    reduce_scatter x1, waiting for transfers between devices, per_device(): lax.psum_scatter(partial_value, 'tx', scatter_dimension=1, tiled=True)  14.2 us
    all_to_all x1, starting transfers between devices, carry_out(): return lax.all_to_all(window, 'dp', split_axis=0, concat_axis=0, tiled=True)  12.3 us
    reduce_scatter x1, waiting for transfers between devices, per_device(): lax.psum_scatter(across_cores, 'ty', scatter_dimension=1, tiled=True)  9 us
    all_to_all x2, waiting for transfers between devices, carry_in(): return lax.all_to_all(window, 'dp', split_axis=0, concat_axis=0, tiled=True)  8.53 us
    dot_general x4, matrix products, one_head(): jnp.einsum('qd,kd->qk', query_rows, keys_all, preferred_element_type=jnp....  7.91 us
    all_to_all x1, waiting for transfers between devices, carry_out(): return lax.all_to_all(window, 'dp', split_axis=0, concat_axis=0, tiled=True)  7.24 us
    dot_general x4, matrix products, one_head(): summed = jnp.dot(weights, values_all, preferred_element_type=jnp.float32)  6.47 us
  transfers between devices with their start and end apart: 6, of which 5 were waited for; matrix products, arithmetic and copies ran while one was open for 15% of the time, Pallas kernels for 0%

profile of v2, /device:TPU:1, one launch (start us, length us, event | category | flops | bytes accessed | tf_op | source)
XLA Modules:
  0.0 161.7 jit_solution(17513352402918082125)
XLA Ops:
  7.9 1.7 %constant_dynamic-slice_fusion = bf16[1,1,1024,128]{3,2,1,0:T(8,128)(2,1)} fusion(bf16[1,1,2048,128]{3,2,1,0:T(8,128)(2,1)} %param.16, s32[]{:T(128)S(6)} %select_n.74), kind=kLoop, calls=%fused_computation.85 | loop fusion | bytes 524292 | tf_op jit(solution)/shard_map/dynamic_slice | solution.py:60
  9.6 17.1 %all-to-all-start = ((bf16[64,16,128]{2,1,0:T(8,128)(2,1)}), bf16[64,16,128]{2,1,0:T(8,128)(2,1)S(1)}, u32[]{:S(2)}, u32[]{:S(2)}) async-start(bf16[64,16,128]{2,1,0:T(8,128)(2,1)} %bitcast.8), calls=%async_computation | async-start | bytes 524288 | tf_op jit(solution)/shard_map/all_to_all | solution.py:30
  37.6 1.7 %all-to-all-done = bf16[64,16,128]{2,1,0:T(8,128)(2,1)S(1)} async-done(((bf16[64,16,128]{2,1,0:T(8,128)(2,1)}), bf16[64,16,128]{2,1,0:T(8,128)(2,1)S(1)}, u32[]{:S(2)}, u32[]{:S(2)}) %all-to-all-start) | async-done | bytes 262176 | tf_op jit(solution)/shard_map/all_to_all | solution.py:30
  40.1 2.1 %fusion.20 = f32[512]{0:T(512)S(1)} fusion(bf16[512,2048]{1,0:T(8,128)(2,1)} %all-gather.2.cloned.1.call-done), kind=kLoop, calls=%fused_computation.18 | loop fusion | flops 3145216 | bytes 2099200 | tf_op jit(solution)/shard_map/reduce_sum | solution.py:53
  42.2 2.5 %fusion.26 = f32[512,128]{0,1:T(8,128)S(1)} fusion(bf16[512,2048]{1,0:T(8,128)(2,1)} %all-gather.2.cloned.1.call-done, f32[512]{0:T(512)S(1)} %add_rsqrt_fusion, bf16[2048,1,128]{2,0,1:T(8,128)(2,1)S(1)} %copy-done.3), kind=kOutput, calls=%fused_computation.32 | convolution fusion | flops 271581184 | bytes 2885632 | tf_op jit(solution)/shard_map/dot_general | solution.py:69
  46.0 10.4 %all-to-all-start.1 = ((bf16[64,24,128]{2,1,0:T(8,128)(2,1)}), bf16[64,24,128]{2,1,0:T(8,128)(2,1)S(1)}, u32[]{:S(2)}, u32[]{:S(2)}) async-start(bf16[64,24,128]{2,1,0:T(8,128)(2,1)} %pad_maximum_fusion.2), calls=%async_computation.1 | async-start | bytes 786432 | tf_op jit(solution)/shard_map/all_to_all | solution.py:30
  56.8 2.3 %copy.20 = bf16[2048,1,256]{0,2,1:T(8,128)(2,1)} copy(bf16[2048,1,256]{2,0,1:T(8,128)(2,1)} %param.13) | data formatting | bytes 2097152 | tf_op args[1]
  60.0 2.7 %fusion.22 = f32[512,4,64]{0,2,1:T(8,128)S(1)} fusion(bf16[4,64,2048]{2,1,0:T(8,128)(2,1)} %bitcast.62, bf16[512,2048]{1,0:T(8,128)(2,1)} %all-gather.2.cloned.1.call-done, f32[512]{0:T(512)S(1)} %add_rsqrt_fusion), kind=kOutput, calls=%fused_computation.21 | convolution fusion | flops 540016640 | bytes 3672064 | tf_op jit(solution)/shard_map/dot_general | solution.py:64
  63.5 6.8 %all-to-all-done.1 = bf16[64,24,128]{2,1,0:T(8,128)(2,1)S(1)} async-done(((bf16[64,24,128]{2,1,0:T(8,128)(2,1)}), bf16[64,24,128]{2,1,0:T(8,128)(2,1)S(1)}, u32[]{:S(2)}, u32[]{:S(2)}) %all-to-all-start.1) | async-done | bytes 393248 | tf_op jit(solution)/shard_map/all_to_all | solution.py:30
  70.3 6.0 %all_gather.7 = bf16[2048,128]{1,0:T(8,128)(2,1)S(1)} all-gather(bf16[1024,128]{1,0:T(8,128)(2,1)S(1)} %bitcast.61), channel_id=1, replica_groups=mesh['dp'=64,'tx'=2,'ty'=4] {'tx'}, dimensions={0}, use_global_device_ids=true | all-gather | bytes 786432 | tf_op jit(solution)/shard_map/all_gather | solution.py:97
  76.5 2.0 %pad_maximum_fusion = (bf16[2560,64]{1,0:T(8,128)(2,1)S(1)}, bf16[2560,64]{1,0:T(8,128)(2,1)}) fusion(bf16[512,64]{1,0:T(8,128)(2,1)S(1)} %copy.22, bf16[2048,64]{1,0:T(8,128)(2,1)S(1)} %get-tuple-element.71, bf16[512,64]{1,0:T(8,128)(2,1)} %copy.23, bf16[2048,64]{1,0:T(8,128)(2,1)S(1)} %get-tuple-element.70), kind=kLoop, calls=%fused_computation.33 | loop fusion | flops 1310720 | bytes 1310720 | tf_op jit(solution)/shard_map/concatenate | solution.py:105
  78.5 18.8 %while.10 = (s32[]{:T(128)}, bf16[4,512,64]{1,2,0:T(8,128)(2,1)}, bf16[4,512,64]{1,2,0:T(8,128)(2,1)}, bf16[2560,64]{1,0:T(8,128)(2,1)S(1)}, pred[512,2560]{1,0:...) while((s32[]{:T(128)}, bf16[4,512,64]{1,2,0:T(8,128)(2,1)}, bf16[4,512,64]{1,2,0:T(8,128)(2,1)}, ...), condition=%wide.region_4.5_spmd, body=%wide.region_1.4_spmd.sunk | while | flops 344783872 | bytes 19147880 | solution.py:121
  78.5 2.0 %fusion.67 = (f32[512]{0:T(512)S(1)}, f32[512,2560]{1,0:T(8,128)S(1)}) fusion(pred[512,2560]{1,0:T(32,128)(4,1)S(1)} %get-tuple-element.139, bf16[2560,64]{1,0:T(8,128)(2,1)S(1)} %get-tuple-element.138, bf16[4,512,64]{1,2,0:T(8,128)(2,1)} %get-tuple-element.137, s32[]{:T(128)} %get-tuple-element.128), kind=kOutput, calls=%fused_computation.88.clone.1 | convolution fusion | flops 171703808 | bytes 6949376 | tf_op jit(solution)/shard_map/while/body/eval_jaxpr/qd,kd->qk/dot_general | solution.py:110
  83.2 2.0 %fusion.67 = (f32[512]{0:T(512)S(1)}, f32[512,2560]{1,0:T(8,128)S(1)}) fusion(pred[512,2560]{1,0:T(32,128)(4,1)S(1)} %get-tuple-element.139, bf16[2560,64]{1,0:T(8,128)(2,1)S(1)} %get-tuple-element.138, bf16[4,512,64]{1,2,0:T(8,128)(2,1)} %get-tuple-element.137, s32[]{:T(128)} %get-tuple-element.128), kind=kOutput, calls=%fused_computation.88.clone.1 | convolution fusion | flops 171703808 | bytes 6949376 | tf_op jit(solution)/shard_map/while/body/eval_jaxpr/qd,kd->qk/dot_general | solution.py:110
  87.9 2.0 %fusion.67 = (f32[512]{0:T(512)S(1)}, f32[512,2560]{1,0:T(8,128)S(1)}) fusion(pred[512,2560]{1,0:T(32,128)(4,1)S(1)} %get-tuple-element.139, bf16[2560,64]{1,0:T(8,128)(2,1)S(1)} %get-tuple-element.138, bf16[4,512,64]{1,2,0:T(8,128)(2,1)} %get-tuple-element.137, s32[]{:T(128)} %get-tuple-element.128), kind=kOutput, calls=%fused_computation.88.clone.1 | convolution fusion | flops 171703808 | bytes 6949376 | tf_op jit(solution)/shard_map/while/body/eval_jaxpr/qd,kd->qk/dot_general | solution.py:110
  92.6 2.0 %fusion.67 = (f32[512]{0:T(512)S(1)}, f32[512,2560]{1,0:T(8,128)S(1)}) fusion(pred[512,2560]{1,0:T(32,128)(4,1)S(1)} %get-tuple-element.139, bf16[2560,64]{1,0:T(8,128)(2,1)S(1)} %get-tuple-element.138, bf16[4,512,64]{1,2,0:T(8,128)(2,1)} %get-tuple-element.137, s32[]{:T(128)} %get-tuple-element.128), kind=kOutput, calls=%fused_computation.88.clone.1 | convolution fusion | flops 171703808 | bytes 6949376 | tf_op jit(solution)/shard_map/while/body/eval_jaxpr/qd,kd->qk/dot_general | solution.py:110
  95.7 1.6 %fusion.69 = bf16[4,512,64]{1,2,0:T(8,128)(2,1)} fusion(bf16[4,512,64]{1,2,0:T(8,128)(2,1)} %get-tuple-element.129, s32[]{:T(128)} %get-tuple-element.128, bf16[2560,64]{1,0:T(8,128)(2,1)S(1)} %copy-done.1, f32[512,2560]{1,0:T(8,128)S(1)} %get-tuple-element.119, f32[512]{0:T(512)S(1)} %get-tuple-element.120, f32[512]{0:T(512)S(1)} %fusion.68), kind=kOutput, calls=%fused_computation.11.clone.1 | convolution fusion | flops 170459136 | bytes 5640704 | tf_op jit(solution)/shard_map/while/body/eval_jaxpr/dot_general | solution.py:118
  97.3 3.6 %fusion.24 = f32[512,2048]{1,0:T(8,128)} fusion(bf16[512,256]{0,1:T(8,128)(2,1)} %bitcast.16, bf16[1,256,2048]{2,1,0:T(8,128)(2,1)S(1)} %copy-done), kind=kOutput, calls=%fused_computation.29 | convolution fusion | flops 536870912 | bytes 5505024 | tf_op jit(solution)/shard_map/dot_general | solution.py:129
  101.0 14.2 %reduce-scatter.3.cloned.1.call-done = f32[512,1024]{1,0:T(8,128)} async-done(((f32[512,2048]{1,0:T(8,128)}), f32[512,1024]{1,0:T(8,128)}) %reduce-scatter.3.cloned.1.call-update) | async-done | bytes 2097168 | tf_op jit(solution)/shard_map/reduce_scatter | solution.py:130
  116.7 12.3 %all-to-all-start.2 = ((bf16[64,8,128]{2,1,0:T(8,128)(2,1)}), bf16[64,8,128]{2,1,0:T(8,128)(2,1)S(1)}, u32[]{:S(2)}, u32[]{:S(2)}) async-start(bf16[64,8,128]{2,1,0:T(8,128)(2,1)} %broadcast_select_fusion.1), calls=%async_computation.4 | async-start | bytes 262144 | tf_op jit(solution)/shard_map/all_to_all | solution.py:34
  133.1 7.2 %all-to-all-done.2 = bf16[64,8,128]{2,1,0:T(8,128)(2,1)S(1)} async-done(((bf16[64,8,128]{2,1,0:T(8,128)(2,1)}), bf16[64,8,128]{2,1,0:T(8,128)(2,1)S(1)}, u32[]{:S(2)}, u32[]{:S(2)}) %all-to-all-start.2) | async-done | bytes 131104 | tf_op jit(solution)/shard_map/all_to_all | solution.py:34
  140.3 4.1 %fusion.31 = bf16[1,1,2048,128]{3,2,1,0:T(8,128)(2,1)} fusion(s32[]{:T(128)S(6)} %select_n.87, bf16[512,128]{1,0:T(8,128)(2,1)S(1)} %bitcast.64, bf16[1536,128]{1,0:T(8,128)(2,1)S(1)} %fusion.34), kind=kLoop, calls=%fused_computation.37 | loop fusion | flops 2097152 | bytes 1048580 | tf_op jit(solution)/shard_map/broadcast_in_dim | solution.py:127
  144.4 9.0 %reduce-scatter.5.cloned.1.call-done = f32[512,256]{1,0:T(8,128)} async-done(((f32[512,1024]{1,0:T(8,128)}), f32[512,256]{1,0:T(8,128)}) %reduce-scatter.5.cloned.1.call-update) | async-done | bytes 524304 | tf_op jit(solution)/shard_map/reduce_scatter | solution.py:131
  153.4 1.8 %convert_element_type.33 = bf16[512,256]{1,0:T(8,128)(2,1)} convert(f32[512,256]{1,0:T(8,128)} %reduce-scatter.5.cloned.1.call-done) | non-fusion elementwise | flops 131072 | bytes 786432 | tf_op jit(solution)/shard_map/convert_element_type | solution.py:132
  (68 shorter events, 24.9 us)
Async XLA Ops:
  7.2 90.1 %copy-start = (bf16[1,256,2048]{2,1,0:T(8,128)(2,1)S(1)}, bf16[1,256,2048]{2,1,0:T(8,128)(2,1)}, u32[]{:S(2)}) copy-start(bf16[1,256,2048]{2,1,0:T(8,128)(2,1)} %param.15) | copy-start | bytes 3145732
  7.2 32.9 %all-gather.2.cloned.1.call-start = ((), (), s32[]{:S(2)}) async-start(), calls=%async_computation.5 | async-start | bytes 3145728 | tf_op jit(solution)/shard_map/all_gather | solution.py:48
  9.6 29.7 %all-to-all-start = ((bf16[64,16,128]{2,1,0:T(8,128)(2,1)}), bf16[64,16,128]{2,1,0:T(8,128)(2,1)S(1)}, u32[]{:S(2)}, u32[]{:S(2)}) async-start(bf16[64,16,128]{2,1,0:T(8,128)(2,1)} %bitcast.8), calls=%async_computation | async-start | bytes 524288 | tf_op jit(solution)/shard_map/all_to_all | solution.py:30
  37.5 4.7 %copy-start.3 = (bf16[2048,1,128]{2,0,1:T(8,128)(2,1)S(1)}, bf16[2048,1,128]{2,0,1:T(8,128)(2,1)}, u32[]{:S(2)}) copy-start(bf16[2048,1,128]{2,0,1:T(8,128)(2,1)} %param.14) | copy-start | bytes 1572868
  46.0 24.2 %all-to-all-start.1 = ((bf16[64,24,128]{2,1,0:T(8,128)(2,1)}), bf16[64,24,128]{2,1,0:T(8,128)(2,1)S(1)}, u32[]{:S(2)}, u32[]{:S(2)}) async-start(bf16[64,24,128]{2,1,0:T(8,128)(2,1)} %pad_maximum_fusion.2), calls=%async_computation.1 | async-start | bytes 786432 | tf_op jit(solution)/shard_map/all_to_all | solution.py:30
  56.4 58.7 %reduce-scatter.3.cloned.1.call-start = ((), (), s32[]{:S(2)}) async-start(), calls=%async_computation.6 | async-start | bytes 6291456 | tf_op jit(solution)/shard_map/reduce_scatter | solution.py:130
  80.5 1.1 copy-start.1
  85.2 1.1 copy-start.1
  89.9 1.1 copy-start.1
  94.6 1.1 copy-start.1
  100.9 30.6 %copy-start.2 = (bf16[1,1,2048,128]{3,2,1,0:T(8,128)(2,1)S(1)}, bf16[1,1,2048,128]{3,2,1,0:T(8,128)(2,1)}, u32[]{:S(2)}) copy-start(bf16[1,1,2048,128]{3,2,1,0:T(8,128)(2,1)} %param.16) | copy-start | bytes 1572868
  101.0 52.5 %reduce-scatter.5.cloned.1.call-start = ((), (), s32[]{:S(2)}) async-start(), calls=%async_computation.7 | async-start | bytes 2621440 | tf_op jit(solution)/shard_map/reduce_scatter | solution.py:131
  116.7 23.6 %all-to-all-start.2 = ((bf16[64,8,128]{2,1,0:T(8,128)(2,1)}), bf16[64,8,128]{2,1,0:T(8,128)(2,1)S(1)}, u32[]{:S(2)}, u32[]{:S(2)}) async-start(bf16[64,8,128]{2,1,0:T(8,128)(2,1)} %broadcast_select_fusion.1), calls=%async_computation.4 | async-start | bytes 262144 | tf_op jit(solution)/shard_map/all_to_all | solution.py:34
Sparse Core Ops, SparseCore 0:
  10.1 25.6 all-gather.1
  101.1 14.0 reduce-scatter.2
  118.3 35.1 reduce-scatter.4

commit v3 on v1

--- a/solution.py
+++ b/solution.py
@@ -45,7 +45,17 @@
 ):
     request = lax.axis_index("dp")
     groups = lax.axis_size("dp")
-    whole = lax.all_gather(tokens, "tx", axis=1, tiled=True)
+    halves = lax.axis_size("tx")
+    core = lax.axis_index("tx")
+    if halves == 2:
+        other = lax.ppermute(tokens, "tx", [(0, 1), (1, 0)])
+        whole = jnp.where(
+            core == 0,
+            jnp.concatenate([tokens, other], axis=1),
+            jnp.concatenate([other, tokens], axis=1),
+        )
+    else:
+        whole = lax.all_gather(tokens, "tx", axis=1, tiled=True)
     rows_new = whole.shape[0]
     width = whole.shape[1]
     floats = whole.astype(jnp.float32)
@@ -54,13 +64,43 @@
     ).astype(jnp.bfloat16)
     owners = jnp.arange(slots.shape[0], dtype=jnp.int32)
     inverse = jnp.sum(jnp.where(slots[None, :] == owners[:, None], owners[None, :], 0), axis=1)
+    length = lengths[request]
+    offset = offsets[request]
+    token_positions = length + jnp.arange(rows_new, dtype=jnp.int32)
+    rotation_pairs = jnp.dot(
+        normalized_input,
+        key_value_weight.reshape(width, 2 * HEAD_SIZE),
+        preferred_element_type=jnp.float32,
+    )
+    new_keys = apply_rotary(rotation_pairs[:, None, :HEAD_SIZE], token_positions)[:, 0].astype(
+        jnp.bfloat16
+    )
+    new_values = rotation_pairs[:, HEAD_SIZE:].astype(jnp.bfloat16)
+    entry = jnp.concatenate([new_keys, new_values], axis=1)
+
     stored = cache[0, 0]
-    halves = lax.axis_size("tx")
     half_rows = stored.shape[0] // halves
-    mine = lax.dynamic_slice_in_dim(stored, lax.axis_index("tx") * half_rows, half_rows, axis=0)
-    spread_in = carry_in(mine)
-    window_part = carry_in(reorder(spread_in, slots, groups))
+    mine = lax.dynamic_slice_in_dim(stored, core * half_rows, half_rows, axis=0)
+    window_chunk = half_rows // groups
+    entry_chunk = rows_new // groups
+    lanes = stored.shape[1]
+    first = jnp.concatenate(
+        [mine.reshape(groups, window_chunk, lanes), entry.reshape(groups, entry_chunk, lanes)],
+        axis=1,
+    ).reshape(groups * (window_chunk + entry_chunk), lanes)
+    spread = carry_in(first).reshape(groups, window_chunk + entry_chunk, lanes)
+    second = jnp.concatenate(
+        [
+            jnp.take(spread[:, :window_chunk], slots, axis=0),
+            jnp.take(spread[:, window_chunk:], inverse, axis=0),
+        ],
+        axis=1,
+    ).reshape(groups * (window_chunk + entry_chunk), lanes)
+    delivered = carry_out(second).reshape(groups, window_chunk + entry_chunk, lanes)
+    window_part = delivered[:, :window_chunk].reshape(half_rows, lanes)
+    arrived = delivered[:, window_chunk:].reshape(rows_new, lanes)
     window = lax.all_gather(window_part, "tx", axis=0, tiled=True)
+
     query_cols = query_weight.shape[2]
     heads = query_cols // HEAD_SIZE
     queries = jnp.dot(
@@ -68,21 +108,9 @@
         query_weight.reshape(width, query_cols),
         preferred_element_type=jnp.float32,
     )
-    rotation_pairs = jnp.dot(
-        normalized_input,
-        key_value_weight.reshape(width, 2 * HEAD_SIZE),
-        preferred_element_type=jnp.float32,
-    )
-    length = lengths[request]
-    offset = offsets[request]
-    token_positions = length + jnp.arange(rows_new, dtype=jnp.int32)
     query_rotated = apply_rotary(
         queries.reshape(rows_new, heads, HEAD_SIZE), token_positions
     ).astype(jnp.bfloat16)
-    new_keys = apply_rotary(rotation_pairs[:, None, :HEAD_SIZE], token_positions)[:, 0].astype(
-        jnp.bfloat16
-    )
-    new_values = rotation_pairs[:, HEAD_SIZE:].astype(jnp.bfloat16)
     factor = 1.0 / math.sqrt(HEAD_SIZE)
     rows = jnp.arange(rows_new, dtype=jnp.int32)
     new_mask = rows[None, :] <= rows[:, None]
@@ -108,17 +136,17 @@
 
     outputs = lax.map(one_head, jnp.transpose(query_rotated, (1, 0, 2)))
     attended = jnp.transpose(outputs, (1, 0, 2)).reshape(rows_new, heads * HEAD_SIZE)
-    entry = jnp.concatenate([new_keys, new_values], axis=1)
-    spread_out = carry_out(entry)
-    arrived = carry_out(reorder(spread_out, inverse, groups))
+
     own_offset = offsets[inverse[request]]
     rolled = jnp.roll(stored, -own_offset, axis=0)
     updated = jnp.roll(jnp.concatenate([arrived, rolled[rows_new:]], axis=0), own_offset, axis=0)
     new_cache = updated[None, None]
     out_rows = output_weight.reshape(output_weight.shape[1], width)
     partial_value = jnp.dot(attended, out_rows, preferred_element_type=jnp.float32)
-    summed_out = lax.psum_scatter(partial_value, ("tx", "ty"), scatter_dimension=1, tiled=True)
-    mixed = summed_out.astype(jnp.bfloat16)
+    across_cores = lax.psum_scatter(
+        partial_value.astype(jnp.bfloat16), "tx", scatter_dimension=1, tiled=True
+    )
+    mixed = lax.psum_scatter(across_cores, "ty", scatter_dimension=1, tiled=True)
     return (mixed, new_cache)
 
 

time: 165 us -> 167 us (1.012)
  waiting for transfers between devices: 41 us -> 57.7 us
  starting transfers between devices: 37.1 us -> 26.4 us
  local copies, waits for them, and re-layouts: 12.8 us -> 9.01 us
  other arithmetic: 24 us -> 21.8 us
  matrix products: 23.4 us -> 25.1 us
    reduce_scatter x1 -> x2, waiting for transfers between devices: 10.4 us -> 33.9 us  [the longest x1 22.3 us: per_device(): lax.psum_scatter(across_cores, 'ty', scatter_dimension=1, tiled=True)]
    all_to_all x2 -> x1, starting transfers between devices: 27.6 us -> 10.9 us  [carry_in(): return lax.all_to_all(window, 'dp', split_axis=0, concat_axis=0, tiled=True)]
    all_to_all x2 -> x1, waiting for transfers between devices: 19.1 us -> 10 us  [carry_out(): return lax.all_to_all(window, 'dp', split_axis=0, concat_axis=0, tiled=True)]
    ppermute x0 -> x1, starting transfers between devices: none -> 8.92 us  [per_device(): other = lax.ppermute(tokens, 'tx', [(0, 1), (1, 0)])]
    all_to_all x2 -> x1, starting transfers between devices: 9.42 us -> 6.24 us  [carry_out(): return lax.all_to_all(window, 'dp', split_axis=0, concat_axis=0, tiled=True)]
    all_to_all x2 -> x1, waiting for transfers between devices: 10.7 us -> 13.7 us  [carry_in(): return lax.all_to_all(window, 'dp', split_axis=0, concat_axis=0, tiled=True)]
    concatenate x0 -> x3, other arithmetic: none -> 2.62 us  [the longest x1 1.03 us: per_device(): values_all = jnp.concatenate([window[:, HEAD_SIZE:], new_values], axis=0)]
    convert_element_type x1 -> x0, other arithmetic: 1.77 us -> none  [per_device(): mixed = summed_out.astype(jnp.bfloat16)]
  transfers between devices with their start and end apart: 6 -> 5, of which waited for: 5 -> 4; matrix products, arithmetic and copies ran while one was open for 14% -> 13% of each run, Pallas kernels for 0% -> 0%
where the time goes in v3:
time: 167 us; the launch traced here: 165 us
  waiting for transfers between devices  57.7 us (35%)
  starting transfers between devices  26.4 us (16%)
  matrix products  25.1 us (15%)
  other arithmetic  21.8 us (13%)
  between operations  20.3 us (12%)
  local copies, waits for them, and re-layouts  9.01 us (5%)
  blocking collectives  5.29 us (3%)
    reduce_scatter x1, waiting for transfers between devices, per_device(): lax.psum_scatter(across_cores, 'ty', scatter_dimension=1, tiled=True)  22.3 us
    all_to_all x1, waiting for transfers between devices, carry_in(): return lax.all_to_all(window, 'dp', split_axis=0, concat_axis=0, tiled=True)  13.7 us
    reduce_scatter x1, waiting for transfers between devices, per_device(): lax.psum_scatter(partial_value.astype(jnp.bfloat16), 'tx', scatter_dimens...  11.6 us
    all_to_all x1, starting transfers between devices, carry_in(): return lax.all_to_all(window, 'dp', split_axis=0, concat_axis=0, tiled=True)  10.9 us
    all_to_all x1, waiting for transfers between devices, carry_out(): return lax.all_to_all(window, 'dp', split_axis=0, concat_axis=0, tiled=True)  10 us
    dot_general x4, matrix products, one_head(): jnp.einsum('qd,kd->qk', query_rows, keys_all, preferred_element_type=jnp....  9.05 us
    ppermute x1, starting transfers between devices, per_device(): other = lax.ppermute(tokens, 'tx', [(0, 1), (1, 0)])  8.92 us
    dot_general x4, matrix products, one_head(): summed = jnp.dot(weights, values_all, preferred_element_type=jnp.float32)  6.51 us
  transfers between devices with their start and end apart: 5, of which 4 were waited for; matrix products, arithmetic and copies ran while one was open for 13% of the time, Pallas kernels for 0%

profile of v3, /device:TPU:1, one launch (start us, length us, event | category | flops | bytes accessed | tf_op | source)
XLA Modules:
  0.0 165.5 jit_solution(18260670358882764556)
XLA Ops:
  7.2 8.9 %collective-permute-start = (bf16[512,1024]{1,0:T(8,128)(2,1)}, bf16[512,1024]{1,0:T(8,128)(2,1)}, u32[]{:S(2)}, u32[]{:S(2)}) collective-permute-start(bf16[512,1024]{1,0:T(8,128)(2,1)} %param.12), channel_id=1, source_target_pairs={{0,4},{4,0},{1,5},{5,1},{2,6},{6,2},{3,7},{7,3},{8,12},{12,8},{9,1... | collective-permute-start | bytes 3145736 | tf_op jit(solution)/shard_map/ppermute | solution.py:51
  25.4 2.3 %copy.20 = bf16[2048,1,256]{0,2,1:T(8,128)(2,1)} copy(bf16[2048,1,256]{2,0,1:T(8,128)(2,1)} %param.13) | data formatting | bytes 2097152 | tf_op args[1]
  29.7 3.1 %fusion.20 = f32[512]{0:T(512)S(1)} fusion(bf16[512,1024]{1,0:T(8,128)(2,1)} %param.12, bf16[512,1024]{1,0:T(8,128)(2,1)} %collective-permute-done, pred[]{:T(512)S(6)} %eq.20), kind=kLoop, calls=%fused_computation.18 | loop fusion | flops 12582400 | bytes 2099201 | tf_op jit(solution)/shard_map/reduce_sum | solution.py:63
  32.8 3.0 %fusion.25 = f32[512,128]{0,1:T(8,128)S(1)} fusion(f32[512]{0:T(512)S(1)} %add_rsqrt_fusion, bf16[2048,1,128]{2,0,1:T(8,128)(2,1)} %param.14, bf16[512,1024]{1,0:T(8,128)(2,1)} %collective-permute-done, bf16[512,1024]{1,0:T(8,128)(2,1)S(1)} %copy-done.2, pred[]{:T(512)S(6)} %eq.20), kind=kOutput, calls=%fused_computation.33 | convolution fusion | flops 281018368 | bytes 2885633 | tf_op jit(solution)/shard_map/dot_general | solution.py:70
  37.1 10.9 %all-to-all-start = ((bf16[64,24,128]{2,1,0:T(8,128)(2,1)}), bf16[64,24,128]{2,1,0:T(8,128)(2,1)S(1)}, u32[]{:S(2)}, u32[]{:S(2)}) async-start(bf16[64,24,128]{2,1,0:T(8,128)(2,1)} %pad_maximum_fusion.2), calls=%async_computation | async-start | bytes 786432 | tf_op jit(solution)/shard_map/all_to_all | solution.py:30
  49.8 13.7 %all-to-all-done = bf16[64,24,128]{2,1,0:T(8,128)(2,1)S(1)} async-done(((bf16[64,24,128]{2,1,0:T(8,128)(2,1)}), bf16[64,24,128]{2,1,0:T(8,128)(2,1)S(1)}, u32[]{:S(2)}, u32[]{:S(2)}) %all-to-all-start) | async-done | bytes 393248 | tf_op jit(solution)/shard_map/all_to_all | solution.py:30
  65.9 6.2 %all-to-all-start.1 = ((bf16[64,24,128]{2,1,0:T(8,128)(2,1)}), bf16[64,24,128]{2,1,0:T(8,128)(2,1)S(1)}, u32[]{:S(2)}, u32[]{:S(2)}) async-start(bf16[64,24,128]{2,1,0:T(8,128)(2,1)} %pad_maximum_fusion.3), calls=%async_computation.1 | async-start | bytes 786432 | tf_op jit(solution)/shard_map/all_to_all | solution.py:34
  72.1 3.5 %fusion.22 = f32[512,4,64]{0,2,1:T(8,128)S(1)} fusion(bf16[4,64,2048]{2,1,0:T(8,128)(2,1)} %bitcast.64, f32[512]{0:T(512)S(1)} %add_rsqrt_fusion, bf16[512,1024]{1,0:T(8,128)(2,1)} %collective-permute-done, bf16[512,1024]{1,0:T(8,128)(2,1)} %param.12, pred[]{:T(512)S(6)} %eq.20), kind=kOutput, calls=%fused_computation.23 | convolution fusion | flops 549453824 | bytes 3672065 | tf_op jit(solution)/shard_map/dot_general | solution.py:106
  76.5 10.0 %all-to-all-done.1 = bf16[64,24,128]{2,1,0:T(8,128)(2,1)S(1)} async-done(((bf16[64,24,128]{2,1,0:T(8,128)(2,1)}), bf16[64,24,128]{2,1,0:T(8,128)(2,1)S(1)}, u32[]{:S(2)}, u32[]{:S(2)}) %all-to-all-start.1) | async-done | bytes 393248 | tf_op jit(solution)/shard_map/all_to_all | solution.py:34
  86.6 5.3 %all_gather.3 = bf16[2048,128]{1,0:T(8,128)(2,1)S(1)} all-gather(bf16[1024,128]{1,0:T(8,128)(2,1)S(1)} %bitcast.63), channel_id=1, replica_groups=mesh['dp'=64,'tx'=2,'ty'=4] {'tx'}, dimensions={0}, use_global_device_ids=true | all-gather | bytes 786432 | tf_op jit(solution)/shard_map/all_gather | solution.py:102
  94.1 19.0 %while.10 = (s32[]{:T(128)}, bf16[4,512,64]{1,2,0:T(8,128)(2,1)}, bf16[4,512,64]{1,2,0:T(8,128)(2,1)}, bf16[2560,64]{1,0:T(8,128)(2,1)}, pred[512,2560]{1,0:T(32...) while((s32[]{:T(128)}, bf16[4,512,64]{1,2,0:T(8,128)(2,1)}, bf16[4,512,64]{1,2,0:T(8,128)(2,1)}, ...), condition=%wide.region_5.6_spmd, body=%wide.region_2.5_spmd.sunk | while | flops 344783872 | bytes 18164812 | solution.py:137
  94.1 2.3 %fusion.66 = (f32[512]{0:T(512)S(1)}, f32[512,2560]{1,0:T(8,128)S(1)}) fusion(pred[512,2560]{1,0:T(32,128)(4,1)S(1)} %get-tuple-element.139, bf16[2560,64]{1,0:T(8,128)(2,1)} %get-tuple-element.138, bf16[4,512,64]{1,2,0:T(8,128)(2,1)} %get-tuple-element.137, s32[]{:T(128)} %get-tuple-element.128), kind=kOutput, calls=%fused_computation.91.clone.1 | convolution fusion | flops 171703808 | bytes 7277056 | tf_op jit(solution)/shard_map/while/body/eval_jaxpr/qd,kd->qk/dot_general | solution.py:126
  97.2 1.6 fusion.68
  98.8 2.3 %fusion.66 = (f32[512]{0:T(512)S(1)}, f32[512,2560]{1,0:T(8,128)S(1)}) fusion(pred[512,2560]{1,0:T(32,128)(4,1)S(1)} %get-tuple-element.139, bf16[2560,64]{1,0:T(8,128)(2,1)} %get-tuple-element.138, bf16[4,512,64]{1,2,0:T(8,128)(2,1)} %get-tuple-element.137, s32[]{:T(128)} %get-tuple-element.128), kind=kOutput, calls=%fused_computation.91.clone.1 | convolution fusion | flops 171703808 | bytes 7277056 | tf_op jit(solution)/shard_map/while/body/eval_jaxpr/qd,kd->qk/dot_general | solution.py:126
  101.9 1.6 fusion.68
  103.6 2.3 %fusion.66 = (f32[512]{0:T(512)S(1)}, f32[512,2560]{1,0:T(8,128)S(1)}) fusion(pred[512,2560]{1,0:T(32,128)(4,1)S(1)} %get-tuple-element.139, bf16[2560,64]{1,0:T(8,128)(2,1)} %get-tuple-element.138, bf16[4,512,64]{1,2,0:T(8,128)(2,1)} %get-tuple-element.137, s32[]{:T(128)} %get-tuple-element.128), kind=kOutput, calls=%fused_computation.91.clone.1 | convolution fusion | flops 171703808 | bytes 7277056 | tf_op jit(solution)/shard_map/while/body/eval_jaxpr/qd,kd->qk/dot_general | solution.py:126
  106.7 1.6 fusion.68
  108.3 2.3 %fusion.66 = (f32[512]{0:T(512)S(1)}, f32[512,2560]{1,0:T(8,128)S(1)}) fusion(pred[512,2560]{1,0:T(32,128)(4,1)S(1)} %get-tuple-element.139, bf16[2560,64]{1,0:T(8,128)(2,1)} %get-tuple-element.138, bf16[4,512,64]{1,2,0:T(8,128)(2,1)} %get-tuple-element.137, s32[]{:T(128)} %get-tuple-element.128), kind=kOutput, calls=%fused_computation.91.clone.1 | convolution fusion | flops 171703808 | bytes 7277056 | tf_op jit(solution)/shard_map/while/body/eval_jaxpr/qd,kd->qk/dot_general | solution.py:126
  111.4 1.6 fusion.68
  113.0 3.1 %convolution_convert_fusion = bf16[512,2048]{1,0:T(8,128)(2,1)} fusion(bf16[512,256]{0,1:T(8,128)(2,1)} %bitcast.18, bf16[1,256,2048]{2,1,0:T(8,128)(2,1)S(1)} %copy-done), kind=kOutput, calls=%fused_computation.21 | convolution fusion | flops 537919488 | bytes 3407872 | tf_op jit(solution)/shard_map/dot_general | solution.py:145
  116.4 11.6 %reduce-scatter.3.cloned.1.call-done = bf16[512,1024]{1,0:T(8,128)(2,1)} async-done(((bf16[512,2048]{1,0:T(8,128)(2,1)}), bf16[512,1024]{1,0:T(8,128)(2,1)}) %reduce-scatter.3.cloned.1.call-update) | async-done | bytes 1048592 | tf_op jit(solution)/shard_map/reduce_scatter | solution.py:146
  130.7 1.5 fusion.33
  132.2 4.1 %fusion.30 = bf16[1,1,2048,128]{3,2,1,0:T(8,128)(2,1)} fusion(s32[]{:T(128)S(6)} %select_n.95, bf16[512,128]{1,0:T(8,128)(2,1)S(1)} %slice_bitcast_fusion, bf16[1536,128]{1,0:T(8,128)(2,1)S(1)} %fusion.33), kind=kLoop, calls=%fused_computation.38 | loop fusion | flops 2097152 | bytes 1048580 | tf_op jit(solution)/shard_map/broadcast_in_dim | solution.py:143
  136.3 22.3 %reduce-scatter.5.cloned.1.call-done = bf16[512,256]{1,0:T(8,128)(2,1)} async-done(((bf16[512,1024]{1,0:T(8,128)(2,1)}), bf16[512,256]{1,0:T(8,128)(2,1)}) %reduce-scatter.5.cloned.1.call-update) | async-done | bytes 262160 | tf_op jit(solution)/shard_map/reduce_scatter | solution.py:149
  (59 shorter events, 20.1 us)
Async XLA Ops:
  7.2 105.9 %copy-start = (bf16[1,256,2048]{2,1,0:T(8,128)(2,1)S(1)}, bf16[1,256,2048]{2,1,0:T(8,128)(2,1)}, u32[]{:S(2)}) copy-start(bf16[1,256,2048]{2,1,0:T(8,128)(2,1)} %param.15) | copy-start | bytes 3145732
  7.2 25.6 %copy-start.2 = (bf16[512,1024]{1,0:T(8,128)(2,1)S(1)}, bf16[512,1024]{1,0:T(8,128)(2,1)}, u32[]{:S(2)}) copy-start(bf16[512,1024]{1,0:T(8,128)(2,1)} %param.12) | copy-start | bytes 3145732
  7.2 22.5 %collective-permute-start = (bf16[512,1024]{1,0:T(8,128)(2,1)}, bf16[512,1024]{1,0:T(8,128)(2,1)}, u32[]{:S(2)}, u32[]{:S(2)}) collective-permute-start(bf16[512,1024]{1,0:T(8,128)(2,1)} %param.12), channel_id=1, source_target_pairs={{0,4},{4,0},{1,5},{5,1},{2,6},{6,2},{3,7},{7,3},{8,12},{12,8},{9,1... | collective-permute-start | bytes 3145736 | tf_op jit(solution)/shard_map/ppermute | solution.py:51
  37.1 26.4 %all-to-all-start = ((bf16[64,24,128]{2,1,0:T(8,128)(2,1)}), bf16[64,24,128]{2,1,0:T(8,128)(2,1)S(1)}, u32[]{:S(2)}, u32[]{:S(2)}) async-start(bf16[64,24,128]{2,1,0:T(8,128)(2,1)} %pad_maximum_fusion.2), calls=%async_computation | async-start | bytes 786432 | tf_op jit(solution)/shard_map/all_to_all | solution.py:30
  65.9 20.7 %all-to-all-start.1 = ((bf16[64,24,128]{2,1,0:T(8,128)(2,1)}), bf16[64,24,128]{2,1,0:T(8,128)(2,1)S(1)}, u32[]{:S(2)}, u32[]{:S(2)}) async-start(bf16[64,24,128]{2,1,0:T(8,128)(2,1)} %pad_maximum_fusion.3), calls=%async_computation.1 | async-start | bytes 786432 | tf_op jit(solution)/shard_map/all_to_all | solution.py:34
  72.1 55.8 %reduce-scatter.3.cloned.1.call-start = ((), (), s32[]{:S(2)}) async-start(), calls=%async_computation.4 | async-start | bytes 3145728 | tf_op jit(solution)/shard_map/reduce_scatter | solution.py:146
  113.0 17.6 %copy-start.1 = (bf16[1,1,2048,128]{3,2,1,0:T(8,128)(2,1)S(1)}, bf16[1,1,2048,128]{3,2,1,0:T(8,128)(2,1)}, u32[]{:S(2)}) copy-start(bf16[1,1,2048,128]{3,2,1,0:T(8,128)(2,1)} %param.16) | copy-start | bytes 1572868
  116.1 42.5 %reduce-scatter.5.cloned.1.call-start = ((), (), s32[]{:S(2)}) async-start(), calls=%async_computation.5 | async-start | bytes 1310720 | tf_op jit(solution)/shard_map/reduce_scatter | solution.py:149
Sparse Core Ops, SparseCore 0:
  116.3 11.6 reduce-scatter.2
  131.6 27.0 reduce-scatter.4

commit v4 on v3

--- a/solution.py
+++ b/solution.py
@@ -47,15 +47,11 @@
     groups = lax.axis_size("dp")
     halves = lax.axis_size("tx")
     core = lax.axis_index("tx")
-    if halves == 2:
-        other = lax.ppermute(tokens, "tx", [(0, 1), (1, 0)])
-        whole = jnp.where(
-            core == 0,
-            jnp.concatenate([tokens, other], axis=1),
-            jnp.concatenate([other, tokens], axis=1),
-        )
-    else:
-        whole = lax.all_gather(tokens, "tx", axis=1, tiled=True)
+    stored = cache[0, 0]
+    half_rows = stored.shape[0] // halves
+    mine = lax.dynamic_slice_in_dim(stored, core * half_rows, half_rows, axis=0)
+    spread = carry_in(mine)
+    whole = lax.all_gather(tokens, "tx", axis=1, tiled=True)
     rows_new = whole.shape[0]
     width = whole.shape[1]
     floats = whole.astype(jnp.float32)
@@ -78,27 +74,19 @@
     new_values = rotation_pairs[:, HEAD_SIZE:].astype(jnp.bfloat16)
     entry = jnp.concatenate([new_keys, new_values], axis=1)
 
-    stored = cache[0, 0]
-    half_rows = stored.shape[0] // halves
-    mine = lax.dynamic_slice_in_dim(stored, core * half_rows, half_rows, axis=0)
     window_chunk = half_rows // groups
     entry_chunk = rows_new // groups
     lanes = stored.shape[1]
-    first = jnp.concatenate(
-        [mine.reshape(groups, window_chunk, lanes), entry.reshape(groups, entry_chunk, lanes)],
-        axis=1,
-    ).reshape(groups * (window_chunk + entry_chunk), lanes)
-    spread = carry_in(first).reshape(groups, window_chunk + entry_chunk, lanes)
     second = jnp.concatenate(
         [
-            jnp.take(spread[:, :window_chunk], slots, axis=0),
-            jnp.take(spread[:, window_chunk:], inverse, axis=0),
+            jnp.take(spread.reshape(groups, window_chunk, lanes), slots, axis=0),
+            entry.reshape(groups, entry_chunk, lanes),
         ],
         axis=1,
     ).reshape(groups * (window_chunk + entry_chunk), lanes)
-    delivered = carry_out(second).reshape(groups, window_chunk + entry_chunk, lanes)
+    delivered = carry_in(second).reshape(groups, window_chunk + entry_chunk, lanes)
     window_part = delivered[:, :window_chunk].reshape(half_rows, lanes)
-    arrived = delivered[:, window_chunk:].reshape(rows_new, lanes)
+    entry_parts = delivered[:, window_chunk:]
     window = lax.all_gather(window_part, "tx", axis=0, tiled=True)
 
     query_cols = query_weight.shape[2]
@@ -137,16 +125,16 @@
     outputs = lax.map(one_head, jnp.transpose(query_rotated, (1, 0, 2)))
     attended = jnp.transpose(outputs, (1, 0, 2)).reshape(rows_new, heads * HEAD_SIZE)
 
+    arrived = carry_out(jnp.take(entry_parts, inverse, axis=0).reshape(rows_new, lanes))
     own_offset = offsets[inverse[request]]
     rolled = jnp.roll(stored, -own_offset, axis=0)
     updated = jnp.roll(jnp.concatenate([arrived, rolled[rows_new:]], axis=0), own_offset, axis=0)
     new_cache = updated[None, None]
     out_rows = output_weight.reshape(output_weight.shape[1], width)
     partial_value = jnp.dot(attended, out_rows, preferred_element_type=jnp.float32)
-    across_cores = lax.psum_scatter(
-        partial_value.astype(jnp.bfloat16), "tx", scatter_dimension=1, tiled=True
+    mixed = lax.psum_scatter(
+        partial_value.astype(jnp.bfloat16), ("tx", "ty"), scatter_dimension=1, tiled=True
     )
-    mixed = lax.psum_scatter(across_cores, "ty", scatter_dimension=1, tiled=True)
     return (mixed, new_cache)
 
 

time: 167 us -> 144 us (0.86)
  waiting for transfers between devices: 57.7 us -> 30.3 us
  starting transfers between devices: 26.4 us -> 32.5 us
  matrix products: 25.1 us -> 22.7 us
  local copies, waits for them, and re-layouts: 9.01 us -> 10.8 us
    reduce_scatter x2 -> x1, waiting for transfers between devices: 33.9 us -> 14.1 us  [per_device(): lax.psum_scatter(partial_value.astype(jnp.bfloat16), ('tx', 'ty'), scatte...]
    all_to_all x1 -> x2, starting transfers between devices: 10.9 us -> 27.7 us  [carry_in(): return lax.all_to_all(window, 'dp', split_axis=0, concat_axis=0, tiled=True)]
    ppermute x1 -> x0, starting transfers between devices: 8.92 us -> none  [per_device(): other = lax.ppermute(tokens, 'tx', [(0, 1), (1, 0)])]
    all_to_all x1 -> x2, waiting for transfers between devices: 13.7 us -> 8.42 us  [carry_in(): return lax.all_to_all(window, 'dp', split_axis=0, concat_axis=0, tiled=True)]
    all_to_all x1, waiting for transfers between devices: 10 us -> 7.12 us  [carry_out(): return lax.all_to_all(window, 'dp', split_axis=0, concat_axis=0, tiled=True)]
    concatenate x3 -> x1, other arithmetic: 2.62 us -> 0.79 us  [per_device(): jnp.concatenate([jnp.take(spread.reshape(groups, window_chunk, lanes), sl...]
  transfers between devices with their start and end apart: 5 -> 5, of which waited for: 4 -> 4; matrix products, arithmetic and copies ran while one was open for 13% -> 17% of each run, Pallas kernels for 0% -> 0%
where the time goes in v4:
time: 144 us; the launch traced here: 143 us
  starting transfers between devices  32.5 us (23%)
  waiting for transfers between devices  30.3 us (21%)
  matrix products  22.7 us (16%)
  other arithmetic  20.6 us (14%)
  between operations  20.3 us (14%)
  local copies, waits for them, and re-layouts  10.8 us (8%)
  blocking collectives  6.03 us (4%)
    all_to_all x2, starting transfers between devices, carry_in(): return lax.all_to_all(window, 'dp', split_axis=0, concat_axis=0, tiled=True)  27.7 us
    reduce_scatter x1, waiting for transfers between devices, per_device(): lax.psum_scatter(partial_value.astype(jnp.bfloat16), ('tx', 'ty'), scatte...  14.1 us
    all_to_all x2, waiting for transfers between devices, carry_in(): return lax.all_to_all(window, 'dp', split_axis=0, concat_axis=0, tiled=True)  8.42 us
    dot_general x4, matrix products, one_head(): jnp.einsum('qd,kd->qk', query_rows, keys_all, preferred_element_type=jnp....  7.92 us
    all_to_all x1, waiting for transfers between devices, carry_out(): return lax.all_to_all(window, 'dp', split_axis=0, concat_axis=0, tiled=True)  7.12 us
    dot_general x4, matrix products, one_head(): summed = jnp.dot(weights, values_all, preferred_element_type=jnp.float32)  6.48 us
    all_gather x1, blocking collectives, per_device(): window = lax.all_gather(window_part, 'tx', axis=0, tiled=True)  6.03 us
    all_to_all x1, starting transfers between devices, carry_out(): return lax.all_to_all(window, 'dp', split_axis=0, concat_axis=0, tiled=True)  4.8 us
  transfers between devices with their start and end apart: 5, of which 4 were waited for; matrix products, arithmetic and copies ran while one was open for 17% of the time, Pallas kernels for 0%

profile of v4, /device:TPU:1, one launch (start us, length us, event | category | flops | bytes accessed | tf_op | source)
XLA Modules:
  0.0 143.3 jit_solution(11156101658553420245)
XLA Ops:
  7.9 1.7 %constant_dynamic-slice_fusion = bf16[1,1,1024,128]{3,2,1,0:T(8,128)(2,1)} fusion(bf16[1,1,2048,128]{3,2,1,0:T(8,128)(2,1)} %param.16, s32[]{:T(128)S(6)} %select_n.74), kind=kLoop, calls=%fused_computation.85 | loop fusion | bytes 524292 | tf_op jit(solution)/shard_map/dynamic_slice | solution.py:52
  9.6 17.1 %all-to-all-start = ((bf16[64,16,128]{2,1,0:T(8,128)(2,1)}), bf16[64,16,128]{2,1,0:T(8,128)(2,1)S(1)}, u32[]{:S(2)}, u32[]{:S(2)}) async-start(bf16[64,16,128]{2,1,0:T(8,128)(2,1)} %bitcast.8), calls=%async_computation | async-start | bytes 524288 | tf_op jit(solution)/shard_map/all_to_all | solution.py:30
  37.7 1.6 %all-to-all-done = bf16[64,16,128]{2,1,0:T(8,128)(2,1)S(1)} async-done(((bf16[64,16,128]{2,1,0:T(8,128)(2,1)}), bf16[64,16,128]{2,1,0:T(8,128)(2,1)S(1)}, u32[]{:S(2)}, u32[]{:S(2)}) %all-to-all-start) | async-done | bytes 262176 | tf_op jit(solution)/shard_map/all_to_all | solution.py:30
  40.1 2.1 %fusion.20 = f32[512]{0:T(512)S(1)} fusion(bf16[512,2048]{1,0:T(8,128)(2,1)} %all-gather.2.cloned.1.call-done), kind=kLoop, calls=%fused_computation.18 | loop fusion | flops 3145216 | bytes 2099200 | tf_op jit(solution)/shard_map/reduce_sum | solution.py:59
  42.2 2.6 %fusion.25 = f32[512,128]{0,1:T(8,128)S(1)} fusion(bf16[512,2048]{1,0:T(8,128)(2,1)} %all-gather.2.cloned.1.call-done, f32[512]{0:T(512)S(1)} %add_rsqrt_fusion, bf16[2048,1,128]{2,0,1:T(8,128)(2,1)} %param.14), kind=kOutput, calls=%fused_computation.32 | convolution fusion | flops 271581184 | bytes 2885632 | tf_op jit(solution)/shard_map/dot_general | solution.py:66
  46.1 10.5 %all-to-all-start.1 = ((bf16[64,24,128]{2,1,0:T(8,128)(2,1)}), bf16[64,24,128]{2,1,0:T(8,128)(2,1)S(1)}, u32[]{:S(2)}, u32[]{:S(2)}) async-start(bf16[64,24,128]{2,1,0:T(8,128)(2,1)} %pad_maximum_fusion.2), calls=%async_computation.1 | async-start | bytes 786432 | tf_op jit(solution)/shard_map/all_to_all | solution.py:30
  57.0 2.3 %copy.20 = bf16[2048,1,256]{0,2,1:T(8,128)(2,1)} copy(bf16[2048,1,256]{2,0,1:T(8,128)(2,1)} %param.13) | data formatting | bytes 2097152 | tf_op args[1]
  60.1 2.7 %fusion.22 = f32[512,4,64]{0,2,1:T(8,128)S(1)} fusion(bf16[4,64,2048]{2,1,0:T(8,128)(2,1)} %bitcast.62, bf16[512,2048]{1,0:T(8,128)(2,1)} %all-gather.2.cloned.1.call-done, f32[512]{0:T(512)S(1)} %add_rsqrt_fusion), kind=kOutput, calls=%fused_computation.22 | convolution fusion | flops 540016640 | bytes 3672064 | tf_op jit(solution)/shard_map/dot_general | solution.py:94
  63.6 6.8 %all-to-all-done.1 = bf16[64,24,128]{2,1,0:T(8,128)(2,1)S(1)} async-done(((bf16[64,24,128]{2,1,0:T(8,128)(2,1)}), bf16[64,24,128]{2,1,0:T(8,128)(2,1)S(1)}, u32[]{:S(2)}, u32[]{:S(2)}) %all-to-all-start.1) | async-done | bytes 393248 | tf_op jit(solution)/shard_map/all_to_all | solution.py:30
  70.4 6.0 %all_gather.7 = bf16[2048,128]{1,0:T(8,128)(2,1)S(1)} all-gather(bf16[1024,128]{1,0:T(8,128)(2,1)S(1)} %bitcast.61), channel_id=1, replica_groups=mesh['dp'=64,'tx'=2,'ty'=4] {'tx'}, dimensions={0}, use_global_device_ids=true | all-gather | bytes 786432 | tf_op jit(solution)/shard_map/all_gather | solution.py:90
  76.7 2.0 %pad_maximum_fusion = (bf16[2560,64]{1,0:T(8,128)(2,1)S(1)}, bf16[2560,64]{1,0:T(8,128)(2,1)}) fusion(bf16[512,64]{1,0:T(8,128)(2,1)S(1)} %copy.22, bf16[2048,64]{1,0:T(8,128)(2,1)S(1)} %get-tuple-element.71, bf16[512,64]{1,0:T(8,128)(2,1)} %copy.23, bf16[2048,64]{1,0:T(8,128)(2,1)S(1)} %get-tuple-element.70), kind=kLoop, calls=%fused_computation.33 | loop fusion | flops 1310720 | bytes 1310720 | tf_op jit(solution)/shard_map/concatenate | solution.py:109
  78.7 18.8 %while.10 = (s32[]{:T(128)}, bf16[4,512,64]{1,2,0:T(8,128)(2,1)}, bf16[4,512,64]{1,2,0:T(8,128)(2,1)}, bf16[2560,64]{1,0:T(8,128)(2,1)S(1)}, pred[512,2560]{1,0:...) while((s32[]{:T(128)}, bf16[4,512,64]{1,2,0:T(8,128)(2,1)}, bf16[4,512,64]{1,2,0:T(8,128)(2,1)}, ...), condition=%wide.region_4.5_spmd, body=%wide.region_1.4_spmd.sunk | while | flops 344783872 | bytes 19147880 | solution.py:125
  78.7 2.0 %fusion.66 = (f32[512]{0:T(512)S(1)}, f32[512,2560]{1,0:T(8,128)S(1)}) fusion(pred[512,2560]{1,0:T(32,128)(4,1)S(1)} %get-tuple-element.139, bf16[2560,64]{1,0:T(8,128)(2,1)S(1)} %get-tuple-element.138, bf16[4,512,64]{1,2,0:T(8,128)(2,1)} %get-tuple-element.137, s32[]{:T(128)} %get-tuple-element.128), kind=kOutput, calls=%fused_computation.88.clone.1 | convolution fusion | flops 171703808 | bytes 6949376 | tf_op jit(solution)/shard_map/while/body/eval_jaxpr/qd,kd->qk/dot_general | solution.py:114
  81.8 1.6 %fusion.68 = bf16[4,512,64]{1,2,0:T(8,128)(2,1)} fusion(bf16[4,512,64]{1,2,0:T(8,128)(2,1)} %get-tuple-element.129, s32[]{:T(128)} %get-tuple-element.128, bf16[2560,64]{1,0:T(8,128)(2,1)S(1)} %copy-done.1, f32[512,2560]{1,0:T(8,128)S(1)} %get-tuple-element.119, f32[512]{0:T(512)S(1)} %get-tuple-element.120, f32[512]{0:T(512)S(1)} %fusion.67), kind=kOutput, calls=%fused_computation.11.clone.1 | convolution fusion | flops 170459136 | bytes 5640704 | tf_op jit(solution)/shard_map/while/body/eval_jaxpr/dot_general | solution.py:122
  83.4 2.0 %fusion.66 = (f32[512]{0:T(512)S(1)}, f32[512,2560]{1,0:T(8,128)S(1)}) fusion(pred[512,2560]{1,0:T(32,128)(4,1)S(1)} %get-tuple-element.139, bf16[2560,64]{1,0:T(8,128)(2,1)S(1)} %get-tuple-element.138, bf16[4,512,64]{1,2,0:T(8,128)(2,1)} %get-tuple-element.137, s32[]{:T(128)} %get-tuple-element.128), kind=kOutput, calls=%fused_computation.88.clone.1 | convolution fusion | flops 171703808 | bytes 6949376 | tf_op jit(solution)/shard_map/while/body/eval_jaxpr/qd,kd->qk/dot_general | solution.py:114
  86.5 1.6 %fusion.68 = bf16[4,512,64]{1,2,0:T(8,128)(2,1)} fusion(bf16[4,512,64]{1,2,0:T(8,128)(2,1)} %get-tuple-element.129, s32[]{:T(128)} %get-tuple-element.128, bf16[2560,64]{1,0:T(8,128)(2,1)S(1)} %copy-done.1, f32[512,2560]{1,0:T(8,128)S(1)} %get-tuple-element.119, f32[512]{0:T(512)S(1)} %get-tuple-element.120, f32[512]{0:T(512)S(1)} %fusion.67), kind=kOutput, calls=%fused_computation.11.clone.1 | convolution fusion | flops 170459136 | bytes 5640704 | tf_op jit(solution)/shard_map/while/body/eval_jaxpr/dot_general | solution.py:122
  88.1 2.0 %fusion.66 = (f32[512]{0:T(512)S(1)}, f32[512,2560]{1,0:T(8,128)S(1)}) fusion(pred[512,2560]{1,0:T(32,128)(4,1)S(1)} %get-tuple-element.139, bf16[2560,64]{1,0:T(8,128)(2,1)S(1)} %get-tuple-element.138, bf16[4,512,64]{1,2,0:T(8,128)(2,1)} %get-tuple-element.137, s32[]{:T(128)} %get-tuple-element.128), kind=kOutput, calls=%fused_computation.88.clone.1 | convolution fusion | flops 171703808 | bytes 6949376 | tf_op jit(solution)/shard_map/while/body/eval_jaxpr/qd,kd->qk/dot_general | solution.py:114
  91.1 1.6 %fusion.68 = bf16[4,512,64]{1,2,0:T(8,128)(2,1)} fusion(bf16[4,512,64]{1,2,0:T(8,128)(2,1)} %get-tuple-element.129, s32[]{:T(128)} %get-tuple-element.128, bf16[2560,64]{1,0:T(8,128)(2,1)S(1)} %copy-done.1, f32[512,2560]{1,0:T(8,128)S(1)} %get-tuple-element.119, f32[512]{0:T(512)S(1)} %get-tuple-element.120, f32[512]{0:T(512)S(1)} %fusion.67), kind=kOutput, calls=%fused_computation.11.clone.1 | convolution fusion | flops 170459136 | bytes 5640704 | tf_op jit(solution)/shard_map/while/body/eval_jaxpr/dot_general | solution.py:122
  92.8 2.0 %fusion.66 = (f32[512]{0:T(512)S(1)}, f32[512,2560]{1,0:T(8,128)S(1)}) fusion(pred[512,2560]{1,0:T(32,128)(4,1)S(1)} %get-tuple-element.139, bf16[2560,64]{1,0:T(8,128)(2,1)S(1)} %get-tuple-element.138, bf16[4,512,64]{1,2,0:T(8,128)(2,1)} %get-tuple-element.137, s32[]{:T(128)} %get-tuple-element.128), kind=kOutput, calls=%fused_computation.88.clone.1 | convolution fusion | flops 171703808 | bytes 6949376 | tf_op jit(solution)/shard_map/while/body/eval_jaxpr/qd,kd->qk/dot_general | solution.py:114
  97.5 3.0 %convolution_convert_fusion = bf16[512,2048]{1,0:T(8,128)(2,1)} fusion(bf16[512,256]{0,1:T(8,128)(2,1)} %bitcast.16, bf16[1,256,2048]{2,1,0:T(8,128)(2,1)S(1)} %copy-done), kind=kOutput, calls=%fused_computation.21 | convolution fusion | flops 537919488 | bytes 3407872 | tf_op jit(solution)/shard_map/dot_general | solution.py:134
  102.0 4.8 %all-to-all-start.2 = ((bf16[64,8,128]{2,1,0:T(8,128)(2,1)}), bf16[64,8,128]{2,1,0:T(8,128)(2,1)S(1)}, u32[]{:S(2)}, u32[]{:S(2)}) async-start(bf16[64,8,128]{2,1,0:T(8,128)(2,1)} %broadcast_select_fusion.1), calls=%async_computation.3 | async-start | bytes 262144 | tf_op jit(solution)/shard_map/all_to_all | solution.py:34
  111.1 7.1 %all-to-all-done.2 = bf16[64,8,128]{2,1,0:T(8,128)(2,1)S(1)} async-done(((bf16[64,8,128]{2,1,0:T(8,128)(2,1)}), bf16[64,8,128]{2,1,0:T(8,128)(2,1)S(1)}, u32[]{:S(2)}, u32[]{:S(2)}) %all-to-all-start.2) | async-done | bytes 131104 | tf_op jit(solution)/shard_map/all_to_all | solution.py:34
  118.2 4.1 %fusion.30 = bf16[1,1,2048,128]{3,2,1,0:T(8,128)(2,1)} fusion(s32[]{:T(128)S(6)} %select_n.87, bf16[512,128]{1,0:T(8,128)(2,1)S(1)} %bitcast.64, bf16[1536,128]{1,0:T(8,128)(2,1)S(1)} %fusion.33), kind=kLoop, calls=%fused_computation.37 | loop fusion | flops 2097152 | bytes 1048580 | tf_op jit(solution)/shard_map/broadcast_in_dim | solution.py:132
  122.3 14.1 %reduce-scatter.2.cloned.1.call-done = bf16[512,256]{1,0:T(8,128)(2,1)} async-done(((bf16[512,2048]{1,0:T(8,128)(2,1)}), bf16[512,256]{1,0:T(8,128)(2,1)}) %reduce-scatter.2.cloned.1.call-update) | async-done | bytes 262160 | tf_op jit(solution)/shard_map/reduce_scatter | solution.py:135
  (62 shorter events, 21.6 us)
Async XLA Ops:
  7.2 90.3 %copy-start = (bf16[1,256,2048]{2,1,0:T(8,128)(2,1)S(1)}, bf16[1,256,2048]{2,1,0:T(8,128)(2,1)}, u32[]{:S(2)}) copy-start(bf16[1,256,2048]{2,1,0:T(8,128)(2,1)} %param.15) | copy-start | bytes 3145732
  7.2 32.9 %all-gather.2.cloned.1.call-start = ((), (), s32[]{:S(2)}) async-start(), calls=%async_computation.4 | async-start | bytes 3145728 | tf_op jit(solution)/shard_map/all_gather | solution.py:54
  9.6 29.7 %all-to-all-start = ((bf16[64,16,128]{2,1,0:T(8,128)(2,1)}), bf16[64,16,128]{2,1,0:T(8,128)(2,1)S(1)}, u32[]{:S(2)}, u32[]{:S(2)}) async-start(bf16[64,16,128]{2,1,0:T(8,128)(2,1)} %bitcast.8), calls=%async_computation | async-start | bytes 524288 | tf_op jit(solution)/shard_map/all_to_all | solution.py:30
  46.1 24.4 %all-to-all-start.1 = ((bf16[64,24,128]{2,1,0:T(8,128)(2,1)}), bf16[64,24,128]{2,1,0:T(8,128)(2,1)S(1)}, u32[]{:S(2)}, u32[]{:S(2)}) async-start(bf16[64,24,128]{2,1,0:T(8,128)(2,1)} %pad_maximum_fusion.2), calls=%async_computation.1 | async-start | bytes 786432 | tf_op jit(solution)/shard_map/all_to_all | solution.py:30
  56.6 79.8 %reduce-scatter.2.cloned.1.call-start = ((), (), s32[]{:S(2)}) async-start(), calls=%async_computation.5 | async-start | bytes 2359296 | tf_op jit(solution)/shard_map/reduce_scatter | solution.py:135
  80.7 1.1 copy-start.1
  85.4 1.1 copy-start.1
  90.1 1.1 copy-start.1
  94.8 1.1 copy-start.1
  100.5 9.1 %copy-start.2 = (bf16[1,1,2048,128]{3,2,1,0:T(8,128)(2,1)S(1)}, bf16[1,1,2048,128]{3,2,1,0:T(8,128)(2,1)}, u32[]{:S(2)}) copy-start(bf16[1,1,2048,128]{3,2,1,0:T(8,128)(2,1)} %param.16) | copy-start | bytes 1572868
  102.0 16.2 %all-to-all-start.2 = ((bf16[64,8,128]{2,1,0:T(8,128)(2,1)}), bf16[64,8,128]{2,1,0:T(8,128)(2,1)S(1)}, u32[]{:S(2)}, u32[]{:S(2)}) async-start(bf16[64,8,128]{2,1,0:T(8,128)(2,1)} %broadcast_select_fusion.1), calls=%async_computation.3 | async-start | bytes 262144 | tf_op jit(solution)/shard_map/all_to_all | solution.py:34
Sparse Core Ops, SparseCore 0:
  10.1 25.6 all-gather.1
  100.6 35.7 reduce-scatter.1

commit v5 on v4

--- a/solution.py
+++ b/solution.py
@@ -45,12 +45,9 @@
 ):
     request = lax.axis_index("dp")
     groups = lax.axis_size("dp")
-    halves = lax.axis_size("tx")
-    core = lax.axis_index("tx")
     stored = cache[0, 0]
-    half_rows = stored.shape[0] // halves
-    mine = lax.dynamic_slice_in_dim(stored, core * half_rows, half_rows, axis=0)
-    spread = carry_in(mine)
+    half_rows = stored.shape[0]
+    spread = carry_in(stored)
     whole = lax.all_gather(tokens, "tx", axis=1, tiled=True)
     rows_new = whole.shape[0]
     width = whole.shape[1]
@@ -85,9 +82,8 @@
         axis=1,
     ).reshape(groups * (window_chunk + entry_chunk), lanes)
     delivered = carry_in(second).reshape(groups, window_chunk + entry_chunk, lanes)
-    window_part = delivered[:, :window_chunk].reshape(half_rows, lanes)
+    window = delivered[:, :window_chunk].reshape(half_rows, lanes)
     entry_parts = delivered[:, window_chunk:]
-    window = lax.all_gather(window_part, "tx", axis=0, tiled=True)
 
     query_cols = query_weight.shape[2]
     heads = query_cols // HEAD_SIZE

time: 144 us -> 141 us (0.979)
  waiting for transfers between devices: 30.3 us -> 40.8 us
  matrix products: 22.7 us -> 15.3 us
  blocking collectives: 6.03 us -> 0 us
  starting transfers between devices: 32.5 us -> 34.1 us
    all_to_all x2, waiting for transfers between devices: 8.42 us -> 18.4 us  [carry_in(): return lax.all_to_all(window, 'dp', split_axis=0, concat_axis=0, tiled=True)]
    all_gather x1 -> x0, blocking collectives: 6.03 us -> none  [per_device(): window = lax.all_gather(window_part, 'tx', axis=0, tiled=True)]
    all_to_all x1, starting transfers between devices: 4.8 us -> 8.7 us  [carry_out(): return lax.all_to_all(window, 'dp', split_axis=0, concat_axis=0, tiled=True)]
    dot_general x4, matrix products: 7.92 us -> 4.66 us  [one_head(): jnp.einsum('qd,kd->qk', query_rows, keys_all, preferred_element_type=jnp....]
    dot_general x4, matrix products: 6.48 us -> 3.94 us  [one_head(): summed = jnp.dot(weights, values_all, preferred_element_type=jnp.float32)]
    all_to_all x2, starting transfers between devices: 27.7 us -> 25.3 us  [carry_in(): return lax.all_to_all(window, 'dp', split_axis=0, concat_axis=0, tiled=True)]
    dynamic_slice x1 -> x0, local copies, waits for them, and re-layouts: 1.67 us -> none  [per_device(): mine = lax.dynamic_slice_in_dim(stored, core * half_rows, half_rows, axis=0)]
  transfers between devices with their start and end apart: 5 -> 5, of which waited for: 4 -> 4; matrix products, arithmetic and copies ran while one was open for 17% -> 15% of each run, Pallas kernels for 0% -> 0%
where the time goes in v5:
time: 141 us
  waiting for transfers between devices  40.8 us (29%)
  starting transfers between devices  34.1 us (24%)
  other arithmetic  20.6 us (15%)
  between operations  20.2 us (14%)
  matrix products  15.3 us (11%)
  local copies, waits for them, and re-layouts  9.51 us (7%)
    all_to_all x2, starting transfers between devices, carry_in(): return lax.all_to_all(window, 'dp', split_axis=0, concat_axis=0, tiled=True)  25.3 us
    all_to_all x2, waiting for transfers between devices, carry_in(): return lax.all_to_all(window, 'dp', split_axis=0, concat_axis=0, tiled=True)  18.4 us
    reduce_scatter x1, waiting for transfers between devices, per_device(): lax.psum_scatter(partial_value.astype(jnp.bfloat16), ('tx', 'ty'), scatte...  14.4 us
    all_to_all x1, starting transfers between devices, carry_out(): return lax.all_to_all(window, 'dp', split_axis=0, concat_axis=0, tiled=True)  8.7 us
    all_to_all x1, waiting for transfers between devices, carry_out(): return lax.all_to_all(window, 'dp', split_axis=0, concat_axis=0, tiled=True)  7.3 us
    dot_general x4, matrix products, one_head(): jnp.einsum('qd,kd->qk', query_rows, keys_all, preferred_element_type=jnp....  4.66 us
    broadcast_in_dim x1, other arithmetic, per_device(): new_cache = updated[None, None]  4.12 us
    dot_general x4, matrix products, one_head(): summed = jnp.dot(weights, values_all, preferred_element_type=jnp.float32)  3.94 us
  transfers between devices with their start and end apart: 5, of which 4 were waited for; matrix products, arithmetic and copies ran while one was open for 15% of the time, Pallas kernels for 0%

profile of v5, /device:TPU:1, one launch (start us, length us, event | category | flops | bytes accessed | tf_op | source)
XLA Modules:
  0.0 140.6 jit_solution(9416224815407990209)
XLA Ops:
  7.9 17.1 %all-to-all-start = ((bf16[64,32,128]{2,1,0:T(8,128)(2,1)}), bf16[64,32,128]{2,1,0:T(8,128)(2,1)S(1)}, u32[]{:S(2)}, u32[]{:S(2)}) async-start(bf16[64,32,128]{2,1,0:T(8,128)(2,1)} %bitcast.61), calls=%async_computation | async-start | bytes 1048576 | tf_op jit(solution)/shard_map/all_to_all | solution.py:30
  32.5 8.9 %all-to-all-done = bf16[64,32,128]{2,1,0:T(8,128)(2,1)S(1)} async-done(((bf16[64,32,128]{2,1,0:T(8,128)(2,1)}), bf16[64,32,128]{2,1,0:T(8,128)(2,1)S(1)}, u32[]{:S(2)}, u32[]{:S(2)}) %all-to-all-start) | async-done | bytes 524320 | tf_op jit(solution)/shard_map/all_to_all | solution.py:30
  42.3 2.2 %fusion.20 = f32[512]{0:T(512)S(1)} fusion(bf16[512,2048]{1,0:T(8,128)(2,1)} %all-gather.2.cloned.1.call-done), kind=kLoop, calls=%fused_computation.18 | loop fusion | flops 3145216 | bytes 2099200 | tf_op jit(solution)/shard_map/reduce_sum | solution.py:56
  44.5 2.0 %fusion.25 = f32[512,128]{0,1:T(8,128)S(1)} fusion(bf16[512,2048]{1,0:T(8,128)(2,1)S(1)} %copy-done.2, f32[512]{0:T(512)S(1)} %add_rsqrt_fusion, bf16[2048,1,128]{2,0,1:T(8,128)(2,1)} %param.14), kind=kOutput, calls=%fused_computation.32 | convolution fusion | flops 271581184 | bytes 2885632 | tf_op jit(solution)/shard_map/dot_general | solution.py:63
  47.9 8.2 %all-to-all-start.1 = ((bf16[64,40,128]{2,1,0:T(8,128)(2,1)}), bf16[64,40,128]{2,1,0:T(8,128)(2,1)}, u32[]{:S(2)}, u32[]{:S(2)}) async-start(bf16[64,40,128]{2,1,0:T(8,128)(2,1)} %pad_maximum_fusion), calls=%async_computation.1 | async-start | bytes 1310720 | tf_op jit(solution)/shard_map/all_to_all | solution.py:30
  56.9 1.4 %copy.20 = bf16[2048,1,256]{0,2,1:T(8,128)(2,1)} copy(bf16[2048,1,256]{2,0,1:T(8,128)(2,1)S(1)} %copy-done.4) | data formatting | bytes 2097152 | tf_op args[1]
  59.3 1.1 pad_add_fusion
  61.9 2.7 %fusion.22 = f32[512,4,64]{0,2,1:T(8,128)S(1)} fusion(bf16[4,64,2048]{2,1,0:T(8,128)(2,1)} %bitcast.63, bf16[512,2048]{1,0:T(8,128)(2,1)} %all-gather.2.cloned.1.call-done, f32[512]{0:T(512)S(1)} %add_rsqrt_fusion), kind=kOutput, calls=%fused_computation.22 | convolution fusion | flops 540016640 | bytes 3672064 | tf_op jit(solution)/shard_map/dot_general | solution.py:90
  64.8 9.5 %all-to-all-done.1 = bf16[64,40,128]{2,1,0:T(8,128)(2,1)} async-done(((bf16[64,40,128]{2,1,0:T(8,128)(2,1)}), bf16[64,40,128]{2,1,0:T(8,128)(2,1)}, u32[]{:S(2)}, u32[]{:S(2)}) %all-to-all-start.1) | async-done | bytes 655392 | tf_op jit(solution)/shard_map/all_to_all | solution.py:30
  74.3 1.1 slice.55
  75.6 2.1 %pad_maximum_fusion.1 = (bf16[2560,64]{1,0:T(8,128)(2,1)S(1)}, bf16[2560,64]{1,0:T(8,128)(2,1)}) fusion(bf16[512,64]{1,0:T(8,128)(2,1)} %copy.22, bf16[2048,64]{1,0:T(8,128)(2,1)S(1)} %get-tuple-element.71, bf16[512,64]{1,0:T(8,128)(2,1)} %copy.23, bf16[2048,64]{1,0:T(8,128)(2,1)S(1)} %get-tuple-element.70), kind=kLoop, calls=%fused_computation.34 | loop fusion | flops 1310720 | bytes 1310720 | tf_op jit(solution)/shard_map/concatenate | solution.py:105
  77.6 13.1 %while.10 = (s32[]{:T(128)}, bf16[4,512,64]{1,2,0:T(8,128)(2,1)S(1)}, bf16[4,512,64]{1,2,0:T(8,128)(2,1)S(1)}, bf16[2560,64]{1,0:T(8,128)(2,1)S(1)}, pred[512,25...) while((s32[]{:T(128)}, bf16[4,512,64]{1,2,0:T(8,128)(2,1)S(1)}, ...), condition=%wide.region_4.5_spmd, body=%wide.region_1.4_spmd.sunk | while | flops 344783872 | bytes 19802232 | solution.py:121
  77.6 1.2 fusion.66
  79.9 1.0 fusion.68
  80.9 1.2 fusion.66
  84.2 1.2 fusion.66
  86.4 1.0 fusion.68
  87.4 1.2 fusion.66
  90.7 2.1 %convolution_convert_fusion = bf16[512,2048]{1,0:T(8,128)(2,1)} fusion(bf16[512,256]{0,1:T(8,128)(2,1)S(1)} %bitcast.64, bf16[1,256,2048]{2,1,0:T(8,128)(2,1)S(1)} %copy-done), kind=kOutput, calls=%fused_computation.21 | convolution fusion | flops 537919488 | bytes 3407872 | tf_op jit(solution)/shard_map/dot_general | solution.py:130
  95.2 8.7 %all-to-all-start.2 = ((bf16[64,8,128]{2,1,0:T(8,128)(2,1)}), bf16[64,8,128]{2,1,0:T(8,128)(2,1)S(1)}, u32[]{:S(2)}, u32[]{:S(2)}) async-start(bf16[64,8,128]{2,1,0:T(8,128)(2,1)} %broadcast_select_fusion.1), calls=%async_computation.3 | async-start | bytes 262144 | tf_op jit(solution)/shard_map/all_to_all | solution.py:34
  106.5 1.5 %fusion.33 = bf16[1536,128]{1,0:T(8,128)(2,1)S(1)} fusion(s32[]{:T(128)S(6)} %add.121, bf16[2048,128]{1,0:T(8,128)(2,1)S(1)} %bitcast.62), kind=kLoop, calls=%fused_computation.42 | loop fusion | flops 786432 | bytes 917508 | tf_op jit(solution)/shard_map/jit(_roll_dynamic)/concatenate | solution.py:126
  108.0 7.3 %all-to-all-done.2 = bf16[64,8,128]{2,1,0:T(8,128)(2,1)S(1)} async-done(((bf16[64,8,128]{2,1,0:T(8,128)(2,1)}), bf16[64,8,128]{2,1,0:T(8,128)(2,1)S(1)}, u32[]{:S(2)}, u32[]{:S(2)}) %all-to-all-start.2) | async-done | bytes 131104 | tf_op jit(solution)/shard_map/all_to_all | solution.py:34
  115.3 4.1 %fusion.30 = bf16[1,1,2048,128]{3,2,1,0:T(8,128)(2,1)} fusion(s32[]{:T(128)S(6)} %select_n.83, bf16[512,128]{1,0:T(8,128)(2,1)S(1)} %bitcast.66, bf16[1536,128]{1,0:T(8,128)(2,1)S(1)} %fusion.33), kind=kLoop, calls=%fused_computation.38 | loop fusion | flops 2097152 | bytes 1048580 | tf_op jit(solution)/shard_map/broadcast_in_dim | solution.py:128
  119.4 14.4 %reduce-scatter.2.cloned.1.call-done = bf16[512,256]{1,0:T(8,128)(2,1)} async-done(((bf16[512,2048]{1,0:T(8,128)(2,1)}), bf16[512,256]{1,0:T(8,128)(2,1)}) %reduce-scatter.2.cloned.1.call-update) | async-done | bytes 262160 | tf_op jit(solution)/shard_map/reduce_scatter | solution.py:131
  (76 shorter events, 19.4 us)
Async XLA Ops:
  7.2 83.5 %copy-start = (bf16[1,256,2048]{2,1,0:T(8,128)(2,1)S(1)}, bf16[1,256,2048]{2,1,0:T(8,128)(2,1)}, u32[]{:S(2)}) copy-start(bf16[1,256,2048]{2,1,0:T(8,128)(2,1)} %param.15) | copy-start | bytes 3145732
  7.2 17.9 %copy-start.10 = (s32[64]{0:T(128)S(1)}, s32[64]{0:T(128)}, u32[]{:S(2)}) copy-start(s32[64]{0:T(128)} %param.19) | copy-start | bytes 772
  7.2 19.9 %copy-start.9 = (s32[64]{0:T(128)S(1)}, s32[64]{0:T(128)}, u32[]{:S(2)}) copy-start(s32[64]{0:T(128)} %param.17) | copy-start | bytes 772
  7.2 21.8 %copy-start.8 = (s32[64]{0:T(128)S(1)}, s32[64]{0:T(128)}, u32[]{:S(2)}) copy-start(s32[64]{0:T(128)} %param.18) | copy-start | bytes 772
  7.2 35.1 %all-gather.2.cloned.1.call-start = ((), (), s32[]{:S(2)}) async-start(), calls=%async_computation.4 | async-start | bytes 3145728 | tf_op jit(solution)/shard_map/all_gather | solution.py:51
  7.9 33.5 %all-to-all-start = ((bf16[64,32,128]{2,1,0:T(8,128)(2,1)}), bf16[64,32,128]{2,1,0:T(8,128)(2,1)S(1)}, u32[]{:S(2)}, u32[]{:S(2)}) async-start(bf16[64,32,128]{2,1,0:T(8,128)(2,1)} %bitcast.61), calls=%async_computation | async-start | bytes 1048576 | tf_op jit(solution)/shard_map/all_to_all | solution.py:30
  42.3 2.2 %copy-start.2 = (bf16[512,2048]{1,0:T(8,128)(2,1)S(1)}, bf16[512,2048]{1,0:T(8,128)(2,1)}, u32[]{:S(2)}) copy-start(bf16[512,2048]{1,0:T(8,128)(2,1)} %all-gather.2.cloned.1.call-done) | copy-start | bytes 6291460
  47.9 9.0 %copy-start.4 = (bf16[2048,1,256]{2,0,1:T(8,128)(2,1)S(1)}, bf16[2048,1,256]{2,0,1:T(8,128)(2,1)}, u32[]{:S(2)}) copy-start(bf16[2048,1,256]{2,0,1:T(8,128)(2,1)} %param.13) | copy-start | bytes 3145732
  47.9 26.3 %all-to-all-start.1 = ((bf16[64,40,128]{2,1,0:T(8,128)(2,1)}), bf16[64,40,128]{2,1,0:T(8,128)(2,1)}, u32[]{:S(2)}, u32[]{:S(2)}) async-start(bf16[64,40,128]{2,1,0:T(8,128)(2,1)} %pad_maximum_fusion), calls=%async_computation.1 | async-start | bytes 1310720 | tf_op jit(solution)/shard_map/all_to_all | solution.py:30
  56.1 77.6 %reduce-scatter.2.cloned.1.call-start = ((), (), s32[]{:S(2)}) async-start(), calls=%async_computation.5 | async-start | bytes 2359296 | tf_op jit(solution)/shard_map/reduce_scatter | solution.py:131
  61.9 2.7 %copy-start.6 = (f32[512,32]{0,1:T(8,128)S(1)}, f32[512,32]{0,1:T(8,128)}, u32[]{:S(2)}) copy-start(f32[512,32]{0,1:T(8,128)} %get-tuple-element.74) | copy-start | bytes 196612
  61.9 2.7 %copy-start.7 = (f32[512,32]{0,1:T(8,128)S(1)}, f32[512,32]{0,1:T(8,128)}, u32[]{:S(2)}) copy-start(f32[512,32]{0,1:T(8,128)} %get-tuple-element.75) | copy-start | bytes 196612
  75.3 2.3 %copy-start.5 = (bf16[4,512,64]{1,2,0:T(8,128)(2,1)S(1)}, bf16[4,512,64]{1,2,0:T(8,128)(2,1)}, u32[]{:S(2)}) copy-start(bf16[4,512,64]{1,2,0:T(8,128)(2,1)} %custom-call.4) | copy-start | bytes 786436
  78.8 1.1 copy-start.1
  82.1 1.1 copy-start.1
  85.3 1.1 copy-start.1
  88.6 1.1 copy-start.1
  92.8 13.7 %copy-start.3 = (bf16[1,1,2048,128]{3,2,1,0:T(8,128)(2,1)S(1)}, bf16[1,1,2048,128]{3,2,1,0:T(8,128)(2,1)}, u32[]{:S(2)}) copy-start(bf16[1,1,2048,128]{3,2,1,0:T(8,128)(2,1)} %param.16) | copy-start | bytes 1572868
  95.2 20.0 %all-to-all-start.2 = ((bf16[64,8,128]{2,1,0:T(8,128)(2,1)}), bf16[64,8,128]{2,1,0:T(8,128)(2,1)S(1)}, u32[]{:S(2)}, u32[]{:S(2)}) async-start(bf16[64,8,128]{2,1,0:T(8,128)(2,1)} %broadcast_select_fusion.1), calls=%async_computation.3 | async-start | bytes 262144 | tf_op jit(solution)/shard_map/all_to_all | solution.py:34
Sparse Core Ops, SparseCore 0:
  10.1 25.6 all-gather.1
  92.9 40.7 reduce-scatter.1

commit v6 on v5

--- a/solution.py
+++ b/solution.py
@@ -3,6 +3,7 @@
 import jax
 import jax.numpy as jnp
 from jax import lax
+from jax.experimental import pallas as pl
 from jax.sharding import PartitionSpec as P
 
 HEAD_SIZE = 64
@@ -24,6 +25,56 @@
     return jnp.concatenate(
         [leading * cosine - trailing * sine, trailing * cosine + leading * sine], axis=-1
     )
+
+
+def attention_kernel(q_ref, win_ref, ent_ref, lim_ref, age_ref, o_ref):
+    rows = q_ref.shape[1]
+    block = pl.program_id(0)
+    factor = 1.0 / math.sqrt(HEAD_SIZE)
+    q = q_ref[0]
+    win = win_ref[...]
+    ent = ent_ref[...]
+    dims = (((1,), (1,)), ((), ()))
+    s_old = lax.dot_general(q, win, dims, preferred_element_type=jnp.float32) * factor
+    s_new = lax.dot_general(q, ent, dims, preferred_element_type=jnp.float32) * factor
+    s_old = jnp.where(age_ref[...] < lim_ref[...], s_old, -jnp.inf)
+    row_ids = block * rows + lax.broadcasted_iota(jnp.int32, s_new.shape, 0)
+    col_ids = lax.broadcasted_iota(jnp.int32, s_new.shape, 1)
+    s_new = jnp.where(col_ids <= row_ids, s_new, -jnp.inf)
+    top = jnp.maximum(jnp.max(s_old, axis=1, keepdims=True), jnp.max(s_new, axis=1, keepdims=True))
+    p_old = jnp.exp(s_old - top)
+    p_new = jnp.exp(s_new - top)
+    total = jnp.sum(p_old, axis=1, keepdims=True) + jnp.sum(p_new, axis=1, keepdims=True)
+    acc = jnp.dot(p_old.astype(jnp.bfloat16), win, preferred_element_type=jnp.float32)
+    acc = acc + jnp.dot(p_new.astype(jnp.bfloat16), ent, preferred_element_type=jnp.float32)
+    o_ref[0] = (acc / total).astype(o_ref.dtype)
+
+
+def attend(query_rotated, window, entry, length, offset):
+    rows_new, heads, _ = query_rotated.shape
+    lanes = window.shape[1]
+    padded = jnp.concatenate(
+        [jnp.transpose(query_rotated, (1, 0, 2)),
+         jnp.zeros((heads, rows_new, lanes - HEAD_SIZE), query_rotated.dtype)], axis=2)
+    rows = jnp.arange(rows_new, dtype=jnp.int32)
+    limit = jnp.minimum(length, WINDOW_LENGTH - 1 - rows)[:, None]
+    cycle = jnp.arange(window.shape[0], dtype=jnp.int32)
+    age = jnp.mod(offset - 1 - cycle, WINDOW_LENGTH)[None, :]
+    block = 128
+    out = pl.pallas_call(
+        attention_kernel,
+        grid=(rows_new // block, heads),
+        in_specs=[
+            pl.BlockSpec((1, block, lanes), lambda b, h: (h, b, 0)),
+            pl.BlockSpec(window.shape, lambda b, h: (0, 0)),
+            pl.BlockSpec(entry.shape, lambda b, h: (0, 0)),
+            pl.BlockSpec((block, 1), lambda b, h: (b, 0)),
+            pl.BlockSpec((1, window.shape[0]), lambda b, h: (0, 0)),
+        ],
+        out_specs=pl.BlockSpec((1, block, lanes), lambda b, h: (h, b, 0)),
+        out_shape=jax.ShapeDtypeStruct((heads, rows_new, lanes), jnp.bfloat16),
+    )(padded, window, entry, limit, age)
+    return jnp.transpose(out[:, :, HEAD_SIZE:], (1, 0, 2)).reshape(rows_new, heads * HEAD_SIZE)
 
 
 def carry_in(window):
@@ -95,31 +146,7 @@
     query_rotated = apply_rotary(
         queries.reshape(rows_new, heads, HEAD_SIZE), token_positions
     ).astype(jnp.bfloat16)
-    factor = 1.0 / math.sqrt(HEAD_SIZE)
-    rows = jnp.arange(rows_new, dtype=jnp.int32)
-    new_mask = rows[None, :] <= rows[:, None]
-    cycle = jnp.arange(WINDOW_LENGTH, dtype=jnp.int32)
-    held = length - 1 - jnp.mod(offset - 1 - cycle, WINDOW_LENGTH)
-    cache_mask = (held[None, :] >= 0) & (held[None, :] > token_positions[:, None] - WINDOW_LENGTH)
-    mask_all = jnp.concatenate([cache_mask, new_mask], axis=1)
-    keys_all = jnp.concatenate([window[:, :HEAD_SIZE], new_keys], axis=0)
-    values_all = jnp.concatenate([window[:, HEAD_SIZE:], new_values], axis=0)
-
-    def one_head(query_rows):
-        scores = (
-            jnp.einsum("qd,kd->qk", query_rows, keys_all, preferred_element_type=jnp.float32)
-            * factor
-        )
-        scores = jnp.where(mask_all, scores, -jnp.inf)
-        top = jnp.max(scores, axis=1, keepdims=True)
-        powers = jnp.exp(scores - top)
-        total = jnp.sum(powers, axis=1, keepdims=True)
-        weights = powers.astype(jnp.bfloat16)
-        summed = jnp.dot(weights, values_all, preferred_element_type=jnp.float32)
-        return (summed / total).astype(jnp.bfloat16)
-
-    outputs = lax.map(one_head, jnp.transpose(query_rotated, (1, 0, 2)))
-    attended = jnp.transpose(outputs, (1, 0, 2)).reshape(rows_new, heads * HEAD_SIZE)
+    attended = attend(query_rotated, window, entry, length, offset)
 
     arrived = carry_out(jnp.take(entry_parts, inverse, axis=0).reshape(rows_new, lanes))
     own_offset = offsets[inverse[request]]

time: 141 us -> 142 us (level)
  Pallas kernels: 0 us -> 16 us
  matrix products: 15.3 us -> 5.98 us
  other arithmetic: 20.6 us -> 16.4 us
  local copies, waits for them, and re-layouts: 9.51 us -> 7.86 us
    pallas_call x0 -> x1, Pallas kernels: none -> 16 us  [attend(): pl.pallas_call(attention_kernel, grid=(rows_new // block, heads), in_spec...]
    dot_general x8 -> x0, matrix products: 8.6 us -> none  [the longest x4 4.66 us: one_head(): jnp.einsum('qd,kd->qk', query_rows, keys_all, preferred_element_type=jnp....]
    reduce_sum x4 -> x0, other arithmetic: 3.36 us -> none  [one_head(): total = jnp.sum(powers, axis=1, keepdims=True)]
    concatenate x2 -> x0, other arithmetic: 3.13 us -> none  [the longest x1 2.07 us: per_device(): keys_all = jnp.concatenate([window[:, :HEAD_SIZE], new_keys], axis=0)]
    transpose x0 -> x2, local copies, waits for them, and re-layouts: none -> 1.44 us  [attend(): jnp.transpose(out[:, :, HEAD_SIZE:], (1, 0, 2))]
  transfers between devices with their start and end apart: 5 -> 5, of which waited for: 4 -> 4; matrix products, arithmetic and copies ran while one was open for 15% -> 14% of each run, Pallas kernels for 0% -> 0%
where the time goes in v6:
time: 142 us
  waiting for transfers between devices  42 us (30%)
  starting transfers between devices  34 us (24%)
  between operations  19.5 us (14%)
  other arithmetic  16.4 us (12%)
  Pallas kernels  16 us (11%)
  local copies, waits for them, and re-layouts  7.86 us (6%)
  matrix products  5.98 us (4%)
    all_to_all x2, starting transfers between devices, carry_in(): return lax.all_to_all(window, 'dp', split_axis=0, concat_axis=0, tiled=True)  24.9 us
    all_to_all x2, waiting for transfers between devices, carry_in(): return lax.all_to_all(window, 'dp', split_axis=0, concat_axis=0, tiled=True)  19.3 us
    pallas_call x1, Pallas kernels, attend(): pl.pallas_call(attention_kernel, grid=(rows_new // block, heads), in_spec...  16 us
    reduce_scatter x1, waiting for transfers between devices, per_device(): lax.psum_scatter(partial_value.astype(jnp.bfloat16), ('tx', 'ty'), scatte...  14.7 us
    all_to_all x1, starting transfers between devices, carry_out(): return lax.all_to_all(window, 'dp', split_axis=0, concat_axis=0, tiled=True)  9.01 us
    all_to_all x1, waiting for transfers between devices, carry_out(): return lax.all_to_all(window, 'dp', split_axis=0, concat_axis=0, tiled=True)  7.25 us
    broadcast_in_dim x1, other arithmetic, per_device(): new_cache = updated[None, None]  4.12 us
    dot_general x1, matrix products, per_device(): jnp.dot(normalized_input, query_weight.reshape(width, query_cols), prefer...  3.15 us
  transfers between devices with their start and end apart: 5, of which 4 were waited for; matrix products, arithmetic and copies ran while one was open for 14% of the time, Pallas kernels for 0%

profile of v6, /device:TPU:1, one launch (start us, length us, event | category | flops | bytes accessed | tf_op | source)
XLA Modules:
  0.0 141.7 jit_solution(17525356332853300084)
XLA Ops:
  7.9 17.1 %all-to-all-start = ((bf16[64,32,128]{2,1,0:T(8,128)(2,1)}), bf16[64,32,128]{2,1,0:T(8,128)(2,1)S(1)}, u32[]{:S(2)}, u32[]{:S(2)}) async-start(bf16[64,32,128]{2,1,0:T(8,128)(2,1)} %bitcast.41), calls=%async_computation | async-start | bytes 1048576 | tf_op jit(solution)/shard_map/all_to_all | solution.py:81
  30.4 11.1 %all-to-all-done = bf16[64,32,128]{2,1,0:T(8,128)(2,1)S(1)} async-done(((bf16[64,32,128]{2,1,0:T(8,128)(2,1)}), bf16[64,32,128]{2,1,0:T(8,128)(2,1)S(1)}, u32[]{:S(2)}, u32[]{:S(2)}) %all-to-all-start) | async-done | bytes 524320 | tf_op jit(solution)/shard_map/all_to_all | solution.py:81
  42.3 2.2 %fusion = f32[512]{0:T(512)S(1)} fusion(bf16[512,2048]{1,0:T(8,128)(2,1)} %all-gather.2.cloned.1.call-done), kind=kLoop, calls=%fused_computation.4 | loop fusion | flops 3145216 | bytes 2099200 | tf_op jit(solution)/shard_map/reduce_sum | solution.py:107
  44.5 0.8 fusion.5
  45.5 1.2 fusion.19
  46.9 0.9 pad_maximum_fusion
  47.8 7.8 %all-to-all-start.1 = ((bf16[64,40,128]{2,1,0:T(8,128)(2,1)}), bf16[64,40,128]{2,1,0:T(8,128)(2,1)S(1)}, u32[]{:S(2)}, u32[]{:S(2)}) async-start(bf16[64,40,128]{2,1,0:T(8,128)(2,1)} %pad_maximum_fusion), calls=%async_computation.1 | async-start | bytes 1310720 | tf_op jit(solution)/shard_map/all_to_all | solution.py:81
  56.3 1.4 %copy.27 = bf16[2048,1,256]{0,2,1:T(8,128)(2,1)} copy(bf16[2048,1,256]{2,0,1:T(8,128)(2,1)S(1)} %copy-done.3) | data formatting | bytes 2097152 | tf_op args[1]
  57.7 1.4 subtract_minimum_fusion.lim_ref
  59.1 1.0 multiply_cosine_fusion.1
  60.1 3.1 %fusion.2 = f32[512,4,64]{2,0,1:T(8,128)S(1)} fusion(bf16[4,64,2048]{2,1,0:T(8,128)(2,1)} %bitcast.45, bf16[512,2048]{1,0:T(8,128)(2,1)} %all-gather.2.cloned.1.call-done, f32[512]{0:T(512)S(1)} %add_rsqrt_fusion), kind=kOutput, calls=%fused_computation.7 | convolution fusion | flops 540016640 | bytes 3672064 | tf_op jit(solution)/shard_map/dot_general | solution.py:141
  64.0 0.9 concatenate.24.q_ref
  64.9 0.8 pad_maximum_fusion.1.ent_ref
  65.7 8.2 %all-to-all-done.1 = bf16[64,40,128]{2,1,0:T(8,128)(2,1)S(1)} async-done(((bf16[64,40,128]{2,1,0:T(8,128)(2,1)}), bf16[64,40,128]{2,1,0:T(8,128)(2,1)S(1)}, u32[]{:S(2)}, u32[]{:S(2)}) %all-to-all-start.1) | async-done | bytes 655392 | tf_op jit(solution)/shard_map/all_to_all | solution.py:81
  73.9 0.8 slice.51
  74.7 16.0 %shard_map.95 = bf16[4,512,128]{2,1,0:T(8,128)(2,1)} custom-call(bf16[4,512,128]{2,1,0:T(8,128)(2,1)} %concatenate.24.q_ref, bf16[2048,128]{1,0:T(8,128)(2,1)} %bitcast.43, bf16[512,128]{1,0:T(8,128)(2,1)} %pad_maximum_fusion.1.ent_ref, s32[512,1]{1,0:T(8,128)} %subtract_minimum_fusion.lim_ref, s32[1,2048]{1,0:T(1,128)} %and_select_fusion.age_ref), custom_call_target="tpu_custom_call" | custom-call | tf_op jit(solution)/shard_map/pallas_call | solution.py:64
  90.7 1.2 slice_bitcast_fusion
  92.1 2.1 %convolution_convert_fusion = bf16[512,2048]{1,0:T(8,128)(2,1)} fusion(bf16[512,256]{0,1:T(8,128)(2,1)S(1)} %bitcast.44, bf16[1,256,2048]{2,1,0:T(8,128)(2,1)S(1)} %copy-done), kind=kOutput, calls=%fused_computation.6 | convolution fusion | flops 537919488 | bytes 3407872 | tf_op jit(solution)/shard_map/dot_general | solution.py:157
  94.9 0.8 broadcast_select_fusion.1
  95.7 9.0 %all-to-all-start.2 = ((bf16[64,8,128]{2,1,0:T(8,128)(2,1)}), bf16[64,8,128]{2,1,0:T(8,128)(2,1)S(1)}, u32[]{:S(2)}, u32[]{:S(2)}) async-start(bf16[64,8,128]{2,1,0:T(8,128)(2,1)} %broadcast_select_fusion.1), calls=%async_computation.3 | async-start | bytes 262144 | tf_op jit(solution)/shard_map/all_to_all | solution.py:85
  107.3 1.5 %fusion.13 = bf16[1536,128]{1,0:T(8,128)(2,1)S(1)} fusion(s32[]{:T(128)S(6)} %add.112, bf16[2048,128]{1,0:T(8,128)(2,1)S(1)} %bitcast.42), kind=kLoop, calls=%fused_computation.28 | loop fusion | flops 786432 | bytes 917508 | tf_op jit(solution)/shard_map/jit(_roll_dynamic)/concatenate | solution.py:153
  108.8 7.3 %all-to-all-done.2 = bf16[64,8,128]{2,1,0:T(8,128)(2,1)S(1)} async-done(((bf16[64,8,128]{2,1,0:T(8,128)(2,1)}), bf16[64,8,128]{2,1,0:T(8,128)(2,1)S(1)}, u32[]{:S(2)}, u32[]{:S(2)}) %all-to-all-start.2) | async-done | bytes 131104 | tf_op jit(solution)/shard_map/all_to_all | solution.py:85
  116.1 4.1 %fusion.10 = bf16[1,1,2048,128]{3,2,1,0:T(8,128)(2,1)} fusion(s32[]{:T(128)S(6)} %select_n.79, bf16[512,128]{1,0:T(8,128)(2,1)S(1)} %bitcast.46, bf16[1536,128]{1,0:T(8,128)(2,1)S(1)} %fusion.13), kind=kLoop, calls=%fused_computation.22 | loop fusion | flops 2097152 | bytes 1048580 | tf_op jit(solution)/shard_map/broadcast_in_dim | solution.py:155
  120.2 14.7 %reduce-scatter.2.cloned.1.call-done = bf16[512,256]{1,0:T(8,128)(2,1)} async-done(((bf16[512,2048]{1,0:T(8,128)(2,1)}), bf16[512,256]{1,0:T(8,128)(2,1)}) %reduce-scatter.2.cloned.1.call-update) | async-done | bytes 262160 | tf_op jit(solution)/shard_map/reduce_scatter | solution.py:158
  (46 shorter events, 6.8 us)
Async XLA Ops:
  7.2 85.0 %copy-start = (bf16[1,256,2048]{2,1,0:T(8,128)(2,1)S(1)}, bf16[1,256,2048]{2,1,0:T(8,128)(2,1)}, u32[]{:S(2)}) copy-start(bf16[1,256,2048]{2,1,0:T(8,128)(2,1)} %param.13) | copy-start | bytes 3145732
  7.2 17.9 %copy-start.7 = (s32[64]{0:T(128)S(1)}, s32[64]{0:T(128)}, u32[]{:S(2)}) copy-start(s32[64]{0:T(128)} %param.17) | copy-start | bytes 772
  7.2 19.9 %copy-start.6 = (s32[64]{0:T(128)S(1)}, s32[64]{0:T(128)}, u32[]{:S(2)}) copy-start(s32[64]{0:T(128)} %param.15) | copy-start | bytes 772
  7.2 21.2 %copy-start.4 = (s32[64]{0:T(128)S(1)}, s32[64]{0:T(128)}, u32[]{:S(2)}) copy-start(s32[64]{0:T(128)} %param.16) | copy-start | bytes 772
  7.2 35.1 %all-gather.2.cloned.1.call-start = ((), (), s32[]{:S(2)}) async-start(), calls=%async_computation.4 | async-start | bytes 3145728 | tf_op jit(solution)/shard_map/all_gather | solution.py:102
  7.9 33.5 %all-to-all-start = ((bf16[64,32,128]{2,1,0:T(8,128)(2,1)}), bf16[64,32,128]{2,1,0:T(8,128)(2,1)S(1)}, u32[]{:S(2)}, u32[]{:S(2)}) async-start(bf16[64,32,128]{2,1,0:T(8,128)(2,1)} %bitcast.41), calls=%async_computation | async-start | bytes 1048576 | tf_op jit(solution)/shard_map/all_to_all | solution.py:81
  30.4 14.2 %copy-start.5 = (bf16[2048,1,128]{2,0,1:T(8,128)(2,1)S(1)}, bf16[2048,1,128]{2,0,1:T(8,128)(2,1)}, u32[]{:S(2)}) copy-start(bf16[2048,1,128]{2,0,1:T(8,128)(2,1)} %param.12) | copy-start | bytes 1572868
  42.3 2.3 %copy-start.1 = (bf16[512,2048]{1,0:T(8,128)(2,1)S(1)}, bf16[512,2048]{1,0:T(8,128)(2,1)}, u32[]{:S(2)}) copy-start(bf16[512,2048]{1,0:T(8,128)(2,1)} %all-gather.2.cloned.1.call-done) | copy-start | bytes 6291460
  45.4 10.9 %copy-start.3 = (bf16[2048,1,256]{2,0,1:T(8,128)(2,1)S(1)}, bf16[2048,1,256]{2,0,1:T(8,128)(2,1)}, u32[]{:S(2)}) copy-start(bf16[2048,1,256]{2,0,1:T(8,128)(2,1)} %param.11) | copy-start | bytes 3145732
  47.8 26.1 %all-to-all-start.1 = ((bf16[64,40,128]{2,1,0:T(8,128)(2,1)}), bf16[64,40,128]{2,1,0:T(8,128)(2,1)S(1)}, u32[]{:S(2)}, u32[]{:S(2)}) async-start(bf16[64,40,128]{2,1,0:T(8,128)(2,1)} %pad_maximum_fusion), calls=%async_computation.1 | async-start | bytes 1310720 | tf_op jit(solution)/shard_map/all_to_all | solution.py:81
  55.6 79.3 %reduce-scatter.2.cloned.1.call-start = ((), (), s32[]{:S(2)}) async-start(), calls=%async_computation.5 | async-start | bytes 2359296 | tf_op jit(solution)/shard_map/reduce_scatter | solution.py:158
  94.2 13.1 %copy-start.2 = (bf16[1,1,2048,128]{3,2,1,0:T(8,128)(2,1)S(1)}, bf16[1,1,2048,128]{3,2,1,0:T(8,128)(2,1)}, u32[]{:S(2)}) copy-start(bf16[1,1,2048,128]{3,2,1,0:T(8,128)(2,1)} %param.14) | copy-start | bytes 1572868
  95.7 20.3 %all-to-all-start.2 = ((bf16[64,8,128]{2,1,0:T(8,128)(2,1)}), bf16[64,8,128]{2,1,0:T(8,128)(2,1)S(1)}, u32[]{:S(2)}, u32[]{:S(2)}) async-start(bf16[64,8,128]{2,1,0:T(8,128)(2,1)} %broadcast_select_fusion.1), calls=%async_computation.3 | async-start | bytes 262144 | tf_op jit(solution)/shard_map/all_to_all | solution.py:85
Sparse Core Ops, SparseCore 0:
  10.1 25.6 all-gather.1
  94.3 40.4 reduce-scatter.1

commit v7 on v6

--- a/solution.py
+++ b/solution.py
@@ -27,16 +27,14 @@
     )
 
 
-def attention_kernel(q_ref, win_ref, ent_ref, lim_ref, age_ref, o_ref):
+def attention_kernel(q_ref, win_ref, ent_ref, win_t_ref, ent_t_ref, lim_ref, age_ref, o_ref):
     rows = q_ref.shape[1]
     block = pl.program_id(0)
-    factor = 1.0 / math.sqrt(HEAD_SIZE)
     q = q_ref[0]
     win = win_ref[...]
     ent = ent_ref[...]
-    dims = (((1,), (1,)), ((), ()))
-    s_old = lax.dot_general(q, win, dims, preferred_element_type=jnp.float32) * factor
-    s_new = lax.dot_general(q, ent, dims, preferred_element_type=jnp.float32) * factor
+    s_old = jnp.dot(q, win_t_ref[...], preferred_element_type=jnp.float32)
+    s_new = jnp.dot(q, ent_t_ref[...], preferred_element_type=jnp.float32)
     s_old = jnp.where(age_ref[...] < lim_ref[...], s_old, -jnp.inf)
     row_ids = block * rows + lax.broadcasted_iota(jnp.int32, s_new.shape, 0)
     col_ids = lax.broadcasted_iota(jnp.int32, s_new.shape, 1)
@@ -53,8 +51,10 @@
 def attend(query_rotated, window, entry, length, offset):
     rows_new, heads, _ = query_rotated.shape
     lanes = window.shape[1]
+    factor = 1.0 / math.sqrt(HEAD_SIZE)
+    scaled = query_rotated * jnp.asarray(factor, query_rotated.dtype)
     padded = jnp.concatenate(
-        [jnp.transpose(query_rotated, (1, 0, 2)),
+        [jnp.transpose(scaled, (1, 0, 2)),
          jnp.zeros((heads, rows_new, lanes - HEAD_SIZE), query_rotated.dtype)], axis=2)
     rows = jnp.arange(rows_new, dtype=jnp.int32)
     limit = jnp.minimum(length, WINDOW_LENGTH - 1 - rows)[:, None]
@@ -68,12 +68,14 @@
             pl.BlockSpec((1, block, lanes), lambda b, h: (h, b, 0)),
             pl.BlockSpec(window.shape, lambda b, h: (0, 0)),
             pl.BlockSpec(entry.shape, lambda b, h: (0, 0)),
+            pl.BlockSpec((lanes, window.shape[0]), lambda b, h: (0, 0)),
+            pl.BlockSpec((lanes, entry.shape[0]), lambda b, h: (0, 0)),
             pl.BlockSpec((block, 1), lambda b, h: (b, 0)),
             pl.BlockSpec((1, window.shape[0]), lambda b, h: (0, 0)),
         ],
         out_specs=pl.BlockSpec((1, block, lanes), lambda b, h: (h, b, 0)),
         out_shape=jax.ShapeDtypeStruct((heads, rows_new, lanes), jnp.bfloat16),
-    )(padded, window, entry, limit, age)
+    )(padded, window, entry, window.T, entry.T, limit, age)
     return jnp.transpose(out[:, :, HEAD_SIZE:], (1, 0, 2)).reshape(rows_new, heads * HEAD_SIZE)
 
 

time: 142 us -> 142 us (level)
  no operation moved by 1% of the time
where the time goes in v7:
time: 142 us
  waiting for transfers between devices  43 us (30%)
  starting transfers between devices  34 us (24%)
  between operations  19.3 us (14%)
  Pallas kernels  15.8 us (11%)
  other arithmetic  15.2 us (11%)
  local copies, waits for them, and re-layouts  8.09 us (6%)
  matrix products  6.15 us (4%)
    all_to_all x2, starting transfers between devices, carry_in(): return lax.all_to_all(window, 'dp', split_axis=0, concat_axis=0, tiled=True)  24.9 us
    all_to_all x2, waiting for transfers between devices, carry_in(): return lax.all_to_all(window, 'dp', split_axis=0, concat_axis=0, tiled=True)  20.1 us
    pallas_call x1, Pallas kernels, attend(): pl.pallas_call(attention_kernel, grid=(rows_new // block, heads), in_spec...  15.8 us
    reduce_scatter x1, waiting for transfers between devices, per_device(): lax.psum_scatter(partial_value.astype(jnp.bfloat16), ('tx', 'ty'), scatte...  14.7 us
    all_to_all x1, starting transfers between devices, carry_out(): return lax.all_to_all(window, 'dp', split_axis=0, concat_axis=0, tiled=True)  9.01 us
    all_to_all x1, waiting for transfers between devices, carry_out(): return lax.all_to_all(window, 'dp', split_axis=0, concat_axis=0, tiled=True)  7.49 us
    broadcast_in_dim x1, other arithmetic, per_device(): new_cache = updated[None, None]  4.12 us
    dot_general x1, matrix products, per_device(): jnp.dot(normalized_input, query_weight.reshape(width, query_cols), prefer...  3.15 us
  transfers between devices with their start and end apart: 5, of which 4 were waited for; matrix products, arithmetic and copies ran while one was open for 14% of the time, Pallas kernels for 0%

profile of v7, /device:TPU:1, one launch (start us, length us, event | category | flops | bytes accessed | tf_op | source)
XLA Modules:
  0.0 141.6 jit_solution(17944286606354201909)
XLA Ops:
  7.2 0.7 all-gather.2.cloned.1.call-update
  7.9 17.1 %all-to-all-start = ((bf16[64,32,128]{2,1,0:T(8,128)(2,1)}), bf16[64,32,128]{2,1,0:T(8,128)(2,1)S(1)}, u32[]{:S(2)}, u32[]{:S(2)}) async-start(bf16[64,32,128]{2,1,0:T(8,128)(2,1)} %bitcast.46), calls=%async_computation | async-start | bytes 1048576 | tf_op jit(solution)/shard_map/all_to_all | solution.py:83
  26.4 1.4 subtract_minimum_fusion.lim_ref
  27.8 13.6 %all-to-all-done = bf16[64,32,128]{2,1,0:T(8,128)(2,1)S(1)} async-done(((bf16[64,32,128]{2,1,0:T(8,128)(2,1)}), bf16[64,32,128]{2,1,0:T(8,128)(2,1)S(1)}, u32[]{:S(2)}, u32[]{:S(2)}) %all-to-all-start) | async-done | bytes 524320 | tf_op jit(solution)/shard_map/all_to_all | solution.py:83
  42.3 2.2 %fusion = f32[512]{0:T(512)S(1)} fusion(bf16[512,2048]{1,0:T(8,128)(2,1)} %all-gather.2.cloned.1.call-done), kind=kLoop, calls=%fused_computation.4 | loop fusion | flops 3145216 | bytes 2099200 | tf_op jit(solution)/shard_map/reduce_sum | solution.py:109
  44.5 0.9 fusion.5
  45.9 0.7 fusion.25
  46.7 0.9 pad_maximum_fusion
  47.6 7.8 %all-to-all-start.1 = ((bf16[64,40,128]{2,1,0:T(8,128)(2,1)}), bf16[64,40,128]{2,1,0:T(8,128)(2,1)S(1)}, u32[]{:S(2)}, u32[]{:S(2)}) async-start(bf16[64,40,128]{2,1,0:T(8,128)(2,1)} %pad_maximum_fusion), calls=%async_computation.1 | async-start | bytes 1310720 | tf_op jit(solution)/shard_map/all_to_all | solution.py:83
  57.5 1.4 %copy.23 = bf16[2048,1,256]{0,2,1:T(8,128)(2,1)} copy(bf16[2048,1,256]{2,0,1:T(8,128)(2,1)S(1)} %copy-done.5) | data formatting | bytes 2097152 | tf_op args[1]
  61.4 1.0 multiply_cosine_fusion
  62.4 3.1 %fusion.2 = f32[512,4,64]{2,0,1:T(8,128)S(1)} fusion(bf16[4,64,2048]{2,1,0:T(8,128)(2,1)} %bitcast.50, bf16[512,2048]{1,0:T(8,128)(2,1)} %all-gather.2.cloned.1.call-done, f32[512]{0:T(512)S(1)} %add_rsqrt_fusion), kind=kOutput, calls=%fused_computation.7 | convolution fusion | flops 540016640 | bytes 3672064 | tf_op jit(solution)/shard_map/dot_general | solution.py:143
  66.3 0.9 concatenate.24.q_ref
  67.2 6.4 %all-to-all-done.1 = bf16[64,40,128]{2,1,0:T(8,128)(2,1)S(1)} async-done(((bf16[64,40,128]{2,1,0:T(8,128)(2,1)}), bf16[64,40,128]{2,1,0:T(8,128)(2,1)S(1)}, u32[]{:S(2)}, u32[]{:S(2)}) %all-to-all-start.1) | async-done | bytes 655392 | tf_op jit(solution)/shard_map/all_to_all | solution.py:83
  73.7 1.0 copy.27
  74.7 15.8 %shard_map.95 = bf16[4,512,128]{2,1,0:T(8,128)(2,1)} custom-call(bf16[4,512,128]{2,1,0:T(8,128)(2,1)} %concatenate.24.q_ref, bf16[2048,128]{1,0:T(8,128)(2,1)} %bitcast.44, bf16[512,128]{1,0:T(8,128)(2,1)} %copy-done.4, bf16[128,2048]{1,0:T(8,128)(2,1)} %bitcast.45, bf16[128,512]{1,0:T(8,128)(2,1)} %get-tuple-element.7.ent_t_ref, ...), custom_call_target="tpu_custom_call" | custom-call | tf_op jit(solution)/shard_map/pallas_call | solution.py:64
  90.6 1.2 slice_bitcast_fusion
  92.0 2.1 %convolution_convert_fusion = bf16[512,2048]{1,0:T(8,128)(2,1)} fusion(bf16[512,256]{0,1:T(8,128)(2,1)S(1)} %bitcast.48, bf16[1,256,2048]{2,1,0:T(8,128)(2,1)S(1)} %copy-done), kind=kOutput, calls=%fused_computation.6 | convolution fusion | flops 537919488 | bytes 3407872 | tf_op jit(solution)/shard_map/dot_general | solution.py:159
  94.8 0.8 broadcast_select_fusion.1
  95.6 9.0 %all-to-all-start.2 = ((bf16[64,8,128]{2,1,0:T(8,128)(2,1)}), bf16[64,8,128]{2,1,0:T(8,128)(2,1)S(1)}, u32[]{:S(2)}, u32[]{:S(2)}) async-start(bf16[64,8,128]{2,1,0:T(8,128)(2,1)} %broadcast_select_fusion.1), calls=%async_computation.3 | async-start | bytes 262144 | tf_op jit(solution)/shard_map/all_to_all | solution.py:87
  107.0 1.5 %fusion.14 = bf16[1536,128]{1,0:T(8,128)(2,1)S(1)} fusion(s32[]{:T(128)S(6)} %add.112, bf16[2048,128]{1,0:T(8,128)(2,1)S(1)} %bitcast.47), kind=kLoop, calls=%fused_computation.29 | loop fusion | flops 786432 | bytes 917508 | tf_op jit(solution)/shard_map/jit(_roll_dynamic)/concatenate | solution.py:155
  108.5 7.5 %all-to-all-done.2 = bf16[64,8,128]{2,1,0:T(8,128)(2,1)S(1)} async-done(((bf16[64,8,128]{2,1,0:T(8,128)(2,1)}), bf16[64,8,128]{2,1,0:T(8,128)(2,1)S(1)}, u32[]{:S(2)}, u32[]{:S(2)}) %all-to-all-start.2) | async-done | bytes 131104 | tf_op jit(solution)/shard_map/all_to_all | solution.py:87
  116.0 4.1 %fusion.10 = bf16[1,1,2048,128]{3,2,1,0:T(8,128)(2,1)} fusion(s32[]{:T(128)S(6)} %select_n.79, bf16[512,128]{1,0:T(8,128)(2,1)S(1)} %bitcast.51, bf16[1536,128]{1,0:T(8,128)(2,1)S(1)} %fusion.14), kind=kLoop, calls=%fused_computation.22 | loop fusion | flops 2097152 | bytes 1048580 | tf_op jit(solution)/shard_map/broadcast_in_dim | solution.py:157
  120.1 14.7 %reduce-scatter.2.cloned.1.call-done = bf16[512,256]{1,0:T(8,128)(2,1)} async-done(((bf16[512,2048]{1,0:T(8,128)(2,1)}), bf16[512,256]{1,0:T(8,128)(2,1)}) %reduce-scatter.2.cloned.1.call-update) | async-done | bytes 262160 | tf_op jit(solution)/shard_map/reduce_scatter | solution.py:160
  (51 shorter events, 6.3 us)
Async XLA Ops:
  7.2 84.9 %copy-start = (bf16[1,256,2048]{2,1,0:T(8,128)(2,1)S(1)}, bf16[1,256,2048]{2,1,0:T(8,128)(2,1)}, u32[]{:S(2)}) copy-start(bf16[1,256,2048]{2,1,0:T(8,128)(2,1)} %param.13) | copy-start | bytes 3145732
  7.2 17.9 %copy-start.8 = (s32[64]{0:T(128)S(1)}, s32[64]{0:T(128)}, u32[]{:S(2)}) copy-start(s32[64]{0:T(128)} %param.15) | copy-start | bytes 772
  7.2 19.2 %copy-start.9 = (s32[64]{0:T(128)S(1)}, s32[64]{0:T(128)}, u32[]{:S(2)}) copy-start(s32[64]{0:T(128)} %param.17) | copy-start | bytes 772
  7.2 35.1 %all-gather.2.cloned.1.call-start = ((), (), s32[]{:S(2)}) async-start(), calls=%async_computation.4 | async-start | bytes 3145728 | tf_op jit(solution)/shard_map/all_gather | solution.py:104
  7.9 33.5 %all-to-all-start = ((bf16[64,32,128]{2,1,0:T(8,128)(2,1)}), bf16[64,32,128]{2,1,0:T(8,128)(2,1)S(1)}, u32[]{:S(2)}, u32[]{:S(2)}) async-start(bf16[64,32,128]{2,1,0:T(8,128)(2,1)} %bitcast.46), calls=%async_computation | async-start | bytes 1048576 | tf_op jit(solution)/shard_map/all_to_all | solution.py:83
  27.8 16.7 %copy-start.7 = (bf16[2048,1,128]{2,0,1:T(8,128)(2,1)S(1)}, bf16[2048,1,128]{2,0,1:T(8,128)(2,1)}, u32[]{:S(2)}) copy-start(bf16[2048,1,128]{2,0,1:T(8,128)(2,1)} %param.12) | copy-start | bytes 1572868
  42.3 2.3 %copy-start.2 = (bf16[512,2048]{1,0:T(8,128)(2,1)S(1)}, bf16[512,2048]{1,0:T(8,128)(2,1)}, u32[]{:S(2)}) copy-start(bf16[512,2048]{1,0:T(8,128)(2,1)} %all-gather.2.cloned.1.call-done) | copy-start | bytes 6291460
  45.5 12.0 %copy-start.5 = (bf16[2048,1,256]{2,0,1:T(8,128)(2,1)S(1)}, bf16[2048,1,256]{2,0,1:T(8,128)(2,1)}, u32[]{:S(2)}) copy-start(bf16[2048,1,256]{2,0,1:T(8,128)(2,1)} %param.11) | copy-start | bytes 3145732
  46.7 12.2 %copy-start.4 = (bf16[512,128]{1,0:T(8,128)(2,1)}, bf16[512,128]{1,0:T(8,128)(2,1)S(1)}, u32[]{:S(2)}) copy-start(bf16[512,128]{1,0:T(8,128)(2,1)S(1)} %copy.26.ent_ref) | copy-start | bytes 393220
  46.7 12.9 %copy-start.6 = (s32[64]{0:T(128)S(1)}, s32[64]{0:T(128)}, u32[]{:S(2)}) copy-start(s32[64]{0:T(128)} %param.16) | copy-start | bytes 772
  47.6 26.1 %all-to-all-start.1 = ((bf16[64,40,128]{2,1,0:T(8,128)(2,1)}), bf16[64,40,128]{2,1,0:T(8,128)(2,1)S(1)}, u32[]{:S(2)}, u32[]{:S(2)}) async-start(bf16[64,40,128]{2,1,0:T(8,128)(2,1)} %pad_maximum_fusion), calls=%async_computation.1 | async-start | bytes 1310720 | tf_op jit(solution)/shard_map/all_to_all | solution.py:83
  55.4 79.4 %reduce-scatter.2.cloned.1.call-start = ((), (), s32[]{:S(2)}) async-start(), calls=%async_computation.5 | async-start | bytes 2359296 | tf_op jit(solution)/shard_map/reduce_scatter | solution.py:160
  73.7 1.0 copy-start.1
  94.1 12.9 %copy-start.3 = (bf16[1,1,2048,128]{3,2,1,0:T(8,128)(2,1)S(1)}, bf16[1,1,2048,128]{3,2,1,0:T(8,128)(2,1)}, u32[]{:S(2)}) copy-start(bf16[1,1,2048,128]{3,2,1,0:T(8,128)(2,1)} %param.14) | copy-start | bytes 1572868
  95.6 20.4 %all-to-all-start.2 = ((bf16[64,8,128]{2,1,0:T(8,128)(2,1)}), bf16[64,8,128]{2,1,0:T(8,128)(2,1)S(1)}, u32[]{:S(2)}, u32[]{:S(2)}) async-start(bf16[64,8,128]{2,1,0:T(8,128)(2,1)} %broadcast_select_fusion.1), calls=%async_computation.3 | async-start | bytes 262144 | tf_op jit(solution)/shard_map/all_to_all | solution.py:87
Sparse Core Ops, SparseCore 0:
  10.1 25.6 all-gather.1
  94.3 40.4 reduce-scatter.1

commit v8 on v5

--- a/solution.py
+++ b/solution.py
@@ -128,8 +128,17 @@
     new_cache = updated[None, None]
     out_rows = output_weight.reshape(output_weight.shape[1], width)
     partial_value = jnp.dot(attended, out_rows, preferred_element_type=jnp.float32)
+    halves = lax.axis_size("tx")
+    if halves == 2:
+        core = lax.axis_index("tx")
+        half_cols = width // halves
+        kept = lax.dynamic_slice_in_dim(partial_value, core * half_cols, half_cols, axis=1)
+        sent = lax.dynamic_slice_in_dim(partial_value, (1 - core) * half_cols, half_cols, axis=1)
+        across_cores = kept + lax.ppermute(sent, "tx", [(0, 1), (1, 0)])
+    else:
+        across_cores = lax.psum_scatter(partial_value, "tx", scatter_dimension=1, tiled=True)
     mixed = lax.psum_scatter(
-        partial_value.astype(jnp.bfloat16), ("tx", "ty"), scatter_dimension=1, tiled=True
+        across_cores.astype(jnp.bfloat16), "ty", scatter_dimension=1, tiled=True
     )
     return (mixed, new_cache)
 

time: 141 us -> 139 us (0.986)
  waiting for transfers between devices: 40.8 us -> 30.7 us
  starting transfers between devices: 34.1 us -> 37.2 us
  other arithmetic: 20.6 us -> 23.4 us
  local copies, waits for them, and re-layouts: 9.51 us -> 12 us
    reduce_scatter x1, waiting for transfers between devices: 14.4 us -> 0.01 us  [per_device(): lax.psum_scatter(across_cores.astype(jnp.bfloat16), 'ty', scatter_dimensi...]
    ppermute x0 -> x1, starting transfers between devices: none -> 6.09 us  [per_device(): across_cores = kept + lax.ppermute(sent, 'tx', [(0, 1), (1, 0)])]
    ppermute x0 -> x1, waiting for transfers between devices: none -> 3.97 us  [per_device(): across_cores = kept + lax.ppermute(sent, 'tx', [(0, 1), (1, 0)])]
    all_to_all x1, starting transfers between devices: 8.7 us -> 5.72 us  [carry_out(): return lax.all_to_all(window, 'dp', split_axis=0, concat_axis=0, tiled=True)]
    convert_element_type x0 -> x1, other arithmetic: none -> 2.86 us  [per_device(): across_cores.astype(jnp.bfloat16)]
    dynamic_slice x0 -> x1, local copies, waits for them, and re-layouts: none -> 1.61 us  [per_device(): lax.dynamic_slice_in_dim(partial_value, (1 - core) * half_cols, half_cols...]
  transfers between devices with their start and end apart: 5 -> 6, of which waited for: 4 -> 4; matrix products, arithmetic and copies ran while one was open for 15% -> 16% of each run, Pallas kernels for 0% -> 0%
where the time goes in v8:
time: 139 us; the launch traced here: 138 us
  starting transfers between devices  37.2 us (27%)
  waiting for transfers between devices  30.7 us (22%)
  other arithmetic  23.4 us (17%)
  between operations  20.2 us (15%)
  matrix products  14 us (10%)
  local copies, waits for them, and re-layouts  12 us (9%)
    all_to_all x2, starting transfers between devices, carry_in(): return lax.all_to_all(window, 'dp', split_axis=0, concat_axis=0, tiled=True)  25.3 us
    all_to_all x2, waiting for transfers between devices, carry_in(): return lax.all_to_all(window, 'dp', split_axis=0, concat_axis=0, tiled=True)  18.5 us
    all_to_all x1, waiting for transfers between devices, carry_out(): return lax.all_to_all(window, 'dp', split_axis=0, concat_axis=0, tiled=True)  7.47 us
    ppermute x1, starting transfers between devices, per_device(): across_cores = kept + lax.ppermute(sent, 'tx', [(0, 1), (1, 0)])  6.09 us
    all_to_all x1, starting transfers between devices, carry_out(): return lax.all_to_all(window, 'dp', split_axis=0, concat_axis=0, tiled=True)  5.72 us
    dot_general x4, matrix products, one_head(): jnp.einsum('qd,kd->qk', query_rows, keys_all, preferred_element_type=jnp....  4.67 us
    broadcast_in_dim x1, other arithmetic, per_device(): new_cache = updated[None, None]  4.12 us
    ppermute x1, waiting for transfers between devices, per_device(): across_cores = kept + lax.ppermute(sent, 'tx', [(0, 1), (1, 0)])  3.97 us
  transfers between devices with their start and end apart: 6, of which 4 were waited for; matrix products, arithmetic and copies ran while one was open for 16% of the time, Pallas kernels for 0%

profile of v8, /device:TPU:1, one launch (start us, length us, event | category | flops | bytes accessed | tf_op | source)
XLA Modules:
  0.0 137.6 jit_solution(2005465700926275997)
XLA Ops:
  7.9 17.1 %all-to-all-start = ((bf16[64,32,128]{2,1,0:T(8,128)(2,1)}), bf16[64,32,128]{2,1,0:T(8,128)(2,1)S(1)}, u32[]{:S(2)}, u32[]{:S(2)}) async-start(bf16[64,32,128]{2,1,0:T(8,128)(2,1)} %bitcast.61), calls=%async_computation | async-start | bytes 1048576 | tf_op jit(solution)/shard_map/all_to_all | solution.py:30
  32.5 9.0 %all-to-all-done = bf16[64,32,128]{2,1,0:T(8,128)(2,1)S(1)} async-done(((bf16[64,32,128]{2,1,0:T(8,128)(2,1)}), bf16[64,32,128]{2,1,0:T(8,128)(2,1)S(1)}, u32[]{:S(2)}, u32[]{:S(2)}) %all-to-all-start) | async-done | bytes 524320 | tf_op jit(solution)/shard_map/all_to_all | solution.py:30
  42.3 2.2 %fusion.20 = f32[512]{0:T(512)S(1)} fusion(bf16[512,2048]{1,0:T(8,128)(2,1)} %all-gather.2.cloned.1.call-done), kind=kLoop, calls=%fused_computation.18 | loop fusion | flops 3145216 | bytes 2099200 | tf_op jit(solution)/shard_map/reduce_sum | solution.py:56
  44.5 2.0 %fusion.26 = f32[512,128]{0,1:T(8,128)S(1)} fusion(bf16[512,2048]{1,0:T(8,128)(2,1)S(1)} %copy-done.3, f32[512]{0:T(512)S(1)} %add_rsqrt_fusion, bf16[2048,1,128]{2,0,1:T(8,128)(2,1)} %param.14), kind=kOutput, calls=%fused_computation.33 | convolution fusion | flops 271581184 | bytes 2885632 | tf_op jit(solution)/shard_map/dot_general | solution.py:63
  47.9 8.2 %all-to-all-start.1 = ((bf16[64,40,128]{2,1,0:T(8,128)(2,1)}), bf16[64,40,128]{2,1,0:T(8,128)(2,1)}, u32[]{:S(2)}, u32[]{:S(2)}) async-start(bf16[64,40,128]{2,1,0:T(8,128)(2,1)} %pad_maximum_fusion), calls=%async_computation.1 | async-start | bytes 1310720 | tf_op jit(solution)/shard_map/all_to_all | solution.py:30
  56.9 1.4 %copy.20 = bf16[2048,1,256]{0,2,1:T(8,128)(2,1)} copy(bf16[2048,1,256]{2,0,1:T(8,128)(2,1)S(1)} %copy-done.5) | data formatting | bytes 2097152 | tf_op args[1]
  59.3 1.1 pad_add_fusion
  61.9 2.7 %fusion.22 = f32[512,4,64]{0,2,1:T(8,128)S(1)} fusion(bf16[4,64,2048]{2,1,0:T(8,128)(2,1)} %bitcast.63, bf16[512,2048]{1,0:T(8,128)(2,1)} %all-gather.2.cloned.1.call-done, f32[512]{0:T(512)S(1)} %add_rsqrt_fusion), kind=kOutput, calls=%fused_computation.21 | convolution fusion | flops 540016640 | bytes 3672064 | tf_op jit(solution)/shard_map/dot_general | solution.py:90
  64.8 9.5 %all-to-all-done.1 = bf16[64,40,128]{2,1,0:T(8,128)(2,1)} async-done(((bf16[64,40,128]{2,1,0:T(8,128)(2,1)}), bf16[64,40,128]{2,1,0:T(8,128)(2,1)}, u32[]{:S(2)}, u32[]{:S(2)}) %all-to-all-start.1) | async-done | bytes 655392 | tf_op jit(solution)/shard_map/all_to_all | solution.py:30
  74.3 1.1 slice.55
  75.6 2.1 %pad_maximum_fusion.1 = (bf16[2560,64]{1,0:T(8,128)(2,1)S(1)}, bf16[2560,64]{1,0:T(8,128)(2,1)}) fusion(bf16[512,64]{1,0:T(8,128)(2,1)} %copy.22, bf16[2048,64]{1,0:T(8,128)(2,1)S(1)} %get-tuple-element.71, bf16[512,64]{1,0:T(8,128)(2,1)} %copy.23, bf16[2048,64]{1,0:T(8,128)(2,1)S(1)} %get-tuple-element.70), kind=kLoop, calls=%fused_computation.35 | loop fusion | flops 1310720 | bytes 1310720 | tf_op jit(solution)/shard_map/concatenate | solution.py:105
  77.6 13.1 %while.10 = (s32[]{:T(128)}, bf16[4,512,64]{1,2,0:T(8,128)(2,1)S(1)}, bf16[4,512,64]{1,2,0:T(8,128)(2,1)S(1)}, bf16[2560,64]{1,0:T(8,128)(2,1)S(1)}, pred[512,25...) while((s32[]{:T(128)}, bf16[4,512,64]{1,2,0:T(8,128)(2,1)S(1)}, ...), condition=%wide.region_4.5_spmd, body=%wide.region_1.4_spmd.sunk | while | flops 344783872 | bytes 19802232 | solution.py:121
  77.6 1.2 fusion.67
  80.9 1.2 fusion.67
  84.2 1.2 fusion.67
  87.4 1.2 fusion.67
  91.5 1.6 %constant_dynamic-slice_fusion = f32[512,1024]{1,0:T(8,128)} fusion(f32[512,2048]{1,0:T(8,128)S(1)} %fusion.24, s32[]{:T(128)S(6)} %select_n.80), kind=kLoop, calls=%fused_computation.84 | loop fusion | bytes 4194308 | tf_op jit(solution)/shard_map/dynamic_slice | solution.py:136
  94.0 6.1 %collective-permute-start = (f32[512,1024]{1,0:T(8,128)}, f32[512,1024]{1,0:T(8,128)S(1)}, u32[]{:S(2)}, u32[]{:S(2)}) collective-permute-start(f32[512,1024]{1,0:T(8,128)} %constant_dynamic-slice_fusion), channel_id=1, source_target_pairs={{0,4},{4,0},{1,5},{5,1},{2,6},{6,2},{3,7},{7,3},{8,12},{12,8},{9,1... | collective-permute-start | bytes 6291464 | tf_op jit(solution)/shard_map/ppermute | solution.py:137
  100.1 4.0 %collective-permute-done = f32[512,1024]{1,0:T(8,128)S(1)} collective-permute-done((f32[512,1024]{1,0:T(8,128)}, f32[512,1024]{1,0:T(8,128)S(1)}, u32[]{:S(2)}, u32[]{:S(2)}) %collective-permute-start) | collective-permute-done | bytes 2097184 | tf_op jit(solution)/shard_map/ppermute | solution.py:137
  104.1 2.9 %add_convert_fusion = bf16[512,1024]{1,0:T(8,128)(2,1)} fusion(f32[512,1024]{1,0:T(8,128)S(1)} %collective-permute-done, f32[512,2048]{1,0:T(8,128)} %copy-done.1, s32[]{:T(128)S(6)} %select_n.79), kind=kLoop, calls=%fused_computation.23 | loop fusion | flops 1048576 | bytes 5242884 | tf_op jit(solution)/shard_map/convert_element_type | solution.py:141
  109.4 5.7 %all-to-all-start.2 = ((bf16[64,8,128]{2,1,0:T(8,128)(2,1)}), bf16[64,8,128]{2,1,0:T(8,128)(2,1)S(1)}, u32[]{:S(2)}, u32[]{:S(2)}) async-start(bf16[64,8,128]{2,1,0:T(8,128)(2,1)} %broadcast_select_fusion.1), calls=%async_computation.3 | async-start | bytes 262144 | tf_op jit(solution)/shard_map/all_to_all | solution.py:34
  117.7 1.5 %fusion.34 = bf16[1536,128]{1,0:T(8,128)(2,1)S(1)} fusion(s32[]{:T(128)S(6)} %add.133, bf16[2048,128]{1,0:T(8,128)(2,1)S(1)} %bitcast.62), kind=kLoop, calls=%fused_computation.43 | loop fusion | flops 786432 | bytes 917508 | tf_op jit(solution)/shard_map/jit(_roll_dynamic)/concatenate | solution.py:126
  119.2 7.5 %all-to-all-done.2 = bf16[64,8,128]{2,1,0:T(8,128)(2,1)S(1)} async-done(((bf16[64,8,128]{2,1,0:T(8,128)(2,1)}), bf16[64,8,128]{2,1,0:T(8,128)(2,1)S(1)}, u32[]{:S(2)}, u32[]{:S(2)}) %all-to-all-start.2) | async-done | bytes 131104 | tf_op jit(solution)/shard_map/all_to_all | solution.py:34
  126.7 4.1 %fusion.31 = bf16[1,1,2048,128]{3,2,1,0:T(8,128)(2,1)} fusion(s32[]{:T(128)S(6)} %select_n.91, bf16[512,128]{1,0:T(8,128)(2,1)S(1)} %bitcast.66, bf16[1536,128]{1,0:T(8,128)(2,1)S(1)} %fusion.34), kind=kLoop, calls=%fused_computation.39 | loop fusion | flops 2097152 | bytes 1048580 | tf_op jit(solution)/shard_map/broadcast_in_dim | solution.py:128
  (82 shorter events, 23.0 us)
Async XLA Ops:
  7.2 83.5 %copy-start = (bf16[1,256,2048]{2,1,0:T(8,128)(2,1)S(1)}, bf16[1,256,2048]{2,1,0:T(8,128)(2,1)}, u32[]{:S(2)}) copy-start(bf16[1,256,2048]{2,1,0:T(8,128)(2,1)} %param.15) | copy-start | bytes 3145732
  7.2 17.9 %copy-start.11 = (s32[64]{0:T(128)S(1)}, s32[64]{0:T(128)}, u32[]{:S(2)}) copy-start(s32[64]{0:T(128)} %param.19) | copy-start | bytes 772
  7.2 19.9 %copy-start.10 = (s32[64]{0:T(128)S(1)}, s32[64]{0:T(128)}, u32[]{:S(2)}) copy-start(s32[64]{0:T(128)} %param.17) | copy-start | bytes 772
  7.2 21.8 %copy-start.9 = (s32[64]{0:T(128)S(1)}, s32[64]{0:T(128)}, u32[]{:S(2)}) copy-start(s32[64]{0:T(128)} %param.18) | copy-start | bytes 772
  7.2 35.1 %all-gather.2.cloned.1.call-start = ((), (), s32[]{:S(2)}) async-start(), calls=%async_computation.4 | async-start | bytes 3145728 | tf_op jit(solution)/shard_map/all_gather | solution.py:51
  7.9 33.5 %all-to-all-start = ((bf16[64,32,128]{2,1,0:T(8,128)(2,1)}), bf16[64,32,128]{2,1,0:T(8,128)(2,1)S(1)}, u32[]{:S(2)}, u32[]{:S(2)}) async-start(bf16[64,32,128]{2,1,0:T(8,128)(2,1)} %bitcast.61), calls=%async_computation | async-start | bytes 1048576 | tf_op jit(solution)/shard_map/all_to_all | solution.py:30
  42.3 2.2 %copy-start.3 = (bf16[512,2048]{1,0:T(8,128)(2,1)S(1)}, bf16[512,2048]{1,0:T(8,128)(2,1)}, u32[]{:S(2)}) copy-start(bf16[512,2048]{1,0:T(8,128)(2,1)} %all-gather.2.cloned.1.call-done) | copy-start | bytes 6291460
  47.9 9.0 %copy-start.5 = (bf16[2048,1,256]{2,0,1:T(8,128)(2,1)S(1)}, bf16[2048,1,256]{2,0,1:T(8,128)(2,1)}, u32[]{:S(2)}) copy-start(bf16[2048,1,256]{2,0,1:T(8,128)(2,1)} %param.13) | copy-start | bytes 3145732
  47.9 26.3 %all-to-all-start.1 = ((bf16[64,40,128]{2,1,0:T(8,128)(2,1)}), bf16[64,40,128]{2,1,0:T(8,128)(2,1)}, u32[]{:S(2)}, u32[]{:S(2)}) async-start(bf16[64,40,128]{2,1,0:T(8,128)(2,1)} %pad_maximum_fusion), calls=%async_computation.1 | async-start | bytes 1310720 | tf_op jit(solution)/shard_map/all_to_all | solution.py:30
  56.1 74.7 %reduce-scatter.2.cloned.1.call-start = ((), (), s32[]{:S(2)}) async-start(), calls=%async_computation.5 | async-start | bytes 1310720 | tf_op jit(solution)/shard_map/reduce_scatter | solution.py:140
  61.9 2.7 %copy-start.7 = (f32[512,32]{0,1:T(8,128)S(1)}, f32[512,32]{0,1:T(8,128)}, u32[]{:S(2)}) copy-start(f32[512,32]{0,1:T(8,128)} %get-tuple-element.74) | copy-start | bytes 196612
  61.9 2.7 %copy-start.8 = (f32[512,32]{0,1:T(8,128)S(1)}, f32[512,32]{0,1:T(8,128)}, u32[]{:S(2)}) copy-start(f32[512,32]{0,1:T(8,128)} %get-tuple-element.75) | copy-start | bytes 196612
  75.4 2.3 %copy-start.6 = (bf16[4,512,64]{1,2,0:T(8,128)(2,1)S(1)}, bf16[4,512,64]{1,2,0:T(8,128)(2,1)}, u32[]{:S(2)}) copy-start(bf16[4,512,64]{1,2,0:T(8,128)(2,1)} %custom-call.4) | copy-start | bytes 786436
  78.8 1.1 copy-start.2
  82.1 1.1 copy-start.2
  85.3 1.1 copy-start.2
  88.6 1.1 copy-start.2
  91.5 2.6 %copy-start.1 = (f32[512,2048]{1,0:T(8,128)}, f32[512,2048]{1,0:T(8,128)S(1)}, u32[]{:S(2)}) copy-start(f32[512,2048]{1,0:T(8,128)S(1)} %fusion.24) | copy-start | bytes 12582916
  94.0 10.1 %collective-permute-start = (f32[512,1024]{1,0:T(8,128)}, f32[512,1024]{1,0:T(8,128)S(1)}, u32[]{:S(2)}, u32[]{:S(2)}) collective-permute-start(f32[512,1024]{1,0:T(8,128)} %constant_dynamic-slice_fusion), channel_id=1, source_target_pairs={{0,4},{4,0},{1,5},{5,1},{2,6},{6,2},{3,7},{7,3},{8,12},{12,8},{9,1... | collective-permute-start | bytes 6291464 | tf_op jit(solution)/shard_map/ppermute | solution.py:137
  107.0 10.7 %copy-start.4 = (bf16[1,1,2048,128]{3,2,1,0:T(8,128)(2,1)S(1)}, bf16[1,1,2048,128]{3,2,1,0:T(8,128)(2,1)}, u32[]{:S(2)}) copy-start(bf16[1,1,2048,128]{3,2,1,0:T(8,128)(2,1)} %param.16) | copy-start | bytes 1572868
  109.4 17.2 %all-to-all-start.2 = ((bf16[64,8,128]{2,1,0:T(8,128)(2,1)}), bf16[64,8,128]{2,1,0:T(8,128)(2,1)S(1)}, u32[]{:S(2)}, u32[]{:S(2)}) async-start(bf16[64,8,128]{2,1,0:T(8,128)(2,1)} %broadcast_select_fusion.1), calls=%async_computation.3 | async-start | bytes 262144 | tf_op jit(solution)/shard_map/all_to_all | solution.py:34
Sparse Core Ops, SparseCore 0:
  10.1 25.6 all-gather.1
  107.1 21.2 reduce-scatter.1

commit v9 on v8

--- a/solution.py
+++ b/solution.py
@@ -123,19 +123,32 @@
 
     arrived = carry_out(jnp.take(entry_parts, inverse, axis=0).reshape(rows_new, lanes))
     own_offset = offsets[inverse[request]]
-    rolled = jnp.roll(stored, -own_offset, axis=0)
-    updated = jnp.roll(jnp.concatenate([arrived, rolled[rows_new:]], axis=0), own_offset, axis=0)
+    extended = jnp.concatenate([stored, stored[:rows_new]], axis=0)
+    extended = lax.dynamic_update_slice_in_dim(extended, arrived, own_offset, axis=0)
+    wrap = own_offset + rows_new - WINDOW_LENGTH
+    head_rows = jnp.arange(rows_new, dtype=jnp.int32)[:, None]
+    head = jnp.where(head_rows < wrap, extended[WINDOW_LENGTH:], extended[:rows_new])
+    updated = jnp.concatenate([head, extended[rows_new:WINDOW_LENGTH]], axis=0)
     new_cache = updated[None, None]
     out_rows = output_weight.reshape(output_weight.shape[1], width)
-    partial_value = jnp.dot(attended, out_rows, preferred_element_type=jnp.float32)
     halves = lax.axis_size("tx")
     if halves == 2:
         core = lax.axis_index("tx")
         half_cols = width // halves
-        kept = lax.dynamic_slice_in_dim(partial_value, core * half_cols, half_cols, axis=1)
-        sent = lax.dynamic_slice_in_dim(partial_value, (1 - core) * half_cols, half_cols, axis=1)
-        across_cores = kept + lax.ppermute(sent, "tx", [(0, 1), (1, 0)])
+        sent = jnp.dot(
+            attended,
+            lax.dynamic_slice_in_dim(out_rows, (1 - core) * half_cols, half_cols, axis=1),
+            preferred_element_type=jnp.float32,
+        )
+        received = lax.ppermute(sent, "tx", [(0, 1), (1, 0)])
+        kept = jnp.dot(
+            attended,
+            lax.dynamic_slice_in_dim(out_rows, core * half_cols, half_cols, axis=1),
+            preferred_element_type=jnp.float32,
+        )
+        across_cores = kept + received
     else:
+        partial_value = jnp.dot(attended, out_rows, preferred_element_type=jnp.float32)
         across_cores = lax.psum_scatter(partial_value, "tx", scatter_dimension=1, tiled=True)
     mixed = lax.psum_scatter(
         across_cores.astype(jnp.bfloat16), "ty", scatter_dimension=1, tiled=True

time: 139 us -> 138 us (level)
  other arithmetic: 23.4 us -> 16 us
  matrix products: 14 us -> 18.1 us
  waiting for transfers between devices: 30.7 us -> 34.7 us
  local copies, waits for them, and re-layouts: 12 us -> 9.92 us
    dot_general x1 -> x2, matrix products: 0.73 us -> 4.8 us  [the longest x1 3.01 us: per_device(): jnp.dot(attended, lax.dynamic_slice_in_dim(out_rows, core * half_cols, ha...]
    all_to_all x1, waiting for transfers between devices: 7.47 us -> 11.4 us  [carry_out(): return lax.all_to_all(window, 'dp', split_axis=0, concat_axis=0, tiled=True)]
    broadcast_in_dim x1, other arithmetic: 4.12 us -> 0.83 us  [per_device(): new_cache = updated[None, None]]
    convert_element_type x1 -> x0, other arithmetic: 2.86 us -> none  [per_device(): across_cores.astype(jnp.bfloat16)]
    dynamic_slice x1 -> x0, local copies, waits for them, and re-layouts: 1.61 us -> none  [per_device(): lax.dynamic_slice_in_dim(partial_value, (1 - core) * half_cols, half_cols...]
    concatenate x1, other arithmetic: 1.49 us -> 0.04 us  [per_device(): extended = jnp.concatenate([stored, stored[:rows_new]], axis=0)]
  transfers between devices with their start and end apart: 6 -> 6, of which waited for: 4 -> 4; matrix products, arithmetic and copies ran while one was open for 16% -> 13% of each run, Pallas kernels for 0% -> 0%
where the time goes in v9:
time: 138 us; the launch traced here: 136 us
  starting transfers between devices  37.2 us (27%)
  waiting for transfers between devices  34.7 us (25%)
  between operations  20.4 us (15%)
  matrix products  18.1 us (13%)
  other arithmetic  16 us (12%)
  local copies, waits for them, and re-layouts  9.92 us (7%)
    all_to_all x2, starting transfers between devices, carry_in(): return lax.all_to_all(window, 'dp', split_axis=0, concat_axis=0, tiled=True)  25.3 us
    all_to_all x2, waiting for transfers between devices, carry_in(): return lax.all_to_all(window, 'dp', split_axis=0, concat_axis=0, tiled=True)  18.5 us
    all_to_all x1, waiting for transfers between devices, carry_out(): return lax.all_to_all(window, 'dp', split_axis=0, concat_axis=0, tiled=True)  11.4 us
    ppermute x1, starting transfers between devices, per_device(): received = lax.ppermute(sent, 'tx', [(0, 1), (1, 0)])  6.09 us
    all_to_all x1, starting transfers between devices, carry_out(): return lax.all_to_all(window, 'dp', split_axis=0, concat_axis=0, tiled=True)  5.73 us
    dot_general x4, matrix products, one_head(): jnp.einsum('qd,kd->qk', query_rows, keys_all, preferred_element_type=jnp....  4.66 us
    ppermute x1, waiting for transfers between devices, per_device(): received = lax.ppermute(sent, 'tx', [(0, 1), (1, 0)])  4.09 us
    dot_general x4, matrix products, one_head(): summed = jnp.dot(weights, values_all, preferred_element_type=jnp.float32)  3.94 us
  transfers between devices with their start and end apart: 6, of which 4 were waited for; matrix products, arithmetic and copies ran while one was open for 13% of the time, Pallas kernels for 0%

profile of v9, /device:TPU:1, one launch (start us, length us, event | category | flops | bytes accessed | tf_op | source)
XLA Modules:
  0.0 136.4 jit_solution(14646439306922281457)
XLA Ops:
  7.9 17.1 %all-to-all-start = ((bf16[64,32,128]{2,1,0:T(8,128)(2,1)}), bf16[64,32,128]{2,1,0:T(8,128)(2,1)S(1)}, u32[]{:S(2)}, u32[]{:S(2)}) async-start(bf16[64,32,128]{2,1,0:T(8,128)(2,1)} %bitcast.67), calls=%async_computation | async-start | bytes 1048576 | tf_op jit(solution)/shard_map/all_to_all | solution.py:30
  32.5 8.9 %all-to-all-done = bf16[64,32,128]{2,1,0:T(8,128)(2,1)S(1)} async-done(((bf16[64,32,128]{2,1,0:T(8,128)(2,1)}), bf16[64,32,128]{2,1,0:T(8,128)(2,1)S(1)}, u32[]{:S(2)}, u32[]{:S(2)}) %all-to-all-start) | async-done | bytes 524320 | tf_op jit(solution)/shard_map/all_to_all | solution.py:30
  42.3 2.2 %fusion.20 = f32[512]{0:T(512)S(1)} fusion(bf16[512,2048]{1,0:T(8,128)(2,1)} %all-gather.2.cloned.1.call-done), kind=kLoop, calls=%fused_computation.18 | loop fusion | flops 3145216 | bytes 2099200 | tf_op jit(solution)/shard_map/reduce_sum | solution.py:56
  44.5 2.0 %fusion.24 = f32[512,128]{0,1:T(8,128)S(1)} fusion(bf16[512,2048]{1,0:T(8,128)(2,1)S(1)} %copy-done.3, f32[512]{0:T(512)S(1)} %add_rsqrt_fusion, bf16[2048,1,128]{2,0,1:T(8,128)(2,1)} %param.12), kind=kOutput, calls=%fused_computation.25 | convolution fusion | flops 271581184 | bytes 2885632 | tf_op jit(solution)/shard_map/dot_general | solution.py:63
  47.9 8.2 %all-to-all-start.1 = ((bf16[64,40,128]{2,1,0:T(8,128)(2,1)}), bf16[64,40,128]{2,1,0:T(8,128)(2,1)}, u32[]{:S(2)}, u32[]{:S(2)}) async-start(bf16[64,40,128]{2,1,0:T(8,128)(2,1)} %pad_maximum_fusion), calls=%async_computation.1 | async-start | bytes 1310720 | tf_op jit(solution)/shard_map/all_to_all | solution.py:30
  56.9 1.4 %copy.20 = bf16[2048,1,256]{0,2,1:T(8,128)(2,1)} copy(bf16[2048,1,256]{2,0,1:T(8,128)(2,1)S(1)} %copy-done.5) | data formatting | bytes 2097152 | tf_op args[1]
  59.3 1.1 pad_add_fusion
  61.9 2.7 %fusion.22 = f32[512,4,64]{0,2,1:T(8,128)S(1)} fusion(bf16[4,64,2048]{2,1,0:T(8,128)(2,1)} %bitcast.71, bf16[512,2048]{1,0:T(8,128)(2,1)} %all-gather.2.cloned.1.call-done, f32[512]{0:T(512)S(1)} %add_rsqrt_fusion), kind=kOutput, calls=%fused_computation.21 | convolution fusion | flops 540016640 | bytes 3672064 | tf_op jit(solution)/shard_map/dot_general | solution.py:90
  64.7 9.5 %all-to-all-done.1 = bf16[64,40,128]{2,1,0:T(8,128)(2,1)} async-done(((bf16[64,40,128]{2,1,0:T(8,128)(2,1)}), bf16[64,40,128]{2,1,0:T(8,128)(2,1)}, u32[]{:S(2)}, u32[]{:S(2)}) %all-to-all-start.1) | async-done | bytes 655392 | tf_op jit(solution)/shard_map/all_to_all | solution.py:30
  74.3 1.1 slice.71
  75.6 2.1 %pad_maximum_fusion.1 = (bf16[2560,64]{1,0:T(8,128)(2,1)S(1)}, bf16[2560,64]{1,0:T(8,128)(2,1)}) fusion(bf16[512,64]{1,0:T(8,128)(2,1)} %copy.22, bf16[2048,64]{1,0:T(8,128)(2,1)S(1)} %get-tuple-element.70, bf16[512,64]{1,0:T(8,128)(2,1)} %copy.23, bf16[2048,64]{1,0:T(8,128)(2,1)S(1)} %get-tuple-element.69), kind=kLoop, calls=%fused_computation.27 | loop fusion | flops 1310720 | bytes 1310720 | tf_op jit(solution)/shard_map/concatenate | solution.py:105
  77.6 13.1 %while.10 = (s32[]{:T(128)}, bf16[4,512,64]{1,2,0:T(8,128)(2,1)S(1)}, bf16[4,512,64]{1,2,0:T(8,128)(2,1)S(1)}, bf16[2560,64]{1,0:T(8,128)(2,1)S(1)}, pred[512,25...) while((s32[]{:T(128)}, bf16[4,512,64]{1,2,0:T(8,128)(2,1)S(1)}, ...), condition=%wide.region_4.5_spmd, body=%wide.region_1.4_spmd.sunk | while | flops 344783872 | bytes 19802232 | solution.py:121
  77.6 1.2 fusion.68
  80.9 1.2 fusion.68
  83.2 1.0 fusion.70
  84.2 1.2 fusion.68
  86.4 1.0 fusion.70
  87.4 1.2 fusion.68
  90.7 1.8 %fusion.27 = f32[512,1024]{1,0:T(8,128)} fusion(bf16[512,256]{0,1:T(8,128)(2,1)S(1)} %bitcast.69, bf16[1,256,2048]{2,1,0:T(8,128)(2,1)S(1)} %copy-done, s32[]{:T(128)S(6)} %select_n.78), kind=kOutput, calls=%fused_computation.31 | convolution fusion | flops 268435456 | bytes 2883588 | tf_op jit(solution)/shard_map/dot_general | solution.py:138
  92.5 6.1 %collective-permute-start = (f32[512,1024]{1,0:T(8,128)}, f32[512,1024]{1,0:T(8,128)}, u32[]{:S(2)}, u32[]{:S(2)}) collective-permute-start(f32[512,1024]{1,0:T(8,128)} %fusion.27), channel_id=1, source_target_pairs={{0,4},{4,0},{1,5},{5,1},{2,6},{6,2},{3,7},{7,3},{8,12},{12,8},{9,1... | collective-permute-start | bytes 6291464 | tf_op jit(solution)/shard_map/ppermute | solution.py:143
  98.6 4.1 %collective-permute-done = f32[512,1024]{1,0:T(8,128)} collective-permute-done((f32[512,1024]{1,0:T(8,128)}, f32[512,1024]{1,0:T(8,128)}, u32[]{:S(2)}, u32[]{:S(2)}) %collective-permute-start) | collective-permute-done | bytes 2097184 | tf_op jit(solution)/shard_map/ppermute | solution.py:143
  102.7 3.0 %add_convert_fusion = bf16[512,1024]{1,0:T(8,128)(2,1)} fusion(f32[512,1024]{1,0:T(8,128)} %collective-permute-done, bf16[512,256]{0,1:T(8,128)(2,1)S(1)} %bitcast.70, bf16[1,256,2048]{2,1,0:T(8,128)(2,1)S(1)} %copy-done, s32[]{:T(128)S(6)} %select_n.77), kind=kOutput, calls=%fused_computation.23 | convolution fusion | flops 269484032 | bytes 3932164 | tf_op jit(solution)/shard_map/dot_general | solution.py:144
  110.9 5.7 %all-to-all-start.2 = ((bf16[64,8,128]{2,1,0:T(8,128)(2,1)}), bf16[64,8,128]{2,1,0:T(8,128)(2,1)S(1)}, u32[]{:S(2)}, u32[]{:S(2)}) async-start(bf16[64,8,128]{2,1,0:T(8,128)(2,1)} %broadcast_select_fusion.1), calls=%async_computation.3 | async-start | bytes 262144 | tf_op jit(solution)/shard_map/all_to_all | solution.py:34
  116.6 11.4 %all-to-all-done.2 = bf16[64,8,128]{2,1,0:T(8,128)(2,1)S(1)} async-done(((bf16[64,8,128]{2,1,0:T(8,128)(2,1)}), bf16[64,8,128]{2,1,0:T(8,128)(2,1)S(1)}, u32[]{:S(2)}, u32[]{:S(2)}) %all-to-all-start.2) | async-done | bytes 131104 | tf_op jit(solution)/shard_map/all_to_all | solution.py:34
  (84 shorter events, 20.8 us)
Async XLA Ops:
  7.2 83.5 %copy-start = (bf16[1,256,2048]{2,1,0:T(8,128)(2,1)S(1)}, bf16[1,256,2048]{2,1,0:T(8,128)(2,1)}, u32[]{:S(2)}) copy-start(bf16[1,256,2048]{2,1,0:T(8,128)(2,1)} %param.13) | copy-start | bytes 3145732
  7.2 17.9 %copy-start.10 = (s32[64]{0:T(128)S(1)}, s32[64]{0:T(128)}, u32[]{:S(2)}) copy-start(s32[64]{0:T(128)} %param.17) | copy-start | bytes 772
  7.2 19.9 %copy-start.9 = (s32[64]{0:T(128)S(1)}, s32[64]{0:T(128)}, u32[]{:S(2)}) copy-start(s32[64]{0:T(128)} %param.15) | copy-start | bytes 772
  7.2 21.8 %copy-start.8 = (s32[64]{0:T(128)S(1)}, s32[64]{0:T(128)}, u32[]{:S(2)}) copy-start(s32[64]{0:T(128)} %param.16) | copy-start | bytes 772
  7.2 35.1 %all-gather.2.cloned.1.call-start = ((), (), s32[]{:S(2)}) async-start(), calls=%async_computation.4 | async-start | bytes 3145728 | tf_op jit(solution)/shard_map/all_gather | solution.py:51
  7.9 33.5 %all-to-all-start = ((bf16[64,32,128]{2,1,0:T(8,128)(2,1)}), bf16[64,32,128]{2,1,0:T(8,128)(2,1)S(1)}, u32[]{:S(2)}, u32[]{:S(2)}) async-start(bf16[64,32,128]{2,1,0:T(8,128)(2,1)} %bitcast.67), calls=%async_computation | async-start | bytes 1048576 | tf_op jit(solution)/shard_map/all_to_all | solution.py:30
  42.3 2.2 %copy-start.3 = (bf16[512,2048]{1,0:T(8,128)(2,1)S(1)}, bf16[512,2048]{1,0:T(8,128)(2,1)}, u32[]{:S(2)}) copy-start(bf16[512,2048]{1,0:T(8,128)(2,1)} %all-gather.2.cloned.1.call-done) | copy-start | bytes 6291460
  47.9 9.0 %copy-start.5 = (bf16[2048,1,256]{2,0,1:T(8,128)(2,1)S(1)}, bf16[2048,1,256]{2,0,1:T(8,128)(2,1)}, u32[]{:S(2)}) copy-start(bf16[2048,1,256]{2,0,1:T(8,128)(2,1)} %param.11) | copy-start | bytes 3145732
  47.9 26.3 %all-to-all-start.1 = ((bf16[64,40,128]{2,1,0:T(8,128)(2,1)}), bf16[64,40,128]{2,1,0:T(8,128)(2,1)}, u32[]{:S(2)}, u32[]{:S(2)}) async-start(bf16[64,40,128]{2,1,0:T(8,128)(2,1)} %pad_maximum_fusion), calls=%async_computation.1 | async-start | bytes 1310720 | tf_op jit(solution)/shard_map/all_to_all | solution.py:30
  56.1 73.4 %reduce-scatter.2.cloned.1.call-start = ((), (), s32[]{:S(2)}) async-start(), calls=%async_computation.5 | async-start | bytes 1310720 | tf_op jit(solution)/shard_map/reduce_scatter | solution.py:153
  61.9 2.7 %copy-start.6 = (f32[512,32]{0,1:T(8,128)S(1)}, f32[512,32]{0,1:T(8,128)}, u32[]{:S(2)}) copy-start(f32[512,32]{0,1:T(8,128)} %get-tuple-element.73) | copy-start | bytes 196612
  61.9 2.7 %copy-start.7 = (f32[512,32]{0,1:T(8,128)S(1)}, f32[512,32]{0,1:T(8,128)}, u32[]{:S(2)}) copy-start(f32[512,32]{0,1:T(8,128)} %get-tuple-element.74) | copy-start | bytes 196612
  75.4 2.3 %copy-start.4 = (bf16[4,512,64]{1,2,0:T(8,128)(2,1)S(1)}, bf16[4,512,64]{1,2,0:T(8,128)(2,1)}, u32[]{:S(2)}) copy-start(bf16[4,512,64]{1,2,0:T(8,128)(2,1)} %custom-call.4) | copy-start | bytes 786436
  78.8 1.1 copy-start.1
  82.1 1.1 copy-start.1
  85.3 1.1 copy-start.1
  88.6 1.1 copy-start.1
  92.5 10.2 %collective-permute-start = (f32[512,1024]{1,0:T(8,128)}, f32[512,1024]{1,0:T(8,128)}, u32[]{:S(2)}, u32[]{:S(2)}) collective-permute-start(f32[512,1024]{1,0:T(8,128)} %fusion.27), channel_id=1, source_target_pairs={{0,4},{4,0},{1,5},{5,1},{2,6},{6,2},{3,7},{7,3},{8,12},{12,8},{9,1... | collective-permute-start | bytes 6291464 | tf_op jit(solution)/shard_map/ppermute | solution.py:143
  98.6 9.9 %copy-start.2 = (bf16[1,1,2048,128]{3,2,1,0:T(8,128)(2,1)S(1)}, bf16[1,1,2048,128]{3,2,1,0:T(8,128)(2,1)}, u32[]{:S(2)}) copy-start(bf16[1,1,2048,128]{3,2,1,0:T(8,128)(2,1)} %param.14) | copy-start | bytes 1572868
  110.9 17.2 %all-to-all-start.2 = ((bf16[64,8,128]{2,1,0:T(8,128)(2,1)}), bf16[64,8,128]{2,1,0:T(8,128)(2,1)S(1)}, u32[]{:S(2)}, u32[]{:S(2)}) async-start(bf16[64,8,128]{2,1,0:T(8,128)(2,1)} %broadcast_select_fusion.1), calls=%async_computation.3 | async-start | bytes 262144 | tf_op jit(solution)/shard_map/all_to_all | solution.py:34
Sparse Core Ops, SparseCore 0:
  10.1 25.6 all-gather.1
  105.9 21.2 reduce-scatter.1

commit v10 on v9

--- a/solution.py
+++ b/solution.py
@@ -48,7 +48,16 @@
     stored = cache[0, 0]
     half_rows = stored.shape[0]
     spread = carry_in(stored)
-    whole = lax.all_gather(tokens, "tx", axis=1, tiled=True)
+    if lax.axis_size("tx") == 2:
+        core = lax.axis_index("tx")
+        other = lax.ppermute(tokens, "tx", [(0, 1), (1, 0)])
+        whole = jnp.where(
+            core == 0,
+            jnp.concatenate([tokens, other], axis=1),
+            jnp.concatenate([other, tokens], axis=1),
+        )
+    else:
+        whole = lax.all_gather(tokens, "tx", axis=1, tiled=True)
     rows_new = whole.shape[0]
     width = whole.shape[1]
     floats = whole.astype(jnp.float32)
@@ -71,6 +80,7 @@
     new_values = rotation_pairs[:, HEAD_SIZE:].astype(jnp.bfloat16)
     entry = jnp.concatenate([new_keys, new_values], axis=1)
 
+    spread, entry = lax.optimization_barrier((spread, entry))
     window_chunk = half_rows // groups
     entry_chunk = rows_new // groups
     lanes = stored.shape[1]
@@ -139,14 +149,14 @@
             attended,
             lax.dynamic_slice_in_dim(out_rows, (1 - core) * half_cols, half_cols, axis=1),
             preferred_element_type=jnp.float32,
-        )
+        ).astype(jnp.bfloat16)
         received = lax.ppermute(sent, "tx", [(0, 1), (1, 0)])
         kept = jnp.dot(
             attended,
             lax.dynamic_slice_in_dim(out_rows, core * half_cols, half_cols, axis=1),
             preferred_element_type=jnp.float32,
         )
-        across_cores = kept + received
+        across_cores = kept + received.astype(jnp.float32)
     else:
         partial_value = jnp.dot(attended, out_rows, preferred_element_type=jnp.float32)
         across_cores = lax.psum_scatter(partial_value, "tx", scatter_dimension=1, tiled=True)

time: 138 us -> 140 us (1.014)
  waiting for transfers between devices: 34.7 us -> 27 us
  starting transfers between devices: 37.2 us -> 43.8 us
  local copies, waits for them, and re-layouts: 9.92 us -> 12.6 us
    ppermute x0 -> x1, starting transfers between devices: none -> 8.92 us  [per_device(): other = lax.ppermute(tokens, 'tx', [(0, 1), (1, 0)])]
    all_to_all x2, waiting for transfers between devices: 18.5 us -> 13 us  [carry_in(): return lax.all_to_all(window, 'dp', split_axis=0, concat_axis=0, tiled=True)]
    all_to_all x2, starting transfers between devices: 25.3 us -> 23.3 us  [carry_in(): return lax.all_to_all(window, 'dp', split_axis=0, concat_axis=0, tiled=True)]
    dot_general x1, matrix products: 1.97 us -> 3.62 us  [per_device(): jnp.dot(normalized_input, key_value_weight.reshape(width, 2 * HEAD_SIZE),...]
    ppermute x1, waiting for transfers between devices: 4.09 us -> 2.47 us  [per_device(): received = lax.ppermute(sent, 'tx', [(0, 1), (1, 0)])]
    dot_general x1, matrix products: 3.01 us -> 1.43 us  [per_device(): jnp.dot(attended, lax.dynamic_slice_in_dim(out_rows, core * half_cols, ha...]
  transfers between devices with their start and end apart: 6 -> 6, of which waited for: 4 -> 3; matrix products, arithmetic and copies ran while one was open for 13% -> 19% of each run, Pallas kernels for 0% -> 0%
where the time goes in v10:
time: 140 us; the launch traced here: 139 us
  starting transfers between devices  43.8 us (31%)
  waiting for transfers between devices  27 us (19%)
  between operations  20.2 us (14%)
  matrix products  18.6 us (13%)
  other arithmetic  16.5 us (12%)
  local copies, waits for them, and re-layouts  12.6 us (9%)
    all_to_all x2, starting transfers between devices, carry_in(): return lax.all_to_all(window, 'dp', split_axis=0, concat_axis=0, tiled=True)  23.3 us
    all_to_all x2, waiting for transfers between devices, carry_in(): return lax.all_to_all(window, 'dp', split_axis=0, concat_axis=0, tiled=True)  13 us
    all_to_all x1, waiting for transfers between devices, carry_out(): return lax.all_to_all(window, 'dp', split_axis=0, concat_axis=0, tiled=True)  11.4 us
    ppermute x1, starting transfers between devices, per_device(): other = lax.ppermute(tokens, 'tx', [(0, 1), (1, 0)])  8.92 us
    all_to_all x1, starting transfers between devices, carry_out(): return lax.all_to_all(window, 'dp', split_axis=0, concat_axis=0, tiled=True)  5.95 us
    ppermute x1, starting transfers between devices, per_device(): received = lax.ppermute(sent, 'tx', [(0, 1), (1, 0)])  5.61 us
    dot_general x4, matrix products, one_head(): jnp.einsum('qd,kd->qk', query_rows, keys_all, preferred_element_type=jnp....  4.67 us
    dot_general x4, matrix products, one_head(): summed = jnp.dot(weights, values_all, preferred_element_type=jnp.float32)  3.95 us
  transfers between devices with their start and end apart: 6, of which 3 were waited for; matrix products, arithmetic and copies ran while one was open for 19% of the time, Pallas kernels for 0%

profile of v10, /device:TPU:1, one launch (start us, length us, event | category | flops | bytes accessed | tf_op | source)
XLA Modules:
  0.0 138.9 jit_solution(7582639391845653197)
XLA Ops:
  7.2 8.9 %collective-permute-start = (bf16[512,1024]{1,0:T(8,128)(2,1)}, bf16[512,1024]{1,0:T(8,128)(2,1)}, u32[]{:S(2)}, u32[]{:S(2)}) collective-permute-start(bf16[512,1024]{1,0:T(8,128)(2,1)} %param.10), channel_id=1, source_target_pairs={{0,4},{4,0},{1,5},{5,1},{2,6},{6,2},{3,7},{7,3},{8,12},{12,8},{9,1... | collective-permute-start | bytes 3145736 | tf_op jit(solution)/shard_map/ppermute | solution.py:53
  16.1 10.9 %all-to-all-start = ((bf16[64,32,128]{2,1,0:T(8,128)(2,1)}), bf16[64,32,128]{2,1,0:T(8,128)(2,1)S(1)}, u32[]{:S(2)}, u32[]{:S(2)}) async-start(bf16[64,32,128]{2,1,0:T(8,128)(2,1)} %bitcast.71), calls=%async_computation | async-start | bytes 1048576 | tf_op jit(solution)/shard_map/all_to_all | solution.py:30
  30.4 1.2 dynamic_slice.26
  34.3 1.3 fusion.55
  36.3 2.3 %copy.20 = bf16[2048,1,256]{0,2,1:T(8,128)(2,1)} copy(bf16[2048,1,256]{2,0,1:T(8,128)(2,1)} %param.11) | data formatting | bytes 2097152 | tf_op args[1]
  40.4 3.1 %fusion.20 = f32[512]{0:T(512)S(1)} fusion(bf16[512,1024]{1,0:T(8,128)(2,1)} %param.10, bf16[512,1024]{1,0:T(8,128)(2,1)} %collective-permute-done, pred[]{:T(512)S(6)} %eq.18), kind=kLoop, calls=%fused_computation.18 | loop fusion | flops 12582400 | bytes 2099201 | tf_op jit(solution)/shard_map/reduce_sum | solution.py:65
  43.5 3.6 %fusion.24 = f32[512,128]{0,1:T(8,128)S(1)} fusion(f32[512]{0:T(512)S(1)} %add_rsqrt_fusion, bf16[2048,1,128]{2,0,1:T(8,128)(2,1)} %param.12, bf16[512,1024]{1,0:T(8,128)(2,1)} %collective-permute-done, bf16[512,1024]{1,0:T(8,128)(2,1)} %param.10, pred[]{:T(512)S(6)} %eq.18), kind=kOutput, calls=%fused_computation.27 | convolution fusion | flops 281018368 | bytes 2885633 | tf_op jit(solution)/shard_map/dot_general | solution.py:72
  49.3 12.4 %all-to-all-start.1 = ((bf16[64,40,128]{2,1,0:T(8,128)(2,1)}), bf16[64,40,128]{2,1,0:T(8,128)(2,1)}, u32[]{:S(2)}, u32[]{:S(2)}) async-start(bf16[64,40,128]{2,1,0:T(8,128)(2,1)} %pad_maximum_fusion), calls=%async_computation.1 | async-start | bytes 1310720 | tf_op jit(solution)/shard_map/all_to_all | solution.py:30
  63.5 3.5 %fusion.22 = f32[512,4,64]{0,2,1:T(8,128)S(1)} fusion(bf16[4,64,2048]{2,1,0:T(8,128)(2,1)} %bitcast.73, f32[512]{0:T(512)S(1)} %add_rsqrt_fusion, bf16[512,1024]{1,0:T(8,128)(2,1)} %collective-permute-done, bf16[512,1024]{1,0:T(8,128)(2,1)} %param.10, pred[]{:T(512)S(6)} %eq.18), kind=kOutput, calls=%fused_computation.22 | convolution fusion | flops 549453824 | bytes 3672065 | tf_op jit(solution)/shard_map/dot_general | solution.py:100
  67.2 13.0 %all-to-all-done.1 = bf16[64,40,128]{2,1,0:T(8,128)(2,1)} async-done(((bf16[64,40,128]{2,1,0:T(8,128)(2,1)}), bf16[64,40,128]{2,1,0:T(8,128)(2,1)}, u32[]{:S(2)}, u32[]{:S(2)}) %all-to-all-start.1) | async-done | bytes 655392 | tf_op jit(solution)/shard_map/all_to_all | solution.py:30
  80.2 1.1 slice.71
  81.5 2.1 %pad_maximum_fusion.1 = (bf16[2560,64]{1,0:T(8,128)(2,1)S(1)}, bf16[2560,64]{1,0:T(8,128)(2,1)}) fusion(bf16[512,64]{1,0:T(8,128)(2,1)} %copy.22, bf16[2048,64]{1,0:T(8,128)(2,1)S(1)} %get-tuple-element.74, bf16[512,64]{1,0:T(8,128)(2,1)} %copy.23, bf16[2048,64]{1,0:T(8,128)(2,1)S(1)} %get-tuple-element.73), kind=kLoop, calls=%fused_computation.29 | loop fusion | flops 1310720 | bytes 1310720 | tf_op jit(solution)/shard_map/concatenate | solution.py:115
  83.6 13.1 %while.10 = (s32[]{:T(128)}, bf16[4,512,64]{1,2,0:T(8,128)(2,1)S(1)}, bf16[4,512,64]{1,2,0:T(8,128)(2,1)S(1)}, bf16[2560,64]{1,0:T(8,128)(2,1)S(1)}, pred[512,25...) while((s32[]{:T(128)}, bf16[4,512,64]{1,2,0:T(8,128)(2,1)S(1)}, ...), condition=%wide.region_4.5_spmd, body=%wide.region_1.0_spmd.sunk | while | flops 344783872 | bytes 19802224 | solution.py:131
  83.6 1.2 fusion.70
  85.8 1.0 fusion.72
  86.8 1.2 fusion.70
  90.1 1.2 fusion.70
  93.4 1.2 fusion.70
  96.7 1.4 %convolution_convert_fusion = bf16[512,1024]{1,0:T(8,128)(2,1)} fusion(bf16[512,256]{0,1:T(8,128)(2,1)S(1)} %bitcast.74, bf16[1,256,2048]{2,1,0:T(8,128)(2,1)S(1)} %copy-done, s32[]{:T(128)S(6)} %select_n.88), kind=kOutput, calls=%fused_computation.25 | convolution fusion | flops 268959744 | bytes 1835012 | tf_op jit(solution)/shard_map/dot_general | solution.py:148
  98.1 5.6 %collective-permute-start.1 = (bf16[512,1024]{1,0:T(8,128)(2,1)}, bf16[512,1024]{1,0:T(8,128)(2,1)S(1)}, u32[]{:S(2)}, u32[]{:S(2)}) collective-permute-start(bf16[512,1024]{1,0:T(8,128)(2,1)} %convolution_convert_fusion), channel_id=1, source_target_pairs={{0,4},{4,0},{1,5},{5,1},{2,6},{6,2},{3,7},{7,3},{8,12},{12,8},{9,1... | collective-permute-start | bytes 3145736 | tf_op jit(solution)/shard_map/ppermute | solution.py:153
  103.7 2.5 %collective-permute-done.1 = bf16[512,1024]{1,0:T(8,128)(2,1)S(1)} collective-permute-done((bf16[512,1024]{1,0:T(8,128)(2,1)}, bf16[512,1024]{1,0:T(8,128)(2,1)S(1)}, u32[]{:S(2)}, u32[]{:S(2)}) %collective-permute-start.1) | collective-permute-done | bytes 1048608 | tf_op jit(solution)/shard_map/ppermute | solution.py:153
  106.2 1.4 %add_convert_fusion = bf16[512,1024]{1,0:T(8,128)(2,1)} fusion(bf16[512,1024]{1,0:T(8,128)(2,1)S(1)} %collective-permute-done.1, bf16[512,256]{0,1:T(8,128)(2,1)S(1)} %bitcast.75, bf16[1,256,2048]{2,1,0:T(8,128)(2,1)S(1)} %copy-done, s32[]{:T(128)S(6)} %select_n.87), kind=kOutput, calls=%fused_computation.24 | convolution fusion | flops 270008320 | bytes 2883588 | tf_op jit(solution)/shard_map/dot_general | solution.py:154
  112.6 5.9 %all-to-all-start.2 = ((bf16[64,8,128]{2,1,0:T(8,128)(2,1)}), bf16[64,8,128]{2,1,0:T(8,128)(2,1)S(1)}, u32[]{:S(2)}, u32[]{:S(2)}) async-start(bf16[64,8,128]{2,1,0:T(8,128)(2,1)} %broadcast_select_fusion.1), calls=%async_computation.3 | async-start | bytes 262144 | tf_op jit(solution)/shard_map/all_to_all | solution.py:34
  118.6 11.4 %all-to-all-done.2 = bf16[64,8,128]{2,1,0:T(8,128)(2,1)S(1)} async-done(((bf16[64,8,128]{2,1,0:T(8,128)(2,1)}), bf16[64,8,128]{2,1,0:T(8,128)(2,1)S(1)}, u32[]{:S(2)}, u32[]{:S(2)}) %all-to-all-start.2) | async-done | bytes 131104 | tf_op jit(solution)/shard_map/all_to_all | solution.py:34
  (75 shorter events, 21.1 us)
Async XLA Ops:
  7.2 89.5 %copy-start = (bf16[1,256,2048]{2,1,0:T(8,128)(2,1)S(1)}, bf16[1,256,2048]{2,1,0:T(8,128)(2,1)}, u32[]{:S(2)}) copy-start(bf16[1,256,2048]{2,1,0:T(8,128)(2,1)} %param.13) | copy-start | bytes 3145732
  7.2 31.4 %copy-start.6 = (s32[64]{0:T(128)S(1)}, s32[64]{0:T(128)}, u32[]{:S(2)}) copy-start(s32[64]{0:T(128)} %param.17) | copy-start | bytes 772
  7.2 33.2 %collective-permute-start = (bf16[512,1024]{1,0:T(8,128)(2,1)}, bf16[512,1024]{1,0:T(8,128)(2,1)}, u32[]{:S(2)}, u32[]{:S(2)}) collective-permute-start(bf16[512,1024]{1,0:T(8,128)(2,1)} %param.10), channel_id=1, source_target_pairs={{0,4},{4,0},{1,5},{5,1},{2,6},{6,2},{3,7},{7,3},{8,12},{12,8},{9,1... | collective-permute-start | bytes 3145736 | tf_op jit(solution)/shard_map/ppermute | solution.py:53
  16.1 31.4 %all-to-all-start = ((bf16[64,32,128]{2,1,0:T(8,128)(2,1)}), bf16[64,32,128]{2,1,0:T(8,128)(2,1)S(1)}, u32[]{:S(2)}, u32[]{:S(2)}) async-start(bf16[64,32,128]{2,1,0:T(8,128)(2,1)} %bitcast.71), calls=%async_computation | async-start | bytes 1048576 | tf_op jit(solution)/shard_map/all_to_all | solution.py:30
  49.3 30.9 %all-to-all-start.1 = ((bf16[64,40,128]{2,1,0:T(8,128)(2,1)}), bf16[64,40,128]{2,1,0:T(8,128)(2,1)}, u32[]{:S(2)}, u32[]{:S(2)}) async-start(bf16[64,40,128]{2,1,0:T(8,128)(2,1)} %pad_maximum_fusion), calls=%async_computation.1 | async-start | bytes 1310720 | tf_op jit(solution)/shard_map/all_to_all | solution.py:30
  61.7 70.3 %reduce-scatter.2.cloned.1.call-start = ((), (), s32[]{:S(2)}) async-start(), calls=%async_computation.4 | async-start | bytes 1310720 | tf_op jit(solution)/shard_map/reduce_scatter | solution.py:163
  63.5 3.6 %copy-start.4 = (f32[512,32]{0,1:T(8,128)S(1)}, f32[512,32]{0,1:T(8,128)}, u32[]{:S(2)}) copy-start(f32[512,32]{0,1:T(8,128)} %get-tuple-element.77) | copy-start | bytes 196612
  63.5 3.6 %copy-start.5 = (f32[512,32]{0,1:T(8,128)S(1)}, f32[512,32]{0,1:T(8,128)}, u32[]{:S(2)}) copy-start(f32[512,32]{0,1:T(8,128)} %get-tuple-element.78) | copy-start | bytes 196612
  81.3 2.3 %copy-start.3 = (bf16[4,512,64]{1,2,0:T(8,128)(2,1)S(1)}, bf16[4,512,64]{1,2,0:T(8,128)(2,1)}, u32[]{:S(2)}) copy-start(bf16[4,512,64]{1,2,0:T(8,128)(2,1)} %custom-call.4) | copy-start | bytes 786436
  84.7 1.1 copy-start.1
  88.0 1.1 copy-start.1
  91.3 1.1 copy-start.1
  94.5 1.1 copy-start.1
  98.1 12.1 %copy-start.2 = (bf16[1,1,2048,128]{3,2,1,0:T(8,128)(2,1)S(1)}, bf16[1,1,2048,128]{3,2,1,0:T(8,128)(2,1)}, u32[]{:S(2)}) copy-start(bf16[1,1,2048,128]{3,2,1,0:T(8,128)(2,1)} %param.14) | copy-start | bytes 1572868
  98.1 8.1 %collective-permute-start.1 = (bf16[512,1024]{1,0:T(8,128)(2,1)}, bf16[512,1024]{1,0:T(8,128)(2,1)S(1)}, u32[]{:S(2)}, u32[]{:S(2)}) collective-permute-start(bf16[512,1024]{1,0:T(8,128)(2,1)} %convolution_convert_fusion), channel_id=1, source_target_pairs={{0,4},{4,0},{1,5},{5,1},{2,6},{6,2},{3,7},{7,3},{8,12},{12,8},{9,1... | collective-permute-start | bytes 3145736 | tf_op jit(solution)/shard_map/ppermute | solution.py:153
  112.6 17.5 %all-to-all-start.2 = ((bf16[64,8,128]{2,1,0:T(8,128)(2,1)}), bf16[64,8,128]{2,1,0:T(8,128)(2,1)S(1)}, u32[]{:S(2)}, u32[]{:S(2)}) async-start(bf16[64,8,128]{2,1,0:T(8,128)(2,1)} %broadcast_select_fusion.1), calls=%async_computation.3 | async-start | bytes 262144 | tf_op jit(solution)/shard_map/all_to_all | solution.py:34
Sparse Core Ops, SparseCore 0:
  107.8 21.4 reduce-scatter.1

commit v11 on v9

--- a/solution.py
+++ b/solution.py
@@ -139,14 +139,14 @@
             attended,
             lax.dynamic_slice_in_dim(out_rows, (1 - core) * half_cols, half_cols, axis=1),
             preferred_element_type=jnp.float32,
-        )
+        ).astype(jnp.bfloat16)
         received = lax.ppermute(sent, "tx", [(0, 1), (1, 0)])
         kept = jnp.dot(
             attended,
             lax.dynamic_slice_in_dim(out_rows, core * half_cols, half_cols, axis=1),
             preferred_element_type=jnp.float32,
         )
-        across_cores = kept + received
+        across_cores = kept + received.astype(jnp.float32)
     else:
         partial_value = jnp.dot(attended, out_rows, preferred_element_type=jnp.float32)
         across_cores = lax.psum_scatter(partial_value, "tx", scatter_dimension=1, tiled=True)

time: 138 us -> 134 us (0.971)
  matrix products: 18.1 us -> 16.2 us
  waiting for transfers between devices: 34.7 us -> 33.1 us
    ppermute x1, waiting for transfers between devices: 4.09 us -> 2.47 us  [per_device(): received = lax.ppermute(sent, 'tx', [(0, 1), (1, 0)])]
    dot_general x1, matrix products: 3.01 us -> 1.45 us  [per_device(): jnp.dot(attended, lax.dynamic_slice_in_dim(out_rows, core * half_cols, ha...]
where the time goes in v11:
time: 134 us; the launch traced here: 133 us
  starting transfers between devices  37.3 us (28%)
  waiting for transfers between devices  33.1 us (25%)
  between operations  19.9 us (15%)
  matrix products  16.2 us (12%)
  other arithmetic  16 us (12%)
  local copies, waits for them, and re-layouts  9.87 us (7%)
    all_to_all x2, starting transfers between devices, carry_in(): return lax.all_to_all(window, 'dp', split_axis=0, concat_axis=0, tiled=True)  25.3 us
    all_to_all x2, waiting for transfers between devices, carry_in(): return lax.all_to_all(window, 'dp', split_axis=0, concat_axis=0, tiled=True)  18.5 us
    all_to_all x1, waiting for transfers between devices, carry_out(): return lax.all_to_all(window, 'dp', split_axis=0, concat_axis=0, tiled=True)  11.4 us
    ppermute x1, starting transfers between devices, per_device(): received = lax.ppermute(sent, 'tx', [(0, 1), (1, 0)])  6.22 us
    all_to_all x1, starting transfers between devices, carry_out(): return lax.all_to_all(window, 'dp', split_axis=0, concat_axis=0, tiled=True)  5.72 us
    dot_general x4, matrix products, one_head(): jnp.einsum('qd,kd->qk', query_rows, keys_all, preferred_element_type=jnp....  4.67 us
    dot_general x4, matrix products, one_head(): summed = jnp.dot(weights, values_all, preferred_element_type=jnp.float32)  3.94 us
    reduce_sum x4, other arithmetic, one_head(): total = jnp.sum(powers, axis=1, keepdims=True)  3.36 us
  transfers between devices with their start and end apart: 6, of which 4 were waited for; matrix products, arithmetic and copies ran while one was open for 13% of the time, Pallas kernels for 0%

profile of v11, /device:TPU:1, one launch (start us, length us, event | category | flops | bytes accessed | tf_op | source)
XLA Modules:
  0.0 132.5 jit_solution(6687395612877186987)
XLA Ops:
  7.9 17.1 %all-to-all-start = ((bf16[64,32,128]{2,1,0:T(8,128)(2,1)}), bf16[64,32,128]{2,1,0:T(8,128)(2,1)S(1)}, u32[]{:S(2)}, u32[]{:S(2)}) async-start(bf16[64,32,128]{2,1,0:T(8,128)(2,1)} %bitcast.69), calls=%async_computation | async-start | bytes 1048576 | tf_op jit(solution)/shard_map/all_to_all | solution.py:30
  32.5 9.0 %all-to-all-done = bf16[64,32,128]{2,1,0:T(8,128)(2,1)S(1)} async-done(((bf16[64,32,128]{2,1,0:T(8,128)(2,1)}), bf16[64,32,128]{2,1,0:T(8,128)(2,1)S(1)}, u32[]{:S(2)}, u32[]{:S(2)}) %all-to-all-start) | async-done | bytes 524320 | tf_op jit(solution)/shard_map/all_to_all | solution.py:30
  42.3 2.2 %fusion.20 = f32[512]{0:T(512)S(1)} fusion(bf16[512,2048]{1,0:T(8,128)(2,1)} %all-gather.2.cloned.1.call-done), kind=kLoop, calls=%fused_computation.18 | loop fusion | flops 3145216 | bytes 2099200 | tf_op jit(solution)/shard_map/reduce_sum | solution.py:56
  44.5 2.0 %fusion.24 = f32[512,128]{0,1:T(8,128)S(1)} fusion(bf16[512,2048]{1,0:T(8,128)(2,1)S(1)} %copy-done.3, f32[512]{0:T(512)S(1)} %add_rsqrt_fusion, bf16[2048,1,128]{2,0,1:T(8,128)(2,1)} %param.12), kind=kOutput, calls=%fused_computation.26 | convolution fusion | flops 271581184 | bytes 2885632 | tf_op jit(solution)/shard_map/dot_general | solution.py:63
  47.9 8.2 %all-to-all-start.1 = ((bf16[64,40,128]{2,1,0:T(8,128)(2,1)}), bf16[64,40,128]{2,1,0:T(8,128)(2,1)}, u32[]{:S(2)}, u32[]{:S(2)}) async-start(bf16[64,40,128]{2,1,0:T(8,128)(2,1)} %pad_maximum_fusion), calls=%async_computation.1 | async-start | bytes 1310720 | tf_op jit(solution)/shard_map/all_to_all | solution.py:30
  56.9 1.4 %copy.20 = bf16[2048,1,256]{0,2,1:T(8,128)(2,1)} copy(bf16[2048,1,256]{2,0,1:T(8,128)(2,1)S(1)} %copy-done.4) | data formatting | bytes 2097152 | tf_op args[1]
  59.3 1.1 pad_add_fusion
  61.9 2.7 %fusion.22 = f32[512,4,64]{0,2,1:T(8,128)S(1)} fusion(bf16[4,64,2048]{2,1,0:T(8,128)(2,1)} %bitcast.71, bf16[512,2048]{1,0:T(8,128)(2,1)} %all-gather.2.cloned.1.call-done, f32[512]{0:T(512)S(1)} %add_rsqrt_fusion), kind=kOutput, calls=%fused_computation.21 | convolution fusion | flops 540016640 | bytes 3672064 | tf_op jit(solution)/shard_map/dot_general | solution.py:90
  64.7 9.5 %all-to-all-done.1 = bf16[64,40,128]{2,1,0:T(8,128)(2,1)} async-done(((bf16[64,40,128]{2,1,0:T(8,128)(2,1)}), bf16[64,40,128]{2,1,0:T(8,128)(2,1)}, u32[]{:S(2)}, u32[]{:S(2)}) %all-to-all-start.1) | async-done | bytes 655392 | tf_op jit(solution)/shard_map/all_to_all | solution.py:30
  74.3 1.1 slice.71
  75.6 2.1 %pad_maximum_fusion.1 = (bf16[2560,64]{1,0:T(8,128)(2,1)S(1)}, bf16[2560,64]{1,0:T(8,128)(2,1)}) fusion(bf16[512,64]{1,0:T(8,128)(2,1)} %copy.22, bf16[2048,64]{1,0:T(8,128)(2,1)S(1)} %get-tuple-element.70, bf16[512,64]{1,0:T(8,128)(2,1)} %copy.23, bf16[2048,64]{1,0:T(8,128)(2,1)S(1)} %get-tuple-element.69), kind=kLoop, calls=%fused_computation.28 | loop fusion | flops 1310720 | bytes 1310720 | tf_op jit(solution)/shard_map/concatenate | solution.py:105
  77.6 13.1 %while.10 = (s32[]{:T(128)}, bf16[4,512,64]{1,2,0:T(8,128)(2,1)S(1)}, bf16[4,512,64]{1,2,0:T(8,128)(2,1)S(1)}, bf16[2560,64]{1,0:T(8,128)(2,1)S(1)}, pred[512,25...) while((s32[]{:T(128)}, bf16[4,512,64]{1,2,0:T(8,128)(2,1)S(1)}, ...), condition=%wide.region_4.5_spmd, body=%wide.region_1.4_spmd.sunk | while | flops 344783872 | bytes 19802232 | solution.py:121
  77.6 1.2 fusion.70
  80.9 1.2 fusion.70
  83.2 1.0 fusion.72
  84.2 1.2 fusion.70
  87.4 1.2 fusion.70
  89.7 1.0 fusion.72
  90.7 1.5 %convolution_convert_fusion = bf16[512,1024]{1,0:T(8,128)(2,1)} fusion(bf16[512,256]{0,1:T(8,128)(2,1)S(1)} %bitcast.72, bf16[1,256,2048]{2,1,0:T(8,128)(2,1)S(1)} %copy-done, s32[]{:T(128)S(6)} %select_n.78), kind=kOutput, calls=%fused_computation.24 | convolution fusion | flops 268959744 | bytes 1835012 | tf_op jit(solution)/shard_map/dot_general | solution.py:138
  92.2 6.2 %collective-permute-start = (bf16[512,1024]{1,0:T(8,128)(2,1)}, bf16[512,1024]{1,0:T(8,128)(2,1)S(1)}, u32[]{:S(2)}, u32[]{:S(2)}) collective-permute-start(bf16[512,1024]{1,0:T(8,128)(2,1)} %convolution_convert_fusion), channel_id=1, source_target_pairs={{0,4},{4,0},{1,5},{5,1},{2,6},{6,2},{3,7},{7,3},{8,12},{12,8},{9,1... | collective-permute-start | bytes 3145736 | tf_op jit(solution)/shard_map/ppermute | solution.py:143
  98.4 2.5 %collective-permute-done = bf16[512,1024]{1,0:T(8,128)(2,1)S(1)} collective-permute-done((bf16[512,1024]{1,0:T(8,128)(2,1)}, bf16[512,1024]{1,0:T(8,128)(2,1)S(1)}, u32[]{:S(2)}, u32[]{:S(2)}) %collective-permute-start) | collective-permute-done | bytes 1048608 | tf_op jit(solution)/shard_map/ppermute | solution.py:143
  100.9 1.4 %add_convert_fusion = bf16[512,1024]{1,0:T(8,128)(2,1)} fusion(bf16[512,1024]{1,0:T(8,128)(2,1)S(1)} %collective-permute-done, bf16[512,256]{0,1:T(8,128)(2,1)S(1)} %bitcast.73, bf16[1,256,2048]{2,1,0:T(8,128)(2,1)S(1)} %copy-done, s32[]{:T(128)S(6)} %select_n.77), kind=kOutput, calls=%fused_computation.23 | convolution fusion | flops 270008320 | bytes 2883588 | tf_op jit(solution)/shard_map/dot_general | solution.py:144
  107.0 5.7 %all-to-all-start.2 = ((bf16[64,8,128]{2,1,0:T(8,128)(2,1)}), bf16[64,8,128]{2,1,0:T(8,128)(2,1)S(1)}, u32[]{:S(2)}, u32[]{:S(2)}) async-start(bf16[64,8,128]{2,1,0:T(8,128)(2,1)} %broadcast_select_fusion.1), calls=%async_computation.3 | async-start | bytes 262144 | tf_op jit(solution)/shard_map/all_to_all | solution.py:34
  112.8 11.4 %all-to-all-done.2 = bf16[64,8,128]{2,1,0:T(8,128)(2,1)S(1)} async-done(((bf16[64,8,128]{2,1,0:T(8,128)(2,1)}), bf16[64,8,128]{2,1,0:T(8,128)(2,1)S(1)}, u32[]{:S(2)}, u32[]{:S(2)}) %all-to-all-start.2) | async-done | bytes 131104 | tf_op jit(solution)/shard_map/all_to_all | solution.py:34
  (84 shorter events, 20.8 us)
Async XLA Ops:
  7.2 83.5 %copy-start = (bf16[1,256,2048]{2,1,0:T(8,128)(2,1)S(1)}, bf16[1,256,2048]{2,1,0:T(8,128)(2,1)}, u32[]{:S(2)}) copy-start(bf16[1,256,2048]{2,1,0:T(8,128)(2,1)} %param.13) | copy-start | bytes 3145732
  7.2 17.9 %copy-start.10 = (s32[64]{0:T(128)S(1)}, s32[64]{0:T(128)}, u32[]{:S(2)}) copy-start(s32[64]{0:T(128)} %param.17) | copy-start | bytes 772
  7.2 19.9 %copy-start.9 = (s32[64]{0:T(128)S(1)}, s32[64]{0:T(128)}, u32[]{:S(2)}) copy-start(s32[64]{0:T(128)} %param.15) | copy-start | bytes 772
  7.2 21.8 %copy-start.8 = (s32[64]{0:T(128)S(1)}, s32[64]{0:T(128)}, u32[]{:S(2)}) copy-start(s32[64]{0:T(128)} %param.16) | copy-start | bytes 772
  7.2 35.1 %all-gather.2.cloned.1.call-start = ((), (), s32[]{:S(2)}) async-start(), calls=%async_computation.4 | async-start | bytes 3145728 | tf_op jit(solution)/shard_map/all_gather | solution.py:51
  7.9 33.5 %all-to-all-start = ((bf16[64,32,128]{2,1,0:T(8,128)(2,1)}), bf16[64,32,128]{2,1,0:T(8,128)(2,1)S(1)}, u32[]{:S(2)}, u32[]{:S(2)}) async-start(bf16[64,32,128]{2,1,0:T(8,128)(2,1)} %bitcast.69), calls=%async_computation | async-start | bytes 1048576 | tf_op jit(solution)/shard_map/all_to_all | solution.py:30
  42.3 2.2 %copy-start.3 = (bf16[512,2048]{1,0:T(8,128)(2,1)S(1)}, bf16[512,2048]{1,0:T(8,128)(2,1)}, u32[]{:S(2)}) copy-start(bf16[512,2048]{1,0:T(8,128)(2,1)} %all-gather.2.cloned.1.call-done) | copy-start | bytes 6291460
  47.9 9.0 %copy-start.4 = (bf16[2048,1,256]{2,0,1:T(8,128)(2,1)S(1)}, bf16[2048,1,256]{2,0,1:T(8,128)(2,1)}, u32[]{:S(2)}) copy-start(bf16[2048,1,256]{2,0,1:T(8,128)(2,1)} %param.11) | copy-start | bytes 3145732
  47.9 26.3 %all-to-all-start.1 = ((bf16[64,40,128]{2,1,0:T(8,128)(2,1)}), bf16[64,40,128]{2,1,0:T(8,128)(2,1)}, u32[]{:S(2)}, u32[]{:S(2)}) async-start(bf16[64,40,128]{2,1,0:T(8,128)(2,1)} %pad_maximum_fusion), calls=%async_computation.1 | async-start | bytes 1310720 | tf_op jit(solution)/shard_map/all_to_all | solution.py:30
  56.1 69.6 %reduce-scatter.2.cloned.1.call-start = ((), (), s32[]{:S(2)}) async-start(), calls=%async_computation.5 | async-start | bytes 1310720 | tf_op jit(solution)/shard_map/reduce_scatter | solution.py:153
  61.9 2.7 %copy-start.6 = (f32[512,32]{0,1:T(8,128)S(1)}, f32[512,32]{0,1:T(8,128)}, u32[]{:S(2)}) copy-start(f32[512,32]{0,1:T(8,128)} %get-tuple-element.73) | copy-start | bytes 196612
  61.9 2.7 %copy-start.7 = (f32[512,32]{0,1:T(8,128)S(1)}, f32[512,32]{0,1:T(8,128)}, u32[]{:S(2)}) copy-start(f32[512,32]{0,1:T(8,128)} %get-tuple-element.74) | copy-start | bytes 196612
  75.3 2.3 %copy-start.5 = (bf16[4,512,64]{1,2,0:T(8,128)(2,1)S(1)}, bf16[4,512,64]{1,2,0:T(8,128)(2,1)}, u32[]{:S(2)}) copy-start(bf16[4,512,64]{1,2,0:T(8,128)(2,1)} %custom-call.4) | copy-start | bytes 786436
  78.8 1.1 copy-start.1
  82.1 1.1 copy-start.1
  85.3 1.1 copy-start.1
  88.6 1.1 copy-start.1
  92.2 12.5 %copy-start.2 = (bf16[1,1,2048,128]{3,2,1,0:T(8,128)(2,1)S(1)}, bf16[1,1,2048,128]{3,2,1,0:T(8,128)(2,1)}, u32[]{:S(2)}) copy-start(bf16[1,1,2048,128]{3,2,1,0:T(8,128)(2,1)} %param.14) | copy-start | bytes 1572868
  92.2 8.7 %collective-permute-start = (bf16[512,1024]{1,0:T(8,128)(2,1)}, bf16[512,1024]{1,0:T(8,128)(2,1)S(1)}, u32[]{:S(2)}, u32[]{:S(2)}) collective-permute-start(bf16[512,1024]{1,0:T(8,128)(2,1)} %convolution_convert_fusion), channel_id=1, source_target_pairs={{0,4},{4,0},{1,5},{5,1},{2,6},{6,2},{3,7},{7,3},{8,12},{12,8},{9,1... | collective-permute-start | bytes 3145736 | tf_op jit(solution)/shard_map/ppermute | solution.py:143
  107.0 17.2 %all-to-all-start.2 = ((bf16[64,8,128]{2,1,0:T(8,128)(2,1)}), bf16[64,8,128]{2,1,0:T(8,128)(2,1)S(1)}, u32[]{:S(2)}, u32[]{:S(2)}) async-start(bf16[64,8,128]{2,1,0:T(8,128)(2,1)} %broadcast_select_fusion.1), calls=%async_computation.3 | async-start | bytes 262144 | tf_op jit(solution)/shard_map/all_to_all | solution.py:34
Sparse Core Ops, SparseCore 0:
  10.1 25.6 all-gather.1
  102.5 21.2 reduce-scatter.1

commit v12 on v11

--- a/solution.py
+++ b/solution.py
@@ -71,6 +71,7 @@
     new_values = rotation_pairs[:, HEAD_SIZE:].astype(jnp.bfloat16)
     entry = jnp.concatenate([new_keys, new_values], axis=1)
 
+    spread, entry = lax.optimization_barrier((spread, entry))
     window_chunk = half_rows // groups
     entry_chunk = rows_new // groups
     lanes = stored.shape[1]

time: 134 us -> 133 us (level)
  waiting for transfers between devices: 33.1 us -> 29 us
  starting transfers between devices: 37.3 us -> 39.4 us
    all_to_all x2, waiting for transfers between devices: 18.5 us -> 11.5 us  [carry_in(): return lax.all_to_all(window, 'dp', split_axis=0, concat_axis=0, tiled=True)]
    all_to_all x2, starting transfers between devices: 25.3 us -> 28.4 us  [carry_in(): return lax.all_to_all(window, 'dp', split_axis=0, concat_axis=0, tiled=True)]
    all_gather x1, waiting for transfers between devices: 0.02 us -> 2.86 us  [per_device(): whole = lax.all_gather(tokens, 'tx', axis=1, tiled=True)]
    ppermute x1, starting transfers between devices: 6.22 us -> 4.72 us  [per_device(): received = lax.ppermute(sent, 'tx', [(0, 1), (1, 0)])]
  transfers between devices with their start and end apart: 6 -> 6, of which waited for: 4 -> 5; matrix products, arithmetic and copies ran while one was open for 13% -> 16% of each run, Pallas kernels for 0% -> 0%
where the time goes in v12:
time: 133 us; the launch traced here: 132 us
  starting transfers between devices  39.4 us (30%)
  waiting for transfers between devices  29 us (22%)
  between operations  19.9 us (15%)
  other arithmetic  17.1 us (13%)
  matrix products  16.2 us (12%)
  local copies, waits for them, and re-layouts  9.86 us (7%)
    all_to_all x2, starting transfers between devices, carry_in(): return lax.all_to_all(window, 'dp', split_axis=0, concat_axis=0, tiled=True)  28.4 us
    all_to_all x2, waiting for transfers between devices, carry_in(): return lax.all_to_all(window, 'dp', split_axis=0, concat_axis=0, tiled=True)  11.5 us
    all_to_all x1, waiting for transfers between devices, carry_out(): return lax.all_to_all(window, 'dp', split_axis=0, concat_axis=0, tiled=True)  11.4 us
    all_to_all x1, starting transfers between devices, carry_out(): return lax.all_to_all(window, 'dp', split_axis=0, concat_axis=0, tiled=True)  6.22 us
    ppermute x1, starting transfers between devices, per_device(): received = lax.ppermute(sent, 'tx', [(0, 1), (1, 0)])  4.72 us
    dot_general x4, matrix products, one_head(): jnp.einsum('qd,kd->qk', query_rows, keys_all, preferred_element_type=jnp....  4.66 us
    dot_general x4, matrix products, one_head(): summed = jnp.dot(weights, values_all, preferred_element_type=jnp.float32)  3.94 us
    reduce_sum x4, other arithmetic, one_head(): total = jnp.sum(powers, axis=1, keepdims=True)  3.36 us
  transfers between devices with their start and end apart: 6, of which 5 were waited for; matrix products, arithmetic and copies ran while one was open for 16% of the time, Pallas kernels for 0%

profile of v12, /device:TPU:1, one launch (start us, length us, event | category | flops | bytes accessed | tf_op | source)
XLA Modules:
  0.0 131.5 jit_solution(488929932526855462)
XLA Ops:
  7.9 17.1 %all-to-all-start = ((bf16[64,32,128]{2,1,0:T(8,128)(2,1)}), bf16[64,32,128]{2,1,0:T(8,128)(2,1)S(1)}, u32[]{:S(2)}, u32[]{:S(2)}) async-start(bf16[64,32,128]{2,1,0:T(8,128)(2,1)} %bitcast.71), calls=%async_computation | async-start | bytes 1048576 | tf_op jit(solution)/shard_map/all_to_all | solution.py:30
  33.0 2.9 %all-gather.2.cloned.1.call-done = bf16[512,2048]{1,0:T(8,128)(2,1)} async-done(((bf16[512,1024]{1,0:T(8,128)(2,1)}), bf16[512,2048]{1,0:T(8,128)(2,1)}) %all-gather.2.cloned.1.call-update) | async-done | bytes 2097168 | tf_op jit(solution)/shard_map/all_gather | solution.py:51
  35.8 2.2 %fusion.20 = f32[512]{0:T(512)S(1)} fusion(bf16[512,2048]{1,0:T(8,128)(2,1)} %all-gather.2.cloned.1.call-done), kind=kLoop, calls=%fused_computation.18 | loop fusion | flops 3145216 | bytes 2099200 | tf_op jit(solution)/shard_map/reduce_sum | solution.py:56
  38.1 2.0 %fusion.24 = f32[512,128]{0,1:T(8,128)S(1)} fusion(bf16[512,2048]{1,0:T(8,128)(2,1)S(1)} %copy-done.3, f32[512]{0:T(512)S(1)} %add_rsqrt_fusion, bf16[2048,1,128]{2,0,1:T(8,128)(2,1)} %param.12), kind=kOutput, calls=%fused_computation.26 | convolution fusion | flops 271581184 | bytes 2885632 | tf_op jit(solution)/shard_map/dot_general | solution.py:63
  40.4 1.0 all-to-all-done
  43.9 11.3 %all-to-all-start.1 = ((bf16[64,40,128]{2,1,0:T(8,128)(2,1)}), bf16[64,40,128]{2,1,0:T(8,128)(2,1)}, u32[]{:S(2)}, u32[]{:S(2)}) async-start(bf16[64,40,128]{2,1,0:T(8,128)(2,1)} %pad_maximum_fusion), calls=%async_computation.1 | async-start | bytes 1310720 | tf_op jit(solution)/shard_map/all_to_all | solution.py:30
  56.0 1.4 %copy.20 = bf16[2048,1,256]{0,2,1:T(8,128)(2,1)} copy(bf16[2048,1,256]{2,0,1:T(8,128)(2,1)S(1)} %copy-done.4) | data formatting | bytes 2097152 | tf_op args[1]
  58.4 1.1 pad_add_fusion
  61.0 2.7 %fusion.22 = f32[512,4,64]{0,2,1:T(8,128)S(1)} fusion(bf16[4,64,2048]{2,1,0:T(8,128)(2,1)} %bitcast.73, bf16[512,2048]{1,0:T(8,128)(2,1)} %all-gather.2.cloned.1.call-done, f32[512]{0:T(512)S(1)} %add_rsqrt_fusion), kind=kOutput, calls=%fused_computation.21 | convolution fusion | flops 540016640 | bytes 3672064 | tf_op jit(solution)/shard_map/dot_general | solution.py:91
  63.8 10.5 %all-to-all-done.1 = bf16[64,40,128]{2,1,0:T(8,128)(2,1)} async-done(((bf16[64,40,128]{2,1,0:T(8,128)(2,1)}), bf16[64,40,128]{2,1,0:T(8,128)(2,1)}, u32[]{:S(2)}, u32[]{:S(2)}) %all-to-all-start.1) | async-done | bytes 655392 | tf_op jit(solution)/shard_map/all_to_all | solution.py:30
  74.3 1.1 slice.71
  75.6 2.1 %pad_maximum_fusion.1 = (bf16[2560,64]{1,0:T(8,128)(2,1)S(1)}, bf16[2560,64]{1,0:T(8,128)(2,1)}) fusion(bf16[512,64]{1,0:T(8,128)(2,1)} %copy.22, bf16[2048,64]{1,0:T(8,128)(2,1)S(1)} %get-tuple-element.74, bf16[512,64]{1,0:T(8,128)(2,1)} %copy.23, bf16[2048,64]{1,0:T(8,128)(2,1)S(1)} %get-tuple-element.73), kind=kLoop, calls=%fused_computation.28 | loop fusion | flops 1310720 | bytes 1310720 | tf_op jit(solution)/shard_map/concatenate | solution.py:106
  77.7 13.1 %while.10 = (s32[]{:T(128)}, bf16[4,512,64]{1,2,0:T(8,128)(2,1)S(1)}, bf16[4,512,64]{1,2,0:T(8,128)(2,1)S(1)}, bf16[2560,64]{1,0:T(8,128)(2,1)S(1)}, pred[512,25...) while((s32[]{:T(128)}, bf16[4,512,64]{1,2,0:T(8,128)(2,1)S(1)}, ...), condition=%wide.region_4.5_spmd, body=%wide.region_1.4_spmd.sunk | while | flops 344783872 | bytes 19802224 | solution.py:122
  77.7 1.2 fusion.70
  80.0 1.0 fusion.72
  81.0 1.2 fusion.70
  84.2 1.2 fusion.70
  87.5 1.2 fusion.70
  90.8 1.4 %convolution_convert_fusion = bf16[512,1024]{1,0:T(8,128)(2,1)} fusion(bf16[512,256]{0,1:T(8,128)(2,1)S(1)} %bitcast.74, bf16[1,256,2048]{2,1,0:T(8,128)(2,1)S(1)} %copy-done, s32[]{:T(128)S(6)} %select_n.78), kind=kOutput, calls=%fused_computation.24 | convolution fusion | flops 268959744 | bytes 1835012 | tf_op jit(solution)/shard_map/dot_general | solution.py:139
  92.2 4.7 %collective-permute-start = (bf16[512,1024]{1,0:T(8,128)(2,1)}, bf16[512,1024]{1,0:T(8,128)(2,1)S(1)}, u32[]{:S(2)}, u32[]{:S(2)}) collective-permute-start(bf16[512,1024]{1,0:T(8,128)(2,1)} %convolution_convert_fusion), channel_id=1, source_target_pairs={{0,4},{4,0},{1,5},{5,1},{2,6},{6,2},{3,7},{7,3},{8,12},{12,8},{9,1... | collective-permute-start | bytes 3145736 | tf_op jit(solution)/shard_map/ppermute | solution.py:144
  97.0 2.5 %collective-permute-done = bf16[512,1024]{1,0:T(8,128)(2,1)S(1)} collective-permute-done((bf16[512,1024]{1,0:T(8,128)(2,1)}, bf16[512,1024]{1,0:T(8,128)(2,1)S(1)}, u32[]{:S(2)}, u32[]{:S(2)}) %collective-permute-start) | collective-permute-done | bytes 1048608 | tf_op jit(solution)/shard_map/ppermute | solution.py:144
  99.4 1.4 %add_convert_fusion = bf16[512,1024]{1,0:T(8,128)(2,1)} fusion(bf16[512,1024]{1,0:T(8,128)(2,1)S(1)} %collective-permute-done, bf16[512,256]{0,1:T(8,128)(2,1)S(1)} %bitcast.75, bf16[1,256,2048]{2,1,0:T(8,128)(2,1)S(1)} %copy-done, s32[]{:T(128)S(6)} %select_n.77), kind=kOutput, calls=%fused_computation.23 | convolution fusion | flops 270008320 | bytes 2883588 | tf_op jit(solution)/shard_map/dot_general | solution.py:145
  105.5 6.2 %all-to-all-start.2 = ((bf16[64,8,128]{2,1,0:T(8,128)(2,1)}), bf16[64,8,128]{2,1,0:T(8,128)(2,1)S(1)}, u32[]{:S(2)}, u32[]{:S(2)}) async-start(bf16[64,8,128]{2,1,0:T(8,128)(2,1)} %broadcast_select_fusion.1), calls=%async_computation.3 | async-start | bytes 262144 | tf_op jit(solution)/shard_map/all_to_all | solution.py:34
  111.8 11.4 %all-to-all-done.2 = bf16[64,8,128]{2,1,0:T(8,128)(2,1)S(1)} async-done(((bf16[64,8,128]{2,1,0:T(8,128)(2,1)}), bf16[64,8,128]{2,1,0:T(8,128)(2,1)S(1)}, u32[]{:S(2)}, u32[]{:S(2)}) %all-to-all-start.2) | async-done | bytes 131104 | tf_op jit(solution)/shard_map/all_to_all | solution.py:34
  (88 shorter events, 22.9 us)
Async XLA Ops:
  7.2 83.6 %copy-start = (bf16[1,256,2048]{2,1,0:T(8,128)(2,1)S(1)}, bf16[1,256,2048]{2,1,0:T(8,128)(2,1)}, u32[]{:S(2)}) copy-start(bf16[1,256,2048]{2,1,0:T(8,128)(2,1)} %param.13) | copy-start | bytes 3145732
  7.2 17.9 %copy-start.10 = (s32[64]{0:T(128)S(1)}, s32[64]{0:T(128)}, u32[]{:S(2)}) copy-start(s32[64]{0:T(128)} %param.17) | copy-start | bytes 772
  7.2 19.9 %copy-start.9 = (s32[64]{0:T(128)S(1)}, s32[64]{0:T(128)}, u32[]{:S(2)}) copy-start(s32[64]{0:T(128)} %param.15) | copy-start | bytes 772
  7.2 21.2 %copy-start.8 = (s32[64]{0:T(128)S(1)}, s32[64]{0:T(128)}, u32[]{:S(2)}) copy-start(s32[64]{0:T(128)} %param.16) | copy-start | bytes 772
  7.2 28.6 %all-gather.2.cloned.1.call-start = ((), (), s32[]{:S(2)}) async-start(), calls=%async_computation.4 | async-start | bytes 3145728 | tf_op jit(solution)/shard_map/all_gather | solution.py:51
  7.9 33.5 %all-to-all-start = ((bf16[64,32,128]{2,1,0:T(8,128)(2,1)}), bf16[64,32,128]{2,1,0:T(8,128)(2,1)S(1)}, u32[]{:S(2)}, u32[]{:S(2)}) async-start(bf16[64,32,128]{2,1,0:T(8,128)(2,1)} %bitcast.71), calls=%async_computation | async-start | bytes 1048576 | tf_op jit(solution)/shard_map/all_to_all | solution.py:30
  25.2 14.8 %copy-start.11 = (s32[64]{0:T(128)}, s32[64]{0:T(128)S(1)}, u32[]{:S(2)}) copy-start(s32[64]{0:T(128)S(1)} %select_reduce_fusion) | copy-start | bytes 772
  35.8 2.2 %copy-start.3 = (bf16[512,2048]{1,0:T(8,128)(2,1)S(1)}, bf16[512,2048]{1,0:T(8,128)(2,1)}, u32[]{:S(2)}) copy-start(bf16[512,2048]{1,0:T(8,128)(2,1)} %all-gather.2.cloned.1.call-done) | copy-start | bytes 6291460
  43.0 13.0 %copy-start.4 = (bf16[2048,1,256]{2,0,1:T(8,128)(2,1)S(1)}, bf16[2048,1,256]{2,0,1:T(8,128)(2,1)}, u32[]{:S(2)}) copy-start(bf16[2048,1,256]{2,0,1:T(8,128)(2,1)} %param.11) | copy-start | bytes 3145732
  43.9 30.4 %all-to-all-start.1 = ((bf16[64,40,128]{2,1,0:T(8,128)(2,1)}), bf16[64,40,128]{2,1,0:T(8,128)(2,1)}, u32[]{:S(2)}, u32[]{:S(2)}) async-start(bf16[64,40,128]{2,1,0:T(8,128)(2,1)} %pad_maximum_fusion), calls=%async_computation.1 | async-start | bytes 1310720 | tf_op jit(solution)/shard_map/all_to_all | solution.py:30
  55.2 69.5 %reduce-scatter.2.cloned.1.call-start = ((), (), s32[]{:S(2)}) async-start(), calls=%async_computation.5 | async-start | bytes 1310720 | tf_op jit(solution)/shard_map/reduce_scatter | solution.py:154
  61.0 2.7 %copy-start.6 = (f32[512,32]{0,1:T(8,128)S(1)}, f32[512,32]{0,1:T(8,128)}, u32[]{:S(2)}) copy-start(f32[512,32]{0,1:T(8,128)} %get-tuple-element.77) | copy-start | bytes 196612
  61.0 2.7 %copy-start.7 = (f32[512,32]{0,1:T(8,128)S(1)}, f32[512,32]{0,1:T(8,128)}, u32[]{:S(2)}) copy-start(f32[512,32]{0,1:T(8,128)} %get-tuple-element.78) | copy-start | bytes 196612
  75.4 2.3 %copy-start.5 = (bf16[4,512,64]{1,2,0:T(8,128)(2,1)S(1)}, bf16[4,512,64]{1,2,0:T(8,128)(2,1)}, u32[]{:S(2)}) copy-start(bf16[4,512,64]{1,2,0:T(8,128)(2,1)} %custom-call.4) | copy-start | bytes 786436
  78.9 1.1 copy-start.1
  82.1 1.1 copy-start.1
  85.4 1.1 copy-start.1
  88.7 1.1 copy-start.1
  92.2 10.9 %copy-start.12 = (s32[64]{0:T(128)S(1)}, s32[64]{0:T(128)}, u32[]{:S(2)}) copy-start(s32[64]{0:T(128)} %copy-done.11) | copy-start | bytes 772
  92.2 10.9 %copy-start.2 = (bf16[1,1,2048,128]{3,2,1,0:T(8,128)(2,1)S(1)}, bf16[1,1,2048,128]{3,2,1,0:T(8,128)(2,1)}, u32[]{:S(2)}) copy-start(bf16[1,1,2048,128]{3,2,1,0:T(8,128)(2,1)} %param.14) | copy-start | bytes 1572868
  92.2 7.2 %collective-permute-start = (bf16[512,1024]{1,0:T(8,128)(2,1)}, bf16[512,1024]{1,0:T(8,128)(2,1)S(1)}, u32[]{:S(2)}, u32[]{:S(2)}) collective-permute-start(bf16[512,1024]{1,0:T(8,128)(2,1)} %convolution_convert_fusion), channel_id=1, source_target_pairs={{0,4},{4,0},{1,5},{5,1},{2,6},{6,2},{3,7},{7,3},{8,12},{12,8},{9,1... | collective-permute-start | bytes 3145736 | tf_op jit(solution)/shard_map/ppermute | solution.py:144
  105.5 17.7 %all-to-all-start.2 = ((bf16[64,8,128]{2,1,0:T(8,128)(2,1)}), bf16[64,8,128]{2,1,0:T(8,128)(2,1)S(1)}, u32[]{:S(2)}, u32[]{:S(2)}) async-start(bf16[64,8,128]{2,1,0:T(8,128)(2,1)} %broadcast_select_fusion.1), calls=%async_computation.3 | async-start | bytes 262144 | tf_op jit(solution)/shard_map/all_to_all | solution.py:34
Sparse Core Ops, SparseCore 0:
  10.1 25.6 all-gather.1
  101.0 21.6 reduce-scatter.1

commit v13 on v12

--- a/solution.py
+++ b/solution.py
@@ -102,21 +102,31 @@
     cycle = jnp.arange(WINDOW_LENGTH, dtype=jnp.int32)
     held = length - 1 - jnp.mod(offset - 1 - cycle, WINDOW_LENGTH)
     cache_mask = (held[None, :] >= 0) & (held[None, :] > token_positions[:, None] - WINDOW_LENGTH)
-    mask_all = jnp.concatenate([cache_mask, new_mask], axis=1)
-    keys_all = jnp.concatenate([window[:, :HEAD_SIZE], new_keys], axis=0)
-    values_all = jnp.concatenate([window[:, HEAD_SIZE:], new_values], axis=0)
+    window_keys = window[:, :HEAD_SIZE]
+    window_values = window[:, HEAD_SIZE:]
 
     def one_head(query_rows):
-        scores = (
-            jnp.einsum("qd,kd->qk", query_rows, keys_all, preferred_element_type=jnp.float32)
+        old_scores = (
+            jnp.einsum("qd,kd->qk", query_rows, window_keys, preferred_element_type=jnp.float32)
             * factor
         )
-        scores = jnp.where(mask_all, scores, -jnp.inf)
-        top = jnp.max(scores, axis=1, keepdims=True)
-        powers = jnp.exp(scores - top)
-        total = jnp.sum(powers, axis=1, keepdims=True)
-        weights = powers.astype(jnp.bfloat16)
-        summed = jnp.dot(weights, values_all, preferred_element_type=jnp.float32)
+        new_scores = (
+            jnp.einsum("qd,kd->qk", query_rows, new_keys, preferred_element_type=jnp.float32)
+            * factor
+        )
+        old_scores = jnp.where(cache_mask, old_scores, -jnp.inf)
+        new_scores = jnp.where(new_mask, new_scores, -jnp.inf)
+        top = jnp.maximum(
+            jnp.max(old_scores, axis=1, keepdims=True), jnp.max(new_scores, axis=1, keepdims=True)
+        )
+        old_powers = jnp.exp(old_scores - top)
+        new_powers = jnp.exp(new_scores - top)
+        total = jnp.sum(old_powers, axis=1, keepdims=True) + jnp.sum(
+            new_powers, axis=1, keepdims=True
+        )
+        summed = jnp.dot(
+            old_powers.astype(jnp.bfloat16), window_values, preferred_element_type=jnp.float32
+        ) + jnp.dot(new_powers.astype(jnp.bfloat16), new_values, preferred_element_type=jnp.float32)
         return (summed / total).astype(jnp.bfloat16)
 
     outputs = lax.map(one_head, jnp.transpose(query_rotated, (1, 0, 2)))

time: 133 us -> 133 us (level)
  matrix products: 16.2 us -> 19.8 us
  waiting for transfers between devices: 29 us -> 26.9 us
  other arithmetic: 17.1 us -> 15.1 us
    all_to_all x2, waiting for transfers between devices: 11.5 us -> 5.41 us  [carry_in(): return lax.all_to_all(window, 'dp', split_axis=0, concat_axis=0, tiled=True)]
    all_gather x1, waiting for transfers between devices: 2.86 us -> 6.87 us  [per_device(): whole = lax.all_gather(tokens, 'tx', axis=1, tiled=True)]
    concatenate x2 -> x0, other arithmetic: 3.13 us -> none  [the longest x1 2.08 us: per_device(): keys_all = jnp.concatenate([window[:, :HEAD_SIZE], new_keys], axis=0)]
    dot_general x8 -> x16, matrix products: 8.6 us -> 11.7 us  [the longest x4 5.79 us: one_head(): jnp.einsum('qd,kd->qk', query_rows, window_keys, preferred_element_type=j...]
    unnamed x25 -> x27, local copies, waits for them, and re-layouts: 1.47 us -> 4.01 us
    reduce_sum x4 -> x8, other arithmetic: 3.36 us -> 3.61 us  [the longest x4 2.82 us: one_head(): jnp.sum(old_powers, axis=1, keepdims=True)]
  transfers between devices with their start and end apart: 6 -> 6, of which waited for: 5 -> 4; matrix products, arithmetic and copies ran while one was open for 16% -> 17% of each run, Pallas kernels for 0% -> 0%
where the time goes in v13:
time: 133 us; the launch traced here: 132 us
  starting transfers between devices  40 us (30%)
  waiting for transfers between devices  26.9 us (20%)
  between operations  20.4 us (15%)
  matrix products  19.8 us (15%)
  other arithmetic  15.1 us (11%)
  local copies, waits for them, and re-layouts  9.3 us (7%)
    all_to_all x2, starting transfers between devices, carry_in(): return lax.all_to_all(window, 'dp', split_axis=0, concat_axis=0, tiled=True)  29.2 us
    all_to_all x1, waiting for transfers between devices, carry_out(): return lax.all_to_all(window, 'dp', split_axis=0, concat_axis=0, tiled=True)  11.4 us
    all_gather x1, waiting for transfers between devices, per_device(): whole = lax.all_gather(tokens, 'tx', axis=1, tiled=True)  6.87 us
    all_to_all x1, starting transfers between devices, carry_out(): return lax.all_to_all(window, 'dp', split_axis=0, concat_axis=0, tiled=True)  6.2 us
    dot_general x4, matrix products, one_head(): jnp.einsum('qd,kd->qk', query_rows, window_keys, preferred_element_type=j...  5.79 us
    all_to_all x2, waiting for transfers between devices, carry_in(): return lax.all_to_all(window, 'dp', split_axis=0, concat_axis=0, tiled=True)  5.41 us
    ppermute x1, starting transfers between devices, per_device(): received = lax.ppermute(sent, 'tx', [(0, 1), (1, 0)])  4.58 us
    unnamed x27, local copies, waits for them, and re-layouts  4.01 us
  transfers between devices with their start and end apart: 6, of which 4 were waited for; matrix products, arithmetic and copies ran while one was open for 17% of the time, Pallas kernels for 0%

profile of v13, /device:TPU:1, one launch (start us, length us, event | category | flops | bytes accessed | tf_op | source)
XLA Modules:
  0.0 131.6 jit_solution(7883901654500336060)
XLA Ops:
  7.9 17.1 %all-to-all-start = ((bf16[64,32,128]{2,1,0:T(8,128)(2,1)}), bf16[64,32,128]{2,1,0:T(8,128)(2,1)S(1)}, u32[]{:S(2)}, u32[]{:S(2)}) async-start(bf16[64,32,128]{2,1,0:T(8,128)(2,1)} %bitcast.84), calls=%async_computation | async-start | bytes 1048576 | tf_op jit(solution)/shard_map/all_to_all | solution.py:30
  25.1 1.3 dynamic_slice.26
  27.7 1.2 compare_and_fusion.1
  28.9 6.9 %all-gather.2.cloned.1.call-done = bf16[512,2048]{1,0:T(8,128)(2,1)} async-done(((bf16[512,1024]{1,0:T(8,128)(2,1)}), bf16[512,2048]{1,0:T(8,128)(2,1)}) %all-gather.2.cloned.1.call-update) | async-done | bytes 2097168 | tf_op jit(solution)/shard_map/all_gather | solution.py:51
  35.8 2.1 %fusion.24 = f32[512]{0:T(512)S(1)} fusion(bf16[512,2048]{1,0:T(8,128)(2,1)} %all-gather.2.cloned.1.call-done), kind=kLoop, calls=%fused_computation.30 | loop fusion | flops 3145216 | bytes 2099200 | tf_op jit(solution)/shard_map/reduce_sum | solution.py:56
  38.5 2.6 %fusion.28 = f32[512,128]{0,1:T(8,128)S(1)} fusion(bf16[512,2048]{1,0:T(8,128)(2,1)} %all-gather.2.cloned.1.call-done, f32[512]{0:T(512)S(1)} %add_rsqrt_fusion, bf16[2048,1,128]{2,0,1:T(8,128)(2,1)S(1)} %copy-done.9), kind=kOutput, calls=%fused_computation.36 | convolution fusion | flops 271581184 | bytes 2885632 | tf_op jit(solution)/shard_map/dot_general | solution.py:63
  44.0 12.0 %all-to-all-start.1 = ((bf16[64,40,128]{2,1,0:T(8,128)(2,1)}), bf16[64,40,128]{2,1,0:T(8,128)(2,1)S(1)}, u32[]{:S(2)}, u32[]{:S(2)}) async-start(bf16[64,40,128]{2,1,0:T(8,128)(2,1)} %pad_maximum_fusion), calls=%async_computation.1 | async-start | bytes 1310720 | tf_op jit(solution)/shard_map/all_to_all | solution.py:30
  58.9 1.4 %copy.20 = bf16[2048,1,256]{0,2,1:T(8,128)(2,1)} copy(bf16[2048,1,256]{2,0,1:T(8,128)(2,1)S(1)} %copy-done.2) | data formatting | bytes 2097152 | tf_op args[1]
  63.0 1.2 fusion.52
  66.1 1.0 copy.24
  67.1 2.7 %fusion.26 = f32[512,4,64]{0,2,1:T(8,128)S(1)} fusion(bf16[4,64,2048]{2,1,0:T(8,128)(2,1)} %bitcast.86, bf16[512,2048]{1,0:T(8,128)(2,1)} %all-gather.2.cloned.1.call-done, f32[512]{0:T(512)} %copy-done.8), kind=kOutput, calls=%fused_computation.32 | convolution fusion | flops 540016640 | bytes 3672064 | tf_op jit(solution)/shard_map/dot_general | solution.py:91
  69.9 5.4 %all-to-all-done.1 = bf16[64,40,128]{2,1,0:T(8,128)(2,1)S(1)} async-done(((bf16[64,40,128]{2,1,0:T(8,128)(2,1)}), bf16[64,40,128]{2,1,0:T(8,128)(2,1)S(1)}, u32[]{:S(2)}, u32[]{:S(2)}) %all-to-all-start.1) | async-done | bytes 655392 | tf_op jit(solution)/shard_map/all_to_all | solution.py:30
  75.6 15.5 %while.11 = (s32[]{:T(128)}, bf16[4,512,64]{1,2,0:T(8,128)(2,1)S(1)}, bf16[4,512,64]{1,2,0:T(8,128)(2,1)S(1)}, bf16[2048,64]{1,0:T(8,128)(2,1)S(1)}, bf16[512,64...) while((s32[]{:T(128)}, ...), condition=%wide.region_6.7_spmd.clone, body=%wide.region_1.6_spmd.clone.sunk | while | flops 347175936 | bytes 17279096 | solution.py:132
  75.6 1.4 %fusion.86 = (f32[512]{0:T(512)S(1)}, f32[512,2048]{1,0:T(8,128)S(1)}) fusion(bf16[2048,64]{1,0:T(8,128)(2,1)S(1)} %get-tuple-element.238, bf16[4,512,64]{1,2,0:T(8,128)(2,1)S(1)} %get-tuple-element.237, s32[]{:T(128)} %get-tuple-element.224, s32[512]{0:T(512)S(1)} %get-tuple-element.242, s32[2048]{0:T(1024)S(1)} %get-tuple-element.243, ...), kind=kOutput, calls=%fused_computation.96.clone.1 | convolution fusion | flops 139460096 | bytes 4798468 | tf_op jit(solution)/shard_map/while/body/eval_jaxpr/qd,kd->qk/dot_general | solution.py:110
  79.4 1.4 %fusion.86 = (f32[512]{0:T(512)S(1)}, f32[512,2048]{1,0:T(8,128)S(1)}) fusion(bf16[2048,64]{1,0:T(8,128)(2,1)S(1)} %get-tuple-element.238, bf16[4,512,64]{1,2,0:T(8,128)(2,1)S(1)} %get-tuple-element.237, s32[]{:T(128)} %get-tuple-element.224, s32[512]{0:T(512)S(1)} %get-tuple-element.242, s32[2048]{0:T(1024)S(1)} %get-tuple-element.243, ...), kind=kOutput, calls=%fused_computation.96.clone.1 | convolution fusion | flops 139460096 | bytes 4798468 | tf_op jit(solution)/shard_map/while/body/eval_jaxpr/qd,kd->qk/dot_general | solution.py:110
  83.3 1.4 %fusion.86 = (f32[512]{0:T(512)S(1)}, f32[512,2048]{1,0:T(8,128)S(1)}) fusion(bf16[2048,64]{1,0:T(8,128)(2,1)S(1)} %get-tuple-element.238, bf16[4,512,64]{1,2,0:T(8,128)(2,1)S(1)} %get-tuple-element.237, s32[]{:T(128)} %get-tuple-element.224, s32[512]{0:T(512)S(1)} %get-tuple-element.242, s32[2048]{0:T(1024)S(1)} %get-tuple-element.243, ...), kind=kOutput, calls=%fused_computation.96.clone.1 | convolution fusion | flops 139460096 | bytes 4798468 | tf_op jit(solution)/shard_map/while/body/eval_jaxpr/qd,kd->qk/dot_general | solution.py:110
  87.2 1.4 %fusion.86 = (f32[512]{0:T(512)S(1)}, f32[512,2048]{1,0:T(8,128)S(1)}) fusion(bf16[2048,64]{1,0:T(8,128)(2,1)S(1)} %get-tuple-element.238, bf16[4,512,64]{1,2,0:T(8,128)(2,1)S(1)} %get-tuple-element.237, s32[]{:T(128)} %get-tuple-element.224, s32[512]{0:T(512)S(1)} %get-tuple-element.242, s32[2048]{0:T(1024)S(1)} %get-tuple-element.243, ...), kind=kOutput, calls=%fused_computation.96.clone.1 | convolution fusion | flops 139460096 | bytes 4798468 | tf_op jit(solution)/shard_map/while/body/eval_jaxpr/qd,kd->qk/dot_general | solution.py:110
  91.1 1.4 %convolution_convert_fusion = bf16[512,1024]{1,0:T(8,128)(2,1)} fusion(bf16[512,256]{0,1:T(8,128)(2,1)S(1)} %bitcast.87, bf16[1,256,2048]{2,1,0:T(8,128)(2,1)S(1)} %copy-done, s32[]{:T(128)S(6)} %select_n.82), kind=kOutput, calls=%fused_computation.35 | convolution fusion | flops 268959744 | bytes 1835012 | tf_op jit(solution)/shard_map/dot_general | solution.py:149
  92.5 4.6 %collective-permute-start = (bf16[512,1024]{1,0:T(8,128)(2,1)}, bf16[512,1024]{1,0:T(8,128)(2,1)S(1)}, u32[]{:S(2)}, u32[]{:S(2)}) collective-permute-start(bf16[512,1024]{1,0:T(8,128)(2,1)} %convolution_convert_fusion), channel_id=1, source_target_pairs={{0,4},{4,0},{1,5},{5,1},{2,6},{6,2},{3,7},{7,3},{8,12},{12,8},{9,1... | collective-permute-start | bytes 3145736 | tf_op jit(solution)/shard_map/ppermute | solution.py:154
  97.1 2.5 %collective-permute-done = bf16[512,1024]{1,0:T(8,128)(2,1)S(1)} collective-permute-done((bf16[512,1024]{1,0:T(8,128)(2,1)}, bf16[512,1024]{1,0:T(8,128)(2,1)S(1)}, u32[]{:S(2)}, u32[]{:S(2)}) %collective-permute-start) | collective-permute-done | bytes 1048608 | tf_op jit(solution)/shard_map/ppermute | solution.py:154
  99.6 1.4 %add_convert_fusion = bf16[512,1024]{1,0:T(8,128)(2,1)} fusion(bf16[512,1024]{1,0:T(8,128)(2,1)S(1)} %collective-permute-done, bf16[512,256]{0,1:T(8,128)(2,1)S(1)} %bitcast.88, bf16[1,256,2048]{2,1,0:T(8,128)(2,1)S(1)} %copy-done, s32[]{:T(128)S(6)} %select_n.81), kind=kOutput, calls=%fused_computation.34 | convolution fusion | flops 270008320 | bytes 2883588 | tf_op jit(solution)/shard_map/dot_general | solution.py:155
  105.1 6.2 %all-to-all-start.2 = ((bf16[64,8,128]{2,1,0:T(8,128)(2,1)}), bf16[64,8,128]{2,1,0:T(8,128)(2,1)S(1)}, u32[]{:S(2)}, u32[]{:S(2)}) async-start(bf16[64,8,128]{2,1,0:T(8,128)(2,1)} %broadcast_select_fusion.1), calls=%async_computation.3 | async-start | bytes 262144 | tf_op jit(solution)/shard_map/all_to_all | solution.py:34
  111.3 11.4 %all-to-all-done.2 = bf16[64,8,128]{2,1,0:T(8,128)(2,1)S(1)} async-done(((bf16[64,8,128]{2,1,0:T(8,128)(2,1)}), bf16[64,8,128]{2,1,0:T(8,128)(2,1)S(1)}, u32[]{:S(2)}, u32[]{:S(2)}) %all-to-all-start.2) | async-done | bytes 131104 | tf_op jit(solution)/shard_map/all_to_all | solution.py:34
  122.8 1.0 dynamic_update_slice.7
  (96 shorter events, 21.9 us)
Async XLA Ops:
  7.2 83.9 %copy-start = (bf16[1,256,2048]{2,1,0:T(8,128)(2,1)S(1)}, bf16[1,256,2048]{2,1,0:T(8,128)(2,1)}, u32[]{:S(2)}) copy-start(bf16[1,256,2048]{2,1,0:T(8,128)(2,1)} %param.13) | copy-start | bytes 3145732
  7.2 31.3 %copy-start.9 = (bf16[2048,1,128]{2,0,1:T(8,128)(2,1)S(1)}, bf16[2048,1,128]{2,0,1:T(8,128)(2,1)}, u32[]{:S(2)}) copy-start(bf16[2048,1,128]{2,0,1:T(8,128)(2,1)} %param.12) | copy-start | bytes 1572868
  7.2 28.6 %all-gather.2.cloned.1.call-start = ((), (), s32[]{:S(2)}) async-start(), calls=%async_computation.4 | async-start | bytes 3145728 | tf_op jit(solution)/shard_map/all_gather | solution.py:51
  7.9 33.6 %all-to-all-start = ((bf16[64,32,128]{2,1,0:T(8,128)(2,1)}), bf16[64,32,128]{2,1,0:T(8,128)(2,1)S(1)}, u32[]{:S(2)}, u32[]{:S(2)}) async-start(bf16[64,32,128]{2,1,0:T(8,128)(2,1)} %bitcast.84), calls=%async_computation | async-start | bytes 1048576 | tf_op jit(solution)/shard_map/all_to_all | solution.py:30
  37.9 0.6 copy-start.8
  38.5 20.4 %copy-start.2 = (bf16[2048,1,256]{2,0,1:T(8,128)(2,1)S(1)}, bf16[2048,1,256]{2,0,1:T(8,128)(2,1)}, u32[]{:S(2)}) copy-start(bf16[2048,1,256]{2,0,1:T(8,128)(2,1)} %param.11) | copy-start | bytes 3145732
  41.1 20.6 %copy-start.5 = (s32[64]{0:T(128)S(1)}, s32[64]{0:T(128)}, u32[]{:S(2)}) copy-start(s32[64]{0:T(128)} %param.16) | copy-start | bytes 772
  41.1 2.9 %copy-start.3 = (bf16[512,64]{0,1:T(8,128)(2,1)}, bf16[512,64]{0,1:T(8,128)(2,1)S(1)}, u32[]{:S(2)}) copy-start(bf16[512,64]{0,1:T(8,128)(2,1)S(1)} %slice.91) | copy-start | bytes 196612
  41.5 2.5 %copy-start.4 = (bf16[512,64]{0,1:T(8,128)(2,1)}, bf16[512,64]{0,1:T(8,128)(2,1)S(1)}, u32[]{:S(2)}) copy-start(bf16[512,64]{0,1:T(8,128)(2,1)S(1)} %maximum_bitcast_fusion.2) | copy-start | bytes 196612
  44.0 31.3 %all-to-all-start.1 = ((bf16[64,40,128]{2,1,0:T(8,128)(2,1)}), bf16[64,40,128]{2,1,0:T(8,128)(2,1)S(1)}, u32[]{:S(2)}, u32[]{:S(2)}) async-start(bf16[64,40,128]{2,1,0:T(8,128)(2,1)} %pad_maximum_fusion), calls=%async_computation.1 | async-start | bytes 1310720 | tf_op jit(solution)/shard_map/all_to_all | solution.py:30
  56.0 68.7 %reduce-scatter.2.cloned.1.call-start = ((), (), s32[]{:S(2)}) async-start(), calls=%async_computation.5 | async-start | bytes 1310720 | tf_op jit(solution)/shard_map/reduce_scatter | solution.py:164
  56.8 7.4 %copy-start.10 = (s32[64]{0:T(128)}, s32[64]{0:T(128)S(1)}, u32[]{:S(2)}) copy-start(s32[64]{0:T(128)S(1)} %select_reduce_fusion) | copy-start | bytes 772
  67.1 8.5 %copy-start.6 = (s32[512]{0:T(512)S(1)}, s32[512]{0:T(512)}, u32[]{:S(2)}) copy-start(s32[512]{0:T(512)} %fusion.52) | copy-start | bytes 6148
  67.1 8.5 %copy-start.7 = (pred[2048]{0:T(1024)(128)(4,1)S(1)}, pred[2048]{0:T(1024)(128)(4,1)}, u32[]{:S(2)}) copy-start(pred[2048]{0:T(1024)(128)(4,1)} %broadcast_compare_fusion) | copy-start | bytes 6148
  91.0 12.5 %copy-start.11 = (s32[64]{0:T(128)S(1)}, s32[64]{0:T(128)}, u32[]{:S(2)}) copy-start(s32[64]{0:T(128)} %copy-done.10) | copy-start | bytes 772
  91.0 12.6 %copy-start.1 = (bf16[1,1,2048,128]{3,2,1,0:T(8,128)(2,1)S(1)}, bf16[1,1,2048,128]{3,2,1,0:T(8,128)(2,1)}, u32[]{:S(2)}) copy-start(bf16[1,1,2048,128]{3,2,1,0:T(8,128)(2,1)} %param.14) | copy-start | bytes 1572868
  92.5 7.1 %collective-permute-start = (bf16[512,1024]{1,0:T(8,128)(2,1)}, bf16[512,1024]{1,0:T(8,128)(2,1)S(1)}, u32[]{:S(2)}, u32[]{:S(2)}) collective-permute-start(bf16[512,1024]{1,0:T(8,128)(2,1)} %convolution_convert_fusion), channel_id=1, source_target_pairs={{0,4},{4,0},{1,5},{5,1},{2,6},{6,2},{3,7},{7,3},{8,12},{12,8},{9,1... | collective-permute-start | bytes 3145736 | tf_op jit(solution)/shard_map/ppermute | solution.py:154
  105.1 17.7 %all-to-all-start.2 = ((bf16[64,8,128]{2,1,0:T(8,128)(2,1)}), bf16[64,8,128]{2,1,0:T(8,128)(2,1)S(1)}, u32[]{:S(2)}, u32[]{:S(2)}) async-start(bf16[64,8,128]{2,1,0:T(8,128)(2,1)} %broadcast_select_fusion.1), calls=%async_computation.3 | async-start | bytes 262144 | tf_op jit(solution)/shard_map/all_to_all | solution.py:34
Sparse Core Ops, SparseCore 0:
  10.1 25.6 all-gather.1
  101.1 21.1 reduce-scatter.1

commit v14 on v13

--- a/solution.py
+++ b/solution.py
@@ -129,7 +129,7 @@
         ) + jnp.dot(new_powers.astype(jnp.bfloat16), new_values, preferred_element_type=jnp.float32)
         return (summed / total).astype(jnp.bfloat16)
 
-    outputs = lax.map(one_head, jnp.transpose(query_rotated, (1, 0, 2)))
+    outputs = jnp.stack([one_head(query_rotated[:, h]) for h in range(heads)])
     attended = jnp.transpose(outputs, (1, 0, 2)).reshape(rows_new, heads * HEAD_SIZE)
 
     arrived = carry_out(jnp.take(entry_parts, inverse, axis=0).reshape(rows_new, lanes))

time: 133 us -> 142 us (1.068)
  matrix products: 19.8 us -> 25.2 us
  waiting for transfers between devices: 26.9 us -> 23.9 us
  local copies, waits for them, and re-layouts: 9.3 us -> 12 us
  other arithmetic: 15.1 us -> 17.2 us
  starting transfers between devices: 40 us -> 41.8 us
    all_gather x1, waiting for transfers between devices: 6.87 us -> 0.01 us  [per_device(): whole = lax.all_gather(tokens, 'tx', axis=1, tiled=True)]
    dot_general x4, matrix products: 1.19 us -> 5.43 us  [one_head(): jnp.einsum('qd,kd->qk', query_rows, new_keys, preferred_element_type=jnp....]
    all_to_all x2, waiting for transfers between devices: 5.41 us -> 9.38 us  [carry_in(): return lax.all_to_all(window, 'dp', split_axis=0, concat_axis=0, tiled=True)]
    gather x1, local copies, waits for them, and re-layouts: 0.66 us -> 2.46 us  [per_device(): jnp.take(spread.reshape(groups, window_chunk, lanes), slots, axis=0)]
    ppermute x1, starting transfers between devices: 4.58 us -> 6.17 us  [per_device(): received = lax.ppermute(sent, 'tx', [(0, 1), (1, 0)])]
    unnamed x27 -> x41, local copies, waits for them, and re-layouts: 4.01 us -> 3.01 us
  transfers between devices with their start and end apart: 6 -> 6, of which waited for: 4 -> 3; matrix products, arithmetic and copies ran while one was open for 17% -> 20% of each run, Pallas kernels for 0% -> 0%
where the time goes in v14:
time: 142 us; the launch traced here: 140 us
  starting transfers between devices  41.8 us (29%)
  matrix products  25.2 us (18%)
  waiting for transfers between devices  23.9 us (17%)
  between operations  20 us (14%)
  other arithmetic  17.2 us (12%)
  local copies, waits for them, and re-layouts  12 us (8%)
    all_to_all x2, starting transfers between devices, carry_in(): return lax.all_to_all(window, 'dp', split_axis=0, concat_axis=0, tiled=True)  29.7 us
    all_to_all x1, waiting for transfers between devices, carry_out(): return lax.all_to_all(window, 'dp', split_axis=0, concat_axis=0, tiled=True)  11.4 us
    all_to_all x2, waiting for transfers between devices, carry_in(): return lax.all_to_all(window, 'dp', split_axis=0, concat_axis=0, tiled=True)  9.38 us
    dot_general x4, matrix products, one_head(): jnp.einsum('qd,kd->qk', query_rows, window_keys, preferred_element_type=j...  6.56 us
    ppermute x1, starting transfers between devices, per_device(): received = lax.ppermute(sent, 'tx', [(0, 1), (1, 0)])  6.17 us
    all_to_all x1, starting transfers between devices, carry_out(): return lax.all_to_all(window, 'dp', split_axis=0, concat_axis=0, tiled=True)  5.67 us
    dot_general x4, matrix products, one_head(): jnp.einsum('qd,kd->qk', query_rows, new_keys, preferred_element_type=jnp....  5.43 us
    dot_general x4, matrix products, one_head(): jnp.dot(old_powers.astype(jnp.bfloat16), window_values, preferred_element...  4.09 us
  transfers between devices with their start and end apart: 6, of which 3 were waited for; matrix products, arithmetic and copies ran while one was open for 20% of the time, Pallas kernels for 0%

profile of v14, /device:TPU:1, one launch (start us, length us, event | category | flops | bytes accessed | tf_op | source)
XLA Modules:
  0.0 140.2 jit_solution(12696079919663774056)
XLA Ops:
  7.9 17.4 %all-to-all-start = ((bf16[64,32,128]{2,1,0:T(8,128)(2,1)}), bf16[64,32,128]{2,1,0:T(8,128)(2,1)}, u32[]{:S(2)}, u32[]{:S(2)}) async-start(bf16[64,32,128]{2,1,0:T(8,128)(2,1)} %bitcast.94), calls=%async_computation | async-start | bytes 1048576 | tf_op jit(solution)/shard_map/all_to_all | solution.py:30
  28.0 1.2 dynamic_slice.22
  29.3 2.3 %copy.14 = bf16[2048,1,256]{0,2,1:T(8,128)(2,1)} copy(bf16[2048,1,256]{2,0,1:T(8,128)(2,1)} %param.9) | data formatting | bytes 2097152 | tf_op args[1]
  34.8 1.2 fusion.96
  38.2 2.1 %fusion = f32[512]{0:T(512)S(1)} fusion(bf16[512,2048]{1,0:T(8,128)(2,1)} %all-gather.2.cloned.1.call-done), kind=kLoop, calls=%fused_computation.4 | loop fusion | flops 3145216 | bytes 2099200 | tf_op jit(solution)/shard_map/reduce_sum | solution.py:56
  40.3 2.7 %fusion.48 = f32[512,128]{0,1:T(8,128)S(1)} fusion(bf16[512,2048]{1,0:T(8,128)(2,1)} %all-gather.2.cloned.1.call-done, f32[512]{0:T(512)S(1)} %add_rsqrt_fusion, bf16[2048,1,128]{2,0,1:T(8,128)(2,1)} %param.10), kind=kOutput, calls=%fused_computation.72 | convolution fusion | flops 271581184 | bytes 2885632 | tf_op jit(solution)/shard_map/dot_general | solution.py:63
  45.7 2.5 %gather_fusion = bf16[64,32,128]{2,1,0:T(8,128)(2,1)} fusion(bf16[64,32,128]{2,1,0:T(8,128)(2,1)} %bitcast.12, s32[1024]{0:T(1024)S(1)} %pad_clamp_fusion.1), kind=kCustom, calls=%fused_computation | custom fusion | bytes 1048832 | tf_op jit(solution)/shard_map/jit(_take)/gather | solution.py:80
  48.1 1.2 broadcast_select_fusion
  50.2 12.3 %all-to-all-start.1 = ((bf16[64,40,128]{2,1,0:T(8,128)(2,1)}), bf16[64,40,128]{2,1,0:T(8,128)(2,1)}, u32[]{:S(2)}, u32[]{:S(2)}) async-start(bf16[64,40,128]{2,1,0:T(8,128)(2,1)} %pad_maximum_fusion), calls=%async_computation.1 | async-start | bytes 1310720 | tf_op jit(solution)/shard_map/all_to_all | solution.py:30
  62.7 2.0 %fusion.18 = f32[512,4,64]{0,2,1:T(8,128)S(1)} fusion(bf16[4,64,2048]{2,1,0:T(8,128)(2,1)} %bitcast.98, bf16[512,2048]{1,0:T(8,128)(2,1)S(1)} %copy-done.4, f32[512]{0:T(512)S(1)} %add_rsqrt_fusion), kind=kOutput, calls=%fused_computation.27 | convolution fusion | flops 540016640 | bytes 3672064 | tf_op jit(solution)/shard_map/dot_general | solution.py:91
  65.8 2.7 %fusion.114 = (f32[512]{0:T(512)}, f32[512,512]{0,1:T(8,128)}) fusion(bf16[512,32]{0,1:T(8,128)(2,1)} %bitcast.105, bf16[512,32]{0,1:T(8,128)(2,1)} %bitcast.101, bf16[512,4,32]{0,2,1:T(8,128)(2,1)S(1)} %get-tuple-element.6, bf16[512,4,32]{0,2,1:T(8,128)(2,1)S(1)} %get-tuple-element.7), kind=kOutput, calls=%fused_computation.167 | convolution fusion | flops 34864640 | bytes 1378304 | tf_op jit(solution)/shard_map/qd,kd->qk/dot_general | solution.py:114
  68.5 2.0 %fusion.112 = (f32[512]{0:T(512)}, f32[512,512]{0,1:T(8,128)}) fusion(bf16[512,32]{0,1:T(8,128)(2,1)S(1)} %bitcast.106, bf16[512,32]{0,1:T(8,128)(2,1)S(1)} %bitcast.102, bf16[512,4,32]{0,2,1:T(8,128)(2,1)S(1)} %get-tuple-element.6, bf16[512,4,32]{0,2,1:T(8,128)(2,1)S(1)} %get-tuple-element.7), kind=kOutput, calls=%fused_computation.165 | convolution fusion | flops 34864640 | bytes 1378304 | tf_op jit(solution)/shard_map/qd,kd->qk/dot_general | solution.py:114
  71.2 9.4 %all-to-all-done.1 = bf16[64,40,128]{2,1,0:T(8,128)(2,1)} async-done(((bf16[64,40,128]{2,1,0:T(8,128)(2,1)}), bf16[64,40,128]{2,1,0:T(8,128)(2,1)}, u32[]{:S(2)}, u32[]{:S(2)}) %all-to-all-start.1) | async-done | bytes 655392 | tf_op jit(solution)/shard_map/all_to_all | solution.py:30
  80.6 1.1 slice.89
  81.7 2.2 %fusion.113 = (f32[512]{0:T(512)S(1)}, f32[512,2048]{1,0:T(8,128)S(1)}) fusion(bf16[2048,128]{1,0:T(8,128)(2,1)S(1)} %bitcast.86, bf16[512,4,32]{0,2,1:T(8,128)(2,1)S(1)} %get-tuple-element.6, bf16[512,4,32]{0,2,1:T(8,128)(2,1)} %copy-done.5, s32[512]{0:T(512)} %fusion.96, s32[2048]{0:T(1024)S(1)} %fusion.91, pred[2048]{0:T(1024)(128)(4,1)} %broadcast_compare_fusion), kind=kOutput, calls=%fused_computation.166 | convolution fusion | flops 139591168 | bytes 4995072 | tf_op jit(solution)/shard_map/qd,kd->qk/dot_general | solution.py:110
  86.4 1.4 %fusion.111 = (f32[512]{0:T(512)S(1)}, f32[512,2048]{1,0:T(8,128)S(1)}) fusion(bf16[2048,128]{1,0:T(8,128)(2,1)S(1)} %bitcast.88, bf16[512,4,32]{0,2,1:T(8,128)(2,1)S(1)} %get-tuple-element.6, bf16[512,4,32]{0,2,1:T(8,128)(2,1)S(1)} %copy-done.6, s32[512]{0:T(512)S(1)} %copy-done.15, s32[2048]{0:T(1024)S(1)} %fusion.91, pred[2048]{0:T(1024)(128)(4,1)S(1)} %copy-done.16), kind=kOutput, calls=%fused_computation.164 | convolution fusion | flops 139591168 | bytes 4995072 | tf_op jit(solution)/shard_map/qd,kd->qk/dot_general | solution.py:110
  88.5 1.0 fusion.14
  89.6 1.5 %fusion.109 = (f32[512]{0:T(512)S(1)}, f32[512,2048]{1,0:T(8,128)S(1)}) fusion(bf16[2048,128]{1,0:T(8,128)(2,1)S(1)} %bitcast.90, bf16[512,4,32]{0,2,1:T(8,128)(2,1)S(1)} %get-tuple-element.6, bf16[512,4,32]{0,2,1:T(8,128)(2,1)S(1)} %copy-done.6, s32[512]{0:T(512)S(1)} %copy-done.15, s32[2048]{0:T(1024)S(1)} %fusion.91, pred[2048]{0:T(1024)(128)(4,1)S(1)} %copy-done.16), kind=kOutput, calls=%fused_computation.162 | convolution fusion | flops 139591168 | bytes 4995072 | tf_op jit(solution)/shard_map/qd,kd->qk/dot_general | solution.py:110
  92.8 1.4 %fusion.107 = (f32[512]{0:T(512)S(1)}, f32[512,2048]{1,0:T(8,128)S(1)}) fusion(bf16[512,64]{0,1:T(8,128)(2,1)S(1)} %copy-done.12, bf16[2048,128]{1,0:T(8,128)(2,1)S(1)} %bitcast.92, s32[512]{0:T(512)S(1)} %copy-done.15, s32[2048]{0:T(1024)S(1)} %fusion.91, pred[2048]{0:T(1024)(128)(4,1)S(1)} %copy-done.16), kind=kOutput, calls=%fused_computation.160 | convolution fusion | flops 139460096 | bytes 4798464 | tf_op jit(solution)/shard_map/qd,kd->qk/dot_general | solution.py:110
  98.8 6.2 %collective-permute-start = (bf16[512,1024]{1,0:T(8,128)(2,1)S(1)}, bf16[512,1024]{1,0:T(8,128)(2,1)}, u32[]{:S(2)}, u32[]{:S(2)}) collective-permute-start(bf16[512,1024]{1,0:T(8,128)(2,1)S(1)} %convolution_convert_fusion), channel_id=1, source_target_pairs={{0,4},{4,0},{1,5},{5,1},{2,6},{6,2},{3,7},{7,3},{8,12},{12,8},{9,1... | collective-permute-start | bytes 3145736 | tf_op jit(solution)/shard_map/ppermute | solution.py:154
  104.9 2.4 %collective-permute-done = bf16[512,1024]{1,0:T(8,128)(2,1)} collective-permute-done((bf16[512,1024]{1,0:T(8,128)(2,1)S(1)}, bf16[512,1024]{1,0:T(8,128)(2,1)}, u32[]{:S(2)}, u32[]{:S(2)}) %collective-permute-start) | collective-permute-done | bytes 1048608 | tf_op jit(solution)/shard_map/ppermute | solution.py:154
  107.3 2.7 %add_convert_fusion = bf16[512,1024]{1,0:T(8,128)(2,1)} fusion(bf16[512,1024]{1,0:T(8,128)(2,1)} %collective-permute-done, bf16[512,256]{0,1:T(8,128)(2,1)S(1)} %bitcast.97, bf16[1,256,2048]{2,1,0:T(8,128)(2,1)S(1)} %copy-done, s32[]{:T(128)S(6)} %select_n.107), kind=kOutput, calls=%fused_computation.29 | convolution fusion | flops 270008320 | bytes 2883588 | tf_op jit(solution)/shard_map/dot_general | solution.py:155
  114.7 5.7 %all-to-all-start.2 = ((bf16[64,8,128]{2,1,0:T(8,128)(2,1)}), bf16[64,8,128]{2,1,0:T(8,128)(2,1)S(1)}, u32[]{:S(2)}, u32[]{:S(2)}) async-start(bf16[64,8,128]{2,1,0:T(8,128)(2,1)} %broadcast_select_fusion.1), calls=%async_computation.3 | async-start | bytes 262144 | tf_op jit(solution)/shard_map/all_to_all | solution.py:34
  120.4 11.4 %all-to-all-done.2 = bf16[64,8,128]{2,1,0:T(8,128)(2,1)S(1)} async-done(((bf16[64,8,128]{2,1,0:T(8,128)(2,1)}), bf16[64,8,128]{2,1,0:T(8,128)(2,1)S(1)}, u32[]{:S(2)}, u32[]{:S(2)}) %all-to-all-start.2) | async-done | bytes 131104 | tf_op jit(solution)/shard_map/all_to_all | solution.py:34
  (108 shorter events, 24.1 us)
Async XLA Ops:
  7.2 91.1 %copy-start = (bf16[1,256,2048]{2,1,0:T(8,128)(2,1)S(1)}, bf16[1,256,2048]{2,1,0:T(8,128)(2,1)}, u32[]{:S(2)}) copy-start(bf16[1,256,2048]{2,1,0:T(8,128)(2,1)} %param.11) | copy-start | bytes 3145732
  7.2 29.5 %copy-start.17 = (s32[64]{0:T(128)S(1)}, s32[64]{0:T(128)}, u32[]{:S(2)}) copy-start(s32[64]{0:T(128)} %param.15) | copy-start | bytes 772
  7.2 25.1 %copy-start.14 = (s32[64]{0:T(128)S(1)}, s32[64]{0:T(128)}, u32[]{:S(2)}) copy-start(s32[64]{0:T(128)} %param.14) | copy-start | bytes 772
  7.2 31.0 %all-gather.2.cloned.1.call-start = ((), (), s32[]{:S(2)}) async-start(), calls=%async_computation.4 | async-start | bytes 3145728 | tf_op jit(solution)/shard_map/all_gather | solution.py:51
  7.9 36.7 %all-to-all-start = ((bf16[64,32,128]{2,1,0:T(8,128)(2,1)}), bf16[64,32,128]{2,1,0:T(8,128)(2,1)}, u32[]{:S(2)}, u32[]{:S(2)}) async-start(bf16[64,32,128]{2,1,0:T(8,128)(2,1)} %bitcast.94), calls=%async_computation | async-start | bytes 1048576 | tf_op jit(solution)/shard_map/all_to_all | solution.py:30
  26.1 14.1 %copy-start.18 = (s32[64]{0:T(128)}, s32[64]{0:T(128)S(1)}, u32[]{:S(2)}) copy-start(s32[64]{0:T(128)S(1)} %select_reduce_fusion) | copy-start | bytes 772
  40.3 22.5 %copy-start.4 = (bf16[512,2048]{1,0:T(8,128)(2,1)S(1)}, bf16[512,2048]{1,0:T(8,128)(2,1)}, u32[]{:S(2)}) copy-start(bf16[512,2048]{1,0:T(8,128)(2,1)} %all-gather.2.cloned.1.call-done) | copy-start | bytes 6291460
  50.2 30.4 %all-to-all-start.1 = ((bf16[64,40,128]{2,1,0:T(8,128)(2,1)}), bf16[64,40,128]{2,1,0:T(8,128)(2,1)}, u32[]{:S(2)}, u32[]{:S(2)}) async-start(bf16[64,40,128]{2,1,0:T(8,128)(2,1)} %pad_maximum_fusion), calls=%async_computation.1 | async-start | bytes 1310720 | tf_op jit(solution)/shard_map/all_to_all | solution.py:30
  62.5 70.9 %reduce-scatter.2.cloned.1.call-start = ((), (), s32[]{:S(2)}) async-start(), calls=%async_computation.5 | async-start | bytes 1310720 | tf_op jit(solution)/shard_map/reduce_scatter | solution.py:164
  62.7 5.8 %copy-start.8 = (bf16[512,1,32]{0,2,1:T(8,128)(2,1)S(1)}, bf16[512,1,32]{0,2,1:T(8,128)(2,1)}, u32[]{:S(2)}) copy-start(bf16[512,1,32]{0,2,1:T(8,128)(2,1)} %copy-done.7) | copy-start | bytes 98308
  62.7 5.8 %copy-start.10 = (bf16[512,1,32]{0,2,1:T(8,128)(2,1)S(1)}, bf16[512,1,32]{0,2,1:T(8,128)(2,1)}, u32[]{:S(2)}) copy-start(bf16[512,1,32]{0,2,1:T(8,128)(2,1)} %copy-done.9) | copy-start | bytes 98308
  65.8 4.8 %copy-start.5 = (bf16[512,4,32]{0,2,1:T(8,128)(2,1)}, bf16[512,4,32]{0,2,1:T(8,128)(2,1)S(1)}, u32[]{:S(2)}) copy-start(bf16[512,4,32]{0,2,1:T(8,128)(2,1)S(1)} %get-tuple-element.7) | copy-start | bytes 393220
  65.8 5.1 %copy-start.11 = (bf16[512,64]{0,1:T(8,128)(2,1)}, bf16[512,64]{0,1:T(8,128)(2,1)S(1)}, u32[]{:S(2)}) copy-start(bf16[512,64]{0,1:T(8,128)(2,1)S(1)} %fusion.89) | copy-start | bytes 196612
  84.6 1.7 %copy-start.6 = (bf16[512,4,32]{0,2,1:T(8,128)(2,1)S(1)}, bf16[512,4,32]{0,2,1:T(8,128)(2,1)}, u32[]{:S(2)}) copy-start(bf16[512,4,32]{0,2,1:T(8,128)(2,1)} %copy-done.5) | copy-start | bytes 393220
  84.6 1.7 %copy-start.15 = (s32[512]{0:T(512)S(1)}, s32[512]{0:T(512)}, u32[]{:S(2)}) copy-start(s32[512]{0:T(512)} %fusion.96) | copy-start | bytes 6148
  84.6 1.7 %copy-start.16 = (pred[2048]{0:T(1024)(128)(4,1)S(1)}, pred[2048]{0:T(1024)(128)(4,1)}, u32[]{:S(2)}) copy-start(pred[2048]{0:T(1024)(128)(4,1)} %broadcast_compare_fusion) | copy-start | bytes 6148
  86.3 1.5 %copy-start.13 = (f32[512]{0:T(512)S(1)}, f32[512]{0:T(512)}, u32[]{:S(2)}) copy-start(f32[512]{0:T(512)} %get-tuple-element.24) | copy-start | bytes 6148
  91.0 1.7 %copy-start.12 = (bf16[512,64]{0,1:T(8,128)(2,1)S(1)}, bf16[512,64]{0,1:T(8,128)(2,1)}, u32[]{:S(2)}) copy-start(bf16[512,64]{0,1:T(8,128)(2,1)} %copy-done.11) | copy-start | bytes 196612
  94.2 2.0 %copy-start.2 = (f32[512,512]{0,1:T(8,128)S(1)}, f32[512,512]{0,1:T(8,128)}, u32[]{:S(2)}) copy-start(f32[512,512]{0,1:T(8,128)} %get-tuple-element.29) | copy-start | bytes 3145732
  94.2 2.2 %copy-start.1 = (f32[512,512]{0,1:T(8,128)S(1)}, f32[512,512]{0,1:T(8,128)}, u32[]{:S(2)}) copy-start(f32[512,512]{0,1:T(8,128)} %get-tuple-element.25) | copy-start | bytes 3145732
  97.9 14.4 %copy-start.19 = (s32[64]{0:T(128)S(1)}, s32[64]{0:T(128)}, u32[]{:S(2)}) copy-start(s32[64]{0:T(128)} %copy-done.18) | copy-start | bytes 772
  97.9 14.4 %copy-start.3 = (bf16[1,1,2048,128]{3,2,1,0:T(8,128)(2,1)S(1)}, bf16[1,1,2048,128]{3,2,1,0:T(8,128)(2,1)}, u32[]{:S(2)}) copy-start(bf16[1,1,2048,128]{3,2,1,0:T(8,128)(2,1)} %param.12) | copy-start | bytes 1572868
  98.8 8.6 %collective-permute-start = (bf16[512,1024]{1,0:T(8,128)(2,1)S(1)}, bf16[512,1024]{1,0:T(8,128)(2,1)}, u32[]{:S(2)}, u32[]{:S(2)}) collective-permute-start(bf16[512,1024]{1,0:T(8,128)(2,1)S(1)} %convolution_convert_fusion), channel_id=1, source_target_pairs={{0,4},{4,0},{1,5},{5,1},{2,6},{6,2},{3,7},{7,3},{8,12},{12,8},{9,1... | collective-permute-start | bytes 3145736 | tf_op jit(solution)/shard_map/ppermute | solution.py:154
  114.7 17.2 %all-to-all-start.2 = ((bf16[64,8,128]{2,1,0:T(8,128)(2,1)}), bf16[64,8,128]{2,1,0:T(8,128)(2,1)S(1)}, u32[]{:S(2)}, u32[]{:S(2)}) async-start(bf16[64,8,128]{2,1,0:T(8,128)(2,1)} %broadcast_select_fusion.1), calls=%async_computation.3 | async-start | bytes 262144 | tf_op jit(solution)/shard_map/all_to_all | solution.py:34
  (2 other events, 1.2 us)
Sparse Core Ops, SparseCore 0:
  10.1 25.6 all-gather.1
  110.2 21.1 reduce-scatter.1

commit v15 on v13

--- a/solution.py
+++ b/solution.py
@@ -132,16 +132,8 @@
     outputs = lax.map(one_head, jnp.transpose(query_rotated, (1, 0, 2)))
     attended = jnp.transpose(outputs, (1, 0, 2)).reshape(rows_new, heads * HEAD_SIZE)
 
-    arrived = carry_out(jnp.take(entry_parts, inverse, axis=0).reshape(rows_new, lanes))
-    own_offset = offsets[inverse[request]]
-    extended = jnp.concatenate([stored, stored[:rows_new]], axis=0)
-    extended = lax.dynamic_update_slice_in_dim(extended, arrived, own_offset, axis=0)
-    wrap = own_offset + rows_new - WINDOW_LENGTH
-    head_rows = jnp.arange(rows_new, dtype=jnp.int32)[:, None]
-    head = jnp.where(head_rows < wrap, extended[WINDOW_LENGTH:], extended[:rows_new])
-    updated = jnp.concatenate([head, extended[rows_new:WINDOW_LENGTH]], axis=0)
-    new_cache = updated[None, None]
     out_rows = output_weight.reshape(output_weight.shape[1], width)
+    sorted_entries = jnp.take(entry_parts, inverse, axis=0).reshape(rows_new, lanes)
     halves = lax.axis_size("tx")
     if halves == 2:
         core = lax.axis_index("tx")
@@ -152,6 +144,7 @@
             preferred_element_type=jnp.float32,
         ).astype(jnp.bfloat16)
         received = lax.ppermute(sent, "tx", [(0, 1), (1, 0)])
+        sorted_entries, received = lax.optimization_barrier((sorted_entries, received))
         kept = jnp.dot(
             attended,
             lax.dynamic_slice_in_dim(out_rows, core * half_cols, half_cols, axis=1),
@@ -161,6 +154,15 @@
     else:
         partial_value = jnp.dot(attended, out_rows, preferred_element_type=jnp.float32)
         across_cores = lax.psum_scatter(partial_value, "tx", scatter_dimension=1, tiled=True)
+    arrived = carry_out(sorted_entries)
+    own_offset = offsets[inverse[request]]
+    extended = jnp.concatenate([stored, stored[:rows_new]], axis=0)
+    extended = lax.dynamic_update_slice_in_dim(extended, arrived, own_offset, axis=0)
+    wrap = own_offset + rows_new - WINDOW_LENGTH
+    head_rows = jnp.arange(rows_new, dtype=jnp.int32)[:, None]
+    head = jnp.where(head_rows < wrap, extended[WINDOW_LENGTH:], extended[:rows_new])
+    updated = jnp.concatenate([head, extended[rows_new:WINDOW_LENGTH]], axis=0)
+    new_cache = updated[None, None]
     mixed = lax.psum_scatter(
         across_cores.astype(jnp.bfloat16), "ty", scatter_dimension=1, tiled=True
     )

time: 133 us -> 138 us (1.038)
  matrix products: 19.8 us -> 24.8 us
  other arithmetic: 15.1 us -> 16.8 us
  local copies, waits for them, and re-layouts: 9.3 us -> 7.74 us
    dot_general x4, matrix products: 5.79 us -> 9.26 us  [one_head(): jnp.einsum('qd,kd->qk', query_rows, window_keys, preferred_element_type=j...]
    dot_general x4, matrix products: 1.19 us -> 4.59 us  [one_head(): jnp.einsum('qd,kd->qk', query_rows, new_keys, preferred_element_type=jnp....]
    all_to_all x2, waiting for transfers between devices: 5.41 us -> 8.19 us  [carry_in(): return lax.all_to_all(window, 'dp', split_axis=0, concat_axis=0, tiled=True)]
    convert_element_type x0 -> x1, other arithmetic: none -> 2.66 us  [per_device(): across_cores.astype(jnp.bfloat16)]
    ppermute x1, waiting for transfers between devices: 2.47 us -> 0.01 us  [per_device(): received = lax.ppermute(sent, 'tx', [(0, 1), (1, 0)])]
    unnamed x27 -> x15, local copies, waits for them, and re-layouts: 4.01 us -> 2.35 us
  transfers between devices with their start and end apart: 6 -> 6, of which waited for: 4 -> 4; matrix products, arithmetic and copies ran while one was open for 17% -> 16% of each run, Pallas kernels for 0% -> 0%
where the time goes in v15:
time: 138 us; the launch traced here: 137 us
  starting transfers between devices  39.6 us (29%)
  waiting for transfers between devices  28.1 us (20%)
  matrix products  24.8 us (18%)
  between operations  20.2 us (15%)
  other arithmetic  16.8 us (12%)
  local copies, waits for them, and re-layouts  7.74 us (6%)
    all_to_all x2, starting transfers between devices, carry_in(): return lax.all_to_all(window, 'dp', split_axis=0, concat_axis=0, tiled=True)  28.7 us
    all_to_all x1, waiting for transfers between devices, carry_out(): return lax.all_to_all(window, 'dp', split_axis=0, concat_axis=0, tiled=True)  11.7 us
    dot_general x4, matrix products, one_head(): jnp.einsum('qd,kd->qk', query_rows, window_keys, preferred_element_type=j...  9.26 us
    all_to_all x2, waiting for transfers between devices, carry_in(): return lax.all_to_all(window, 'dp', split_axis=0, concat_axis=0, tiled=True)  8.19 us
    all_gather x1, waiting for transfers between devices, per_device(): whole = lax.all_gather(tokens, 'tx', axis=1, tiled=True)  7.47 us
    all_to_all x1, starting transfers between devices, carry_out(): return lax.all_to_all(window, 'dp', split_axis=0, concat_axis=0, tiled=True)  6.22 us
    ppermute x1, starting transfers between devices, per_device(): received = lax.ppermute(sent, 'tx', [(0, 1), (1, 0)])  4.59 us
    dot_general x4, matrix products, one_head(): jnp.einsum('qd,kd->qk', query_rows, new_keys, preferred_element_type=jnp....  4.59 us
  transfers between devices with their start and end apart: 6, of which 4 were waited for; matrix products, arithmetic and copies ran while one was open for 16% of the time, Pallas kernels for 0%

profile of v15, /device:TPU:1, one launch (start us, length us, event | category | flops | bytes accessed | tf_op | source)
XLA Modules:
  0.0 137.3 jit_solution(18155062680117657028)
XLA Ops:
  7.9 17.1 %all-to-all-start = ((bf16[64,32,128]{2,1,0:T(8,128)(2,1)}), bf16[64,32,128]{2,1,0:T(8,128)(2,1)S(1)}, u32[]{:S(2)}, u32[]{:S(2)}) async-start(bf16[64,32,128]{2,1,0:T(8,128)(2,1)} %bitcast.85), calls=%async_computation | async-start | bytes 1048576 | tf_op jit(solution)/shard_map/all_to_all | solution.py:30
  25.1 1.2 dynamic_slice.26
  28.3 7.5 %all-gather.2.cloned.1.call-done = bf16[512,2048]{1,0:T(8,128)(2,1)} async-done(((bf16[512,1024]{1,0:T(8,128)(2,1)}), bf16[512,2048]{1,0:T(8,128)(2,1)}) %all-gather.2.cloned.1.call-update) | async-done | bytes 2097168 | tf_op jit(solution)/shard_map/all_gather | solution.py:51
  35.8 2.1 %fusion.24 = f32[512]{0:T(512)S(1)} fusion(bf16[512,2048]{1,0:T(8,128)(2,1)} %all-gather.2.cloned.1.call-done), kind=kLoop, calls=%fused_computation.30 | loop fusion | flops 3145216 | bytes 2099200 | tf_op jit(solution)/shard_map/reduce_sum | solution.py:56
  37.9 2.7 %fusion.28 = f32[512,128]{0,1:T(8,128)S(1)} fusion(bf16[512,2048]{1,0:T(8,128)(2,1)} %all-gather.2.cloned.1.call-done, f32[512]{0:T(512)S(1)} %add_rsqrt_fusion, bf16[2048,1,128]{2,0,1:T(8,128)(2,1)} %param.12), kind=kOutput, calls=%fused_computation.36 | convolution fusion | flops 271581184 | bytes 2885632 | tf_op jit(solution)/shard_map/dot_general | solution.py:63
  42.4 0.9 pad_maximum_fusion
  43.2 11.6 %all-to-all-start.1 = ((bf16[64,40,128]{2,1,0:T(8,128)(2,1)}), bf16[64,40,128]{2,1,0:T(8,128)(2,1)S(1)}, u32[]{:S(2)}, u32[]{:S(2)}) async-start(bf16[64,40,128]{2,1,0:T(8,128)(2,1)} %pad_maximum_fusion), calls=%async_computation.1 | async-start | bytes 1310720 | tf_op jit(solution)/shard_map/all_to_all | solution.py:30
  56.9 1.4 %copy.20 = bf16[2048,1,256]{0,2,1:T(8,128)(2,1)} copy(bf16[2048,1,256]{2,0,1:T(8,128)(2,1)S(1)} %copy-done.2) | data formatting | bytes 2097152 | tf_op args[1]
  62.8 2.7 %fusion.26 = f32[512,4,64]{0,2,1:T(8,128)S(1)} fusion(bf16[4,64,2048]{2,1,0:T(8,128)(2,1)} %bitcast.87, bf16[512,2048]{1,0:T(8,128)(2,1)} %all-gather.2.cloned.1.call-done, f32[512]{0:T(512)S(1)} %add_rsqrt_fusion), kind=kOutput, calls=%fused_computation.32 | convolution fusion | flops 540016640 | bytes 3672064 | tf_op jit(solution)/shard_map/dot_general | solution.py:91
  66.3 7.8 %all-to-all-done.1 = bf16[64,40,128]{2,1,0:T(8,128)(2,1)S(1)} async-done(((bf16[64,40,128]{2,1,0:T(8,128)(2,1)}), bf16[64,40,128]{2,1,0:T(8,128)(2,1)S(1)}, u32[]{:S(2)}, u32[]{:S(2)}) %all-to-all-start.1) | async-done | bytes 655392 | tf_op jit(solution)/shard_map/all_to_all | solution.py:30
  74.3 22.4 %while.11 = (s32[]{:T(128)}, bf16[4,512,64]{1,2,0:T(8,128)(2,1)S(1)}, bf16[4,512,64]{1,2,0:T(8,128)(2,1)}, bf16[2048,64]{1,0:T(8,128)(2,1)S(1)}, bf16[512,64]{1,...) while((s32[]{:T(128)}, ...), condition=%wide.region_6.7_spmd.clone, body=%wide.region_1.6_spmd.clone.sunk | while | flops 347175936 | bytes 17214604 | solution.py:132
  74.4 2.3 %fusion.84 = (f32[512]{0:T(512)S(1)}, f32[512,2048]{1,0:T(8,128)S(1)}) fusion(bf16[2048,64]{1,0:T(8,128)(2,1)S(1)} %get-tuple-element.242, bf16[4,512,64]{1,2,0:T(8,128)(2,1)} %get-tuple-element.241, s32[]{:T(128)} %get-tuple-element.228, s32[512]{0:T(512)S(1)} %get-tuple-element.246, s32[2048]{0:T(1024)S(1)} %get-tuple-element.247, ...), kind=kOutput, calls=%fused_computation.96.clone.1 | convolution fusion | flops 139460096 | bytes 4536832 | tf_op jit(solution)/shard_map/while/body/eval_jaxpr/qd,kd->qk/dot_general | solution.py:110
  76.7 1.1 fusion.85
  80.0 2.3 %fusion.84 = (f32[512]{0:T(512)S(1)}, f32[512,2048]{1,0:T(8,128)S(1)}) fusion(bf16[2048,64]{1,0:T(8,128)(2,1)S(1)} %get-tuple-element.242, bf16[4,512,64]{1,2,0:T(8,128)(2,1)} %get-tuple-element.241, s32[]{:T(128)} %get-tuple-element.228, s32[512]{0:T(512)S(1)} %get-tuple-element.246, s32[2048]{0:T(1024)S(1)} %get-tuple-element.247, ...), kind=kOutput, calls=%fused_computation.96.clone.1 | convolution fusion | flops 139460096 | bytes 4536832 | tf_op jit(solution)/shard_map/while/body/eval_jaxpr/qd,kd->qk/dot_general | solution.py:110
  82.3 1.1 fusion.85
  85.6 2.3 %fusion.84 = (f32[512]{0:T(512)S(1)}, f32[512,2048]{1,0:T(8,128)S(1)}) fusion(bf16[2048,64]{1,0:T(8,128)(2,1)S(1)} %get-tuple-element.242, bf16[4,512,64]{1,2,0:T(8,128)(2,1)} %get-tuple-element.241, s32[]{:T(128)} %get-tuple-element.228, s32[512]{0:T(512)S(1)} %get-tuple-element.246, s32[2048]{0:T(1024)S(1)} %get-tuple-element.247, ...), kind=kOutput, calls=%fused_computation.96.clone.1 | convolution fusion | flops 139460096 | bytes 4536832 | tf_op jit(solution)/shard_map/while/body/eval_jaxpr/qd,kd->qk/dot_general | solution.py:110
  87.9 1.1 fusion.85
  91.2 2.3 %fusion.84 = (f32[512]{0:T(512)S(1)}, f32[512,2048]{1,0:T(8,128)S(1)}) fusion(bf16[2048,64]{1,0:T(8,128)(2,1)S(1)} %get-tuple-element.242, bf16[4,512,64]{1,2,0:T(8,128)(2,1)} %get-tuple-element.241, s32[]{:T(128)} %get-tuple-element.228, s32[512]{0:T(512)S(1)} %get-tuple-element.246, s32[2048]{0:T(1024)S(1)} %get-tuple-element.247, ...), kind=kOutput, calls=%fused_computation.96.clone.1 | convolution fusion | flops 139460096 | bytes 4536832 | tf_op jit(solution)/shard_map/while/body/eval_jaxpr/qd,kd->qk/dot_general | solution.py:110
  93.5 1.1 fusion.85
  97.2 4.6 %collective-permute-start = (bf16[512,1024]{1,0:T(8,128)(2,1)S(1)}, bf16[512,1024]{1,0:T(8,128)(2,1)}, u32[]{:S(2)}, u32[]{:S(2)}) collective-permute-start(bf16[512,1024]{1,0:T(8,128)(2,1)S(1)} %convolution_convert_fusion), channel_id=1, source_target_pairs={{0,4},{4,0},{1,5},{5,1},{2,6},{6,2},{3,7},{7,3},{8,12},{12,8},{9,1... | collective-permute-start | bytes 3145736 | tf_op jit(solution)/shard_map/ppermute | solution.py:146
  105.2 2.7 %add_convert_fusion = bf16[512,1024]{1,0:T(8,128)(2,1)} fusion(f32[512,1024]{1,0:T(8,128)S(1)} %fusion.32, bf16[512,1024]{1,0:T(8,128)(2,1)} %collective-permute-done), kind=kLoop, calls=%fused_computation.34 | loop fusion | flops 1572864 | bytes 4194304 | tf_op jit(solution)/shard_map/convert_element_type | solution.py:167
  110.5 6.2 %all-to-all-start.2 = ((bf16[64,8,128]{2,1,0:T(8,128)(2,1)}), bf16[64,8,128]{2,1,0:T(8,128)(2,1)S(1)}, u32[]{:S(2)}, u32[]{:S(2)}) async-start(bf16[64,8,128]{2,1,0:T(8,128)(2,1)} %bitcast.27), calls=%async_computation.3 | async-start | bytes 262144 | tf_op jit(solution)/shard_map/all_to_all | solution.py:34
  116.7 11.7 %all-to-all-done.2 = bf16[64,8,128]{2,1,0:T(8,128)(2,1)S(1)} async-done(((bf16[64,8,128]{2,1,0:T(8,128)(2,1)}), bf16[64,8,128]{2,1,0:T(8,128)(2,1)S(1)}, u32[]{:S(2)}, u32[]{:S(2)}) %all-to-all-start.2) | async-done | bytes 131104 | tf_op jit(solution)/shard_map/all_to_all | solution.py:34
  128.4 1.0 dynamic_update_slice.7
  (95 shorter events, 22.1 us)
Async XLA Ops:
  7.2 89.6 %copy-start = (bf16[1,256,2048]{2,1,0:T(8,128)(2,1)S(1)}, bf16[1,256,2048]{2,1,0:T(8,128)(2,1)}, u32[]{:S(2)}) copy-start(bf16[1,256,2048]{2,1,0:T(8,128)(2,1)} %param.13) | copy-start | bytes 3145732
  7.2 28.6 %all-gather.2.cloned.1.call-start = ((), (), s32[]{:S(2)}) async-start(), calls=%async_computation.4 | async-start | bytes 3145728 | tf_op jit(solution)/shard_map/all_gather | solution.py:51
  7.9 33.5 %all-to-all-start = ((bf16[64,32,128]{2,1,0:T(8,128)(2,1)}), bf16[64,32,128]{2,1,0:T(8,128)(2,1)S(1)}, u32[]{:S(2)}, u32[]{:S(2)}) async-start(bf16[64,32,128]{2,1,0:T(8,128)(2,1)} %bitcast.85), calls=%async_computation | async-start | bytes 1048576 | tf_op jit(solution)/shard_map/all_to_all | solution.py:30
  37.9 17.0 %copy-start.5 = (s32[64]{0:T(128)S(1)}, s32[64]{0:T(128)}, u32[]{:S(2)}) copy-start(s32[64]{0:T(128)} %param.17) | copy-start | bytes 772
  37.9 19.0 %copy-start.2 = (bf16[2048,1,256]{2,0,1:T(8,128)(2,1)S(1)}, bf16[2048,1,256]{2,0,1:T(8,128)(2,1)}, u32[]{:S(2)}) copy-start(bf16[2048,1,256]{2,0,1:T(8,128)(2,1)} %param.11) | copy-start | bytes 3145732
  40.6 19.1 %copy-start.4 = (s32[64]{0:T(128)S(1)}, s32[64]{0:T(128)}, u32[]{:S(2)}) copy-start(s32[64]{0:T(128)} %param.16) | copy-start | bytes 772
  43.2 30.8 %all-to-all-start.1 = ((bf16[64,40,128]{2,1,0:T(8,128)(2,1)}), bf16[64,40,128]{2,1,0:T(8,128)(2,1)S(1)}, u32[]{:S(2)}, u32[]{:S(2)}) async-start(bf16[64,40,128]{2,1,0:T(8,128)(2,1)} %pad_maximum_fusion), calls=%async_computation.1 | async-start | bytes 1310720 | tf_op jit(solution)/shard_map/all_to_all | solution.py:30
  54.8 75.6 %reduce-scatter.2.cloned.1.call-start = ((), (), s32[]{:S(2)}) async-start(), calls=%async_computation.5 | async-start | bytes 1310720 | tf_op jit(solution)/shard_map/reduce_scatter | solution.py:166
  55.0 10.5 %copy-start.6 = (s32[64]{0:T(128)}, s32[64]{0:T(128)S(1)}, u32[]{:S(2)}) copy-start(s32[64]{0:T(128)S(1)} %select_reduce_fusion) | copy-start | bytes 772
  74.4 2.3 %copy-start.3 = (bf16[512,64]{1,0:T(8,128)(2,1)S(1)}, bf16[512,64]{1,0:T(8,128)(2,1)}, u32[]{:S(2)}) copy-start(bf16[512,64]{1,0:T(8,128)(2,1)} %get-tuple-element.243) | copy-start | bytes 196612 | tf_op jit(solution)/shard_map/while
  80.0 2.3 %copy-start.3 = (bf16[512,64]{1,0:T(8,128)(2,1)S(1)}, bf16[512,64]{1,0:T(8,128)(2,1)}, u32[]{:S(2)}) copy-start(bf16[512,64]{1,0:T(8,128)(2,1)} %get-tuple-element.243) | copy-start | bytes 196612 | tf_op jit(solution)/shard_map/while
  85.6 2.3 %copy-start.3 = (bf16[512,64]{1,0:T(8,128)(2,1)S(1)}, bf16[512,64]{1,0:T(8,128)(2,1)}, u32[]{:S(2)}) copy-start(bf16[512,64]{1,0:T(8,128)(2,1)} %get-tuple-element.243) | copy-start | bytes 196612 | tf_op jit(solution)/shard_map/while
  91.2 2.3 %copy-start.3 = (bf16[512,64]{1,0:T(8,128)(2,1)S(1)}, bf16[512,64]{1,0:T(8,128)(2,1)}, u32[]{:S(2)}) copy-start(bf16[512,64]{1,0:T(8,128)(2,1)} %get-tuple-element.243) | copy-start | bytes 196612 | tf_op jit(solution)/shard_map/while
  97.2 8.0 %collective-permute-start = (bf16[512,1024]{1,0:T(8,128)(2,1)S(1)}, bf16[512,1024]{1,0:T(8,128)(2,1)}, u32[]{:S(2)}, u32[]{:S(2)}) collective-permute-start(bf16[512,1024]{1,0:T(8,128)(2,1)S(1)} %convolution_convert_fusion), channel_id=1, source_target_pairs={{0,4},{4,0},{1,5},{5,1},{2,6},{6,2},{3,7},{7,3},{8,12},{12,8},{9,1... | collective-permute-start | bytes 3145736 | tf_op jit(solution)/shard_map/ppermute | solution.py:146
  103.9 6.5 %copy-start.1 = (bf16[1,1,2048,128]{3,2,1,0:T(8,128)(2,1)S(1)}, bf16[1,1,2048,128]{3,2,1,0:T(8,128)(2,1)}, u32[]{:S(2)}) copy-start(bf16[1,1,2048,128]{3,2,1,0:T(8,128)(2,1)} %param.14) | copy-start | bytes 1572868
  110.5 18.0 %all-to-all-start.2 = ((bf16[64,8,128]{2,1,0:T(8,128)(2,1)}), bf16[64,8,128]{2,1,0:T(8,128)(2,1)S(1)}, u32[]{:S(2)}, u32[]{:S(2)}) async-start(bf16[64,8,128]{2,1,0:T(8,128)(2,1)} %bitcast.27), calls=%async_computation.3 | async-start | bytes 262144 | tf_op jit(solution)/shard_map/all_to_all | solution.py:34
Sparse Core Ops, SparseCore 0:
  10.1 25.6 all-gather.1
  108.0 21.4 reduce-scatter.1

commit v16 on v13

--- a/solution.py
+++ b/solution.py
@@ -46,8 +46,11 @@
     request = lax.axis_index("dp")
     groups = lax.axis_size("dp")
     stored = cache[0, 0]
-    half_rows = stored.shape[0]
-    spread = carry_in(stored)
+    halves = lax.axis_size("tx")
+    core = lax.axis_index("tx")
+    half_rows = stored.shape[0] // halves
+    mine = lax.dynamic_slice_in_dim(stored, core * half_rows, half_rows, axis=0)
+    spread = carry_in(mine)
     whole = lax.all_gather(tokens, "tx", axis=1, tiled=True)
     rows_new = whole.shape[0]
     width = whole.shape[1]
@@ -83,7 +86,16 @@
         axis=1,
     ).reshape(groups * (window_chunk + entry_chunk), lanes)
     delivered = carry_in(second).reshape(groups, window_chunk + entry_chunk, lanes)
-    window = delivered[:, :window_chunk].reshape(half_rows, lanes)
+    window_part = delivered[:, :window_chunk].reshape(half_rows, lanes)
+    if halves == 2:
+        other = lax.ppermute(window_part, "tx", [(0, 1), (1, 0)])
+        window = jnp.where(
+            core == 0,
+            jnp.concatenate([window_part, other], axis=0),
+            jnp.concatenate([other, window_part], axis=0),
+        )
+    else:
+        window = lax.all_gather(window_part, "tx", axis=0, tiled=True)
     entry_parts = delivered[:, window_chunk:]
 
     query_cols = query_weight.shape[2]

time: 133 us -> 141 us (1.060)
  waiting for transfers between devices: 26.9 us -> 18.3 us
  local copies, waits for them, and re-layouts: 9.3 us -> 16.2 us
  starting transfers between devices: 40 us -> 46.5 us
  other arithmetic: 15.1 us -> 19 us
    all_to_all x2, waiting for transfers between devices: 5.41 us -> 0.01 us  [carry_in(): return lax.all_to_all(window, 'dp', split_axis=0, concat_axis=0, tiled=True)]
    ppermute x0 -> x1, starting transfers between devices: none -> 4.52 us  [per_device(): other = lax.ppermute(window_part, 'tx', [(0, 1), (1, 0)])]
    all_to_all x1, starting transfers between devices: 6.2 us -> 10.2 us  [carry_out(): return lax.all_to_all(window, 'dp', split_axis=0, concat_axis=0, tiled=True)]
    all_gather x1, waiting for transfers between devices: 6.87 us -> 3.91 us  [per_device(): whole = lax.all_gather(tokens, 'tx', axis=1, tiled=True)]
    ppermute x1, starting transfers between devices: 4.58 us -> 2.26 us  [per_device(): received = lax.ppermute(sent, 'tx', [(0, 1), (1, 0)])]
    dynamic_slice x0 -> x1, local copies, waits for them, and re-layouts: none -> 1.67 us  [per_device(): mine = lax.dynamic_slice_in_dim(stored, core * half_rows, half_rows, axis=0)]
    optimization_barrier x1, local copies, waits for them, and re-layouts: 0.12 us -> 1.75 us  [per_device(): spread, entry = lax.optimization_barrier((spread, entry))]
    unnamed x27 -> x25, local copies, waits for them, and re-layouts: 4.01 us -> 4.31 us
  transfers between devices with their start and end apart: 6 -> 7, of which waited for: 4 -> 3; matrix products, arithmetic and copies ran while one was open for 17% -> 21% of each run, Pallas kernels for 0% -> 0%
where the time goes in v16:
time: 141 us; the launch traced here: 140 us
  starting transfers between devices  46.5 us (33%)
  between operations  20.5 us (15%)
  matrix products  19.2 us (14%)
  other arithmetic  19 us (13%)
  waiting for transfers between devices  18.3 us (13%)
  local copies, waits for them, and re-layouts  16.2 us (11%)
    all_to_all x2, starting transfers between devices, carry_in(): return lax.all_to_all(window, 'dp', split_axis=0, concat_axis=0, tiled=True)  29.4 us
    all_to_all x1, waiting for transfers between devices, carry_out(): return lax.all_to_all(window, 'dp', split_axis=0, concat_axis=0, tiled=True)  11.4 us
    all_to_all x1, starting transfers between devices, carry_out(): return lax.all_to_all(window, 'dp', split_axis=0, concat_axis=0, tiled=True)  10.2 us
    dot_general x4, matrix products, one_head(): jnp.einsum('qd,kd->qk', query_rows, window_keys, preferred_element_type=j...  5.8 us
    ppermute x1, starting transfers between devices, per_device(): other = lax.ppermute(window_part, 'tx', [(0, 1), (1, 0)])  4.52 us
    unnamed x25, local copies, waits for them, and re-layouts  4.31 us
    all_gather x1, waiting for transfers between devices, per_device(): whole = lax.all_gather(tokens, 'tx', axis=1, tiled=True)  3.91 us
    dot_general x4, matrix products, one_head(): jnp.dot(old_powers.astype(jnp.bfloat16), window_values, preferred_element...  3.53 us
  transfers between devices with their start and end apart: 7, of which 3 were waited for; matrix products, arithmetic and copies ran while one was open for 21% of the time, Pallas kernels for 0%

profile of v16, /device:TPU:1, one launch (start us, length us, event | category | flops | bytes accessed | tf_op | source)
XLA Modules:
  0.0 139.8 jit_solution(10491228486537180188)
XLA Ops:
  7.9 1.7 %constant_dynamic-slice_fusion = bf16[1,1,1024,128]{3,2,1,0:T(8,128)(2,1)} fusion(bf16[1,1,2048,128]{3,2,1,0:T(8,128)(2,1)} %param.14, s32[]{:T(128)S(6)} %select_n.89), kind=kLoop, calls=%fused_computation.95 | loop fusion | bytes 524292 | tf_op jit(solution)/shard_map/dynamic_slice | solution.py:52
  9.6 17.1 %all-to-all-start = ((bf16[64,16,128]{2,1,0:T(8,128)(2,1)}), bf16[64,16,128]{2,1,0:T(8,128)(2,1)S(1)}, u32[]{:S(2)}, u32[]{:S(2)}) async-start(bf16[64,16,128]{2,1,0:T(8,128)(2,1)} %bitcast.6), calls=%async_computation | async-start | bytes 524288 | tf_op jit(solution)/shard_map/all_to_all | solution.py:30
  26.7 1.3 dynamic_slice.29
  29.4 1.3 select_reduce_fusion
  31.9 3.9 %all-gather.2.cloned.1.call-done = bf16[512,2048]{1,0:T(8,128)(2,1)} async-done(((bf16[512,1024]{1,0:T(8,128)(2,1)}), bf16[512,2048]{1,0:T(8,128)(2,1)}) %all-gather.2.cloned.1.call-update) | async-done | bytes 2097168 | tf_op jit(solution)/shard_map/all_gather | solution.py:54
  35.8 2.1 %fusion.24 = f32[512]{0:T(512)S(1)} fusion(bf16[512,2048]{1,0:T(8,128)(2,1)} %all-gather.2.cloned.1.call-done), kind=kLoop, calls=%fused_computation.30 | loop fusion | flops 3145216 | bytes 2099200 | tf_op jit(solution)/shard_map/reduce_sum | solution.py:59
  37.9 2.7 %fusion.28 = f32[512,128]{0,1:T(8,128)S(1)} fusion(bf16[512,2048]{1,0:T(8,128)(2,1)} %all-gather.2.cloned.1.call-done, f32[512]{0:T(512)S(1)} %add_rsqrt_fusion, bf16[2048,1,128]{2,0,1:T(8,128)(2,1)} %param.12), kind=kOutput, calls=%fused_computation.36 | convolution fusion | flops 271581184 | bytes 2885632 | tf_op jit(solution)/shard_map/dot_general | solution.py:66
  42.0 1.7 %copy.21 = bf16[512,128]{1,0:T(8,128)(2,1)} copy(bf16[512,128]{0,1:T(8,128)(2,1)} %pad_maximum_fusion.2) | data formatting | bytes 262144 | tf_op jit(solution)/shard_map/optimization_barrier | solution.py:77
  43.7 1.6 %gather_fusion = bf16[64,16,128]{2,1,0:T(8,128)(2,1)S(1)} fusion(bf16[64,16,128]{2,1,0:T(8,128)(2,1)} %copy-done.3, s32[1024]{0:T(1024)S(1)} %pad_clamp_fusion.1), kind=kCustom, calls=%fused_computation | custom fusion | bytes 524544 | tf_op jit(solution)/shard_map/jit(_take)/gather | solution.py:83
  46.0 1.7 %pad_maximum_fusion.1 = bf16[64,24,128]{2,1,0:T(8,128)(2,1)} fusion(bf16[64,8,128]{2,1,0:T(8,128)(2,1)} %bitcast.90, bf16[64,16,128]{2,1,0:T(8,128)(2,1)S(1)} %broadcast_select_fusion), kind=kLoop, calls=%fused_computation.46 | loop fusion | flops 786432 | bytes 786432 | tf_op jit(solution)/shard_map/concatenate | solution.py:81
  47.8 12.2 %all-to-all-start.1 = ((bf16[64,24,128]{2,1,0:T(8,128)(2,1)}), bf16[64,24,128]{2,1,0:T(8,128)(2,1)}, u32[]{:S(2)}, u32[]{:S(2)}) async-start(bf16[64,24,128]{2,1,0:T(8,128)(2,1)} %pad_maximum_fusion.1), calls=%async_computation.1 | async-start | bytes 786432 | tf_op jit(solution)/shard_map/all_to_all | solution.py:30
  63.8 2.3 %copy.20 = bf16[2048,1,256]{0,2,1:T(8,128)(2,1)} copy(bf16[2048,1,256]{2,0,1:T(8,128)(2,1)} %param.11) | data formatting | bytes 2097152 | tf_op args[1]
  72.1 2.9 %fusion.26 = f32[512,4,64]{0,2,1:T(8,128)} fusion(bf16[4,64,2048]{2,1,0:T(8,128)(2,1)} %bitcast.84, bf16[512,2048]{1,0:T(8,128)(2,1)S(1)} %copy-done.1, f32[512]{0:T(512)} %copy-done.9), kind=kOutput, calls=%fused_computation.32 | convolution fusion | flops 540016640 | bytes 3672064 | tf_op jit(solution)/shard_map/dot_general | solution.py:103
  76.0 4.5 %collective-permute-start = (bf16[1024,128]{1,0:T(8,128)(2,1)S(1)}, bf16[1024,128]{1,0:T(8,128)(2,1)S(1)}, u32[]{:S(2)}, u32[]{:S(2)}) collective-permute-start(bf16[1024,128]{1,0:T(8,128)(2,1)S(1)} %bitcast.87), channel_id=1, source_target_pairs={{0,4},{4,0},{1,5},{5,1},{2,6},{6,2},{3,7},{7,3},{8,12},{12,8},{9,1... | collective-permute-start | bytes 786440 | tf_op jit(solution)/shard_map/ppermute | solution.py:91
  82.0 15.5 %while.11 = (s32[]{:T(128)}, bf16[4,512,64]{1,2,0:T(8,128)(2,1)S(1)}, bf16[4,512,64]{1,2,0:T(8,128)(2,1)S(1)}, bf16[2048,64]{1,0:T(8,128)(2,1)S(1)}, bf16[512,64...) while((s32[]{:T(128)}, ...), condition=%wide.region_6.7_spmd.clone, body=%wide.region_1.6_spmd.clone.sunk | while | flops 347175936 | bytes 17279104 | solution.py:144
  82.1 1.4 %fusion.86 = (f32[512]{0:T(512)S(1)}, f32[512,2048]{1,0:T(8,128)S(1)}) fusion(bf16[2048,64]{1,0:T(8,128)(2,1)S(1)} %get-tuple-element.238, bf16[4,512,64]{1,2,0:T(8,128)(2,1)S(1)} %get-tuple-element.237, s32[]{:T(128)S(6)} %copy.29, s32[512]{0:T(512)S(1)} %get-tuple-element.242, s32[2048]{0:T(1024)S(1)} %get-tuple-element.243, ...), kind=kOutput, calls=%fused_computation.98.clone.1 | convolution fusion | flops 139460096 | bytes 4798468 | tf_op jit(solution)/shard_map/while/body/eval_jaxpr/qd,kd->qk/dot_general | solution.py:122
  85.9 1.4 %fusion.86 = (f32[512]{0:T(512)S(1)}, f32[512,2048]{1,0:T(8,128)S(1)}) fusion(bf16[2048,64]{1,0:T(8,128)(2,1)S(1)} %get-tuple-element.238, bf16[4,512,64]{1,2,0:T(8,128)(2,1)S(1)} %get-tuple-element.237, s32[]{:T(128)S(6)} %copy.29, s32[512]{0:T(512)S(1)} %get-tuple-element.242, s32[2048]{0:T(1024)S(1)} %get-tuple-element.243, ...), kind=kOutput, calls=%fused_computation.98.clone.1 | convolution fusion | flops 139460096 | bytes 4798468 | tf_op jit(solution)/shard_map/while/body/eval_jaxpr/qd,kd->qk/dot_general | solution.py:122
  89.8 1.4 %fusion.86 = (f32[512]{0:T(512)S(1)}, f32[512,2048]{1,0:T(8,128)S(1)}) fusion(bf16[2048,64]{1,0:T(8,128)(2,1)S(1)} %get-tuple-element.238, bf16[4,512,64]{1,2,0:T(8,128)(2,1)S(1)} %get-tuple-element.237, s32[]{:T(128)S(6)} %copy.29, s32[512]{0:T(512)S(1)} %get-tuple-element.242, s32[2048]{0:T(1024)S(1)} %get-tuple-element.243, ...), kind=kOutput, calls=%fused_computation.98.clone.1 | convolution fusion | flops 139460096 | bytes 4798468 | tf_op jit(solution)/shard_map/while/body/eval_jaxpr/qd,kd->qk/dot_general | solution.py:122
  93.6 1.4 %fusion.86 = (f32[512]{0:T(512)S(1)}, f32[512,2048]{1,0:T(8,128)S(1)}) fusion(bf16[2048,64]{1,0:T(8,128)(2,1)S(1)} %get-tuple-element.238, bf16[4,512,64]{1,2,0:T(8,128)(2,1)S(1)} %get-tuple-element.237, s32[]{:T(128)S(6)} %copy.29, s32[512]{0:T(512)S(1)} %get-tuple-element.242, s32[2048]{0:T(1024)S(1)} %get-tuple-element.243, ...), kind=kOutput, calls=%fused_computation.98.clone.1 | convolution fusion | flops 139460096 | bytes 4798468 | tf_op jit(solution)/shard_map/while/body/eval_jaxpr/qd,kd->qk/dot_general | solution.py:122
  98.0 2.3 %collective-permute-start.1 = (bf16[512,1024]{1,0:T(8,128)(2,1)S(1)}, bf16[512,1024]{1,0:T(8,128)(2,1)S(1)}, u32[]{:S(2)}, u32[]{:S(2)}) collective-permute-start(bf16[512,1024]{1,0:T(8,128)(2,1)S(1)} %convolution_convert_fusion), channel_id=1, source_target_pairs={{0,4},{4,0},{1,5},{5,1},{2,6},{6,2},{3,7},{7,3},{8,12},{12,8},{9,1... | collective-permute-start | bytes 3145736 | tf_op jit(solution)/shard_map/ppermute | solution.py:166
  100.3 2.3 %collective-permute-done.1 = bf16[512,1024]{1,0:T(8,128)(2,1)S(1)} collective-permute-done((bf16[512,1024]{1,0:T(8,128)(2,1)S(1)}, bf16[512,1024]{1,0:T(8,128)(2,1)S(1)}, u32[]{:S(2)}, u32[]{:S(2)}) %collective-permute-start.1) | collective-permute-done | bytes 1048608 | tf_op jit(solution)/shard_map/ppermute | solution.py:166
  102.6 1.4 %add_convert_fusion = bf16[512,1024]{1,0:T(8,128)(2,1)} fusion(bf16[512,1024]{1,0:T(8,128)(2,1)S(1)} %collective-permute-done.1, bf16[512,256]{0,1:T(8,128)(2,1)S(1)} %bitcast.86, bf16[1,256,2048]{2,1,0:T(8,128)(2,1)S(1)} %copy-done, s32[]{:T(128)S(6)} %select_n.89), kind=kOutput, calls=%fused_computation.34 | convolution fusion | flops 270008320 | bytes 2883588 | tf_op jit(solution)/shard_map/dot_general | solution.py:167
  109.2 10.2 %all-to-all-start.2 = ((bf16[64,8,128]{2,1,0:T(8,128)(2,1)}), bf16[64,8,128]{2,1,0:T(8,128)(2,1)S(1)}, u32[]{:S(2)}, u32[]{:S(2)}) async-start(bf16[64,8,128]{2,1,0:T(8,128)(2,1)} %broadcast_select_fusion.1), calls=%async_computation.3 | async-start | bytes 262144 | tf_op jit(solution)/shard_map/all_to_all | solution.py:34
  119.5 11.4 %all-to-all-done.2 = bf16[64,8,128]{2,1,0:T(8,128)(2,1)S(1)} async-done(((bf16[64,8,128]{2,1,0:T(8,128)(2,1)}), bf16[64,8,128]{2,1,0:T(8,128)(2,1)S(1)}, u32[]{:S(2)}, u32[]{:S(2)}) %all-to-all-start.2) | async-done | bytes 131104 | tf_op jit(solution)/shard_map/all_to_all | solution.py:34
  (98 shorter events, 28.7 us)
Async XLA Ops:
  7.2 90.4 %copy-start = (bf16[1,256,2048]{2,1,0:T(8,128)(2,1)S(1)}, bf16[1,256,2048]{2,1,0:T(8,128)(2,1)}, u32[]{:S(2)}) copy-start(bf16[1,256,2048]{2,1,0:T(8,128)(2,1)} %param.13) | copy-start | bytes 3145732
  7.2 28.6 %all-gather.2.cloned.1.call-start = ((), (), s32[]{:S(2)}) async-start(), calls=%async_computation.4 | async-start | bytes 3145728 | tf_op jit(solution)/shard_map/all_gather | solution.py:54
  9.6 32.4 %all-to-all-start = ((bf16[64,16,128]{2,1,0:T(8,128)(2,1)}), bf16[64,16,128]{2,1,0:T(8,128)(2,1)S(1)}, u32[]{:S(2)}, u32[]{:S(2)}) async-start(bf16[64,16,128]{2,1,0:T(8,128)(2,1)} %bitcast.6), calls=%async_computation | async-start | bytes 524288 | tf_op jit(solution)/shard_map/all_to_all | solution.py:30
  37.9 3.2 %copy-start.9 = (f32[512]{0:T(512)}, f32[512]{0:T(512)S(1)}, u32[]{:S(2)}) copy-start(f32[512]{0:T(512)S(1)} %add_rsqrt_fusion) | copy-start | bytes 6148
  37.9 29.5 %copy-start.6 = (s32[64]{0:T(128)S(1)}, s32[64]{0:T(128)}, u32[]{:S(2)}) copy-start(s32[64]{0:T(128)} %param.16) | copy-start | bytes 772
  37.9 34.2 %copy-start.1 = (bf16[512,2048]{1,0:T(8,128)(2,1)S(1)}, bf16[512,2048]{1,0:T(8,128)(2,1)}, u32[]{:S(2)}) copy-start(bf16[512,2048]{1,0:T(8,128)(2,1)} %all-gather.2.cloned.1.call-done) | copy-start | bytes 6291460
  40.7 0.6 copy-start.4
  42.0 1.8 %copy-start.3 = (bf16[64,16,128]{2,1,0:T(8,128)(2,1)}, bf16[64,16,128]{2,1,0:T(8,128)(2,1)S(1)}, u32[]{:S(2)}) copy-start(bf16[64,16,128]{2,1,0:T(8,128)(2,1)S(1)} %all-to-all-done) | copy-start | bytes 786436
  47.8 27.2 %all-to-all-start.1 = ((bf16[64,24,128]{2,1,0:T(8,128)(2,1)}), bf16[64,24,128]{2,1,0:T(8,128)(2,1)}, u32[]{:S(2)}, u32[]{:S(2)}) async-start(bf16[64,24,128]{2,1,0:T(8,128)(2,1)} %pad_maximum_fusion.1), calls=%async_computation.1 | async-start | bytes 786432 | tf_op jit(solution)/shard_map/all_to_all | solution.py:30
  60.0 72.9 %reduce-scatter.2.cloned.1.call-start = ((), (), s32[]{:S(2)}) async-start(), calls=%async_computation.5 | async-start | bytes 1310720 | tf_op jit(solution)/shard_map/reduce_scatter | solution.py:176
  72.1 9.9 %copy-start.7 = (s32[512]{0:T(512)S(1)}, s32[512]{0:T(512)}, u32[]{:S(2)}) copy-start(s32[512]{0:T(512)} %fusion.52) | copy-start | bytes 6148
  72.1 9.9 %copy-start.8 = (pred[2048]{0:T(1024)(128)(4,1)S(1)}, pred[2048]{0:T(1024)(128)(4,1)}, u32[]{:S(2)}) copy-start(pred[2048]{0:T(1024)(128)(4,1)} %broadcast_compare_fusion) | copy-start | bytes 6148
  75.0 7.1 %copy-start.5 = (bf16[512,64]{1,0:T(8,128)(2,1)S(1)}, bf16[512,64]{1,0:T(8,128)(2,1)}, u32[]{:S(2)}) copy-start(bf16[512,64]{1,0:T(8,128)(2,1)} %copy.23) | copy-start | bytes 196612
  76.0 5.7 %collective-permute-start = (bf16[1024,128]{1,0:T(8,128)(2,1)S(1)}, bf16[1024,128]{1,0:T(8,128)(2,1)S(1)}, u32[]{:S(2)}, u32[]{:S(2)}) collective-permute-start(bf16[1024,128]{1,0:T(8,128)(2,1)S(1)} %bitcast.87), channel_id=1, source_target_pairs={{0,4},{4,0},{1,5},{5,1},{2,6},{6,2},{3,7},{7,3},{8,12},{12,8},{9,1... | collective-permute-start | bytes 786440 | tf_op jit(solution)/shard_map/ppermute | solution.py:91
  97.5 9.3 %copy-start.10 = (s32[64]{0:T(128)S(1)}, s32[64]{0:T(128)}, u32[]{:S(2)}) copy-start(s32[64]{0:T(128)} %select_reduce_fusion) | copy-start | bytes 772
  97.5 9.3 %copy-start.2 = (bf16[1,1,2048,128]{3,2,1,0:T(8,128)(2,1)S(1)}, bf16[1,1,2048,128]{3,2,1,0:T(8,128)(2,1)}, u32[]{:S(2)}) copy-start(bf16[1,1,2048,128]{3,2,1,0:T(8,128)(2,1)} %param.14) | copy-start | bytes 1572868
  98.0 4.6 %collective-permute-start.1 = (bf16[512,1024]{1,0:T(8,128)(2,1)S(1)}, bf16[512,1024]{1,0:T(8,128)(2,1)S(1)}, u32[]{:S(2)}, u32[]{:S(2)}) collective-permute-start(bf16[512,1024]{1,0:T(8,128)(2,1)S(1)} %convolution_convert_fusion), channel_id=1, source_target_pairs={{0,4},{4,0},{1,5},{5,1},{2,6},{6,2},{3,7},{7,3},{8,12},{12,8},{9,1... | collective-permute-start | bytes 3145736 | tf_op jit(solution)/shard_map/ppermute | solution.py:166
  109.2 21.7 %all-to-all-start.2 = ((bf16[64,8,128]{2,1,0:T(8,128)(2,1)}), bf16[64,8,128]{2,1,0:T(8,128)(2,1)S(1)}, u32[]{:S(2)}, u32[]{:S(2)}) async-start(bf16[64,8,128]{2,1,0:T(8,128)(2,1)} %broadcast_select_fusion.1), calls=%async_computation.3 | async-start | bytes 262144 | tf_op jit(solution)/shard_map/all_to_all | solution.py:34
Sparse Core Ops, SparseCore 0:
  10.1 25.6 all-gather.1
  104.1 25.7 reduce-scatter.1

commit v17 on v13

--- a/solution.py
+++ b/solution.py
@@ -146,18 +146,15 @@
     if halves == 2:
         core = lax.axis_index("tx")
         half_cols = width // halves
-        sent = jnp.dot(
-            attended,
-            lax.dynamic_slice_in_dim(out_rows, (1 - core) * half_cols, half_cols, axis=1),
-            preferred_element_type=jnp.float32,
-        ).astype(jnp.bfloat16)
-        received = lax.ppermute(sent, "tx", [(0, 1), (1, 0)])
-        kept = jnp.dot(
-            attended,
-            lax.dynamic_slice_in_dim(out_rows, core * half_cols, half_cols, axis=1),
-            preferred_element_type=jnp.float32,
+        pairs = [(0, 1), (1, 0)]
+        other_weight = lax.ppermute(
+            lax.dynamic_slice_in_dim(out_rows, (1 - core) * half_cols, half_cols, axis=1), "tx", pairs
         )
-        across_cores = kept + received.astype(jnp.float32)
+        own_weight = lax.dynamic_slice_in_dim(out_rows, core * half_cols, half_cols, axis=1)
+        other_attended = lax.ppermute(attended, "tx", pairs)
+        across_cores = jnp.dot(attended, own_weight, preferred_element_type=jnp.float32) + jnp.dot(
+            other_attended, other_weight, preferred_element_type=jnp.float32
+        )
     else:
         partial_value = jnp.dot(attended, out_rows, preferred_element_type=jnp.float32)
         across_cores = lax.psum_scatter(partial_value, "tx", scatter_dimension=1, tiled=True)

time: 133 us -> 129 us (0.970)
  other arithmetic: 15.1 us -> 12.1 us
  starting transfers between devices: 40 us -> 42.6 us
  local copies, waits for them, and re-layouts: 9.3 us -> 7.3 us
    all_to_all x2, waiting for transfers between devices: 5.41 us -> 9.49 us  [carry_in(): return lax.all_to_all(window, 'dp', split_axis=0, concat_axis=0, tiled=True)]
    all_gather x1, waiting for transfers between devices: 6.87 us -> 3.68 us  [per_device(): whole = lax.all_gather(tokens, 'tx', axis=1, tiled=True)]
    ppermute x1 -> x2, starting transfers between devices: 4.58 us -> 7.58 us  [the longest x1 4.73 us: per_device(): other_attended = lax.ppermute(attended, 'tx', pairs)]
    unnamed x27 -> x19, local copies, waits for them, and re-layouts: 4.01 us -> 1.72 us
    ppermute x1 -> x2, waiting for transfers between devices: 2.47 us -> 0.67 us  [the longest x1 0.67 us: per_device(): other_attended = lax.ppermute(attended, 'tx', pairs)]
  transfers between devices with their start and end apart: 6 -> 7, of which waited for: 4 -> 5; matrix products, arithmetic and copies ran while one was open for 17% -> 29% of each run, Pallas kernels for 0% -> 0%
where the time goes in v17:
time: 129 us; the launch traced here: 128 us
  starting transfers between devices  42.6 us (33%)
  waiting for transfers between devices  26 us (20%)
  between operations  20.2 us (16%)
  matrix products  19.9 us (15%)
  other arithmetic  12.1 us (9%)
  local copies, waits for them, and re-layouts  7.3 us (6%)
    all_to_all x2, starting transfers between devices, carry_in(): return lax.all_to_all(window, 'dp', split_axis=0, concat_axis=0, tiled=True)  28.8 us
    all_to_all x1, waiting for transfers between devices, carry_out(): return lax.all_to_all(window, 'dp', split_axis=0, concat_axis=0, tiled=True)  11.4 us
    all_to_all x2, waiting for transfers between devices, carry_in(): return lax.all_to_all(window, 'dp', split_axis=0, concat_axis=0, tiled=True)  9.49 us
    all_to_all x1, starting transfers between devices, carry_out(): return lax.all_to_all(window, 'dp', split_axis=0, concat_axis=0, tiled=True)  6.2 us
    dot_general x4, matrix products, one_head(): jnp.einsum('qd,kd->qk', query_rows, window_keys, preferred_element_type=j...  5.77 us
    ppermute x1, starting transfers between devices, per_device(): other_attended = lax.ppermute(attended, 'tx', pairs)  4.73 us
    all_gather x1, waiting for transfers between devices, per_device(): whole = lax.all_gather(tokens, 'tx', axis=1, tiled=True)  3.68 us
    dot_general x4, matrix products, one_head(): jnp.dot(old_powers.astype(jnp.bfloat16), window_values, preferred_element...  3.51 us
  transfers between devices with their start and end apart: 7, of which 5 were waited for; matrix products, arithmetic and copies ran while one was open for 29% of the time, Pallas kernels for 0%

profile of v17, /device:TPU:1, one launch (start us, length us, event | category | flops | bytes accessed | tf_op | source)
XLA Modules:
  0.0 128.2 jit_solution(3373555412275014049)
XLA Ops:
  7.9 17.1 %all-to-all-start = ((bf16[64,32,128]{2,1,0:T(8,128)(2,1)}), bf16[64,32,128]{2,1,0:T(8,128)(2,1)S(1)}, u32[]{:S(2)}, u32[]{:S(2)}) async-start(bf16[64,32,128]{2,1,0:T(8,128)(2,1)} %bitcast.82), calls=%async_computation | async-start | bytes 1048576 | tf_op jit(solution)/shard_map/all_to_all | solution.py:30
  25.9 2.9 %collective-permute-start.1 = (bf16[256,1024]{1,0:T(8,128)(2,1)}, bf16[256,1024]{1,0:T(8,128)(2,1)}, u32[]{:S(2)}, u32[]{:S(2)}) collective-permute-start(bf16[256,1024]{1,0:T(8,128)(2,1)} %dynamic-slice_bitcast_fusion), channel_id=1, source_target_pairs={{0,4},{4,0},{1,5},{5,1},{2,6},{6,2},{3,7},{7,3},{8,12},{12,8},{9,1... | collective-permute-start | bytes 1572872 | tf_op jit(solution)/shard_map/ppermute | solution.py:150
  28.8 1.3 %dynamic_slice.26 = s32[1]{0:T(128)} dynamic-slice(s32[64]{0:T(128)} %param.15, s32[]{:T(128)S(6)} %select_n.77), dynamic_slice_sizes={1} | dynamic-slice | bytes 12 | tf_op jit(solution)/shard_map/dynamic_slice | solution.py:60
  32.1 3.7 %all-gather.2.cloned.1.call-done = bf16[512,2048]{1,0:T(8,128)(2,1)} async-done(((bf16[512,1024]{1,0:T(8,128)(2,1)}), bf16[512,2048]{1,0:T(8,128)(2,1)}) %all-gather.2.cloned.1.call-update) | async-done | bytes 2097168 | tf_op jit(solution)/shard_map/all_gather | solution.py:51
  35.8 2.1 %fusion.24 = f32[512]{0:T(512)S(1)} fusion(bf16[512,2048]{1,0:T(8,128)(2,1)} %all-gather.2.cloned.1.call-done), kind=kLoop, calls=%fused_computation.30 | loop fusion | flops 3145216 | bytes 2099200 | tf_op jit(solution)/shard_map/reduce_sum | solution.py:56
  37.9 2.7 %fusion.28 = f32[512,128]{0,1:T(8,128)S(1)} fusion(bf16[512,2048]{1,0:T(8,128)(2,1)} %all-gather.2.cloned.1.call-done, f32[512]{0:T(512)S(1)} %add_rsqrt_fusion, bf16[2048,1,128]{2,0,1:T(8,128)(2,1)} %param.12), kind=kOutput, calls=%fused_computation.35 | convolution fusion | flops 271581184 | bytes 2885632 | tf_op jit(solution)/shard_map/dot_general | solution.py:63
  42.3 0.9 pad_maximum_fusion
  43.2 11.6 %all-to-all-start.1 = ((bf16[64,40,128]{2,1,0:T(8,128)(2,1)}), bf16[64,40,128]{2,1,0:T(8,128)(2,1)S(1)}, u32[]{:S(2)}, u32[]{:S(2)}) async-start(bf16[64,40,128]{2,1,0:T(8,128)(2,1)} %pad_maximum_fusion), calls=%async_computation.1 | async-start | bytes 1310720 | tf_op jit(solution)/shard_map/all_to_all | solution.py:30
  56.9 1.4 %copy.20 = bf16[2048,1,256]{0,2,1:T(8,128)(2,1)} copy(bf16[2048,1,256]{2,0,1:T(8,128)(2,1)S(1)} %copy-done.2) | data formatting | bytes 2097152 | tf_op args[1]
  62.2 2.7 %fusion.26 = f32[512,4,64]{0,2,1:T(8,128)S(1)} fusion(bf16[4,64,2048]{2,1,0:T(8,128)(2,1)} %bitcast.84, bf16[512,2048]{1,0:T(8,128)(2,1)} %all-gather.2.cloned.1.call-done, f32[512]{0:T(512)} %copy-done.4), kind=kOutput, calls=%fused_computation.32 | convolution fusion | flops 540016640 | bytes 3672064 | tf_op jit(solution)/shard_map/dot_general | solution.py:91
  65.0 9.1 %all-to-all-done.1 = bf16[64,40,128]{2,1,0:T(8,128)(2,1)S(1)} async-done(((bf16[64,40,128]{2,1,0:T(8,128)(2,1)}), bf16[64,40,128]{2,1,0:T(8,128)(2,1)S(1)}, u32[]{:S(2)}, u32[]{:S(2)}) %all-to-all-start.1) | async-done | bytes 655392 | tf_op jit(solution)/shard_map/all_to_all | solution.py:30
  74.4 15.4 %while.11 = (s32[]{:T(128)}, bf16[4,512,64]{1,2,0:T(8,128)(2,1)S(1)}, bf16[4,512,64]{1,2,0:T(8,128)(2,1)S(1)}, bf16[2048,64]{1,0:T(8,128)(2,1)S(1)}, bf16[512,64...) while((s32[]{:T(128)}, ...), condition=%wide.region_6.7_spmd.clone, body=%wide.region_1.6_spmd.clone.sunk | while | flops 347175936 | bytes 17279096 | solution.py:132
  74.4 1.4 %fusion.82 = (f32[512]{0:T(512)S(1)}, f32[512,2048]{1,0:T(8,128)S(1)}) fusion(bf16[2048,64]{1,0:T(8,128)(2,1)S(1)} %get-tuple-element.238, bf16[4,512,64]{1,2,0:T(8,128)(2,1)S(1)} %get-tuple-element.237, s32[]{:T(128)} %get-tuple-element.224, s32[512]{0:T(512)S(1)} %get-tuple-element.242, s32[2048]{0:T(1024)S(1)} %get-tuple-element.243, ...), kind=kOutput, calls=%fused_computation.93.clone.1 | convolution fusion | flops 139460096 | bytes 4798468 | tf_op jit(solution)/shard_map/while/body/eval_jaxpr/qd,kd->qk/dot_general | solution.py:110
  77.0 0.9 fusion.84
  78.2 1.4 %fusion.82 = (f32[512]{0:T(512)S(1)}, f32[512,2048]{1,0:T(8,128)S(1)}) fusion(bf16[2048,64]{1,0:T(8,128)(2,1)S(1)} %get-tuple-element.238, bf16[4,512,64]{1,2,0:T(8,128)(2,1)S(1)} %get-tuple-element.237, s32[]{:T(128)} %get-tuple-element.224, s32[512]{0:T(512)S(1)} %get-tuple-element.242, s32[2048]{0:T(1024)S(1)} %get-tuple-element.243, ...), kind=kOutput, calls=%fused_computation.93.clone.1 | convolution fusion | flops 139460096 | bytes 4798468 | tf_op jit(solution)/shard_map/while/body/eval_jaxpr/qd,kd->qk/dot_general | solution.py:110
  80.9 0.9 fusion.84
  82.1 1.4 %fusion.82 = (f32[512]{0:T(512)S(1)}, f32[512,2048]{1,0:T(8,128)S(1)}) fusion(bf16[2048,64]{1,0:T(8,128)(2,1)S(1)} %get-tuple-element.238, bf16[4,512,64]{1,2,0:T(8,128)(2,1)S(1)} %get-tuple-element.237, s32[]{:T(128)} %get-tuple-element.224, s32[512]{0:T(512)S(1)} %get-tuple-element.242, s32[2048]{0:T(1024)S(1)} %get-tuple-element.243, ...), kind=kOutput, calls=%fused_computation.93.clone.1 | convolution fusion | flops 139460096 | bytes 4798468 | tf_op jit(solution)/shard_map/while/body/eval_jaxpr/qd,kd->qk/dot_general | solution.py:110
  84.7 0.9 fusion.84
  85.9 1.4 %fusion.82 = (f32[512]{0:T(512)S(1)}, f32[512,2048]{1,0:T(8,128)S(1)}) fusion(bf16[2048,64]{1,0:T(8,128)(2,1)S(1)} %get-tuple-element.238, bf16[4,512,64]{1,2,0:T(8,128)(2,1)S(1)} %get-tuple-element.237, s32[]{:T(128)} %get-tuple-element.224, s32[512]{0:T(512)S(1)} %get-tuple-element.242, s32[2048]{0:T(1024)S(1)} %get-tuple-element.243, ...), kind=kOutput, calls=%fused_computation.93.clone.1 | convolution fusion | flops 139460096 | bytes 4798468 | tf_op jit(solution)/shard_map/while/body/eval_jaxpr/qd,kd->qk/dot_general | solution.py:110
  88.6 0.9 fusion.84
  89.8 4.7 %collective-permute-start = (bf16[512,256]{0,1:T(8,128)(2,1)S(1)}, bf16[512,256]{0,1:T(8,128)(2,1)S(1)}, u32[]{:S(2)}, u32[]{:S(2)}) collective-permute-start(bf16[512,256]{0,1:T(8,128)(2,1)S(1)} %bitcast.87), channel_id=1, source_target_pairs={{0,4},{4,0},{1,5},{5,1},{2,6},{6,2},{3,7},{7,3},{8,12},{12,8},{9,1... | collective-permute-start | bytes 786440 | tf_op jit(solution)/shard_map/ppermute | solution.py:154
  95.7 2.5 %add_convert_fusion = bf16[512,1024]{1,0:T(8,128)(2,1)} fusion(f32[512,1024]{1,0:T(8,128)S(1)} %fusion.31, bf16[512,256]{0,1:T(8,128)(2,1)S(1)} %collective-permute-done, bf16[256,1024]{1,0:T(8,128)(2,1)} %collective-permute-done.1), kind=kOutput, calls=%fused_computation.34 | convolution fusion | flops 269484032 | bytes 3932160 | tf_op jit(solution)/shard_map/dot_general | solution.py:155
  102.2 6.2 %all-to-all-start.2 = ((bf16[64,8,128]{2,1,0:T(8,128)(2,1)}), bf16[64,8,128]{2,1,0:T(8,128)(2,1)S(1)}, u32[]{:S(2)}, u32[]{:S(2)}) async-start(bf16[64,8,128]{2,1,0:T(8,128)(2,1)} %broadcast_select_fusion.1), calls=%async_computation.3 | async-start | bytes 262144 | tf_op jit(solution)/shard_map/all_to_all | solution.py:34
  108.5 11.4 %all-to-all-done.2 = bf16[64,8,128]{2,1,0:T(8,128)(2,1)S(1)} async-done(((bf16[64,8,128]{2,1,0:T(8,128)(2,1)}), bf16[64,8,128]{2,1,0:T(8,128)(2,1)S(1)}, u32[]{:S(2)}, u32[]{:S(2)}) %all-to-all-start.2) | async-done | bytes 131104 | tf_op jit(solution)/shard_map/all_to_all | solution.py:34
  (91 shorter events, 18.4 us)
Async XLA Ops:
  7.2 17.9 %copy-start = (bf16[1,256,2048]{2,1,0:T(8,128)(2,1)S(1)}, bf16[1,256,2048]{2,1,0:T(8,128)(2,1)}, u32[]{:S(2)}) copy-start(bf16[1,256,2048]{2,1,0:T(8,128)(2,1)} %param.13) | copy-start | bytes 3145732
  7.2 28.6 %all-gather.2.cloned.1.call-start = ((), (), s32[]{:S(2)}) async-start(), calls=%async_computation.4 | async-start | bytes 3145728 | tf_op jit(solution)/shard_map/all_gather | solution.py:51
  7.9 33.5 %all-to-all-start = ((bf16[64,32,128]{2,1,0:T(8,128)(2,1)}), bf16[64,32,128]{2,1,0:T(8,128)(2,1)S(1)}, u32[]{:S(2)}, u32[]{:S(2)}) async-start(bf16[64,32,128]{2,1,0:T(8,128)(2,1)} %bitcast.82), calls=%async_computation | async-start | bytes 1048576 | tf_op jit(solution)/shard_map/all_to_all | solution.py:30
  25.9 69.1 %collective-permute-start.1 = (bf16[256,1024]{1,0:T(8,128)(2,1)}, bf16[256,1024]{1,0:T(8,128)(2,1)}, u32[]{:S(2)}, u32[]{:S(2)}) collective-permute-start(bf16[256,1024]{1,0:T(8,128)(2,1)} %dynamic-slice_bitcast_fusion), channel_id=1, source_target_pairs={{0,4},{4,0},{1,5},{5,1},{2,6},{6,2},{3,7},{7,3},{8,12},{12,8},{9,1... | collective-permute-start | bytes 1572872 | tf_op jit(solution)/shard_map/ppermute | solution.py:150
  37.9 2.7 %copy-start.4 = (f32[512]{0:T(512)}, f32[512]{0:T(512)S(1)}, u32[]{:S(2)}) copy-start(f32[512]{0:T(512)S(1)} %add_rsqrt_fusion) | copy-start | bytes 6148
  37.9 17.0 %copy-start.5 = (s32[64]{0:T(128)S(1)}, s32[64]{0:T(128)}, u32[]{:S(2)}) copy-start(s32[64]{0:T(128)} %param.17) | copy-start | bytes 772
  37.9 19.0 %copy-start.2 = (bf16[2048,1,256]{2,0,1:T(8,128)(2,1)S(1)}, bf16[2048,1,256]{2,0,1:T(8,128)(2,1)}, u32[]{:S(2)}) copy-start(bf16[2048,1,256]{2,0,1:T(8,128)(2,1)} %param.11) | copy-start | bytes 3145732
  40.6 19.0 %copy-start.3 = (s32[64]{0:T(128)S(1)}, s32[64]{0:T(128)}, u32[]{:S(2)}) copy-start(s32[64]{0:T(128)} %param.16) | copy-start | bytes 772
  43.2 30.9 %all-to-all-start.1 = ((bf16[64,40,128]{2,1,0:T(8,128)(2,1)}), bf16[64,40,128]{2,1,0:T(8,128)(2,1)S(1)}, u32[]{:S(2)}, u32[]{:S(2)}) async-start(bf16[64,40,128]{2,1,0:T(8,128)(2,1)} %pad_maximum_fusion), calls=%async_computation.1 | async-start | bytes 1310720 | tf_op jit(solution)/shard_map/all_to_all | solution.py:30
  54.8 66.5 %reduce-scatter.2.cloned.1.call-start = ((), (), s32[]{:S(2)}) async-start(), calls=%async_computation.5 | async-start | bytes 1310720 | tf_op jit(solution)/shard_map/reduce_scatter | solution.py:161
  55.0 6.6 %copy-start.6 = (s32[64]{0:T(128)}, s32[64]{0:T(128)S(1)}, u32[]{:S(2)}) copy-start(s32[64]{0:T(128)S(1)} %select_reduce_fusion) | copy-start | bytes 772
  89.8 10.9 %copy-start.7 = (s32[64]{0:T(128)S(1)}, s32[64]{0:T(128)}, u32[]{:S(2)}) copy-start(s32[64]{0:T(128)} %copy-done.6) | copy-start | bytes 772
  89.8 10.9 %copy-start.1 = (bf16[1,1,2048,128]{3,2,1,0:T(8,128)(2,1)S(1)}, bf16[1,1,2048,128]{3,2,1,0:T(8,128)(2,1)}, u32[]{:S(2)}) copy-start(bf16[1,1,2048,128]{3,2,1,0:T(8,128)(2,1)} %param.14) | copy-start | bytes 1572868
  89.8 5.9 %collective-permute-start = (bf16[512,256]{0,1:T(8,128)(2,1)S(1)}, bf16[512,256]{0,1:T(8,128)(2,1)S(1)}, u32[]{:S(2)}, u32[]{:S(2)}) collective-permute-start(bf16[512,256]{0,1:T(8,128)(2,1)S(1)} %bitcast.87), channel_id=1, source_target_pairs={{0,4},{4,0},{1,5},{5,1},{2,6},{6,2},{3,7},{7,3},{8,12},{12,8},{9,1... | collective-permute-start | bytes 786440 | tf_op jit(solution)/shard_map/ppermute | solution.py:154
  102.2 17.7 %all-to-all-start.2 = ((bf16[64,8,128]{2,1,0:T(8,128)(2,1)}), bf16[64,8,128]{2,1,0:T(8,128)(2,1)S(1)}, u32[]{:S(2)}, u32[]{:S(2)}) async-start(bf16[64,8,128]{2,1,0:T(8,128)(2,1)} %broadcast_select_fusion.1), calls=%async_computation.3 | async-start | bytes 262144 | tf_op jit(solution)/shard_map/all_to_all | solution.py:34
Sparse Core Ops, SparseCore 0:
  10.1 25.6 all-gather.1
  98.3 21.1 reduce-scatter.1

commit v18 on v17

--- a/solution.py
+++ b/solution.py
@@ -77,7 +77,7 @@
     lanes = stored.shape[1]
     second = jnp.concatenate(
         [
-            jnp.take(spread.reshape(groups, window_chunk, lanes), slots, axis=0),
+            jnp.take(spread.reshape(groups, window_chunk, lanes), slots, axis=0, mode="clip"),
             entry.reshape(groups, entry_chunk, lanes),
         ],
         axis=1,
@@ -132,7 +132,7 @@
     outputs = lax.map(one_head, jnp.transpose(query_rotated, (1, 0, 2)))
     attended = jnp.transpose(outputs, (1, 0, 2)).reshape(rows_new, heads * HEAD_SIZE)
 
-    arrived = carry_out(jnp.take(entry_parts, inverse, axis=0).reshape(rows_new, lanes))
+    arrived = carry_out(jnp.take(entry_parts, inverse, axis=0, mode="clip").reshape(rows_new, lanes))
     own_offset = offsets[inverse[request]]
     extended = jnp.concatenate([stored, stored[:rows_new]], axis=0)
     extended = lax.dynamic_update_slice_in_dim(extended, arrived, own_offset, axis=0)

time: 129 us -> 129 us (level)
  other arithmetic: 12.1 us -> 10.5 us
    select_n x4 -> x0, other arithmetic: 1.6 us -> none  [the longest x2 0.8 us: per_device(): jnp.take(spread.reshape(groups, window_chunk, lanes), slots, axis=0)]
  transfers between devices with their start and end apart: 7 -> 7, of which waited for: 5 -> 5; matrix products, arithmetic and copies ran while one was open for 29% -> 28% of each run, Pallas kernels for 0% -> 0%
where the time goes in v18:
time: 129 us; the launch traced here: 128 us
  starting transfers between devices  42.6 us (33%)
  waiting for transfers between devices  26.7 us (21%)
  between operations  20.1 us (16%)
  matrix products  19.9 us (15%)
  other arithmetic  10.5 us (8%)
  local copies, waits for them, and re-layouts  7.95 us (6%)
    all_to_all x2, starting transfers between devices, carry_in(): return lax.all_to_all(window, 'dp', split_axis=0, concat_axis=0, tiled=True)  28.8 us
    all_to_all x1, waiting for transfers between devices, carry_out(): return lax.all_to_all(window, 'dp', split_axis=0, concat_axis=0, tiled=True)  11.4 us
    all_to_all x2, waiting for transfers between devices, carry_in(): return lax.all_to_all(window, 'dp', split_axis=0, concat_axis=0, tiled=True)  9.5 us
    all_to_all x1, starting transfers between devices, carry_out(): return lax.all_to_all(window, 'dp', split_axis=0, concat_axis=0, tiled=True)  6.2 us
    dot_general x4, matrix products, one_head(): jnp.einsum('qd,kd->qk', query_rows, window_keys, preferred_element_type=j...  5.77 us
    ppermute x1, starting transfers between devices, per_device(): other_attended = lax.ppermute(attended, 'tx', pairs)  4.73 us
    all_gather x1, waiting for transfers between devices, per_device(): whole = lax.all_gather(tokens, 'tx', axis=1, tiled=True)  4.35 us
    dot_general x4, matrix products, one_head(): jnp.dot(old_powers.astype(jnp.bfloat16), window_values, preferred_element...  3.51 us
  transfers between devices with their start and end apart: 7, of which 5 were waited for; matrix products, arithmetic and copies ran while one was open for 28% of the time, Pallas kernels for 0%

profile of v18, /device:TPU:1, one launch (start us, length us, event | category | flops | bytes accessed | tf_op | source)
XLA Modules:
  0.0 127.9 jit_solution(894349284606863015)
XLA Ops:
  7.9 17.1 %all-to-all-start = ((bf16[64,32,128]{2,1,0:T(8,128)(2,1)}), bf16[64,32,128]{2,1,0:T(8,128)(2,1)S(1)}, u32[]{:S(2)}, u32[]{:S(2)}) async-start(bf16[64,32,128]{2,1,0:T(8,128)(2,1)} %bitcast.78), calls=%async_computation | async-start | bytes 1048576 | tf_op jit(solution)/shard_map/all_to_all | solution.py:30
  25.9 2.9 %collective-permute-start.1 = (bf16[256,1024]{1,0:T(8,128)(2,1)}, bf16[256,1024]{1,0:T(8,128)(2,1)}, u32[]{:S(2)}, u32[]{:S(2)}) collective-permute-start(bf16[256,1024]{1,0:T(8,128)(2,1)} %dynamic-slice_bitcast_fusion), channel_id=1, source_target_pairs={{0,4},{4,0},{1,5},{5,1},{2,6},{6,2},{3,7},{7,3},{8,12},{12,8},{9,1... | collective-permute-start | bytes 1572872 | tf_op jit(solution)/shard_map/ppermute | solution.py:150
  28.8 1.3 %dynamic_slice.26 = s32[1]{0:T(128)} dynamic-slice(s32[64]{0:T(128)} %param.15, s32[]{:T(128)S(6)} %select_n.47), dynamic_slice_sizes={1} | dynamic-slice | bytes 12 | tf_op jit(solution)/shard_map/dynamic_slice | solution.py:60
  31.4 4.4 %all-gather.2.cloned.1.call-done = bf16[512,2048]{1,0:T(8,128)(2,1)} async-done(((bf16[512,1024]{1,0:T(8,128)(2,1)}), bf16[512,2048]{1,0:T(8,128)(2,1)}) %all-gather.2.cloned.1.call-update) | async-done | bytes 2097168 | tf_op jit(solution)/shard_map/all_gather | solution.py:51
  35.8 2.1 %fusion.24 = f32[512]{0:T(512)S(1)} fusion(bf16[512,2048]{1,0:T(8,128)(2,1)} %all-gather.2.cloned.1.call-done), kind=kLoop, calls=%fused_computation.30 | loop fusion | flops 3145216 | bytes 2099200 | tf_op jit(solution)/shard_map/reduce_sum | solution.py:56
  37.9 2.7 %fusion.28 = f32[512,128]{0,1:T(8,128)S(1)} fusion(bf16[512,2048]{1,0:T(8,128)(2,1)} %all-gather.2.cloned.1.call-done, f32[512]{0:T(512)S(1)} %add_rsqrt_fusion, bf16[2048,1,128]{2,0,1:T(8,128)(2,1)} %param.12), kind=kOutput, calls=%fused_computation.35 | convolution fusion | flops 271581184 | bytes 2885632 | tf_op jit(solution)/shard_map/dot_general | solution.py:63
  42.2 0.9 pad_maximum_fusion
  43.1 11.6 %all-to-all-start.1 = ((bf16[64,40,128]{2,1,0:T(8,128)(2,1)}), bf16[64,40,128]{2,1,0:T(8,128)(2,1)S(1)}, u32[]{:S(2)}, u32[]{:S(2)}) async-start(bf16[64,40,128]{2,1,0:T(8,128)(2,1)} %pad_maximum_fusion), calls=%async_computation.1 | async-start | bytes 1310720 | tf_op jit(solution)/shard_map/all_to_all | solution.py:30
  56.8 1.4 %copy.20 = bf16[2048,1,256]{0,2,1:T(8,128)(2,1)} copy(bf16[2048,1,256]{2,0,1:T(8,128)(2,1)S(1)} %copy-done.2) | data formatting | bytes 2097152 | tf_op args[1]
  62.1 2.7 %fusion.26 = f32[512,4,64]{0,2,1:T(8,128)S(1)} fusion(bf16[4,64,2048]{2,1,0:T(8,128)(2,1)} %bitcast.80, bf16[512,2048]{1,0:T(8,128)(2,1)} %all-gather.2.cloned.1.call-done, f32[512]{0:T(512)} %copy-done.4), kind=kOutput, calls=%fused_computation.32 | convolution fusion | flops 540016640 | bytes 3672064 | tf_op jit(solution)/shard_map/dot_general | solution.py:91
  64.9 9.1 %all-to-all-done.1 = bf16[64,40,128]{2,1,0:T(8,128)(2,1)S(1)} async-done(((bf16[64,40,128]{2,1,0:T(8,128)(2,1)}), bf16[64,40,128]{2,1,0:T(8,128)(2,1)S(1)}, u32[]{:S(2)}, u32[]{:S(2)}) %all-to-all-start.1) | async-done | bytes 655392 | tf_op jit(solution)/shard_map/all_to_all | solution.py:30
  74.2 15.4 %while.11 = (s32[]{:T(128)}, bf16[4,512,64]{1,2,0:T(8,128)(2,1)S(1)}, bf16[4,512,64]{1,2,0:T(8,128)(2,1)S(1)}, bf16[2048,64]{1,0:T(8,128)(2,1)S(1)}, bf16[512,64...) while((s32[]{:T(128)}, ...), condition=%wide.region_6.7_spmd.clone, body=%wide.region_1.6_spmd.clone.sunk | while | flops 347175936 | bytes 17279096 | solution.py:132
  74.2 1.4 %fusion.81 = (f32[512]{0:T(512)S(1)}, f32[512,2048]{1,0:T(8,128)S(1)}) fusion(bf16[2048,64]{1,0:T(8,128)(2,1)S(1)} %get-tuple-element.238, bf16[4,512,64]{1,2,0:T(8,128)(2,1)S(1)} %get-tuple-element.237, s32[]{:T(128)} %get-tuple-element.224, s32[512]{0:T(512)S(1)} %get-tuple-element.242, s32[2048]{0:T(1024)S(1)} %get-tuple-element.243, ...), kind=kOutput, calls=%fused_computation.85.clone.1 | convolution fusion | flops 139460096 | bytes 4798468 | tf_op jit(solution)/shard_map/while/body/eval_jaxpr/qd,kd->qk/dot_general | solution.py:110
  76.9 0.9 fusion.83
  78.1 1.4 %fusion.81 = (f32[512]{0:T(512)S(1)}, f32[512,2048]{1,0:T(8,128)S(1)}) fusion(bf16[2048,64]{1,0:T(8,128)(2,1)S(1)} %get-tuple-element.238, bf16[4,512,64]{1,2,0:T(8,128)(2,1)S(1)} %get-tuple-element.237, s32[]{:T(128)} %get-tuple-element.224, s32[512]{0:T(512)S(1)} %get-tuple-element.242, s32[2048]{0:T(1024)S(1)} %get-tuple-element.243, ...), kind=kOutput, calls=%fused_computation.85.clone.1 | convolution fusion | flops 139460096 | bytes 4798468 | tf_op jit(solution)/shard_map/while/body/eval_jaxpr/qd,kd->qk/dot_general | solution.py:110
  80.7 0.9 fusion.83
  81.9 1.4 %fusion.81 = (f32[512]{0:T(512)S(1)}, f32[512,2048]{1,0:T(8,128)S(1)}) fusion(bf16[2048,64]{1,0:T(8,128)(2,1)S(1)} %get-tuple-element.238, bf16[4,512,64]{1,2,0:T(8,128)(2,1)S(1)} %get-tuple-element.237, s32[]{:T(128)} %get-tuple-element.224, s32[512]{0:T(512)S(1)} %get-tuple-element.242, s32[2048]{0:T(1024)S(1)} %get-tuple-element.243, ...), kind=kOutput, calls=%fused_computation.85.clone.1 | convolution fusion | flops 139460096 | bytes 4798468 | tf_op jit(solution)/shard_map/while/body/eval_jaxpr/qd,kd->qk/dot_general | solution.py:110
  84.6 0.9 fusion.83
  85.8 1.4 %fusion.81 = (f32[512]{0:T(512)S(1)}, f32[512,2048]{1,0:T(8,128)S(1)}) fusion(bf16[2048,64]{1,0:T(8,128)(2,1)S(1)} %get-tuple-element.238, bf16[4,512,64]{1,2,0:T(8,128)(2,1)S(1)} %get-tuple-element.237, s32[]{:T(128)} %get-tuple-element.224, s32[512]{0:T(512)S(1)} %get-tuple-element.242, s32[2048]{0:T(1024)S(1)} %get-tuple-element.243, ...), kind=kOutput, calls=%fused_computation.85.clone.1 | convolution fusion | flops 139460096 | bytes 4798468 | tf_op jit(solution)/shard_map/while/body/eval_jaxpr/qd,kd->qk/dot_general | solution.py:110
  89.7 4.7 %collective-permute-start = (bf16[512,256]{0,1:T(8,128)(2,1)S(1)}, bf16[512,256]{0,1:T(8,128)(2,1)S(1)}, u32[]{:S(2)}, u32[]{:S(2)}) collective-permute-start(bf16[512,256]{0,1:T(8,128)(2,1)S(1)} %bitcast.83), channel_id=1, source_target_pairs={{0,4},{4,0},{1,5},{5,1},{2,6},{6,2},{3,7},{7,3},{8,12},{12,8},{9,1... | collective-permute-start | bytes 786440 | tf_op jit(solution)/shard_map/ppermute | solution.py:154
  95.5 2.5 %add_convert_fusion = bf16[512,1024]{1,0:T(8,128)(2,1)} fusion(f32[512,1024]{1,0:T(8,128)S(1)} %fusion.31, bf16[512,256]{0,1:T(8,128)(2,1)S(1)} %collective-permute-done, bf16[256,1024]{1,0:T(8,128)(2,1)} %collective-permute-done.1), kind=kOutput, calls=%fused_computation.34 | convolution fusion | flops 269484032 | bytes 3932160 | tf_op jit(solution)/shard_map/dot_general | solution.py:155
  100.6 1.3 gather_fusion.1
  101.9 6.2 %all-to-all-start.2 = ((bf16[64,8,128]{2,1,0:T(8,128)(2,1)}), bf16[64,8,128]{2,1,0:T(8,128)(2,1)S(1)}, u32[]{:S(2)}, u32[]{:S(2)}) async-start(bf16[64,8,128]{2,1,0:T(8,128)(2,1)} %gather_fusion.1), calls=%async_computation.3 | async-start | bytes 262144 | tf_op jit(solution)/shard_map/all_to_all | solution.py:34
  108.2 11.4 %all-to-all-done.2 = bf16[64,8,128]{2,1,0:T(8,128)(2,1)S(1)} async-done(((bf16[64,8,128]{2,1,0:T(8,128)(2,1)}), bf16[64,8,128]{2,1,0:T(8,128)(2,1)S(1)}, u32[]{:S(2)}, u32[]{:S(2)}) %all-to-all-start.2) | async-done | bytes 131104 | tf_op jit(solution)/shard_map/all_to_all | solution.py:34
  (85 shorter events, 17.1 us)
Async XLA Ops:
  7.2 17.9 %copy-start = (bf16[1,256,2048]{2,1,0:T(8,128)(2,1)S(1)}, bf16[1,256,2048]{2,1,0:T(8,128)(2,1)}, u32[]{:S(2)}) copy-start(bf16[1,256,2048]{2,1,0:T(8,128)(2,1)} %param.13) | copy-start | bytes 3145732
  7.2 28.6 %all-gather.2.cloned.1.call-start = ((), (), s32[]{:S(2)}) async-start(), calls=%async_computation.4 | async-start | bytes 3145728 | tf_op jit(solution)/shard_map/all_gather | solution.py:51
  7.9 33.5 %all-to-all-start = ((bf16[64,32,128]{2,1,0:T(8,128)(2,1)}), bf16[64,32,128]{2,1,0:T(8,128)(2,1)S(1)}, u32[]{:S(2)}, u32[]{:S(2)}) async-start(bf16[64,32,128]{2,1,0:T(8,128)(2,1)} %bitcast.78), calls=%async_computation | async-start | bytes 1048576 | tf_op jit(solution)/shard_map/all_to_all | solution.py:30
  25.9 68.9 %collective-permute-start.1 = (bf16[256,1024]{1,0:T(8,128)(2,1)}, bf16[256,1024]{1,0:T(8,128)(2,1)}, u32[]{:S(2)}, u32[]{:S(2)}) collective-permute-start(bf16[256,1024]{1,0:T(8,128)(2,1)} %dynamic-slice_bitcast_fusion), channel_id=1, source_target_pairs={{0,4},{4,0},{1,5},{5,1},{2,6},{6,2},{3,7},{7,3},{8,12},{12,8},{9,1... | collective-permute-start | bytes 1572872 | tf_op jit(solution)/shard_map/ppermute | solution.py:150
  37.9 16.9 %copy-start.5 = (s32[64]{0:T(128)S(1)}, s32[64]{0:T(128)}, u32[]{:S(2)}) copy-start(s32[64]{0:T(128)} %param.17) | copy-start | bytes 772
  37.9 18.9 %copy-start.2 = (bf16[2048,1,256]{2,0,1:T(8,128)(2,1)S(1)}, bf16[2048,1,256]{2,0,1:T(8,128)(2,1)}, u32[]{:S(2)}) copy-start(bf16[2048,1,256]{2,0,1:T(8,128)(2,1)} %param.11) | copy-start | bytes 3145732
  37.9 2.7 %copy-start.4 = (f32[512]{0:T(512)}, f32[512]{0:T(512)S(1)}, u32[]{:S(2)}) copy-start(f32[512]{0:T(512)S(1)} %add_rsqrt_fusion) | copy-start | bytes 6148
  40.6 18.9 %copy-start.3 = (s32[64]{0:T(128)S(1)}, s32[64]{0:T(128)}, u32[]{:S(2)}) copy-start(s32[64]{0:T(128)} %param.16) | copy-start | bytes 772
  43.1 30.9 %all-to-all-start.1 = ((bf16[64,40,128]{2,1,0:T(8,128)(2,1)}), bf16[64,40,128]{2,1,0:T(8,128)(2,1)S(1)}, u32[]{:S(2)}, u32[]{:S(2)}) async-start(bf16[64,40,128]{2,1,0:T(8,128)(2,1)} %pad_maximum_fusion), calls=%async_computation.1 | async-start | bytes 1310720 | tf_op jit(solution)/shard_map/all_to_all | solution.py:30
  54.7 66.4 %reduce-scatter.2.cloned.1.call-start = ((), (), s32[]{:S(2)}) async-start(), calls=%async_computation.5 | async-start | bytes 1310720 | tf_op jit(solution)/shard_map/reduce_scatter | solution.py:161
  54.9 6.6 %copy-start.6 = (s32[64]{0:T(128)}, s32[64]{0:T(128)S(1)}, u32[]{:S(2)}) copy-start(s32[64]{0:T(128)S(1)} %select_reduce_fusion) | copy-start | bytes 772
  89.6 10.9 %copy-start.7 = (s32[64]{0:T(128)S(1)}, s32[64]{0:T(128)}, u32[]{:S(2)}) copy-start(s32[64]{0:T(128)} %copy-done.6) | copy-start | bytes 772
  89.7 10.9 %copy-start.1 = (bf16[1,1,2048,128]{3,2,1,0:T(8,128)(2,1)S(1)}, bf16[1,1,2048,128]{3,2,1,0:T(8,128)(2,1)}, u32[]{:S(2)}) copy-start(bf16[1,1,2048,128]{3,2,1,0:T(8,128)(2,1)} %param.14) | copy-start | bytes 1572868
  89.7 5.9 %collective-permute-start = (bf16[512,256]{0,1:T(8,128)(2,1)S(1)}, bf16[512,256]{0,1:T(8,128)(2,1)S(1)}, u32[]{:S(2)}, u32[]{:S(2)}) collective-permute-start(bf16[512,256]{0,1:T(8,128)(2,1)S(1)} %bitcast.83), channel_id=1, source_target_pairs={{0,4},{4,0},{1,5},{5,1},{2,6},{6,2},{3,7},{7,3},{8,12},{12,8},{9,1... | collective-permute-start | bytes 786440 | tf_op jit(solution)/shard_map/ppermute | solution.py:154
  101.9 17.7 %all-to-all-start.2 = ((bf16[64,8,128]{2,1,0:T(8,128)(2,1)}), bf16[64,8,128]{2,1,0:T(8,128)(2,1)S(1)}, u32[]{:S(2)}, u32[]{:S(2)}) async-start(bf16[64,8,128]{2,1,0:T(8,128)(2,1)} %gather_fusion.1), calls=%async_computation.3 | async-start | bytes 262144 | tf_op jit(solution)/shard_map/all_to_all | solution.py:34
Sparse Core Ops, SparseCore 0:
  10.1 25.6 all-gather.1
  98.2 21.1 reduce-scatter.1

commit v19 on v18

--- a/solution.py
+++ b/solution.py
@@ -134,12 +134,13 @@
 
     arrived = carry_out(jnp.take(entry_parts, inverse, axis=0, mode="clip").reshape(rows_new, lanes))
     own_offset = offsets[inverse[request]]
-    extended = jnp.concatenate([stored, stored[:rows_new]], axis=0)
-    extended = lax.dynamic_update_slice_in_dim(extended, arrived, own_offset, axis=0)
-    wrap = own_offset + rows_new - WINDOW_LENGTH
-    head_rows = jnp.arange(rows_new, dtype=jnp.int32)[:, None]
-    head = jnp.where(head_rows < wrap, extended[WINDOW_LENGTH:], extended[:rows_new])
-    updated = jnp.concatenate([head, extended[rows_new:WINDOW_LENGTH]], axis=0)
+    padded = jnp.concatenate(
+        [arrived, jnp.zeros((stored.shape[0] - rows_new, lanes), arrived.dtype)], axis=0
+    )
+    placed = jnp.roll(padded, own_offset, axis=0)
+    slot_rows = jnp.arange(stored.shape[0], dtype=jnp.int32)[:, None]
+    fresh = jnp.mod(slot_rows - own_offset, WINDOW_LENGTH) < rows_new
+    updated = jnp.where(fresh, placed, stored)
     new_cache = updated[None, None]
     out_rows = output_weight.reshape(output_weight.shape[1], width)
     halves = lax.axis_size("tx")

time: 129 us -> 129 us (level)
  other arithmetic: 10.5 us -> 14.5 us
  waiting for transfers between devices: 26.7 us -> 24.2 us
    broadcast_in_dim x1, other arithmetic: 0.83 us -> 4.36 us  [per_device(): new_cache = updated[None, None]]
    all_to_all x1, waiting for transfers between devices: 11.4 us -> 8.96 us  [carry_out(): return lax.all_to_all(window, 'dp', split_axis=0, concat_axis=0, tiled=True)]
  transfers between devices with their start and end apart: 7 -> 7, of which waited for: 5 -> 5; matrix products, arithmetic and copies ran while one was open for 28% -> 31% of each run, Pallas kernels for 0% -> 0%
where the time goes in v19:
time: 129 us; the launch traced here: 128 us
  starting transfers between devices  42.6 us (33%)
  waiting for transfers between devices  24.2 us (19%)
  matrix products  19.9 us (15%)
  between operations  19.5 us (15%)
  other arithmetic  14.5 us (11%)
  local copies, waits for them, and re-layouts  7.52 us (6%)
    all_to_all x2, starting transfers between devices, carry_in(): return lax.all_to_all(window, 'dp', split_axis=0, concat_axis=0, tiled=True)  28.8 us
    all_to_all x2, waiting for transfers between devices, carry_in(): return lax.all_to_all(window, 'dp', split_axis=0, concat_axis=0, tiled=True)  9.5 us
    all_to_all x1, waiting for transfers between devices, carry_out(): return lax.all_to_all(window, 'dp', split_axis=0, concat_axis=0, tiled=True)  8.96 us
    all_to_all x1, starting transfers between devices, carry_out(): return lax.all_to_all(window, 'dp', split_axis=0, concat_axis=0, tiled=True)  6.2 us
    dot_general x4, matrix products, one_head(): jnp.einsum('qd,kd->qk', query_rows, window_keys, preferred_element_type=j...  5.77 us
    ppermute x1, starting transfers between devices, per_device(): other_attended = lax.ppermute(attended, 'tx', pairs)  4.73 us
    broadcast_in_dim x1, other arithmetic, per_device(): new_cache = updated[None, None]  4.36 us
    all_gather x1, waiting for transfers between devices, per_device(): whole = lax.all_gather(tokens, 'tx', axis=1, tiled=True)  4.35 us
  transfers between devices with their start and end apart: 7, of which 5 were waited for; matrix products, arithmetic and copies ran while one was open for 31% of the time, Pallas kernels for 0%

profile of v19, /device:TPU:1, one launch (start us, length us, event | category | flops | bytes accessed | tf_op | source)
XLA Modules:
  0.0 128.3 jit_solution(17805647008966616219)
XLA Ops:
  7.9 17.1 %all-to-all-start = ((bf16[64,32,128]{2,1,0:T(8,128)(2,1)}), bf16[64,32,128]{2,1,0:T(8,128)(2,1)S(1)}, u32[]{:S(2)}, u32[]{:S(2)}) async-start(bf16[64,32,128]{2,1,0:T(8,128)(2,1)} %bitcast.77), calls=%async_computation | async-start | bytes 1048576 | tf_op jit(solution)/shard_map/all_to_all | solution.py:30
  25.9 2.9 %collective-permute-start.1 = (bf16[256,1024]{1,0:T(8,128)(2,1)}, bf16[256,1024]{1,0:T(8,128)(2,1)}, u32[]{:S(2)}, u32[]{:S(2)}) collective-permute-start(bf16[256,1024]{1,0:T(8,128)(2,1)} %dynamic-slice_bitcast_fusion), channel_id=1, source_target_pairs={{0,4},{4,0},{1,5},{5,1},{2,6},{6,2},{3,7},{7,3},{8,12},{12,8},{9,1... | collective-permute-start | bytes 1572872 | tf_op jit(solution)/shard_map/ppermute | solution.py:151
  28.8 1.3 %dynamic_slice.30 = s32[1]{0:T(128)} dynamic-slice(s32[64]{0:T(128)} %param.15, s32[]{:T(128)S(6)} %select_n.67), dynamic_slice_sizes={1} | dynamic-slice | bytes 12 | tf_op jit(solution)/shard_map/dynamic_slice | solution.py:60
  31.4 4.4 %all-gather.2.cloned.1.call-done = bf16[512,2048]{1,0:T(8,128)(2,1)} async-done(((bf16[512,1024]{1,0:T(8,128)(2,1)}), bf16[512,2048]{1,0:T(8,128)(2,1)}) %all-gather.2.cloned.1.call-update) | async-done | bytes 2097168 | tf_op jit(solution)/shard_map/all_gather | solution.py:51
  35.8 2.1 %fusion.24 = f32[512]{0:T(512)S(1)} fusion(bf16[512,2048]{1,0:T(8,128)(2,1)} %all-gather.2.cloned.1.call-done), kind=kLoop, calls=%fused_computation.30 | loop fusion | flops 3145216 | bytes 2099200 | tf_op jit(solution)/shard_map/reduce_sum | solution.py:56
  37.9 2.7 %fusion.28 = f32[512,128]{0,1:T(8,128)S(1)} fusion(bf16[512,2048]{1,0:T(8,128)(2,1)} %all-gather.2.cloned.1.call-done, f32[512]{0:T(512)S(1)} %add_rsqrt_fusion, bf16[2048,1,128]{2,0,1:T(8,128)(2,1)} %param.12), kind=kOutput, calls=%fused_computation.39 | convolution fusion | flops 271581184 | bytes 2885632 | tf_op jit(solution)/shard_map/dot_general | solution.py:63
  42.2 0.9 pad_maximum_fusion
  43.1 11.6 %all-to-all-start.1 = ((bf16[64,40,128]{2,1,0:T(8,128)(2,1)}), bf16[64,40,128]{2,1,0:T(8,128)(2,1)S(1)}, u32[]{:S(2)}, u32[]{:S(2)}) async-start(bf16[64,40,128]{2,1,0:T(8,128)(2,1)} %pad_maximum_fusion), calls=%async_computation.1 | async-start | bytes 1310720 | tf_op jit(solution)/shard_map/all_to_all | solution.py:30
  56.8 1.4 %copy.20 = bf16[2048,1,256]{0,2,1:T(8,128)(2,1)} copy(bf16[2048,1,256]{2,0,1:T(8,128)(2,1)S(1)} %copy-done.2) | data formatting | bytes 2097152 | tf_op args[1]
  62.1 2.7 %fusion.26 = f32[512,4,64]{0,2,1:T(8,128)S(1)} fusion(bf16[4,64,2048]{2,1,0:T(8,128)(2,1)} %bitcast.78, bf16[512,2048]{1,0:T(8,128)(2,1)} %all-gather.2.cloned.1.call-done, f32[512]{0:T(512)} %copy-done.4), kind=kOutput, calls=%fused_computation.32 | convolution fusion | flops 540016640 | bytes 3672064 | tf_op jit(solution)/shard_map/dot_general | solution.py:91
  64.9 9.1 %all-to-all-done.1 = bf16[64,40,128]{2,1,0:T(8,128)(2,1)S(1)} async-done(((bf16[64,40,128]{2,1,0:T(8,128)(2,1)}), bf16[64,40,128]{2,1,0:T(8,128)(2,1)S(1)}, u32[]{:S(2)}, u32[]{:S(2)}) %all-to-all-start.1) | async-done | bytes 655392 | tf_op jit(solution)/shard_map/all_to_all | solution.py:30
  74.2 15.4 %while.11 = (s32[]{:T(128)}, bf16[4,512,64]{1,2,0:T(8,128)(2,1)S(1)}, bf16[4,512,64]{1,2,0:T(8,128)(2,1)S(1)}, bf16[2048,64]{1,0:T(8,128)(2,1)S(1)}, bf16[512,64...) while((s32[]{:T(128)}, ...), condition=%wide.region_6.7_spmd.clone, body=%wide.region_1.6_spmd.clone.sunk | while | flops 347175936 | bytes 17279096 | solution.py:132
  74.2 1.4 %fusion.91 = (f32[512]{0:T(512)S(1)}, f32[512,2048]{1,0:T(8,128)S(1)}) fusion(bf16[2048,64]{1,0:T(8,128)(2,1)S(1)} %get-tuple-element.238, bf16[4,512,64]{1,2,0:T(8,128)(2,1)S(1)} %get-tuple-element.237, s32[]{:T(128)} %get-tuple-element.224, s32[512]{0:T(512)S(1)} %get-tuple-element.242, s32[2048]{0:T(1024)S(1)} %get-tuple-element.243, ...), kind=kOutput, calls=%fused_computation.97.clone.1 | convolution fusion | flops 139460096 | bytes 4798468 | tf_op jit(solution)/shard_map/while/body/eval_jaxpr/qd,kd->qk/dot_general | solution.py:110
  76.9 0.9 fusion.93
  78.1 1.4 %fusion.91 = (f32[512]{0:T(512)S(1)}, f32[512,2048]{1,0:T(8,128)S(1)}) fusion(bf16[2048,64]{1,0:T(8,128)(2,1)S(1)} %get-tuple-element.238, bf16[4,512,64]{1,2,0:T(8,128)(2,1)S(1)} %get-tuple-element.237, s32[]{:T(128)} %get-tuple-element.224, s32[512]{0:T(512)S(1)} %get-tuple-element.242, s32[2048]{0:T(1024)S(1)} %get-tuple-element.243, ...), kind=kOutput, calls=%fused_computation.97.clone.1 | convolution fusion | flops 139460096 | bytes 4798468 | tf_op jit(solution)/shard_map/while/body/eval_jaxpr/qd,kd->qk/dot_general | solution.py:110
  80.7 0.9 fusion.93
  81.9 1.4 %fusion.91 = (f32[512]{0:T(512)S(1)}, f32[512,2048]{1,0:T(8,128)S(1)}) fusion(bf16[2048,64]{1,0:T(8,128)(2,1)S(1)} %get-tuple-element.238, bf16[4,512,64]{1,2,0:T(8,128)(2,1)S(1)} %get-tuple-element.237, s32[]{:T(128)} %get-tuple-element.224, s32[512]{0:T(512)S(1)} %get-tuple-element.242, s32[2048]{0:T(1024)S(1)} %get-tuple-element.243, ...), kind=kOutput, calls=%fused_computation.97.clone.1 | convolution fusion | flops 139460096 | bytes 4798468 | tf_op jit(solution)/shard_map/while/body/eval_jaxpr/qd,kd->qk/dot_general | solution.py:110
  85.8 1.4 %fusion.91 = (f32[512]{0:T(512)S(1)}, f32[512,2048]{1,0:T(8,128)S(1)}) fusion(bf16[2048,64]{1,0:T(8,128)(2,1)S(1)} %get-tuple-element.238, bf16[4,512,64]{1,2,0:T(8,128)(2,1)S(1)} %get-tuple-element.237, s32[]{:T(128)} %get-tuple-element.224, s32[512]{0:T(512)S(1)} %get-tuple-element.242, s32[2048]{0:T(1024)S(1)} %get-tuple-element.243, ...), kind=kOutput, calls=%fused_computation.97.clone.1 | convolution fusion | flops 139460096 | bytes 4798468 | tf_op jit(solution)/shard_map/while/body/eval_jaxpr/qd,kd->qk/dot_general | solution.py:110
  89.7 4.7 %collective-permute-start = (bf16[512,256]{0,1:T(8,128)(2,1)S(1)}, bf16[512,256]{0,1:T(8,128)(2,1)S(1)}, u32[]{:S(2)}, u32[]{:S(2)}) collective-permute-start(bf16[512,256]{0,1:T(8,128)(2,1)S(1)} %bitcast.81), channel_id=1, source_target_pairs={{0,4},{4,0},{1,5},{5,1},{2,6},{6,2},{3,7},{7,3},{8,12},{12,8},{9,1... | collective-permute-start | bytes 786440 | tf_op jit(solution)/shard_map/ppermute | solution.py:155
  95.5 2.5 %add_convert_fusion = bf16[512,1024]{1,0:T(8,128)(2,1)} fusion(f32[512,1024]{1,0:T(8,128)S(1)} %fusion.36, bf16[512,256]{0,1:T(8,128)(2,1)S(1)} %collective-permute-done, bf16[256,1024]{1,0:T(8,128)(2,1)} %collective-permute-done.1), kind=kOutput, calls=%fused_computation.34 | convolution fusion | flops 269484032 | bytes 3932160 | tf_op jit(solution)/shard_map/dot_general | solution.py:156
  98.1 1.3 gather_fusion.1
  99.3 6.2 %all-to-all-start.2 = ((bf16[64,8,128]{2,1,0:T(8,128)(2,1)}), bf16[64,8,128]{2,1,0:T(8,128)(2,1)S(1)}, u32[]{:S(2)}, u32[]{:S(2)}) async-start(bf16[64,8,128]{2,1,0:T(8,128)(2,1)} %gather_fusion.1), calls=%async_computation.3 | async-start | bytes 262144 | tf_op jit(solution)/shard_map/all_to_all | solution.py:34
  108.1 9.0 %all-to-all-done.2 = bf16[64,8,128]{2,1,0:T(8,128)(2,1)S(1)} async-done(((bf16[64,8,128]{2,1,0:T(8,128)(2,1)}), bf16[64,8,128]{2,1,0:T(8,128)(2,1)S(1)}, u32[]{:S(2)}, u32[]{:S(2)}) %all-to-all-start.2) | async-done | bytes 131104 | tf_op jit(solution)/shard_map/all_to_all | solution.py:34
  117.1 4.4 %fusion.35 = bf16[1,1,2048,128]{3,2,1,0:T(8,128)(2,1)} fusion(s32[]{:T(128)S(6)} %select_n.75, bf16[512,128]{1,0:T(8,128)(2,1)S(1)} %bitcast.79, bf16[1536,128]{1,0:T(8,128)(2,1)S(1)} %broadcast_in_dim.81, bf16[1,1,2048,128]{3,2,1,0:T(8,128)(2,1)S(1)} %copy-done.1, pred[2048]{0:T(1024)(128)(4,1)S(1)} %fusion.51), kind=kLoop, calls=%fused_computation.45 | loop fusion | flops 2359296 | bytes 1574916 | tf_op jit(solution)/shard_map/broadcast_in_dim | solution.py:144
  (81 shorter events, 17.1 us)
Async XLA Ops:
  7.2 17.9 %copy-start = (bf16[1,256,2048]{2,1,0:T(8,128)(2,1)S(1)}, bf16[1,256,2048]{2,1,0:T(8,128)(2,1)}, u32[]{:S(2)}) copy-start(bf16[1,256,2048]{2,1,0:T(8,128)(2,1)} %param.13) | copy-start | bytes 3145732
  7.2 28.6 %all-gather.2.cloned.1.call-start = ((), (), s32[]{:S(2)}) async-start(), calls=%async_computation.4 | async-start | bytes 3145728 | tf_op jit(solution)/shard_map/all_gather | solution.py:51
  7.9 33.5 %all-to-all-start = ((bf16[64,32,128]{2,1,0:T(8,128)(2,1)}), bf16[64,32,128]{2,1,0:T(8,128)(2,1)S(1)}, u32[]{:S(2)}, u32[]{:S(2)}) async-start(bf16[64,32,128]{2,1,0:T(8,128)(2,1)} %bitcast.77), calls=%async_computation | async-start | bytes 1048576 | tf_op jit(solution)/shard_map/all_to_all | solution.py:30
  25.9 68.9 %collective-permute-start.1 = (bf16[256,1024]{1,0:T(8,128)(2,1)}, bf16[256,1024]{1,0:T(8,128)(2,1)}, u32[]{:S(2)}, u32[]{:S(2)}) collective-permute-start(bf16[256,1024]{1,0:T(8,128)(2,1)} %dynamic-slice_bitcast_fusion), channel_id=1, source_target_pairs={{0,4},{4,0},{1,5},{5,1},{2,6},{6,2},{3,7},{7,3},{8,12},{12,8},{9,1... | collective-permute-start | bytes 1572872 | tf_op jit(solution)/shard_map/ppermute | solution.py:151
  37.9 16.9 %copy-start.5 = (s32[64]{0:T(128)S(1)}, s32[64]{0:T(128)}, u32[]{:S(2)}) copy-start(s32[64]{0:T(128)} %param.17) | copy-start | bytes 772
  37.9 18.9 %copy-start.2 = (bf16[2048,1,256]{2,0,1:T(8,128)(2,1)S(1)}, bf16[2048,1,256]{2,0,1:T(8,128)(2,1)}, u32[]{:S(2)}) copy-start(bf16[2048,1,256]{2,0,1:T(8,128)(2,1)} %param.11) | copy-start | bytes 3145732
  37.9 2.7 %copy-start.4 = (f32[512]{0:T(512)}, f32[512]{0:T(512)S(1)}, u32[]{:S(2)}) copy-start(f32[512]{0:T(512)S(1)} %add_rsqrt_fusion) | copy-start | bytes 6148
  40.6 18.9 %copy-start.3 = (s32[64]{0:T(128)S(1)}, s32[64]{0:T(128)}, u32[]{:S(2)}) copy-start(s32[64]{0:T(128)} %param.16) | copy-start | bytes 772
  43.1 30.9 %all-to-all-start.1 = ((bf16[64,40,128]{2,1,0:T(8,128)(2,1)}), bf16[64,40,128]{2,1,0:T(8,128)(2,1)S(1)}, u32[]{:S(2)}, u32[]{:S(2)}) async-start(bf16[64,40,128]{2,1,0:T(8,128)(2,1)} %pad_maximum_fusion), calls=%async_computation.1 | async-start | bytes 1310720 | tf_op jit(solution)/shard_map/all_to_all | solution.py:30
  54.7 66.8 %reduce-scatter.2.cloned.1.call-start = ((), (), s32[]{:S(2)}) async-start(), calls=%async_computation.5 | async-start | bytes 1310720 | tf_op jit(solution)/shard_map/reduce_scatter | solution.py:162
  54.9 6.6 %copy-start.6 = (s32[64]{0:T(128)}, s32[64]{0:T(128)S(1)}, u32[]{:S(2)}) copy-start(s32[64]{0:T(128)S(1)} %select_reduce_fusion) | copy-start | bytes 772
  89.6 8.4 %copy-start.7 = (s32[64]{0:T(128)S(1)}, s32[64]{0:T(128)}, u32[]{:S(2)}) copy-start(s32[64]{0:T(128)} %copy-done.6) | copy-start | bytes 772
  89.7 27.5 %copy-start.1 = (bf16[1,1,2048,128]{3,2,1,0:T(8,128)(2,1)S(1)}, bf16[1,1,2048,128]{3,2,1,0:T(8,128)(2,1)}, u32[]{:S(2)}) copy-start(bf16[1,1,2048,128]{3,2,1,0:T(8,128)(2,1)} %param.14) | copy-start | bytes 1572868
  89.7 5.9 %collective-permute-start = (bf16[512,256]{0,1:T(8,128)(2,1)S(1)}, bf16[512,256]{0,1:T(8,128)(2,1)S(1)}, u32[]{:S(2)}, u32[]{:S(2)}) collective-permute-start(bf16[512,256]{0,1:T(8,128)(2,1)S(1)} %bitcast.81), channel_id=1, source_target_pairs={{0,4},{4,0},{1,5},{5,1},{2,6},{6,2},{3,7},{7,3},{8,12},{12,8},{9,1... | collective-permute-start | bytes 786440 | tf_op jit(solution)/shard_map/ppermute | solution.py:155
  99.3 17.7 %all-to-all-start.2 = ((bf16[64,8,128]{2,1,0:T(8,128)(2,1)}), bf16[64,8,128]{2,1,0:T(8,128)(2,1)S(1)}, u32[]{:S(2)}, u32[]{:S(2)}) async-start(bf16[64,8,128]{2,1,0:T(8,128)(2,1)} %gather_fusion.1), calls=%async_computation.3 | async-start | bytes 262144 | tf_op jit(solution)/shard_map/all_to_all | solution.py:34
Sparse Core Ops, SparseCore 0:
  10.1 25.6 all-gather.1
  98.2 21.1 reduce-scatter.1
